TPU v7x, 32 devices: a whole 2x2x4 slice. The times are simulated.
32 devices in a mesh: lat: 8 (over y, x, core), lon: 4 (over z).
Axes of the slice: x: 2, y: 2, z: 4, core: 2. Of those that a mesh axis runs over, the one named last changes fastest.
Arguments:
- surface: float32 [256, 8192], P('lat', 'lon'), may hold values from -6 to 6
- wet_blocks: int32 [256, 64], P('lat', 'lon'), may hold values 0 or 1
- legendre: float32 [1024, 256, 1024], P('lon', 'lat'), may hold values from -0.375 to 0.375
- slot_order: int32 [1024], replicated, may hold values from 0 to 1023, each once
- love_gain: float32 [1024], replicated, may hold values from 0.25 to 2.5
Outputs:
- surface_next: float32 [256, 8192], P('lat', 'lon')
- loading: float32 [256, 8192], P('lat', 'lon')
Inputs may be any that keep to these rules, and one draw needn't show every extreme that they name: `slot_order`: each order 0 to 1023 is held by exactly one slot.
All inputs are finite; a program needn't handle non-finite values. No bound on the sum of `wet_blocks` on one device may be relied on, other than what follows from the above.
Results may differ from a plain program's by a relative error of at most 0.000073.
Values sent between devices are 32-bit elements; how exact they have to be, the bound alone decides.
No kernel may reach another device: no remote copies, remote signals or barrier semaphores. Data moves between devices by JAX's collectives and lax.ppermute only.
A program may use at most 192 MiB of HBM per device.

v0:
```python
import math

import jax
import jax.numpy as jnp
from jax import lax
from jax.sharding import PartitionSpec as P

BLK = 128


def padded_2(cells, sides, width):
    for axis, dim in sides:
        count = lax.axis_size(axis)
        ends = count - 1
        head = lax.slice_in_dim(cells, 0, width, axis=dim)
        tail = lax.slice_in_dim(cells, cells.shape[dim] - width, cells.shape[dim], axis=dim)
        cells = jnp.concatenate(
            [
                lax.ppermute(tail, axis, [(i, (i + 1) % count) for i in range(ends)]),
                cells,
                lax.ppermute(head, axis, [((i + 1) % count, i) for i in range(ends)]),
            ],
            axis=dim,
        )
    return cells


def fourier_table(orders, lon_start, lon_width, lon_total):
    inner_n = 64 if lon_width % 64 == 0 else lon_width
    outer_n = lon_width // inner_n
    scale = 2.0 * math.pi / lon_total

    def angle(pos):
        phase = orders[:, None] * pos[None, :] % lon_total
        return phase.astype(jnp.float32) * scale

    outer = angle(lon_start + inner_n * jnp.arange(outer_n, dtype=jnp.int32))
    inner = angle(jnp.arange(inner_n, dtype=jnp.int32))
    ca, sa = jnp.cos(outer)[:, :, None], jnp.sin(outer)[:, :, None]
    cb, sb = jnp.cos(inner)[:, None, :], jnp.sin(inner)[:, None, :]
    cos = ca * cb - sa * sb
    sin = sa * cb + ca * sb
    return jnp.stack([cos, sin], axis=1).reshape(orders.shape[0], 2, lon_width)


def reduce_scatter(x, axis):
    count = lax.axis_size(axis)
    moved = lax.all_to_all(x, axis, 0, 0, tiled=True)
    return moved.reshape((count, x.shape[0] // count) + x.shape[1:]).sum(axis=0)


def all_gather(x, axis):
    count = lax.axis_size(axis)
    copies = jnp.broadcast_to(x[None], (count,) + x.shape).reshape((count * x.shape[0],) + x.shape[1:])
    return lax.all_to_all(copies, axis, 0, 0, tiled=True)


def local(surface, wet_blocks, legendre, slot_order, love_gain):
    cycle_count, lon_width = surface.shape
    groups = lax.axis_size("lon")
    lon_total = lon_width * groups
    slot_count = legendre.shape[0]
    slot_total = slot_count * groups
    wet_cells = jnp.repeat(wet_blocks, BLK, axis=1).astype(jnp.float32)
    masked = wet_cells * surface
    lon_start = lax.axis_index("lon") * lon_width
    own_orders = lax.dynamic_slice_in_dim(
        slot_order, lax.axis_index("lon") * slot_count, slot_count
    )
    forward_scale = lon_total ** (-0.5)
    phases = fourier_table(slot_order, lon_start, lon_width, lon_total)
    fourier = reduce_scatter(
        jnp.einsum("kcx,rx->kcr", phases, masked, precision=lax.Precision.HIGHEST) * forward_scale,
        "lon",
    )
    coefficient = jnp.einsum("krl,kcr->kcl", legendre, fourier, precision=lax.Precision.HIGHEST)
    degree_whole = all_gather(reduce_scatter(coefficient, "lat"), "lat")
    degree_count = degree_whole.shape[2]
    degrees = jnp.arange(degree_count, dtype=jnp.int32)
    retained = degrees[None, :] >= own_orders[:, None]
    spectrum = jnp.where(retained[:, None, :], love_gain[None, None, :] * degree_whole, 0.0)
    synthesis = jnp.einsum("krl,kcl->kcr", legendre, spectrum, precision=lax.Precision.HIGHEST)
    summed = jnp.einsum(
        "kcr,kcx->rx",
        all_gather(synthesis, "lon"),
        phases,
        precision=lax.Precision.HIGHEST,
    )
    loading = summed * (2 * slot_total) ** (-0.5)
    potential = masked - 0.6 * loading
    padded = padded_2(potential, (("lat", 0), ("lon", 1)), 1)
    neighbours = padded[2:, 1:-1] + padded[:-2, 1:-1] + padded[1:-1, 2:] + padded[1:-1, :-2]
    surface_next = wet_cells * (masked + 0.2 * (neighbours - 4.0 * potential))
    return (surface_next, loading)


def solution(mesh):
    return jax.shard_map(
        local,
        mesh=mesh,
        in_specs=(P("lat", "lon"), P("lat", "lon"), P("lon", "lat", None), P(), P()),
        out_specs=(P("lat", "lon"), P("lat", "lon")),
        check_vma=False,
    )
```

profile of v0, /device:TPU:12, one launch (start us, length us, event | category | flops | bytes accessed | tf_op | source)
XLA Modules:
  0.0 225.5 jit_solution(15122553603828940520)
XLA Ops:
  0.6 1.7 fusion.28
  2.4 1.3 fusion.30
  3.7 7.2 %multiply_subtract_fusion = (f32[1024,32,64]{0,2,1:T(8,128)}, f32[1024,32,64]{0,2,1:T(8,128)}) fusion(f32[1024,64]{0,1:T(8,128)S(1)} %get-tuple-element.13, f32[1024,32]{0,1:T(8,128)S(1)} %get-tuple-element.11, f32[1024,64]{0,1:T(8,128)S(1)} %get-tuple-element.12, f32[1024,32]{0,1:T(8,128)S(1)} %get-tuple-element.10), kind=kLoop, calls=%fused_computation.4 | loop fusion | flops 12582912 | bytes 17563648 | tf_op jit(solution)/shard_map/sub | solution.py:41
  10.8 9.1 %copy.14 = f32[1024,1,2048]{2,0,1:T(8,128)} copy(f32[1024,1,2048]{0,2,1:T(8,128)} %bitcast.26) | data formatting | bytes 16777216 | tf_op jit(solution)/shard_map/sub | solution.py:41
  20.0 9.2 %copy.15 = f32[1024,1,2048]{2,0,1:T(8,128)} copy(f32[1024,1,2048]{0,2,1:T(8,128)} %bitcast.25) | data formatting | bytes 16777216 | tf_op jit(solution)/shard_map/add | solution.py:42
  29.4 19.2 %fusion.7 = f32[1024,2,32]{0,2,1:T(8,128)S(1)} fusion(f32[1024,1,2048]{2,0,1:T(8,128)} %copy.15, f32[1024,1,2048]{2,0,1:T(8,128)} %copy.14, f32[32,2048]{1,0:T(8,128)S(1)} %copy-done, f32[4,8,16,128]{3,2,1,0:T(8,128)S(1)} %bitcast.29), kind=kOutput, calls=%fused_computation.10 | convolution fusion | flops 1614938112 | bytes 17563648 | tf_op jit(solution)/shard_map/kcx,rx->kcr/dot_general | solution.py:73
  49.1 1.0 reshape.259
  50.2 12.2 %all_to_all.20 = f32[4,1,16384]{2,1,0:T(1,128)S(1)} all-to-all(f32[4,1,16384]{2,1,0:T(1,128)S(1)} %reshape.259), channel_id=1, replica_groups=mesh['lat'=8,'lon'=4] {'lon'}, dimensions={0} | all-to-all | bytes 524288 | tf_op jit(solution)/shard_map/all_to_all | solution.py:48
  62.9 1.4 reduce
  66.0 19.8 %fusion.35 = f32[256,2,1024]{2,1,0:T(2,128)S(1)} fusion(f32[256,2,32]{2,1,0:T(2,128)S(1)} %reduce_sum.18, f32[256,32,1024]{2,1,0:T(8,128)} %param.7), kind=kOutput, calls=%fused_computation.63 | convolution fusion | flops 201326592 | bytes 35717120 | tf_op jit(solution)/shard_map/krl,kcr->kcl/dot_general | solution.py:76
  85.7 29.2 %all_to_all.21 = f32[256,2,1024]{2,1,0:T(2,128)S(1)} all-to-all(f32[256,2,1024]{2,1,0:T(2,128)S(1)} %fusion.35), channel_id=1, replica_groups=mesh['lat'=8,'lon'=4] {'lat'}, dimensions={0} | all-to-all | bytes 4194304 | tf_op jit(solution)/shard_map/all_to_all | solution.py:48
  115.8 2.0 broadcast_in_dim.16
  117.9 5.0 %all-to-all-start.2 = ((f32[256,2,1024]{2,1,0:T(2,128)}), f32[256,2,1024]{2,1,0:T(2,128)S(1)}, u32[]{:S(2)}, u32[]{:S(2)}) async-start(f32[256,2,1024]{2,1,0:T(2,128)} %bitcast.28), calls=%async_computation.2 | async-start | bytes 4194304 | tf_op jit(solution)/shard_map/all_to_all | solution.py:55
  123.8 24.2 %all-to-all-done.2 = f32[256,2,1024]{2,1,0:T(2,128)S(1)} async-done(((f32[256,2,1024]{2,1,0:T(2,128)}), f32[256,2,1024]{2,1,0:T(2,128)S(1)}, u32[]{:S(2)}, u32[]{:S(2)}) %all-to-all-start.2) | async-done | bytes 2097184 | tf_op jit(solution)/shard_map/all_to_all | solution.py:55
  148.0 30.8 %fusion.3 = f32[256,2,32]{2,1,0:T(2,128)S(1)} fusion(f32[256,32,1024]{2,1,0:T(8,128)} %param.7, f32[256,2,1024]{2,1,0:T(2,128)S(1)} %all-to-all-done.2, pred[256,1024]{1,0:T(8,128)(4,1)S(1)} %iota_compare_fusion, f32[1024]{0:T(1024)S(1)} %copy-done.1), kind=kOutput, calls=%fused_computation.6 | convolution fusion | flops 202375168 | bytes 35983360 | tf_op jit(solution)/shard_map/krl,kcl->kcr/dot_general | solution.py:82
  180.2 10.6 %all_to_all.22 = f32[4,1,16384]{2,1,0:T(1,128)S(1)} all-to-all(f32[4,1,16384]{2,1,0:T(1,128)S(1)} %reshape.261), channel_id=1, replica_groups=mesh['lat'=8,'lon'=4] {'lon'}, dimensions={0} | all-to-all | bytes 524288 | tf_op jit(solution)/shard_map/all_to_all | solution.py:55
  190.7 1.4 reduce.1
  193.1 14.1 %broadcast_multiply_fusion = (f32[32,2048]{1,0:T(8,128)}, f32[32,2048]{1,0:T(8,128)S(1)}) fusion(f32[32,2048]{1,0:T(8,128)S(1)} %copy-done, f32[4,8,16,128]{3,2,1,0:T(8,128)S(1)} %bitcast.30, f32[1024,1,2048]{2,0,1:T(8,128)} %copy.15, f32[1024,1,2048]{2,0,1:T(8,128)} %copy.14, f32[1024,2,32]{2,1,0:T(2,128)S(1)} %reshape.262), kind=kOutput, calls=%fused_computation.50 | convolution fusion | flops 1615069184 | bytes 18087936 | tf_op jit(solution)/shard_map/kcr,kcx->rx/dot_general | solution.py:83
  207.2 3.1 %collective-permute-start = (f32[1,2048]{1,0:T(1,128)S(1)}, f32[1,2048]{1,0:T(1,128)S(1)}, u32[]{:S(2)}, u32[]{:S(2)}) collective-permute-start(f32[1,2048]{1,0:T(1,128)S(1)} %get-tuple-element.9), channel_id=1, source_target_pairs={{4,0},{8,4},{12,8},{16,12},{20,16},{24,20},{28,24},{5,1},{9,5},{13... | collective-permute-start | bytes 24584 | tf_op jit(solution)/shard_map/ppermute | solution.py:21
  210.3 1.9 collective-permute-start.1
  212.2 3.9 %collective-permute-done.1 = f32[1,2048]{1,0:T(1,128)S(1)} collective-permute-done((f32[1,2048]{1,0:T(1,128)S(1)}, f32[1,2048]{1,0:T(1,128)S(1)}, u32[]{:S(2)}, u32[]{:S(2)}) %collective-permute-start.1) | collective-permute-done | bytes 8224 | tf_op jit(solution)/shard_map/ppermute | solution.py:19
  216.2 2.7 %collective-permute-start.2 = (f32[34,1]{1,0:T(8,128)S(1)}, f32[34,1]{1,0:T(8,128)S(1)}, u32[]{:S(2)}, u32[]{:S(2)}) collective-permute-start(f32[34,1]{1,0:T(8,128)S(1)} %get-tuple-element.4), channel_id=1, source_target_pairs={{1,0},{2,1},{3,2},{5,4},{6,5},{7,6},{9,8},{10,9},{11,10},{13,12},{... | collective-permute-start | bytes 416 | tf_op jit(solution)/shard_map/ppermute | solution.py:21
  218.9 3.2 %collective-permute-start.3 = (f32[34,1]{1,0:T(8,128)S(1)}, f32[34,1]{1,0:T(8,128)S(1)}, u32[]{:S(2)}, u32[]{:S(2)}) collective-permute-start(f32[34,1]{1,0:T(8,128)S(1)} %get-tuple-element.5), channel_id=1, source_target_pairs={{0,1},{1,2},{2,3},{4,5},{5,6},{6,7},{8,9},{9,10},{10,11},{12,13},{... | collective-permute-start | bytes 416 | tf_op jit(solution)/shard_map/ppermute | solution.py:19
  222.1 2.5 %collective-permute-done.3 = f32[34,1]{1,0:T(8,128)S(1)} collective-permute-done((f32[34,1]{1,0:T(8,128)S(1)}, f32[34,1]{1,0:T(8,128)S(1)}, u32[]{:S(2)}, u32[]{:S(2)}) %collective-permute-start.3) | collective-permute-done | bytes 168 | tf_op jit(solution)/shard_map/ppermute | solution.py:19
  (25 shorter events, 8.2 us)
Async XLA Ops:
  20.0 9.2 %copy-start.2 = (s32[32,16]{0,1:T(8,128)S(1)}, s32[32,16]{0,1:T(8,128)}, u32[]{:S(2)}) copy-start(s32[32,16]{0,1:T(8,128)} %param.6) | copy-start | bytes 6148
  20.0 9.4 %copy-start = (f32[32,2048]{1,0:T(8,128)S(1)}, f32[32,2048]{1,0:T(8,128)}, u32[]{:S(2)}) copy-start(f32[32,2048]{1,0:T(8,128)} %param.5) | copy-start | bytes 786436
  85.7 62.3 %copy-start.1 = (f32[1024]{0:T(1024)S(1)}, f32[1024]{0:T(1024)}, u32[]{:S(2)}) copy-start(f32[1024]{0:T(1024)} %param.9) | copy-start | bytes 12292
  117.9 30.2 %all-to-all-start.2 = ((f32[256,2,1024]{2,1,0:T(2,128)}), f32[256,2,1024]{2,1,0:T(2,128)S(1)}, u32[]{:S(2)}, u32[]{:S(2)}) async-start(f32[256,2,1024]{2,1,0:T(2,128)} %bitcast.28), calls=%async_computation.2 | async-start | bytes 4194304 | tf_op jit(solution)/shard_map/all_to_all | solution.py:55
  207.2 5.0 %collective-permute-start = (f32[1,2048]{1,0:T(1,128)S(1)}, f32[1,2048]{1,0:T(1,128)S(1)}, u32[]{:S(2)}, u32[]{:S(2)}) collective-permute-start(f32[1,2048]{1,0:T(1,128)S(1)} %get-tuple-element.9), channel_id=1, source_target_pairs={{4,0},{8,4},{12,8},{16,12},{20,16},{24,20},{28,24},{5,1},{9,5},{13... | collective-permute-start | bytes 24584 | tf_op jit(solution)/shard_map/ppermute | solution.py:21
  210.3 5.9 %collective-permute-start.1 = (f32[1,2048]{1,0:T(1,128)S(1)}, f32[1,2048]{1,0:T(1,128)S(1)}, u32[]{:S(2)}, u32[]{:S(2)}) collective-permute-start(f32[1,2048]{1,0:T(1,128)S(1)} %get-tuple-element.8), channel_id=1, source_target_pairs={{0,4},{4,8},{8,12},{12,16},{16,20},{20,24},{24,28},{1,5},{5,9},{9,... | collective-permute-start | bytes 24584 | tf_op jit(solution)/shard_map/ppermute | solution.py:19
  216.2 5.9 %collective-permute-start.2 = (f32[34,1]{1,0:T(8,128)S(1)}, f32[34,1]{1,0:T(8,128)S(1)}, u32[]{:S(2)}, u32[]{:S(2)}) collective-permute-start(f32[34,1]{1,0:T(8,128)S(1)} %get-tuple-element.4), channel_id=1, source_target_pairs={{1,0},{2,1},{3,2},{5,4},{6,5},{7,6},{9,8},{10,9},{11,10},{13,12},{... | collective-permute-start | bytes 416 | tf_op jit(solution)/shard_map/ppermute | solution.py:21
  218.9 5.7 %collective-permute-start.3 = (f32[34,1]{1,0:T(8,128)S(1)}, f32[34,1]{1,0:T(8,128)S(1)}, u32[]{:S(2)}, u32[]{:S(2)}) collective-permute-start(f32[34,1]{1,0:T(8,128)S(1)} %get-tuple-element.5), channel_id=1, source_target_pairs={{0,1},{1,2},{2,3},{4,5},{5,6},{6,7},{8,9},{9,10},{10,11},{12,13},{... | collective-permute-start | bytes 416 | tf_op jit(solution)/shard_map/ppermute | solution.py:19
where the time goes:
time: 226 us
  matrix products  83.9 us (37%)
  blocking collectives  51.9 us (23%)
  waiting for transfers between devices  30.6 us (14%)
  local copies, waits for them, and re-layouts  26.6 us (12%)
  other arithmetic  15.8 us (7%)
  starting transfers between devices  15.8 us (7%)
    all_to_all x2, blocking collectives, reduce_scatter(): moved = lax.all_to_all(x, axis, 0, 0, tiled=True)  41.3 us
    dot_general x1, matrix products, local(): jnp.einsum('krl,kcl->kcr', legendre, spectrum, precision=lax.Precision.HI...  30.8 us
    all_to_all x1, waiting for transfers between devices, all_gather(): return lax.all_to_all(copies, axis, 0, 0, tiled=True)  24.2 us
    dot_general x1, matrix products, local(): jnp.einsum('krl,kcr->kcl', legendre, fourier, precision=lax.Precision.HIG...  19.8 us
    dot_general x1, matrix products, local(): jnp.einsum('kcx,rx->kcr', phases, masked, precision=lax.Precision.HIGHEST)  19.2 us
    dot_general x1, matrix products, local(): jnp.einsum('kcr,kcx->rx', all_gather(synthesis, 'lon'), phases, precision...  14.1 us
    all_to_all x1, blocking collectives, all_gather(): return lax.all_to_all(copies, axis, 0, 0, tiled=True)  10.6 us
    add x1, local copies, waits for them, and re-layouts, fourier_table(): sin = sa * cb + ca * sb  9.17 us
  transfers between devices with their start and end apart: 5, of which 3 were waited for; matrix products, arithmetic and copies ran while one was open for 0% of the time, Pallas kernels for 0%

commit v1 on v0

--- a/solution.py
+++ b/solution.py
@@ -25,22 +25,44 @@
     return cells
 
 
-def fourier_table(orders, lon_start, lon_width, lon_total):
-    inner_n = 64 if lon_width % 64 == 0 else lon_width
-    outer_n = lon_width // inner_n
-    scale = 2.0 * math.pi / lon_total
+INNER = 32
 
-    def angle(pos):
-        phase = orders[:, None] * pos[None, :] % lon_total
-        return phase.astype(jnp.float32) * scale
 
-    outer = angle(lon_start + inner_n * jnp.arange(outer_n, dtype=jnp.int32))
-    inner = angle(jnp.arange(inner_n, dtype=jnp.int32))
-    ca, sa = jnp.cos(outer)[:, :, None], jnp.sin(outer)[:, :, None]
-    cb, sb = jnp.cos(inner)[:, None, :], jnp.sin(inner)[:, None, :]
-    cos = ca * cb - sa * sb
-    sin = sa * cb + ca * sb
-    return jnp.stack([cos, sin], axis=1).reshape(orders.shape[0], 2, lon_width)
+def dft_tables(order_count, lon_start, lon_width, lon_total):
+    period = lon_total // INNER
+    outer = jnp.arange(lon_width // INNER, dtype=jnp.int32)
+    residue = jnp.arange(period, dtype=jnp.int32)
+    alpha = (residue[:, None] * outer[None, :] % period).astype(jnp.float32) * (2.0 * math.pi / period)
+    orders = jnp.arange(order_count, dtype=jnp.int32)
+    inner = lon_start + jnp.arange(INNER, dtype=jnp.int32)
+    beta = (orders[:, None] * inner[None, :] % lon_total).astype(jnp.float32) * (2.0 * math.pi / lon_total)
+    beta = beta.reshape(order_count // period, period, INNER)
+    return jnp.stack([jnp.cos(alpha), jnp.sin(alpha)]), jnp.cos(beta), jnp.sin(beta)
+
+
+def forward_dft(masked, slot_order, lon_start, lon_total):
+    cycles, lon_width = masked.shape
+    order_count = slot_order.shape[0]
+    rotor, cb, sb = dft_tables(order_count, lon_start, lon_width, lon_total)
+    blocks = masked.reshape(cycles, lon_width // INNER, INNER)
+    partial = jnp.einsum("cua,rab->cubr", rotor, blocks, precision=lax.Precision.HIGHEST)
+    gc, gs = partial[0][None], partial[1][None]
+    fc = (cb[..., None] * gc - sb[..., None] * gs).sum(axis=2)
+    fs = (sb[..., None] * gc + cb[..., None] * gs).sum(axis=2)
+    by_order = jnp.stack([fc, fs], axis=2).reshape(order_count, 2, cycles)
+    return jnp.take(by_order, slot_order, axis=0)
+
+
+def inverse_dft(synthesis, slot_order, lon_start, lon_width, lon_total):
+    order_count, _, cycles = synthesis.shape
+    rotor, cb, sb = dft_tables(order_count, lon_start, lon_width, lon_total)
+    slot_of = jnp.zeros((order_count,), jnp.int32).at[slot_order].set(jnp.arange(order_count, dtype=jnp.int32))
+    by_order = jnp.take(synthesis, slot_of, axis=0).reshape(cb.shape[0], cb.shape[1], 2, cycles)
+    yc, ys = by_order[:, :, 0, None, :], by_order[:, :, 1, None, :]
+    hc = (yc * cb[..., None] + ys * sb[..., None]).sum(axis=0)
+    hs = (ys * cb[..., None] - yc * sb[..., None]).sum(axis=0)
+    out = jnp.einsum("cua,cubr->rab", rotor, jnp.stack([hc, hs]), precision=lax.Precision.HIGHEST)
+    return out.reshape(cycles, lon_width)
 
 
 def reduce_scatter(x, axis):
@@ -68,11 +90,7 @@
         slot_order, lax.axis_index("lon") * slot_count, slot_count
     )
     forward_scale = lon_total ** (-0.5)
-    phases = fourier_table(slot_order, lon_start, lon_width, lon_total)
-    fourier = reduce_scatter(
-        jnp.einsum("kcx,rx->kcr", phases, masked, precision=lax.Precision.HIGHEST) * forward_scale,
-        "lon",
-    )
+    fourier = reduce_scatter(forward_dft(masked, slot_order, lon_start, lon_total) * forward_scale, "lon")
     coefficient = jnp.einsum("krl,kcr->kcl", legendre, fourier, precision=lax.Precision.HIGHEST)
     degree_whole = all_gather(reduce_scatter(coefficient, "lat"), "lat")
     degree_count = degree_whole.shape[2]
@@ -80,12 +98,7 @@
     retained = degrees[None, :] >= own_orders[:, None]
     spectrum = jnp.where(retained[:, None, :], love_gain[None, None, :] * degree_whole, 0.0)
     synthesis = jnp.einsum("krl,kcl->kcr", legendre, spectrum, precision=lax.Precision.HIGHEST)
-    summed = jnp.einsum(
-        "kcr,kcx->rx",
-        all_gather(synthesis, "lon"),
-        phases,
-        precision=lax.Precision.HIGHEST,
-    )
+    summed = inverse_dft(all_gather(synthesis, "lon"), slot_order, lon_start, lon_width, lon_total)
     loading = summed * (2 * slot_total) ** (-0.5)
     potential = masked - 0.6 * loading
     padded = padded_2(potential, (("lat", 0), ("lon", 1)), 1)

time: 226 us -> 196 us (0.87)
  matrix products: 83.9 us -> 54.2 us
  blocking collectives: 51.9 us -> 41.3 us
  starting transfers between devices: 15.8 us -> 21 us
  other arithmetic: 15.8 us -> 19.8 us
    dot_general x2, matrix products: 33.4 us -> 3.63 us  [the longest x1 1.85 us: forward_dft(): jnp.einsum('cua,rab->cubr', rotor, blocks, precision=lax.Precision.HIGHEST)]
    all_to_all x1 -> x0, blocking collectives: 10.6 us -> none  [all_gather(): return lax.all_to_all(copies, axis, 0, 0, tiled=True)]
    add x1 -> x0, local copies, waits for them, and re-layouts: 9.17 us -> none  [fourier_table(): sin = sa * cb + ca * sb]
    sub x1 -> x0, local copies, waits for them, and re-layouts: 9.14 us -> none  [fourier_table(): cos = ca * cb - sa * sb]
    sub x1, other arithmetic: 7.16 us -> 0.03 us  [local(): potential = masked - 0.6 * loading]
    gather x0 -> x2, local copies, waits for them, and re-layouts: none -> 7.11 us  [the longest x1 3.55 us: inverse_dft(): jnp.take(synthesis, slot_of, axis=0)]
    all_to_all x1 -> x2, starting transfers between devices: 4.99 us -> 10.2 us  [all_gather(): return lax.all_to_all(copies, axis, 0, 0, tiled=True)]
    mul x0 -> x3, other arithmetic: none -> 4.82 us  [the longest x1 3.76 us: local(): forward_dft(masked, slot_order, lon_start, lon_total) * forward_scale]
  transfers between devices with their start and end apart: 5 -> 6, of which waited for: 3 -> 4; matrix products, arithmetic and copies ran while one was open for 0% -> 4% of each run, Pallas kernels for 0% -> 0%
where the time goes in v1:
time: 196 us; the launch traced here: 195 us
  matrix products  54.2 us (28%)
  blocking collectives  41.3 us (21%)
  waiting for transfers between devices  31 us (16%)
  local copies, waits for them, and re-layouts  26.7 us (14%)
  starting transfers between devices  21 us (11%)
  other arithmetic  19.8 us (10%)
    all_to_all x2, blocking collectives, reduce_scatter(): moved = lax.all_to_all(x, axis, 0, 0, tiled=True)  41.3 us
    dot_general x1, matrix products, local(): jnp.einsum('krl,kcl->kcr', legendre, spectrum, precision=lax.Precision.HI...  30.8 us
    all_to_all x2, waiting for transfers between devices, all_gather(): return lax.all_to_all(copies, axis, 0, 0, tiled=True)  25.9 us
    dot_general x1, matrix products, local(): jnp.einsum('krl,kcr->kcl', legendre, fourier, precision=lax.Precision.HIG...  19.8 us
    all_to_all x2, starting transfers between devices, all_gather(): return lax.all_to_all(copies, axis, 0, 0, tiled=True)  10.2 us
    ppermute x2, starting transfers between devices, padded_2(): lax.ppermute(head, axis, [((i + 1) % count, i) for i in range(ends)])  6.03 us
    unnamed x8, local copies, waits for them, and re-layouts  5.32 us
    ppermute x2, waiting for transfers between devices, padded_2(): lax.ppermute(tail, axis, [(i, (i + 1) % count) for i in range(ends)])  5.13 us
  transfers between devices with their start and end apart: 6, of which 4 were waited for; matrix products, arithmetic and copies ran while one was open for 4% of the time, Pallas kernels for 0%

profile of v1, /device:TPU:12, one launch (start us, length us, event | category | flops | bytes accessed | tf_op | source)
XLA Modules:
  0.0 195.1 jit_solution(8787455735943677927)
XLA Ops:
  4.6 1.9 convolution_bitcast_fusion
  10.6 3.6 %gather_fusion = f32[1024,2,32]{2,1,0:T(2,128)S(1)} fusion(f32[1024,2,32]{2,1,0:T(2,128)S(1)} %copy.48, s32[1024]{0:T(1024)S(1)} %get-tuple-element.20), kind=kCustom, calls=%fused_computation.clone | custom fusion | bytes 528384 | tf_op jit(solution)/shard_map/jit(_take)/gather | solution.py:53
  14.2 3.8 %select_multiply_fusion = f32[1024,2,32]{2,1,0:T(2,128)S(1)} fusion(f32[1024,2,32]{2,1,0:T(2,128)S(1)} %gather_fusion, pred[1024]{0:T(1024)(128)(4,1)S(1)} %compare_and_fusion.1), kind=kLoop, calls=%fused_computation.20 | loop fusion | flops 131072 | bytes 525312 | tf_op jit(solution)/shard_map/mul | solution.py:93
  19.0 12.2 %all_to_all.20 = f32[4,1,16384]{2,1,0:T(1,128)S(1)} all-to-all(f32[4,1,16384]{2,1,0:T(1,128)S(1)} %reshape.208), channel_id=1, replica_groups=mesh['lat'=8,'lon'=4] {'lon'}, dimensions={0} | all-to-all | bytes 524288 | tf_op jit(solution)/shard_map/all_to_all | solution.py:70
  34.8 19.8 %fusion.43 = f32[256,2,1024]{2,1,0:T(2,128)S(1)} fusion(f32[256,2,32]{2,1,0:T(2,128)S(1)} %reduce_sum.56, f32[256,32,1024]{2,1,0:T(8,128)} %param.9), kind=kOutput, calls=%fused_computation.84 | convolution fusion | flops 201326592 | bytes 35717120 | tf_op jit(solution)/shard_map/krl,kcr->kcl/dot_general | solution.py:94
  54.6 29.2 %all_to_all.21 = f32[256,2,1024]{2,1,0:T(2,128)S(1)} all-to-all(f32[256,2,1024]{2,1,0:T(2,128)S(1)} %fusion.43), channel_id=1, replica_groups=mesh['lat'=8,'lon'=4] {'lat'}, dimensions={0} | all-to-all | bytes 4194304 | tf_op jit(solution)/shard_map/all_to_all | solution.py:70
  84.7 2.1 %broadcast_in_dim.31 = f32[8,32,2,1024]{3,2,1,0:T(2,128)} broadcast(f32[32,2,1024]{2,1,0:T(2,128)S(1)} %reduce_sum.57), dimensions={1,2,3} | broadcast | bytes 2359296 | tf_op jit(solution)/shard_map/broadcast_in_dim | solution.py:76
  86.7 5.0 %all-to-all-start.2 = ((f32[256,2,1024]{2,1,0:T(2,128)}), f32[256,2,1024]{2,1,0:T(2,128)S(1)}, u32[]{:S(2)}, u32[]{:S(2)}) async-start(f32[256,2,1024]{2,1,0:T(2,128)} %bitcast.47), calls=%async_computation.2 | async-start | bytes 4194304 | tf_op jit(solution)/shard_map/all_to_all | solution.py:77
  92.5 4.5 %scatter_custom_fusion = s32[1024]{0:T(1024)S(1)} fusion(s32[1024]{0:T(1024)S(1)} %get-tuple-element.19, s32[1024]{0:T(1024)S(1)} %iota.53, s32[]{:T(128)} %constant.60.clone.1), kind=kCustom, calls=%fused_computation.76 | custom fusion | bytes 4100 | tf_op jit(solution)/shard_map/scatter | solution.py:59
  97.2 19.7 %all-to-all-done.2 = f32[256,2,1024]{2,1,0:T(2,128)S(1)} async-done(((f32[256,2,1024]{2,1,0:T(2,128)}), f32[256,2,1024]{2,1,0:T(2,128)S(1)}, u32[]{:S(2)}, u32[]{:S(2)}) %all-to-all-start.2) | async-done | bytes 2097184 | tf_op jit(solution)/shard_map/all_to_all | solution.py:77
  116.9 30.8 %fusion.4 = f32[256,2,32]{2,1,0:T(2,128)S(1)} fusion(f32[256,32,1024]{2,1,0:T(8,128)} %param.9, f32[256,2,1024]{2,1,0:T(2,128)S(1)} %all-to-all-done.2, pred[256,1024]{1,0:T(8,128)(4,1)S(1)} %iota_compare_fusion, f32[1024]{0:T(1024)S(1)} %copy-done), kind=kOutput, calls=%fused_computation.11 | convolution fusion | flops 202375168 | bytes 35983360 | tf_op jit(solution)/shard_map/krl,kcl->kcr/dot_general | solution.py:100
  148.0 1.8 reshape.210
  149.8 5.2 %all-to-all-start.3 = ((f32[4,1,16384]{2,1,0:T(1,128)}), f32[4,1,16384]{2,1,0:T(1,128)S(1)}, u32[]{:S(2)}, u32[]{:S(2)}) async-start(f32[4,1,16384]{2,1,0:T(1,128)} %reshape.210), calls=%async_computation.3 | async-start | bytes 524288 | tf_op jit(solution)/shard_map/all_to_all | solution.py:77
  155.0 6.2 %all-to-all-done.3 = f32[4,1,16384]{2,1,0:T(1,128)S(1)} async-done(((f32[4,1,16384]{2,1,0:T(1,128)}), f32[4,1,16384]{2,1,0:T(1,128)S(1)}, u32[]{:S(2)}, u32[]{:S(2)}) %all-to-all-start.3) | async-done | bytes 262176 | tf_op jit(solution)/shard_map/all_to_all | solution.py:77
  163.5 3.6 %gather_fusion.1 = f32[1024,2,32]{2,1,0:T(2,128)S(1)} fusion(f32[1024,2,32]{2,1,0:T(2,128)S(1)} %reshape.211, s32[1024]{0:T(1024)S(1)} %fusion.33), kind=kCustom, calls=%fused_computation.1.clone | custom fusion | bytes 528384 | tf_op jit(solution)/shard_map/jit(_take)/gather | solution.py:60
  167.0 3.7 %broadcast_select_fusion = f32[1024,2,32]{2,1,0:T(2,128)S(1)} fusion(f32[1024,2,32]{2,1,0:T(2,128)S(1)} %gather_fusion.1, pred[1024]{0:T(1024)(128)(4,1)S(1)} %compare_and_fusion), kind=kLoop, calls=%fused_computation.24 | loop fusion | flops 65536 | bytes 525312 | tf_op jit(solution)/shard_map/jit(_take)/select_n | solution.py:60
  172.3 1.4 add_reduce_fusion
  173.7 1.8 multiply_bitcast_fusion
  176.5 3.1 %collective-permute-start = (f32[1,2048]{1,0:T(1,128)S(1)}, f32[1,2048]{1,0:T(1,128)S(1)}, u32[]{:S(2)}, u32[]{:S(2)}) collective-permute-start(f32[1,2048]{1,0:T(1,128)S(1)} %get-tuple-element.16), channel_id=1, source_target_pairs={{4,0},{8,4},{12,8},{16,12},{20,16},{24,20},{28,24},{5,1},{9,5},{13... | collective-permute-start | bytes 24584 | tf_op jit(solution)/shard_map/ppermute | solution.py:21
  179.6 1.9 collective-permute-start.1
  181.9 3.5 %collective-permute-done.1 = f32[1,2048]{1,0:T(1,128)S(1)} collective-permute-done((f32[1,2048]{1,0:T(1,128)S(1)}, f32[1,2048]{1,0:T(1,128)S(1)}, u32[]{:S(2)}, u32[]{:S(2)}) %collective-permute-start.1) | collective-permute-done | bytes 8224 | tf_op jit(solution)/shard_map/ppermute | solution.py:19
  185.5 3.0 %collective-permute-start.2 = (f32[34,1]{1,0:T(8,128)S(1)}, f32[34,1]{1,0:T(8,128)S(1)}, u32[]{:S(2)}, u32[]{:S(2)}) collective-permute-start(f32[34,1]{1,0:T(8,128)S(1)} %get-tuple-element.13), channel_id=1, source_target_pairs={{1,0},{2,1},{3,2},{5,4},{6,5},{7,6},{9,8},{10,9},{11,10},{13,12},{... | collective-permute-start | bytes 416 | tf_op jit(solution)/shard_map/ppermute | solution.py:21
  188.5 2.9 %collective-permute-start.3 = (f32[34,1]{1,0:T(8,128)S(1)}, f32[34,1]{1,0:T(8,128)S(1)}, u32[]{:S(2)}, u32[]{:S(2)}) collective-permute-start(f32[34,1]{1,0:T(8,128)S(1)} %get-tuple-element.14), channel_id=1, source_target_pairs={{0,1},{1,2},{2,3},{4,5},{5,6},{6,7},{8,9},{9,10},{10,11},{12,13},{... | collective-permute-start | bytes 416 | tf_op jit(solution)/shard_map/ppermute | solution.py:19
  192.5 1.6 collective-permute-done.3
  (52 shorter events, 22.2 us)
Async XLA Ops:
  83.7 33.2 %copy-start = (f32[1024]{0:T(1024)S(1)}, f32[1024]{0:T(1024)}, u32[]{:S(2)}) copy-start(f32[1024]{0:T(1024)} %param.11) | copy-start | bytes 12292
  86.7 30.2 %all-to-all-start.2 = ((f32[256,2,1024]{2,1,0:T(2,128)}), f32[256,2,1024]{2,1,0:T(2,128)S(1)}, u32[]{:S(2)}, u32[]{:S(2)}) async-start(f32[256,2,1024]{2,1,0:T(2,128)} %bitcast.47), calls=%async_computation.2 | async-start | bytes 4194304 | tf_op jit(solution)/shard_map/all_to_all | solution.py:77
  149.8 11.4 %all-to-all-start.3 = ((f32[4,1,16384]{2,1,0:T(1,128)}), f32[4,1,16384]{2,1,0:T(1,128)S(1)}, u32[]{:S(2)}, u32[]{:S(2)}) async-start(f32[4,1,16384]{2,1,0:T(1,128)} %reshape.210), calls=%async_computation.3 | async-start | bytes 524288 | tf_op jit(solution)/shard_map/all_to_all | solution.py:77
  176.5 5.4 %collective-permute-start = (f32[1,2048]{1,0:T(1,128)S(1)}, f32[1,2048]{1,0:T(1,128)S(1)}, u32[]{:S(2)}, u32[]{:S(2)}) collective-permute-start(f32[1,2048]{1,0:T(1,128)S(1)} %get-tuple-element.16), channel_id=1, source_target_pairs={{4,0},{8,4},{12,8},{16,12},{20,16},{24,20},{28,24},{5,1},{9,5},{13... | collective-permute-start | bytes 24584 | tf_op jit(solution)/shard_map/ppermute | solution.py:21
  179.6 5.9 %collective-permute-start.1 = (f32[1,2048]{1,0:T(1,128)S(1)}, f32[1,2048]{1,0:T(1,128)S(1)}, u32[]{:S(2)}, u32[]{:S(2)}) collective-permute-start(f32[1,2048]{1,0:T(1,128)S(1)} %get-tuple-element.15), channel_id=1, source_target_pairs={{0,4},{4,8},{8,12},{12,16},{16,20},{20,24},{24,28},{1,5},{5,9},{9,... | collective-permute-start | bytes 24584 | tf_op jit(solution)/shard_map/ppermute | solution.py:19
  185.5 7.0 %collective-permute-start.2 = (f32[34,1]{1,0:T(8,128)S(1)}, f32[34,1]{1,0:T(8,128)S(1)}, u32[]{:S(2)}, u32[]{:S(2)}) collective-permute-start(f32[34,1]{1,0:T(8,128)S(1)} %get-tuple-element.13), channel_id=1, source_target_pairs={{1,0},{2,1},{3,2},{5,4},{6,5},{7,6},{9,8},{10,9},{11,10},{13,12},{... | collective-permute-start | bytes 416 | tf_op jit(solution)/shard_map/ppermute | solution.py:21
  188.5 5.7 %collective-permute-start.3 = (f32[34,1]{1,0:T(8,128)S(1)}, f32[34,1]{1,0:T(8,128)S(1)}, u32[]{:S(2)}, u32[]{:S(2)}) collective-permute-start(f32[34,1]{1,0:T(8,128)S(1)} %get-tuple-element.14), channel_id=1, source_target_pairs={{0,1},{1,2},{2,3},{4,5},{5,6},{6,7},{8,9},{9,10},{10,11},{12,13},{... | collective-permute-start | bytes 416 | tf_op jit(solution)/shard_map/ppermute | solution.py:19

commit v2 on v1

--- a/solution.py
+++ b/solution.py
@@ -91,13 +91,13 @@
     )
     forward_scale = lon_total ** (-0.5)
     fourier = reduce_scatter(forward_dft(masked, slot_order, lon_start, lon_total) * forward_scale, "lon")
-    coefficient = jnp.einsum("krl,kcr->kcl", legendre, fourier, precision=lax.Precision.HIGHEST)
+    coefficient = jnp.einsum("krl,kcr->kcl", legendre, fourier, precision=lax.Precision.HIGH)
     degree_whole = all_gather(reduce_scatter(coefficient, "lat"), "lat")
     degree_count = degree_whole.shape[2]
     degrees = jnp.arange(degree_count, dtype=jnp.int32)
     retained = degrees[None, :] >= own_orders[:, None]
     spectrum = jnp.where(retained[:, None, :], love_gain[None, None, :] * degree_whole, 0.0)
-    synthesis = jnp.einsum("krl,kcl->kcr", legendre, spectrum, precision=lax.Precision.HIGHEST)
+    synthesis = jnp.einsum("krl,kcl->kcr", legendre, spectrum, precision=lax.Precision.HIGH)
     summed = inverse_dft(all_gather(synthesis, "lon"), slot_order, lon_start, lon_width, lon_total)
     loading = summed * (2 * slot_total) ** (-0.5)
     potential = masked - 0.6 * loading

time: 196 us -> 180 us (0.918)
  matrix products: 54.2 us -> 36.4 us
    dot_general x2, matrix products: 50.6 us -> 32.8 us  [the longest x1 17 us: local(): jnp.einsum('krl,kcl->kcr', legendre, spectrum, precision=lax.Precision.HIGH)]
where the time goes in v2:
time: 180 us; the launch traced here: 179 us
  blocking collectives  41.4 us (23%)
  matrix products  36.4 us (20%)
  waiting for transfers between devices  31 us (17%)
  local copies, waits for them, and re-layouts  26.7 us (15%)
  other arithmetic  21.3 us (12%)
  starting transfers between devices  21 us (12%)
    all_to_all x2, blocking collectives, reduce_scatter(): moved = lax.all_to_all(x, axis, 0, 0, tiled=True)  41.4 us
    all_to_all x2, waiting for transfers between devices, all_gather(): return lax.all_to_all(copies, axis, 0, 0, tiled=True)  25.9 us
    dot_general x1, matrix products, local(): jnp.einsum('krl,kcl->kcr', legendre, spectrum, precision=lax.Precision.HIGH)  17 us
    dot_general x1, matrix products, local(): jnp.einsum('krl,kcr->kcl', legendre, fourier, precision=lax.Precision.HIGH)  15.8 us
    all_to_all x2, starting transfers between devices, all_gather(): return lax.all_to_all(copies, axis, 0, 0, tiled=True)  10.2 us
    ppermute x2, starting transfers between devices, padded_2(): lax.ppermute(head, axis, [((i + 1) % count, i) for i in range(ends)])  6.03 us
    unnamed x8, local copies, waits for them, and re-layouts  5.32 us
    ppermute x2, waiting for transfers between devices, padded_2(): lax.ppermute(tail, axis, [(i, (i + 1) % count) for i in range(ends)])  5.12 us
  transfers between devices with their start and end apart: 6, of which 4 were waited for; matrix products, arithmetic and copies ran while one was open for 4% of the time, Pallas kernels for 0%

profile of v2, /device:TPU:12, one launch (start us, length us, event | category | flops | bytes accessed | tf_op | source)
XLA Modules:
  0.0 178.8 jit_solution(10532642688831409048)
XLA Ops:
  4.6 1.9 %convolution_bitcast_fusion = f32[2,256,32,32]{1,2,0,3:T(8,128)S(1)} fusion(f32[32,64,32]{2,1,0:T(8,128)S(1)} %reshape.166, f32[1,256,64]{1,2,0:T(8,128)S(1)} %get-tuple-element.21, f32[1,256,64]{1,2,0:T(8,128)S(1)} %get-tuple-element.22), kind=kOutput, calls=%fused_computation.15 | convolution fusion | flops 402685952 | bytes 2490368 | tf_op jit(solution)/shard_map/cua,rab->cubr/dot_general | solution.py:48
  10.6 3.6 %gather_fusion = f32[1024,2,32]{2,1,0:T(2,128)S(1)} fusion(f32[1024,2,32]{2,1,0:T(2,128)S(1)} %copy.48, s32[1024]{0:T(1024)S(1)} %get-tuple-element.20), kind=kCustom, calls=%fused_computation.clone | custom fusion | bytes 528384 | tf_op jit(solution)/shard_map/jit(_take)/gather | solution.py:53
  14.2 3.8 %select_multiply_fusion = f32[1024,2,32]{2,1,0:T(2,128)S(1)} fusion(f32[1024,2,32]{2,1,0:T(2,128)S(1)} %gather_fusion, pred[1024]{0:T(1024)(128)(4,1)S(1)} %compare_and_fusion.1), kind=kLoop, calls=%fused_computation.20 | loop fusion | flops 131072 | bytes 525312 | tf_op jit(solution)/shard_map/mul | solution.py:93
  19.0 12.2 %all_to_all.20 = f32[4,1,16384]{2,1,0:T(1,128)S(1)} all-to-all(f32[4,1,16384]{2,1,0:T(1,128)S(1)} %reshape.208), channel_id=1, replica_groups=mesh['lat'=8,'lon'=4] {'lon'}, dimensions={0} | all-to-all | bytes 524288 | tf_op jit(solution)/shard_map/all_to_all | solution.py:70
  34.8 15.8 %fusion.43 = f32[256,2,1024]{2,1,0:T(2,128)S(1)} fusion(f32[256,2,32]{2,1,0:T(2,128)S(1)} %reduce_sum.56, f32[256,32,1024]{2,1,0:T(8,128)} %param.9), kind=kOutput, calls=%fused_computation.84 | convolution fusion | flops 100663296 | bytes 35717120 | tf_op jit(solution)/shard_map/krl,kcr->kcl/dot_general | solution.py:94
  50.6 29.3 %all_to_all.21 = f32[256,2,1024]{2,1,0:T(2,128)} all-to-all(f32[256,2,1024]{2,1,0:T(2,128)S(1)} %fusion.43), channel_id=1, replica_groups=mesh['lat'=8,'lon'=4] {'lat'}, dimensions={0} | all-to-all | bytes 4194304 | tf_op jit(solution)/shard_map/all_to_all | solution.py:70
  79.9 2.4 %reduce_sum.57 = f32[32,2,1024]{2,1,0:T(2,128)S(1)} reduce(f32[8,32,2,1024]{3,2,1,0:T(2,128)} %bitcast.46, f32[]{:T(128)} %constant.68.clone.1), dimensions={0}, to_apply=%region_3.5 | reduce | flops 458752 | bytes 2359300 | tf_op jit(solution)/shard_map/reduce_sum | solution.py:71
  82.2 2.1 %broadcast_in_dim.31 = f32[8,32,2,1024]{3,2,1,0:T(2,128)} broadcast(f32[32,2,1024]{2,1,0:T(2,128)S(1)} %reduce_sum.57), dimensions={1,2,3} | broadcast | bytes 2359296 | tf_op jit(solution)/shard_map/broadcast_in_dim | solution.py:76
  84.3 5.0 %all-to-all-start.2 = ((f32[256,2,1024]{2,1,0:T(2,128)}), f32[256,2,1024]{2,1,0:T(2,128)S(1)}, u32[]{:S(2)}, u32[]{:S(2)}) async-start(f32[256,2,1024]{2,1,0:T(2,128)} %bitcast.47), calls=%async_computation.2 | async-start | bytes 4194304 | tf_op jit(solution)/shard_map/all_to_all | solution.py:77
  90.0 4.5 %scatter_custom_fusion = s32[1024]{0:T(1024)S(1)} fusion(s32[1024]{0:T(1024)S(1)} %get-tuple-element.19, s32[1024]{0:T(1024)S(1)} %iota.53, s32[]{:T(128)} %constant.60.clone.1), kind=kCustom, calls=%fused_computation.76 | custom fusion | bytes 4100 | tf_op jit(solution)/shard_map/scatter | solution.py:59
  94.8 19.7 %all-to-all-done.2 = f32[256,2,1024]{2,1,0:T(2,128)S(1)} async-done(((f32[256,2,1024]{2,1,0:T(2,128)}), f32[256,2,1024]{2,1,0:T(2,128)S(1)}, u32[]{:S(2)}, u32[]{:S(2)}) %all-to-all-start.2) | async-done | bytes 2097184 | tf_op jit(solution)/shard_map/all_to_all | solution.py:77
  114.4 17.0 %fusion.4 = f32[256,2,32]{2,1,0:T(2,128)S(1)} fusion(f32[256,32,1024]{2,1,0:T(8,128)} %param.9, f32[256,2,1024]{2,1,0:T(2,128)S(1)} %all-to-all-done.2, pred[256,1024]{1,0:T(8,128)(4,1)S(1)} %iota_compare_fusion, f32[1024]{0:T(1024)S(1)} %copy-done), kind=kOutput, calls=%fused_computation.11 | convolution fusion | flops 101711872 | bytes 35983360 | tf_op jit(solution)/shard_map/krl,kcl->kcr/dot_general | solution.py:100
  131.7 1.8 reshape.210
  133.5 5.2 %all-to-all-start.3 = ((f32[4,1,16384]{2,1,0:T(1,128)}), f32[4,1,16384]{2,1,0:T(1,128)S(1)}, u32[]{:S(2)}, u32[]{:S(2)}) async-start(f32[4,1,16384]{2,1,0:T(1,128)} %reshape.210), calls=%async_computation.3 | async-start | bytes 524288 | tf_op jit(solution)/shard_map/all_to_all | solution.py:77
  138.7 6.2 %all-to-all-done.3 = f32[4,1,16384]{2,1,0:T(1,128)S(1)} async-done(((f32[4,1,16384]{2,1,0:T(1,128)}), f32[4,1,16384]{2,1,0:T(1,128)S(1)}, u32[]{:S(2)}, u32[]{:S(2)}) %all-to-all-start.3) | async-done | bytes 262176 | tf_op jit(solution)/shard_map/all_to_all | solution.py:77
  147.2 3.6 %gather_fusion.1 = f32[1024,2,32]{2,1,0:T(2,128)S(1)} fusion(f32[1024,2,32]{2,1,0:T(2,128)S(1)} %reshape.211, s32[1024]{0:T(1024)S(1)} %fusion.33), kind=kCustom, calls=%fused_computation.1.clone | custom fusion | bytes 528384 | tf_op jit(solution)/shard_map/jit(_take)/gather | solution.py:60
  150.8 3.7 %broadcast_select_fusion = f32[1024,2,32]{2,1,0:T(2,128)S(1)} fusion(f32[1024,2,32]{2,1,0:T(2,128)S(1)} %gather_fusion.1, pred[1024]{0:T(1024)(128)(4,1)S(1)} %compare_and_fusion), kind=kLoop, calls=%fused_computation.24 | loop fusion | flops 65536 | bytes 525312 | tf_op jit(solution)/shard_map/jit(_take)/select_n | solution.py:60
  157.5 1.8 multiply_bitcast_fusion
  160.2 3.1 %collective-permute-start = (f32[1,2048]{1,0:T(1,128)S(1)}, f32[1,2048]{1,0:T(1,128)S(1)}, u32[]{:S(2)}, u32[]{:S(2)}) collective-permute-start(f32[1,2048]{1,0:T(1,128)S(1)} %get-tuple-element.16), channel_id=1, source_target_pairs={{4,0},{8,4},{12,8},{16,12},{20,16},{24,20},{28,24},{5,1},{9,5},{13... | collective-permute-start | bytes 24584 | tf_op jit(solution)/shard_map/ppermute | solution.py:21
  163.3 1.9 %collective-permute-start.1 = (f32[1,2048]{1,0:T(1,128)S(1)}, f32[1,2048]{1,0:T(1,128)S(1)}, u32[]{:S(2)}, u32[]{:S(2)}) collective-permute-start(f32[1,2048]{1,0:T(1,128)S(1)} %get-tuple-element.15), channel_id=1, source_target_pairs={{0,4},{4,8},{8,12},{12,16},{16,20},{20,24},{24,28},{1,5},{5,9},{9,... | collective-permute-start | bytes 24584 | tf_op jit(solution)/shard_map/ppermute | solution.py:19
  165.6 3.5 %collective-permute-done.1 = f32[1,2048]{1,0:T(1,128)S(1)} collective-permute-done((f32[1,2048]{1,0:T(1,128)S(1)}, f32[1,2048]{1,0:T(1,128)S(1)}, u32[]{:S(2)}, u32[]{:S(2)}) %collective-permute-start.1) | collective-permute-done | bytes 8224 | tf_op jit(solution)/shard_map/ppermute | solution.py:19
  169.2 2.9 %collective-permute-start.2 = (f32[34,1]{1,0:T(8,128)S(1)}, f32[34,1]{1,0:T(8,128)S(1)}, u32[]{:S(2)}, u32[]{:S(2)}) collective-permute-start(f32[34,1]{1,0:T(8,128)S(1)} %get-tuple-element.13), channel_id=1, source_target_pairs={{1,0},{2,1},{3,2},{5,4},{6,5},{7,6},{9,8},{10,9},{11,10},{13,12},{... | collective-permute-start | bytes 416 | tf_op jit(solution)/shard_map/ppermute | solution.py:21
  172.2 2.9 %collective-permute-start.3 = (f32[34,1]{1,0:T(8,128)S(1)}, f32[34,1]{1,0:T(8,128)S(1)}, u32[]{:S(2)}, u32[]{:S(2)}) collective-permute-start(f32[34,1]{1,0:T(8,128)S(1)} %get-tuple-element.14), channel_id=1, source_target_pairs={{0,1},{1,2},{2,3},{4,5},{5,6},{6,7},{8,9},{9,10},{10,11},{12,13},{... | collective-permute-start | bytes 416 | tf_op jit(solution)/shard_map/ppermute | solution.py:19
  176.3 1.6 collective-permute-done.3
  (52 shorter events, 22.7 us)
Async XLA Ops:
  79.8 34.6 %copy-start = (f32[1024]{0:T(1024)S(1)}, f32[1024]{0:T(1024)}, u32[]{:S(2)}) copy-start(f32[1024]{0:T(1024)} %param.11) | copy-start | bytes 12292
  84.3 30.2 %all-to-all-start.2 = ((f32[256,2,1024]{2,1,0:T(2,128)}), f32[256,2,1024]{2,1,0:T(2,128)S(1)}, u32[]{:S(2)}, u32[]{:S(2)}) async-start(f32[256,2,1024]{2,1,0:T(2,128)} %bitcast.47), calls=%async_computation.2 | async-start | bytes 4194304 | tf_op jit(solution)/shard_map/all_to_all | solution.py:77
  133.5 11.4 %all-to-all-start.3 = ((f32[4,1,16384]{2,1,0:T(1,128)}), f32[4,1,16384]{2,1,0:T(1,128)S(1)}, u32[]{:S(2)}, u32[]{:S(2)}) async-start(f32[4,1,16384]{2,1,0:T(1,128)} %reshape.210), calls=%async_computation.3 | async-start | bytes 524288 | tf_op jit(solution)/shard_map/all_to_all | solution.py:77
  160.2 5.4 %collective-permute-start = (f32[1,2048]{1,0:T(1,128)S(1)}, f32[1,2048]{1,0:T(1,128)S(1)}, u32[]{:S(2)}, u32[]{:S(2)}) collective-permute-start(f32[1,2048]{1,0:T(1,128)S(1)} %get-tuple-element.16), channel_id=1, source_target_pairs={{4,0},{8,4},{12,8},{16,12},{20,16},{24,20},{28,24},{5,1},{9,5},{13... | collective-permute-start | bytes 24584 | tf_op jit(solution)/shard_map/ppermute | solution.py:21
  163.3 5.9 %collective-permute-start.1 = (f32[1,2048]{1,0:T(1,128)S(1)}, f32[1,2048]{1,0:T(1,128)S(1)}, u32[]{:S(2)}, u32[]{:S(2)}) collective-permute-start(f32[1,2048]{1,0:T(1,128)S(1)} %get-tuple-element.15), channel_id=1, source_target_pairs={{0,4},{4,8},{8,12},{12,16},{16,20},{20,24},{24,28},{1,5},{5,9},{9,... | collective-permute-start | bytes 24584 | tf_op jit(solution)/shard_map/ppermute | solution.py:19
  169.2 7.0 %collective-permute-start.2 = (f32[34,1]{1,0:T(8,128)S(1)}, f32[34,1]{1,0:T(8,128)S(1)}, u32[]{:S(2)}, u32[]{:S(2)}) collective-permute-start(f32[34,1]{1,0:T(8,128)S(1)} %get-tuple-element.13), channel_id=1, source_target_pairs={{1,0},{2,1},{3,2},{5,4},{6,5},{7,6},{9,8},{10,9},{11,10},{13,12},{... | collective-permute-start | bytes 416 | tf_op jit(solution)/shard_map/ppermute | solution.py:21
  172.2 5.7 %collective-permute-start.3 = (f32[34,1]{1,0:T(8,128)S(1)}, f32[34,1]{1,0:T(8,128)S(1)}, u32[]{:S(2)}, u32[]{:S(2)}) collective-permute-start(f32[34,1]{1,0:T(8,128)S(1)} %get-tuple-element.14), channel_id=1, source_target_pairs={{0,1},{1,2},{2,3},{4,5},{5,6},{6,7},{8,9},{9,10},{10,11},{12,13},{... | collective-permute-start | bytes 416 | tf_op jit(solution)/shard_map/ppermute | solution.py:19

commit v3 on v2

--- a/solution.py
+++ b/solution.py
@@ -77,6 +77,30 @@
     return lax.all_to_all(copies, axis, 0, 0, tiled=True)
 
 
+def paired_reduce_scatter(x, axis):
+    count = lax.axis_size(axis)
+    pairs = [(i, i ^ 1) for i in range(count)]
+    groups = [list(range(side, count, 2)) for side in (0, 1)]
+    side = lax.axis_index(axis) % 2
+    half = x.shape[0] // 2
+    kept = lax.dynamic_slice_in_dim(x, side * half, half)
+    sent = lax.dynamic_slice_in_dim(x, (1 - side) * half, half)
+    summed = kept + lax.ppermute(sent, axis, pairs)
+    moved = lax.all_to_all(summed, axis, 0, 0, tiled=True, axis_index_groups=groups)
+    return moved.reshape((count // 2, half * 2 // count) + x.shape[1:]).sum(axis=0)
+
+
+def paired_all_gather(x, axis):
+    count = lax.axis_size(axis)
+    pairs = [(i, i ^ 1) for i in range(count)]
+    groups = [list(range(side, count, 2)) for side in (0, 1)]
+    side = lax.axis_index(axis) % 2
+    copies = jnp.broadcast_to(x[None], (count // 2,) + x.shape).reshape((count // 2 * x.shape[0],) + x.shape[1:])
+    half = lax.all_to_all(copies, axis, 0, 0, tiled=True, axis_index_groups=groups)
+    other = lax.ppermute(half, axis, pairs)
+    return jnp.where(side == 0, jnp.concatenate([half, other]), jnp.concatenate([other, half]))
+
+
 def local(surface, wet_blocks, legendre, slot_order, love_gain):
     cycle_count, lon_width = surface.shape
     groups = lax.axis_size("lon")
@@ -92,7 +116,7 @@
     forward_scale = lon_total ** (-0.5)
     fourier = reduce_scatter(forward_dft(masked, slot_order, lon_start, lon_total) * forward_scale, "lon")
     coefficient = jnp.einsum("krl,kcr->kcl", legendre, fourier, precision=lax.Precision.HIGH)
-    degree_whole = all_gather(reduce_scatter(coefficient, "lat"), "lat")
+    degree_whole = paired_all_gather(paired_reduce_scatter(coefficient, "lat"), "lat")
     degree_count = degree_whole.shape[2]
     degrees = jnp.arange(degree_count, dtype=jnp.int32)
     retained = degrees[None, :] >= own_orders[:, None]

time: 180 us -> 164 us (0.911)
  blocking collectives: 41.4 us -> 32.8 us
  waiting for transfers between devices: 31 us -> 23.3 us
    all_to_all x2 -> x1, waiting for transfers between devices: 25.9 us -> 8 us  [all_gather(): return lax.all_to_all(copies, axis, 0, 0, tiled=True)]
    all_to_all x2, blocking collectives: 41.4 us -> 32.8 us  [the longest x1 17.4 us: paired_reduce_scatter(): lax.all_to_all(summed, axis, 0, 0, tiled=True, axis_index_groups=groups)]
    all_to_all x0 -> x1, waiting for transfers between devices: none -> 7.06 us  [reduce_scatter(): moved = lax.all_to_all(x, axis, 0, 0, tiled=True)]
    all_to_all x0 -> x1, starting transfers between devices: none -> 5.32 us  [reduce_scatter(): moved = lax.all_to_all(x, axis, 0, 0, tiled=True)]
    all_to_all x2 -> x1, starting transfers between devices: 10.2 us -> 5.24 us  [all_gather(): return lax.all_to_all(copies, axis, 0, 0, tiled=True)]
    ppermute x0 -> x2, waiting for transfers between devices: none -> 3 us  [the longest x1 3 us: paired_reduce_scatter(): summed = kept + lax.ppermute(sent, axis, pairs)]
    reduce_sum x2 -> x1, other arithmetic: 3.14 us -> 0.77 us  [reduce_scatter(): return moved.reshape((count, x.shape[0] // count) + x.shape[1:]).sum(axis=0)]
    broadcast_in_dim x2 -> x1, local copies, waits for them, and re-layouts: 2.33 us -> 0.27 us  [all_gather(): jnp.broadcast_to(x[None], (count,) + x.shape)]
  transfers between devices with their start and end apart: 6 -> 8, of which waited for: 4 -> 5; matrix products, arithmetic and copies ran while one was open for 4% -> 4% of each run, Pallas kernels for 0% -> 0%
where the time goes in v3:
time: 164 us; the launch traced here: 163 us
  matrix products  37.1 us (23%)
  blocking collectives  32.8 us (20%)
  local copies, waits for them, and re-layouts  26.7 us (16%)
  waiting for transfers between devices  23.3 us (14%)
  other arithmetic  21.3 us (13%)
  starting transfers between devices  20.9 us (13%)
    dot_general x1, matrix products, local(): jnp.einsum('krl,kcl->kcr', legendre, spectrum, precision=lax.Precision.HIGH)  17.7 us
    all_to_all x1, blocking collectives, paired_reduce_scatter(): lax.all_to_all(summed, axis, 0, 0, tiled=True, axis_index_groups=groups)  17.4 us
    dot_general x1, matrix products, local(): jnp.einsum('krl,kcr->kcl', legendre, fourier, precision=lax.Precision.HIGH)  15.8 us
    all_to_all x1, blocking collectives, paired_all_gather(): lax.all_to_all(copies, axis, 0, 0, tiled=True, axis_index_groups=groups)  15.4 us
    all_to_all x1, waiting for transfers between devices, all_gather(): return lax.all_to_all(copies, axis, 0, 0, tiled=True)  8 us
    all_to_all x1, waiting for transfers between devices, reduce_scatter(): moved = lax.all_to_all(x, axis, 0, 0, tiled=True)  7.06 us
    unnamed x8, local copies, waits for them, and re-layouts  6.03 us
    ppermute x2, starting transfers between devices, padded_2(): lax.ppermute(head, axis, [((i + 1) % count, i) for i in range(ends)])  5.63 us
  transfers between devices with their start and end apart: 8, of which 5 were waited for; matrix products, arithmetic and copies ran while one was open for 4% of the time, Pallas kernels for 0%

profile of v3, /device:TPU:12, one launch (start us, length us, event | category | flops | bytes accessed | tf_op | source)
XLA Modules:
  0.0 163.1 jit_solution(16038739571636776248)
XLA Ops:
  4.6 1.9 %convolution_bitcast_fusion = f32[2,256,32,32]{1,2,0,3:T(8,128)S(1)} fusion(f32[32,64,32]{2,1,0:T(8,128)S(1)} %reshape.166, f32[1,256,64]{1,2,0:T(8,128)S(1)} %get-tuple-element.21, f32[1,256,64]{1,2,0:T(8,128)S(1)} %get-tuple-element.22), kind=kOutput, calls=%fused_computation.22 | convolution fusion | flops 402685952 | bytes 2490368 | tf_op jit(solution)/shard_map/cua,rab->cubr/dot_general | solution.py:48
  10.6 3.6 %gather_fusion = f32[1024,2,32]{2,1,0:T(2,128)S(1)} fusion(f32[1024,2,32]{2,1,0:T(2,128)S(1)} %copy.48, s32[1024]{0:T(1024)S(1)} %get-tuple-element.20), kind=kCustom, calls=%fused_computation.clone | custom fusion | bytes 528384 | tf_op jit(solution)/shard_map/jit(_take)/gather | solution.py:53
  14.2 3.8 %select_multiply_fusion = f32[1024,2,32]{2,1,0:T(2,128)S(1)} fusion(f32[1024,2,32]{2,1,0:T(2,128)S(1)} %gather_fusion, pred[1024]{0:T(1024)(128)(4,1)S(1)} %compare_and_fusion.1), kind=kLoop, calls=%fused_computation.27 | loop fusion | flops 131072 | bytes 525312 | tf_op jit(solution)/shard_map/mul | solution.py:117
  18.0 1.8 %reshape.208 = f32[4,1,16384]{2,1,0:T(1,128)} reshape(f32[1024,2,32]{2,1,0:T(2,128)S(1)} %select_multiply_fusion) | data formatting | bytes 524288
  19.7 5.3 %all-to-all-start = ((f32[4,1,16384]{2,1,0:T(1,128)}), f32[4,1,16384]{2,1,0:T(1,128)S(1)}, u32[]{:S(2)}, u32[]{:S(2)}) async-start(f32[4,1,16384]{2,1,0:T(1,128)} %reshape.208), calls=%async_computation | async-start | bytes 524288 | tf_op jit(solution)/shard_map/all_to_all | solution.py:70
  25.0 7.1 %all-to-all-done = f32[4,1,16384]{2,1,0:T(1,128)S(1)} async-done(((f32[4,1,16384]{2,1,0:T(1,128)}), f32[4,1,16384]{2,1,0:T(1,128)S(1)}, u32[]{:S(2)}, u32[]{:S(2)}) %all-to-all-start) | async-done | bytes 262176 | tf_op jit(solution)/shard_map/all_to_all | solution.py:70
  35.7 15.8 %fusion.51 = f32[256,2,1024]{2,1,0:T(2,128)S(1)} fusion(f32[256,2,32]{2,1,0:T(2,128)S(1)} %reduce_sum.56, f32[256,32,1024]{2,1,0:T(8,128)} %param.9), kind=kOutput, calls=%fused_computation.94 | convolution fusion | flops 100663296 | bytes 35717120 | tf_op jit(solution)/shard_map/krl,kcr->kcl/dot_general | solution.py:118
  52.5 3.0 %collective-permute-done = f32[128,2,1024]{2,1,0:T(2,128)} collective-permute-done((f32[128,2,1024]{2,1,0:T(2,128)}, f32[128,2,1024]{2,1,0:T(2,128)}, u32[]{:S(2)}, u32[]{:S(2)}) %collective-permute-start) | collective-permute-done | bytes 1048608 | tf_op jit(solution)/shard_map/ppermute | solution.py:88
  55.5 1.8 %dynamic-slice_add_fusion = f32[128,2,1024]{2,1,0:T(2,128)S(1)} fusion(f32[128,2,1024]{2,1,0:T(2,128)} %collective-permute-done, f32[256,2,1024]{2,1,0:T(2,128)S(1)} %fusion.51, s32[]{:T(128)S(6)} %select_n.82), kind=kLoop, calls=%fused_computation.29 | loop fusion | flops 262144 | bytes 3145732 | tf_op jit(solution)/shard_map/add | solution.py:88
  57.3 17.4 %all_to_all.20 = f32[128,2,1024]{2,1,0:T(2,128)S(1)} all-to-all(f32[128,2,1024]{2,1,0:T(2,128)S(1)} %dynamic-slice_add_fusion), channel_id=1, replica_groups={{0,8,16,24},{4,12,20,28},{1,9,17,25},{5,13,21,29},{2,10,18,26},{6,14,22..., dimensions={0} | all-to-all | bytes 2097152 | tf_op jit(solution)/shard_map/all_to_all | solution.py:89
  75.6 15.4 %all_to_all.21 = f32[128,2,1024]{2,1,0:T(2,128)S(1)} all-to-all(f32[128,2,1024]{2,1,0:T(2,128)S(1)} %bitcast.50), channel_id=1, replica_groups={{0,8,16,24},{4,12,20,28},{1,9,17,25},{5,13,21,29},{2,10,18,26},{6,14,22..., dimensions={0} | all-to-all | bytes 2097152 | tf_op jit(solution)/shard_map/all_to_all | solution.py:99
  91.8 4.5 %scatter_custom_fusion = s32[1024]{0:T(1024)S(1)} fusion(s32[1024]{0:T(1024)S(1)} %get-tuple-element.19, s32[1024]{0:T(1024)S(1)} %iota.53, s32[]{:T(128)} %constant.77.clone.1), kind=kCustom, calls=%fused_computation.84 | custom fusion | bytes 4100 | tf_op jit(solution)/shard_map/scatter | solution.py:59
  96.6 17.7 %fusion.2 = f32[256,2,32]{2,1,0:T(2,128)S(1)} fusion(f32[256,32,1024]{2,1,0:T(8,128)} %param.9, f32[128,2,1024]{2,1,0:T(2,128)} %collective-permute-done.1, f32[128,2,1024]{2,1,0:T(2,128)S(1)} %all_to_all.21, pred[]{:T(512)S(6)} %eq.12, pred[256,1024]{1,0:T(8,128)(4,1)S(1)} %iota_compare_fusion, f32[1024]{0:T(1024)S(1)} %copy-done), kind=kOutput, calls=%fused_computation.10 | convolution fusion | flops 103284736 | bytes 35983360 | tf_op jit(solution)/shard_map/krl,kcl->kcr/dot_general | solution.py:124
  114.6 1.8 %reshape.210 = f32[4,1,16384]{2,1,0:T(1,128)} reshape(f32[1024,2,32]{2,1,0:T(2,128)S(1)} %bitcast.49) | data formatting | bytes 524288
  116.3 5.2 %all-to-all-start.3 = ((f32[4,1,16384]{2,1,0:T(1,128)}), f32[4,1,16384]{2,1,0:T(1,128)S(1)}, u32[]{:S(2)}, u32[]{:S(2)}) async-start(f32[4,1,16384]{2,1,0:T(1,128)} %reshape.210), calls=%async_computation.3 | async-start | bytes 524288 | tf_op jit(solution)/shard_map/all_to_all | solution.py:77
  121.6 8.0 %all-to-all-done.3 = f32[4,1,16384]{2,1,0:T(1,128)S(1)} async-done(((f32[4,1,16384]{2,1,0:T(1,128)}), f32[4,1,16384]{2,1,0:T(1,128)S(1)}, u32[]{:S(2)}, u32[]{:S(2)}) %all-to-all-start.3) | async-done | bytes 262176 | tf_op jit(solution)/shard_map/all_to_all | solution.py:77
  131.9 3.5 %gather_fusion.1 = f32[1024,2,32]{2,1,0:T(2,128)S(1)} fusion(f32[1024,2,32]{2,1,0:T(2,128)S(1)} %reshape.211, s32[1024]{0:T(1024)S(1)} %fusion.40), kind=kCustom, calls=%fused_computation.1.clone | custom fusion | bytes 528384 | tf_op jit(solution)/shard_map/jit(_take)/gather | solution.py:60
  135.5 3.7 %broadcast_select_fusion = f32[1024,2,32]{2,1,0:T(2,128)S(1)} fusion(f32[1024,2,32]{2,1,0:T(2,128)S(1)} %gather_fusion.1, pred[1024]{0:T(1024)(128)(4,1)S(1)} %compare_and_fusion), kind=kLoop, calls=%fused_computation.32 | loop fusion | flops 65536 | bytes 525312 | tf_op jit(solution)/shard_map/jit(_take)/select_n | solution.py:60
  142.2 1.8 %multiply_bitcast_fusion = (f32[32,64,32]{1,0,2:T(8,128)S(1)}, f32[32,64,32]{1,0,2:T(8,128)S(1)}) fusion(f32[1,256,64]{1,2,0:T(8,128)S(1)} %get-tuple-element.21, f32[1,256,64]{1,2,0:T(8,128)S(1)} %get-tuple-element.22, f32[1,256,32,32]{1,3,0,2:T(8,128)S(1)} %bitcast.47, f32[1,256,32,32]{1,3,0,2:T(8,128)S(1)} %bitcast.46), kind=kOutput, calls=%fused_computation.33 | convolution fusion | flops 403341312 | bytes 2752512 | tf_op jit(solution)/shard_map/cua,cubr->rab/dot_general | solution.py:64
  144.9 2.6 %collective-permute-start.2 = (f32[1,2048]{1,0:T(1,128)S(1)}, f32[1,2048]{1,0:T(1,128)S(1)}, u32[]{:S(2)}, u32[]{:S(2)}) collective-permute-start(f32[1,2048]{1,0:T(1,128)S(1)} %get-tuple-element.16), channel_id=1, source_target_pairs={{4,0},{8,4},{12,8},{16,12},{20,16},{24,20},{28,24},{5,1},{9,5},{13... | collective-permute-start | bytes 24584 | tf_op jit(solution)/shard_map/ppermute | solution.py:21
  147.5 1.9 %collective-permute-start.3 = (f32[1,2048]{1,0:T(1,128)S(1)}, f32[1,2048]{1,0:T(1,128)S(1)}, u32[]{:S(2)}, u32[]{:S(2)}) collective-permute-start(f32[1,2048]{1,0:T(1,128)S(1)} %get-tuple-element.15), channel_id=1, source_target_pairs={{0,4},{4,8},{8,12},{12,16},{16,20},{20,24},{24,28},{1,5},{5,9},{9,... | collective-permute-start | bytes 24584 | tf_op jit(solution)/shard_map/ppermute | solution.py:19
  149.8 3.5 %collective-permute-done.3 = f32[1,2048]{1,0:T(1,128)S(1)} collective-permute-done((f32[1,2048]{1,0:T(1,128)S(1)}, f32[1,2048]{1,0:T(1,128)S(1)}, u32[]{:S(2)}, u32[]{:S(2)}) %collective-permute-start.3) | collective-permute-done | bytes 8224 | tf_op jit(solution)/shard_map/ppermute | solution.py:19
  153.5 3.0 %collective-permute-start.4 = (f32[34,1]{1,0:T(8,128)S(1)}, f32[34,1]{1,0:T(8,128)S(1)}, u32[]{:S(2)}, u32[]{:S(2)}) collective-permute-start(f32[34,1]{1,0:T(8,128)S(1)} %get-tuple-element.13), channel_id=1, source_target_pairs={{1,0},{2,1},{3,2},{5,4},{6,5},{7,6},{9,8},{10,9},{11,10},{13,12},{... | collective-permute-start | bytes 416 | tf_op jit(solution)/shard_map/ppermute | solution.py:21
  156.5 2.8 %collective-permute-start.5 = (f32[34,1]{1,0:T(8,128)S(1)}, f32[34,1]{1,0:T(8,128)S(1)}, u32[]{:S(2)}, u32[]{:S(2)}) collective-permute-start(f32[34,1]{1,0:T(8,128)S(1)} %get-tuple-element.14), channel_id=1, source_target_pairs={{0,1},{1,2},{2,3},{4,5},{5,6},{6,7},{8,9},{9,10},{10,11},{12,13},{... | collective-permute-start | bytes 416 | tf_op jit(solution)/shard_map/ppermute | solution.py:19
  (58 shorter events, 25.3 us)
Async XLA Ops:
  19.7 12.4 %all-to-all-start = ((f32[4,1,16384]{2,1,0:T(1,128)}), f32[4,1,16384]{2,1,0:T(1,128)S(1)}, u32[]{:S(2)}, u32[]{:S(2)}) async-start(f32[4,1,16384]{2,1,0:T(1,128)} %reshape.208), calls=%async_computation | async-start | bytes 524288 | tf_op jit(solution)/shard_map/all_to_all | solution.py:70
  52.5 3.0 %collective-permute-start = (f32[128,2,1024]{2,1,0:T(2,128)}, f32[128,2,1024]{2,1,0:T(2,128)}, u32[]{:S(2)}, u32[]{:S(2)}) collective-permute-start(f32[128,2,1024]{2,1,0:T(2,128)} %constant_dynamic-slice_fusion), channel_id=1, source_target_pairs={{0,4},{4,0},{8,12},{12,8},{16,20},{20,16},{24,28},{28,24},{1,5},{5... | collective-permute-start | bytes 3145736 | tf_op jit(solution)/shard_map/ppermute | solution.py:88
  57.3 39.3 %copy-start = (f32[1024]{0:T(1024)S(1)}, f32[1024]{0:T(1024)}, u32[]{:S(2)}) copy-start(f32[1024]{0:T(1024)} %param.11) | copy-start | bytes 12292
  91.0 5.5 %collective-permute-start.1 = (f32[128,2,1024]{2,1,0:T(2,128)S(1)}, f32[128,2,1024]{2,1,0:T(2,128)}, u32[]{:S(2)}, u32[]{:S(2)}) collective-permute-start(f32[128,2,1024]{2,1,0:T(2,128)S(1)} %all_to_all.21), channel_id=1, source_target_pairs={{0,4},{4,0},{8,12},{12,8},{16,20},{20,16},{24,28},{28,24},{1,5},{5... | collective-permute-start | bytes 3145736 | tf_op jit(solution)/shard_map/ppermute | solution.py:100
  116.3 13.3 %all-to-all-start.3 = ((f32[4,1,16384]{2,1,0:T(1,128)}), f32[4,1,16384]{2,1,0:T(1,128)S(1)}, u32[]{:S(2)}, u32[]{:S(2)}) async-start(f32[4,1,16384]{2,1,0:T(1,128)} %reshape.210), calls=%async_computation.3 | async-start | bytes 524288 | tf_op jit(solution)/shard_map/all_to_all | solution.py:77
  144.9 4.9 %collective-permute-start.2 = (f32[1,2048]{1,0:T(1,128)S(1)}, f32[1,2048]{1,0:T(1,128)S(1)}, u32[]{:S(2)}, u32[]{:S(2)}) collective-permute-start(f32[1,2048]{1,0:T(1,128)S(1)} %get-tuple-element.16), channel_id=1, source_target_pairs={{4,0},{8,4},{12,8},{16,12},{20,16},{24,20},{28,24},{5,1},{9,5},{13... | collective-permute-start | bytes 24584 | tf_op jit(solution)/shard_map/ppermute | solution.py:21
  147.5 5.9 %collective-permute-start.3 = (f32[1,2048]{1,0:T(1,128)S(1)}, f32[1,2048]{1,0:T(1,128)S(1)}, u32[]{:S(2)}, u32[]{:S(2)}) collective-permute-start(f32[1,2048]{1,0:T(1,128)S(1)} %get-tuple-element.15), channel_id=1, source_target_pairs={{0,4},{4,8},{8,12},{12,16},{16,20},{20,24},{24,28},{1,5},{5,9},{9,... | collective-permute-start | bytes 24584 | tf_op jit(solution)/shard_map/ppermute | solution.py:19
  153.5 7.0 %collective-permute-start.4 = (f32[34,1]{1,0:T(8,128)S(1)}, f32[34,1]{1,0:T(8,128)S(1)}, u32[]{:S(2)}, u32[]{:S(2)}) collective-permute-start(f32[34,1]{1,0:T(8,128)S(1)} %get-tuple-element.13), channel_id=1, source_target_pairs={{1,0},{2,1},{3,2},{5,4},{6,5},{7,6},{9,8},{10,9},{11,10},{13,12},{... | collective-permute-start | bytes 416 | tf_op jit(solution)/shard_map/ppermute | solution.py:21
  156.5 5.7 %collective-permute-start.5 = (f32[34,1]{1,0:T(8,128)S(1)}, f32[34,1]{1,0:T(8,128)S(1)}, u32[]{:S(2)}, u32[]{:S(2)}) collective-permute-start(f32[34,1]{1,0:T(8,128)S(1)} %get-tuple-element.14), channel_id=1, source_target_pairs={{0,1},{1,2},{2,3},{4,5},{5,6},{6,7},{8,9},{9,10},{10,11},{12,13},{... | collective-permute-start | bytes 416 | tf_op jit(solution)/shard_map/ppermute | solution.py:19

commit v4 on v3

--- a/solution.py
+++ b/solution.py
@@ -8,21 +8,22 @@
 BLK = 128
 
 
-def padded_2(cells, sides, width):
-    for axis, dim in sides:
-        count = lax.axis_size(axis)
-        ends = count - 1
-        head = lax.slice_in_dim(cells, 0, width, axis=dim)
-        tail = lax.slice_in_dim(cells, cells.shape[dim] - width, cells.shape[dim], axis=dim)
-        cells = jnp.concatenate(
-            [
-                lax.ppermute(tail, axis, [(i, (i + 1) % count) for i in range(ends)]),
-                cells,
-                lax.ppermute(head, axis, [((i + 1) % count, i) for i in range(ends)]),
-            ],
-            axis=dim,
-        )
-    return cells
+def halo(cells, axis, dim):
+    count = lax.axis_size(axis)
+    ends = count - 1
+    head = lax.slice_in_dim(cells, 0, 1, axis=dim)
+    tail = lax.slice_in_dim(cells, cells.shape[dim] - 1, cells.shape[dim], axis=dim)
+    before = lax.ppermute(tail, axis, [(i, (i + 1) % count) for i in range(ends)])
+    after = lax.ppermute(head, axis, [((i + 1) % count, i) for i in range(ends)])
+    return before, after
+
+
+def neighbour_sum(cells):
+    up, down = halo(cells, "lat", 0)
+    left, right = halo(cells, "lon", 1)
+    rows = jnp.concatenate([up, cells[:-1]], axis=0) + jnp.concatenate([cells[1:], down], axis=0)
+    cols = jnp.concatenate([left, cells[:, :-1]], axis=1) + jnp.concatenate([cells[:, 1:], right], axis=1)
+    return rows + cols
 
 
 INNER = 32
@@ -56,7 +57,8 @@
 def inverse_dft(synthesis, slot_order, lon_start, lon_width, lon_total):
     order_count, _, cycles = synthesis.shape
     rotor, cb, sb = dft_tables(order_count, lon_start, lon_width, lon_total)
-    slot_of = jnp.zeros((order_count,), jnp.int32).at[slot_order].set(jnp.arange(order_count, dtype=jnp.int32))
+    slots = jnp.arange(order_count, dtype=jnp.int32)
+    slot_of = jnp.where(slot_order[None, :] == slots[:, None], slots[None, :], 0).sum(axis=1)
     by_order = jnp.take(synthesis, slot_of, axis=0).reshape(cb.shape[0], cb.shape[1], 2, cycles)
     yc, ys = by_order[:, :, 0, None, :], by_order[:, :, 1, None, :]
     hc = (yc * cb[..., None] + ys * sb[..., None]).sum(axis=0)
@@ -65,16 +67,23 @@
     return out.reshape(cycles, lon_width)
 
 
-def reduce_scatter(x, axis):
+def shifted_reduce_scatter(x, axis):
     count = lax.axis_size(axis)
-    moved = lax.all_to_all(x, axis, 0, 0, tiled=True)
-    return moved.reshape((count, x.shape[0] // count) + x.shape[1:]).sum(axis=0)
+    me = lax.axis_index(axis)
+    size = x.shape[0] // count
+    total = lax.dynamic_slice_in_dim(x, me * size, size)
+    for shift in range(1, count):
+        chunk = lax.dynamic_slice_in_dim(x, (me + shift) % count * size, size)
+        total = total + lax.ppermute(chunk, axis, [(i, (i + shift) % count) for i in range(count)])
+    return total
 
 
-def all_gather(x, axis):
+def shifted_all_gather(x, axis):
     count = lax.axis_size(axis)
-    copies = jnp.broadcast_to(x[None], (count,) + x.shape).reshape((count * x.shape[0],) + x.shape[1:])
-    return lax.all_to_all(copies, axis, 0, 0, tiled=True)
+    me = lax.axis_index(axis)
+    ahead = [x] + [lax.ppermute(x, axis, [((i + shift) % count, i) for i in range(count)]) for shift in range(1, count)]
+    stacked = jnp.concatenate(ahead + ahead, axis=0)
+    return lax.dynamic_slice_in_dim(stacked, (count - me) % count * x.shape[0], count * x.shape[0])
 
 
 def paired_reduce_scatter(x, axis):
@@ -114,7 +123,7 @@
         slot_order, lax.axis_index("lon") * slot_count, slot_count
     )
     forward_scale = lon_total ** (-0.5)
-    fourier = reduce_scatter(forward_dft(masked, slot_order, lon_start, lon_total) * forward_scale, "lon")
+    fourier = shifted_reduce_scatter(forward_dft(masked, slot_order, lon_start, lon_total) * forward_scale, "lon")
     coefficient = jnp.einsum("krl,kcr->kcl", legendre, fourier, precision=lax.Precision.HIGH)
     degree_whole = paired_all_gather(paired_reduce_scatter(coefficient, "lat"), "lat")
     degree_count = degree_whole.shape[2]
@@ -122,11 +131,10 @@
     retained = degrees[None, :] >= own_orders[:, None]
     spectrum = jnp.where(retained[:, None, :], love_gain[None, None, :] * degree_whole, 0.0)
     synthesis = jnp.einsum("krl,kcl->kcr", legendre, spectrum, precision=lax.Precision.HIGH)
-    summed = inverse_dft(all_gather(synthesis, "lon"), slot_order, lon_start, lon_width, lon_total)
+    summed = inverse_dft(shifted_all_gather(synthesis, "lon"), slot_order, lon_start, lon_width, lon_total)
     loading = summed * (2 * slot_total) ** (-0.5)
     potential = masked - 0.6 * loading
-    padded = padded_2(potential, (("lat", 0), ("lon", 1)), 1)
-    neighbours = padded[2:, 1:-1] + padded[:-2, 1:-1] + padded[1:-1, 2:] + padded[1:-1, :-2]
+    neighbours = neighbour_sum(potential)
     surface_next = wet_cells * (masked + 0.2 * (neighbours - 4.0 * potential))
     return (surface_next, loading)
 

time: 164 us -> 181 us (1.10)
  waiting for transfers between devices: 23.3 us -> 45.8 us
  local copies, waits for them, and re-layouts: 26.7 us -> 22.2 us
  other arithmetic: 21.3 us -> 18.2 us
    ppermute x4 -> x10, waiting for transfers between devices: 5.21 us -> 41.2 us  [the longest x3 20.6 us: shifted_reduce_scatter(): lax.ppermute(chunk, axis, [(i, (i + shift) % count) for i in range(count)])]
    all_to_all x2 -> x0, waiting for transfers between devices: 15.1 us -> none  [the longest x1 8 us: all_gather(): return lax.all_to_all(copies, axis, 0, 0, tiled=True)]
    ppermute x4 -> x10, starting transfers between devices: 10.4 us -> 22.5 us  [the longest x2 6.46 us: halo(): lax.ppermute(head, axis, [((i + 1) % count, i) for i in range(ends)])]
    all_to_all x2 -> x0, starting transfers between devices: 10.6 us -> none  [the longest x1 5.32 us: reduce_scatter(): moved = lax.all_to_all(x, axis, 0, 0, tiled=True)]
    scatter x1 -> x0, local copies, waits for them, and re-layouts: 4.53 us -> none  [inverse_dft(): jnp.zeros((order_count,), jnp.int32).at[slot_order]]
    all_to_all x2 -> x0, other arithmetic: 2.74 us -> none  [the longest x1 1.37 us: all_gather(): return lax.all_to_all(copies, axis, 0, 0, tiled=True)]
    ppermute x1, waiting for transfers between devices: 0.01 us -> 1.84 us  [paired_all_gather(): other = lax.ppermute(half, axis, pairs)]
    unnamed x8 -> x30, local copies, waits for them, and re-layouts: 6.03 us -> 5.76 us
  transfers between devices with their start and end apart: 8 -> 12, of which waited for: 5 -> 8; matrix products, arithmetic and copies ran while one was open for 4% -> 2% of each run, Pallas kernels for 0% -> 0%
where the time goes in v4:
time: 181 us
  waiting for transfers between devices  45.8 us (25%)
  matrix products  38 us (21%)
  blocking collectives  32.8 us (18%)
  starting transfers between devices  22.6 us (12%)
  local copies, waits for them, and re-layouts  22.2 us (12%)
  other arithmetic  18.2 us (10%)
    ppermute x3, waiting for transfers between devices, shifted_reduce_scatter(): lax.ppermute(chunk, axis, [(i, (i + shift) % count) for i in range(count)])  20.6 us
    ppermute x3, waiting for transfers between devices, shifted_all_gather(): lax.ppermute(x, axis, [((i + shift) % count, i) for i in range(count)])  18.5 us
    dot_general x1, matrix products, local(): jnp.einsum('krl,kcl->kcr', legendre, spectrum, precision=lax.Precision.HIGH)  18.2 us
    all_to_all x1, blocking collectives, paired_reduce_scatter(): lax.all_to_all(summed, axis, 0, 0, tiled=True, axis_index_groups=groups)  17.4 us
    dot_general x1, matrix products, local(): jnp.einsum('krl,kcr->kcl', legendre, fourier, precision=lax.Precision.HIGH)  16.1 us
    all_to_all x1, blocking collectives, paired_all_gather(): lax.all_to_all(copies, axis, 0, 0, tiled=True, axis_index_groups=groups)  15.4 us
    ppermute x2, starting transfers between devices, halo(): lax.ppermute(head, axis, [((i + 1) % count, i) for i in range(ends)])  6.46 us
    ppermute x2, starting transfers between devices, halo(): lax.ppermute(tail, axis, [(i, (i + 1) % count) for i in range(ends)])  6.3 us
  transfers between devices with their start and end apart: 12, of which 8 were waited for; matrix products, arithmetic and copies ran while one was open for 2% of the time, Pallas kernels for 0%

profile of v4, /device:TPU:12, one launch (start us, length us, event | category | flops | bytes accessed | tf_op | source)
XLA Modules:
  0.0 180.7 jit_solution(9194091183103073840)
XLA Ops:
  5.4 1.9 %convolution_bitcast_fusion = f32[2,256,32,32]{1,2,0,3:T(8,128)S(1)} fusion(f32[32,64,32]{2,1,0:T(8,128)S(1)} %reshape.160, f32[1,256,64]{1,2,0:T(8,128)S(1)} %get-tuple-element.28, f32[1,256,64]{1,2,0:T(8,128)S(1)} %get-tuple-element.29), kind=kOutput, calls=%fused_computation.23 | convolution fusion | flops 402685952 | bytes 2490368 | tf_op jit(solution)/shard_map/cua,rab->cubr/dot_general | solution.py:49
  11.6 3.6 %gather_fusion = f32[1024,2,32]{2,1,0:T(2,128)S(1)} fusion(f32[1024,2,32]{2,1,0:T(2,128)S(1)} %copy.65, s32[1024]{0:T(1024)S(1)} %fusion.43), kind=kCustom, calls=%fused_computation.clone | custom fusion | bytes 528384 | tf_op jit(solution)/shard_map/jit(_take)/gather | solution.py:54
  15.1 3.8 %select_multiply_fusion = f32[1024,2,32]{2,1,0:T(2,128)S(1)} fusion(f32[1024,2,32]{2,1,0:T(2,128)S(1)} %gather_fusion, pred[1024]{0:T(1024)(128)(4,1)S(1)} %compare_and_fusion.1), kind=kLoop, calls=%fused_computation.28 | loop fusion | flops 131072 | bytes 525312 | tf_op jit(solution)/shard_map/mul | solution.py:126
  21.8 1.8 collective-permute-start.2
  23.6 14.9 %collective-permute-done = f32[256,2,32]{2,1,0:T(2,128)S(1)} collective-permute-done((f32[256,2,32]{2,1,0:T(2,128)S(1)}, f32[256,2,32]{2,1,0:T(2,128)S(1)}, u32[]{:S(2)}, u32[]{:S(2)}) %collective-permute-start) | collective-permute-done | bytes 65568 | tf_op jit(solution)/shard_map/ppermute | solution.py:77
  38.5 4.5 %collective-permute-done.1 = f32[256,2,32]{2,1,0:T(2,128)S(1)} collective-permute-done((f32[256,2,32]{2,1,0:T(2,128)S(1)}, f32[256,2,32]{2,1,0:T(2,128)S(1)}, u32[]{:S(2)}, u32[]{:S(2)}) %collective-permute-start.1) | collective-permute-done | bytes 65568 | tf_op jit(solution)/shard_map/ppermute | solution.py:77
  44.9 16.1 %fusion.25 = f32[256,2,1024]{2,1,0:T(2,128)S(1)} fusion(f32[256,32,1024]{2,1,0:T(8,128)} %param.9, f32[256,2,32]{2,1,0:T(2,128)} %collective-permute-done.2, f32[256,2,32]{2,1,0:T(2,128)} %copy-done.9, f32[256,2,32]{2,1,0:T(2,128)} %copy-done.8, f32[1024,2,32]{2,1,0:T(2,128)S(1)} %select_multiply_fusion, s32[]{:T(128)S(6)} %select_n.107), kind=kOutput, calls=%fused_computation.45 | convolution fusion | flops 100712448 | bytes 36110340 | tf_op jit(solution)/shard_map/krl,kcr->kcl/dot_general | solution.py:127
  61.2 2.8 %collective-permute-done.3 = f32[128,2,1024]{2,1,0:T(2,128)} collective-permute-done((f32[128,2,1024]{2,1,0:T(2,128)S(1)}, f32[128,2,1024]{2,1,0:T(2,128)}, u32[]{:S(2)}, u32[]{:S(2)}) %collective-permute-start.3) | collective-permute-done | bytes 1048608 | tf_op jit(solution)/shard_map/ppermute | solution.py:97
  65.8 17.4 %all_to_all.10 = f32[128,2,1024]{2,1,0:T(2,128)S(1)} all-to-all(f32[128,2,1024]{2,1,0:T(2,128)S(1)} %dynamic-slice_add_fusion), channel_id=1, replica_groups={{0,8,16,24},{4,12,20,28},{1,9,17,25},{5,13,21,29},{2,10,18,26},{6,14,22..., dimensions={0} | all-to-all | bytes 2097152 | tf_op jit(solution)/shard_map/all_to_all | solution.py:98
  84.0 15.4 %all_to_all.11 = f32[128,2,1024]{2,1,0:T(2,128)S(1)} all-to-all(f32[128,2,1024]{2,1,0:T(2,128)S(1)} %bitcast.45), channel_id=1, replica_groups={{0,8,16,24},{4,12,20,28},{1,9,17,25},{5,13,21,29},{2,10,18,26},{6,14,22..., dimensions={0} | all-to-all | bytes 2097152 | tf_op jit(solution)/shard_map/all_to_all | solution.py:108
  100.3 1.8 %collective-permute-done.4 = f32[128,2,1024]{2,1,0:T(2,128)S(1)} collective-permute-done((f32[128,2,1024]{2,1,0:T(2,128)S(1)}, f32[128,2,1024]{2,1,0:T(2,128)S(1)}, u32[]{:S(2)}, u32[]{:S(2)}) %collective-permute-start.4) | collective-permute-done | bytes 1048608 | tf_op jit(solution)/shard_map/ppermute | solution.py:109
  102.2 18.2 %constant_dynamic-update-slice_fusion.7 = (f32[2048,2,32]{2,1,0:T(2,128)}, f32[256,2,32]{2,1,0:T(2,128)S(1)}) fusion(f32[256,32,1024]{2,1,0:T(8,128)} %param.9, f32[128,2,1024]{2,1,0:T(2,128)S(1)} %collective-permute-done.4, f32[128,2,1024]{2,1,0:T(2,128)S(1)} %all_to_all.11, pred[]{:T(512)S(6)} %eq.29, pred[256,1024]{1,0:T(8,128)(4,1)S(1)} %iota_compare_fusion.1, ...), kind=kOutput, calls=%fused_computation.79 | convolution fusion | flops 103284736 | bytes 36245504 | tf_op jit(solution)/shard_map/krl,kcl->kcr/dot_general | solution.py:133
  120.4 2.3 %collective-permute-start.6 = (f32[256,2,32]{2,1,0:T(2,128)S(1)}, f32[256,2,32]{2,1,0:T(2,128)S(1)}, u32[]{:S(2)}, u32[]{:S(2)}) collective-permute-start(f32[256,2,32]{2,1,0:T(2,128)S(1)} %get-tuple-element.27), channel_id=1, source_target_pairs={{2,0},{3,1},{0,2},{1,3},{6,4},{7,5},{4,6},{5,7},{10,8},{11,9},{8,1... | collective-permute-start | bytes 196616 | tf_op jit(solution)/shard_map/ppermute | solution.py:84
  122.6 2.8 %collective-permute-start.7 = (f32[256,2,32]{2,1,0:T(2,128)S(1)}, f32[256,2,32]{2,1,0:T(2,128)S(1)}, u32[]{:S(2)}, u32[]{:S(2)}) collective-permute-start(f32[256,2,32]{2,1,0:T(2,128)S(1)} %get-tuple-element.27), channel_id=1, source_target_pairs={{3,0},{0,1},{1,2},{2,3},{7,4},{4,5},{5,6},{6,7},{11,8},{8,9},{9,10... | collective-permute-start | bytes 196616 | tf_op jit(solution)/shard_map/ppermute | solution.py:84
  125.5 15.3 %collective-permute-done.5 = f32[256,2,32]{2,1,0:T(2,128)S(1)} collective-permute-done((f32[256,2,32]{2,1,0:T(2,128)S(1)}, f32[256,2,32]{2,1,0:T(2,128)S(1)}, u32[]{:S(2)}, u32[]{:S(2)}) %collective-permute-start.5) | collective-permute-done | bytes 65568 | tf_op jit(solution)/shard_map/ppermute | solution.py:84
  142.1 3.2 %collective-permute-done.7 = f32[256,2,32]{2,1,0:T(2,128)S(1)} collective-permute-done((f32[256,2,32]{2,1,0:T(2,128)S(1)}, f32[256,2,32]{2,1,0:T(2,128)S(1)}, u32[]{:S(2)}, u32[]{:S(2)}) %collective-permute-start.7) | collective-permute-done | bytes 65568 | tf_op jit(solution)/shard_map/ppermute | solution.py:84
  150.3 3.6 %gather_fusion.1 = f32[1024,2,32]{2,1,0:T(2,128)S(1)} fusion(f32[1024,2,32]{2,1,0:T(2,128)S(1)} %constant_dynamic-slice_fusion, s32[1024]{0:T(1024)S(1)} %fusion.44), kind=kCustom, calls=%fused_computation.1.clone | custom fusion | bytes 528384 | tf_op jit(solution)/shard_map/jit(_take)/gather | solution.py:62
  153.9 3.7 %broadcast_select_fusion = f32[1024,2,32]{2,1,0:T(2,128)S(1)} fusion(f32[1024,2,32]{2,1,0:T(2,128)S(1)} %gather_fusion.1, pred[1024]{0:T(1024)(128)(4,1)S(1)} %compare_and_fusion), kind=kLoop, calls=%fused_computation.33 | loop fusion | flops 65536 | bytes 525312 | tf_op jit(solution)/shard_map/jit(_take)/select_n | solution.py:62
  160.2 1.8 multiply_bitcast_fusion
  163.2 1.9 %collective-permute-start.8 = (f32[1,2048]{1,0:T(1,128)S(1)}, f32[1,2048]{1,0:T(1,128)S(1)}, u32[]{:S(2)}, u32[]{:S(2)}) collective-permute-start(f32[1,2048]{1,0:T(1,128)S(1)} %get-tuple-element.23), channel_id=1, source_target_pairs={{0,4},{4,8},{8,12},{12,16},{16,20},{20,24},{24,28},{1,5},{5,9},{9,... | collective-permute-start | bytes 24584 | tf_op jit(solution)/shard_map/ppermute | solution.py:16
  165.1 4.5 %collective-permute-start.9 = (f32[1,2048]{1,0:T(1,128)S(1)}, f32[1,2048]{1,0:T(1,128)S(1)}, u32[]{:S(2)}, u32[]{:S(2)}) collective-permute-start(f32[1,2048]{1,0:T(1,128)S(1)} %get-tuple-element.22), channel_id=1, source_target_pairs={{4,0},{8,4},{12,8},{16,12},{20,16},{24,20},{28,24},{5,1},{9,5},{13... | collective-permute-start | bytes 24584 | tf_op jit(solution)/shard_map/ppermute | solution.py:17
  169.7 4.4 %collective-permute-start.10 = (f32[32,1]{1,0:T(8,128)S(1)}, f32[32,1]{1,0:T(8,128)S(1)}, u32[]{:S(2)}, u32[]{:S(2)}) collective-permute-start(f32[32,1]{1,0:T(8,128)S(1)} %get-tuple-element.19), channel_id=1, source_target_pairs={{0,1},{1,2},{2,3},{4,5},{5,6},{6,7},{8,9},{9,10},{10,11},{12,13},{... | collective-permute-start | bytes 392 | tf_op jit(solution)/shard_map/ppermute | solution.py:16
  174.1 1.9 %collective-permute-start.11 = (f32[32,1]{1,0:T(8,128)S(1)}, f32[32,1]{1,0:T(8,128)S(1)}, u32[]{:S(2)}, u32[]{:S(2)}) collective-permute-start(f32[32,1]{1,0:T(8,128)S(1)} %get-tuple-element.18), channel_id=1, source_target_pairs={{1,0},{2,1},{3,2},{5,4},{6,5},{7,6},{9,8},{10,9},{11,10},{13,12},{... | collective-permute-start | bytes 392 | tf_op jit(solution)/shard_map/ppermute | solution.py:17
  177.6 2.1 %collective-permute-done.11 = f32[32,1]{1,0:T(8,128)S(1)} collective-permute-done((f32[32,1]{1,0:T(8,128)S(1)}, f32[32,1]{1,0:T(8,128)S(1)}, u32[]{:S(2)}, u32[]{:S(2)}) %collective-permute-start.11) | collective-permute-done | bytes 160 | tf_op jit(solution)/shard_map/ppermute | solution.py:17
  (87 shorter events, 29.9 us)
Async XLA Ops:
  0.9 6.3 %copy-start.4 = (f32[1,256,64]{1,2,0:T(8,128)}, f32[1,256,64]{1,2,0:T(8,128)S(1)}, u32[]{:S(2)}) copy-start(f32[1,256,64]{1,2,0:T(8,128)S(1)} %get-tuple-element.28) | copy-start | bytes 196612
  1.0 6.3 %copy-start.6 = (f32[1,256,64]{1,2,0:T(8,128)}, f32[1,256,64]{1,2,0:T(8,128)S(1)}, u32[]{:S(2)}) copy-start(f32[1,256,64]{1,2,0:T(8,128)S(1)} %get-tuple-element.29) | copy-start | bytes 196612
  3.3 0.7 copy-start
  9.4 1.6 copy-start.2
  19.0 19.6 %collective-permute-start = (f32[256,2,32]{2,1,0:T(2,128)S(1)}, f32[256,2,32]{2,1,0:T(2,128)S(1)}, u32[]{:S(2)}, u32[]{:S(2)}) collective-permute-start(f32[256,2,32]{2,1,0:T(2,128)S(1)} %get-tuple-element.11), channel_id=1, source_target_pairs={{0,1},{1,2},{2,3},{3,0},{4,5},{5,6},{6,7},{7,4},{8,9},{9,10},{10,1... | collective-permute-start | bytes 196616 | tf_op jit(solution)/shard_map/ppermute | solution.py:77
  20.6 22.4 %collective-permute-start.1 = (f32[256,2,32]{2,1,0:T(2,128)S(1)}, f32[256,2,32]{2,1,0:T(2,128)S(1)}, u32[]{:S(2)}, u32[]{:S(2)}) collective-permute-start(f32[256,2,32]{2,1,0:T(2,128)S(1)} %get-tuple-element.13), channel_id=1, source_target_pairs={{0,2},{1,3},{2,0},{3,1},{4,6},{5,7},{6,4},{7,5},{8,10},{9,11},{10,... | collective-permute-start | bytes 196616 | tf_op jit(solution)/shard_map/ppermute | solution.py:77
  21.8 23.1 %collective-permute-start.2 = (f32[256,2,32]{2,1,0:T(2,128)S(1)}, f32[256,2,32]{2,1,0:T(2,128)}, u32[]{:S(2)}, u32[]{:S(2)}) collective-permute-start(f32[256,2,32]{2,1,0:T(2,128)S(1)} %get-tuple-element.12), channel_id=1, source_target_pairs={{0,3},{1,0},{2,1},{3,2},{4,7},{5,4},{6,5},{7,6},{8,11},{9,8},{10,9... | collective-permute-start | bytes 196616 | tf_op jit(solution)/shard_map/ppermute | solution.py:77
  38.5 4.5 %copy-start.8 = (f32[256,2,32]{2,1,0:T(2,128)}, f32[256,2,32]{2,1,0:T(2,128)S(1)}, u32[]{:S(2)}) copy-start(f32[256,2,32]{2,1,0:T(2,128)S(1)} %collective-permute-done) | copy-start | bytes 196612
  43.0 0.7 copy-start.9
  61.1 2.9 %collective-permute-start.3 = (f32[128,2,1024]{2,1,0:T(2,128)S(1)}, f32[128,2,1024]{2,1,0:T(2,128)}, u32[]{:S(2)}, u32[]{:S(2)}) collective-permute-start(f32[128,2,1024]{2,1,0:T(2,128)S(1)} %constant_dynamic-slice_fusion.1), channel_id=1, source_target_pairs={{0,4},{4,0},{8,12},{12,8},{16,20},{20,16},{24,28},{28,24},{1,5},{5... | collective-permute-start | bytes 3145736 | tf_op jit(solution)/shard_map/ppermute | solution.py:97
  83.1 16.4 %copy-start.10 = (s32[1024]{0:T(1024)S(1)}, s32[1024]{0:T(1024)}, u32[]{:S(2)}) copy-start(s32[1024]{0:T(1024)} %param.10) | copy-start | bytes 12292
  83.7 18.4 %copy-start.11 = (f32[1024]{0:T(1024)S(1)}, f32[1024]{0:T(1024)}, u32[]{:S(2)}) copy-start(f32[1024]{0:T(1024)} %param.11) | copy-start | bytes 12292
  99.5 2.7 %collective-permute-start.4 = (f32[128,2,1024]{2,1,0:T(2,128)S(1)}, f32[128,2,1024]{2,1,0:T(2,128)S(1)}, u32[]{:S(2)}, u32[]{:S(2)}) collective-permute-start(f32[128,2,1024]{2,1,0:T(2,128)S(1)} %all_to_all.11), channel_id=1, source_target_pairs={{0,4},{4,0},{8,12},{12,8},{16,20},{20,16},{24,28},{28,24},{1,5},{5... | collective-permute-start | bytes 3145736 | tf_op jit(solution)/shard_map/ppermute | solution.py:109
  120.3 20.4 %collective-permute-start.5 = (f32[256,2,32]{2,1,0:T(2,128)S(1)}, f32[256,2,32]{2,1,0:T(2,128)S(1)}, u32[]{:S(2)}, u32[]{:S(2)}) collective-permute-start(f32[256,2,32]{2,1,0:T(2,128)S(1)} %get-tuple-element.27), channel_id=1, source_target_pairs={{1,0},{2,1},{3,2},{0,3},{5,4},{6,5},{7,6},{4,7},{9,8},{10,9},{11,1... | collective-permute-start | bytes 196616 | tf_op jit(solution)/shard_map/ppermute | solution.py:84
  120.4 21.1 %collective-permute-start.6 = (f32[256,2,32]{2,1,0:T(2,128)S(1)}, f32[256,2,32]{2,1,0:T(2,128)S(1)}, u32[]{:S(2)}, u32[]{:S(2)}) collective-permute-start(f32[256,2,32]{2,1,0:T(2,128)S(1)} %get-tuple-element.27), channel_id=1, source_target_pairs={{2,0},{3,1},{0,2},{1,3},{6,4},{7,5},{4,6},{5,7},{10,8},{11,9},{8,1... | collective-permute-start | bytes 196616 | tf_op jit(solution)/shard_map/ppermute | solution.py:84
  122.6 22.8 %collective-permute-start.7 = (f32[256,2,32]{2,1,0:T(2,128)S(1)}, f32[256,2,32]{2,1,0:T(2,128)S(1)}, u32[]{:S(2)}, u32[]{:S(2)}) collective-permute-start(f32[256,2,32]{2,1,0:T(2,128)S(1)} %get-tuple-element.27), channel_id=1, source_target_pairs={{3,0},{0,1},{1,2},{2,3},{7,4},{4,5},{5,6},{6,7},{11,8},{8,9},{9,10... | collective-permute-start | bytes 196616 | tf_op jit(solution)/shard_map/ppermute | solution.py:84
  157.6 1.2 copy-start.3
  158.4 1.8 copy-start.5
  158.5 1.8 copy-start.7
  163.1 16.7 %copy-start.1 = (f32[32,16,128]{2,1,0:T(8,128)S(1)}, f32[32,16,128]{2,1,0:T(8,128)}, u32[]{:S(2)}) copy-start(f32[32,16,128]{2,1,0:T(8,128)} %copy-done) | copy-start | bytes 786436
  163.2 16.6 %collective-permute-start.8 = (f32[1,2048]{1,0:T(1,128)S(1)}, f32[1,2048]{1,0:T(1,128)S(1)}, u32[]{:S(2)}, u32[]{:S(2)}) collective-permute-start(f32[1,2048]{1,0:T(1,128)S(1)} %get-tuple-element.23), channel_id=1, source_target_pairs={{0,4},{4,8},{8,12},{12,16},{16,20},{20,24},{24,28},{1,5},{5,9},{9,... | collective-permute-start | bytes 24584 | tf_op jit(solution)/shard_map/ppermute | solution.py:16
  165.1 14.7 %collective-permute-start.9 = (f32[1,2048]{1,0:T(1,128)S(1)}, f32[1,2048]{1,0:T(1,128)S(1)}, u32[]{:S(2)}, u32[]{:S(2)}) collective-permute-start(f32[1,2048]{1,0:T(1,128)S(1)} %get-tuple-element.22), channel_id=1, source_target_pairs={{4,0},{8,4},{12,8},{16,12},{20,16},{24,20},{28,24},{5,1},{9,5},{13... | collective-permute-start | bytes 24584 | tf_op jit(solution)/shard_map/ppermute | solution.py:17
  169.7 7.9 %collective-permute-start.10 = (f32[32,1]{1,0:T(8,128)S(1)}, f32[32,1]{1,0:T(8,128)S(1)}, u32[]{:S(2)}, u32[]{:S(2)}) collective-permute-start(f32[32,1]{1,0:T(8,128)S(1)} %get-tuple-element.19), channel_id=1, source_target_pairs={{0,1},{1,2},{2,3},{4,5},{5,6},{6,7},{8,9},{9,10},{10,11},{12,13},{... | collective-permute-start | bytes 392 | tf_op jit(solution)/shard_map/ppermute | solution.py:16
  174.1 5.6 %collective-permute-start.11 = (f32[32,1]{1,0:T(8,128)S(1)}, f32[32,1]{1,0:T(8,128)S(1)}, u32[]{:S(2)}, u32[]{:S(2)}) collective-permute-start(f32[32,1]{1,0:T(8,128)S(1)} %get-tuple-element.18), channel_id=1, source_target_pairs={{1,0},{2,1},{3,2},{5,4},{6,5},{7,6},{9,8},{10,9},{11,10},{13,12},{... | collective-permute-start | bytes 392 | tf_op jit(solution)/shard_map/ppermute | solution.py:17

commit v5 on v4

--- a/solution.py
+++ b/solution.py
@@ -67,23 +67,16 @@
     return out.reshape(cycles, lon_width)
 
 
-def shifted_reduce_scatter(x, axis):
+def reduce_scatter(x, axis):
     count = lax.axis_size(axis)
-    me = lax.axis_index(axis)
-    size = x.shape[0] // count
-    total = lax.dynamic_slice_in_dim(x, me * size, size)
-    for shift in range(1, count):
-        chunk = lax.dynamic_slice_in_dim(x, (me + shift) % count * size, size)
-        total = total + lax.ppermute(chunk, axis, [(i, (i + shift) % count) for i in range(count)])
-    return total
+    moved = lax.all_to_all(x, axis, 0, 0, tiled=True)
+    return moved.reshape((count, x.shape[0] // count) + x.shape[1:]).sum(axis=0)
 
 
-def shifted_all_gather(x, axis):
+def all_gather(x, axis):
     count = lax.axis_size(axis)
-    me = lax.axis_index(axis)
-    ahead = [x] + [lax.ppermute(x, axis, [((i + shift) % count, i) for i in range(count)]) for shift in range(1, count)]
-    stacked = jnp.concatenate(ahead + ahead, axis=0)
-    return lax.dynamic_slice_in_dim(stacked, (count - me) % count * x.shape[0], count * x.shape[0])
+    copies = jnp.broadcast_to(x[None], (count,) + x.shape).reshape((count * x.shape[0],) + x.shape[1:])
+    return lax.all_to_all(copies, axis, 0, 0, tiled=True)
 
 
 def paired_reduce_scatter(x, axis):
@@ -123,7 +116,7 @@
         slot_order, lax.axis_index("lon") * slot_count, slot_count
     )
     forward_scale = lon_total ** (-0.5)
-    fourier = shifted_reduce_scatter(forward_dft(masked, slot_order, lon_start, lon_total) * forward_scale, "lon")
+    fourier = reduce_scatter(forward_dft(masked, slot_order, lon_start, lon_total) * forward_scale, "lon")
     coefficient = jnp.einsum("krl,kcr->kcl", legendre, fourier, precision=lax.Precision.HIGH)
     degree_whole = paired_all_gather(paired_reduce_scatter(coefficient, "lat"), "lat")
     degree_count = degree_whole.shape[2]
@@ -131,7 +124,7 @@
     retained = degrees[None, :] >= own_orders[:, None]
     spectrum = jnp.where(retained[:, None, :], love_gain[None, None, :] * degree_whole, 0.0)
     synthesis = jnp.einsum("krl,kcl->kcr", legendre, spectrum, precision=lax.Precision.HIGH)
-    summed = inverse_dft(shifted_all_gather(synthesis, "lon"), slot_order, lon_start, lon_width, lon_total)
+    summed = inverse_dft(all_gather(synthesis, "lon"), slot_order, lon_start, lon_width, lon_total)
     loading = summed * (2 * slot_total) ** (-0.5)
     potential = masked - 0.6 * loading
     neighbours = neighbour_sum(potential)

time: 181 us -> 159 us (0.88)
  waiting for transfers between devices: 45.8 us -> 20.1 us
  other arithmetic: 18.2 us -> 21.7 us
    ppermute x6 -> x0, waiting for transfers between devices: 39.1 us -> none  [the longest x3 20.6 us: shifted_reduce_scatter(): lax.ppermute(chunk, axis, [(i, (i + shift) % count) for i in range(count)])]
    all_to_all x0 -> x2, waiting for transfers between devices: none -> 14.5 us  [the longest x1 7.48 us: all_gather(): return lax.all_to_all(copies, axis, 0, 0, tiled=True)]
    all_to_all x0 -> x2, starting transfers between devices: none -> 10.6 us  [the longest x1 5.32 us: reduce_scatter(): moved = lax.all_to_all(x, axis, 0, 0, tiled=True)]
    ppermute x6 -> x0, starting transfers between devices: 9.76 us -> none  [the longest x3 5.09 us: shifted_all_gather(): lax.ppermute(x, axis, [((i + shift) % count, i) for i in range(count)])]
    all_to_all x0 -> x2, other arithmetic: none -> 2.74 us  [the longest x1 1.37 us: all_gather(): return lax.all_to_all(copies, axis, 0, 0, tiled=True)]
    ppermute x2, starting transfers between devices: 6.3 us -> 4.18 us  [halo(): lax.ppermute(tail, axis, [(i, (i + 1) % count) for i in range(ends)])]
    unnamed x30 -> x10, local copies, waits for them, and re-layouts: 5.76 us -> 6.04 us
  transfers between devices with their start and end apart: 12 -> 8, of which waited for: 8 -> 5; matrix products, arithmetic and copies ran while one was open for 2% -> 2% of each run, Pallas kernels for 0% -> 0%
where the time goes in v5:
time: 159 us; the launch traced here: 157 us
  matrix products  37.1 us (23%)
  blocking collectives  32.8 us (21%)
  starting transfers between devices  22.9 us (14%)
  local copies, waits for them, and re-layouts  21.8 us (14%)
  other arithmetic  21.7 us (14%)
  waiting for transfers between devices  20.1 us (13%)
    dot_general x1, matrix products, local(): jnp.einsum('krl,kcl->kcr', legendre, spectrum, precision=lax.Precision.HIGH)  17.7 us
    all_to_all x1, blocking collectives, paired_reduce_scatter(): lax.all_to_all(summed, axis, 0, 0, tiled=True, axis_index_groups=groups)  17.4 us
    dot_general x1, matrix products, local(): jnp.einsum('krl,kcr->kcl', legendre, fourier, precision=lax.Precision.HIGH)  15.8 us
    all_to_all x1, blocking collectives, paired_all_gather(): lax.all_to_all(copies, axis, 0, 0, tiled=True, axis_index_groups=groups)  15.4 us
    ppermute x2, starting transfers between devices, halo(): lax.ppermute(head, axis, [((i + 1) % count, i) for i in range(ends)])  8.12 us
    all_to_all x1, waiting for transfers between devices, all_gather(): return lax.all_to_all(copies, axis, 0, 0, tiled=True)  7.48 us
    all_to_all x1, waiting for transfers between devices, reduce_scatter(): moved = lax.all_to_all(x, axis, 0, 0, tiled=True)  7.05 us
    unnamed x10, local copies, waits for them, and re-layouts  6.04 us
  transfers between devices with their start and end apart: 8, of which 5 were waited for; matrix products, arithmetic and copies ran while one was open for 2% of the time, Pallas kernels for 0%

profile of v5, /device:TPU:12, one launch (start us, length us, event | category | flops | bytes accessed | tf_op | source)
XLA Modules:
  0.0 157.4 jit_solution(15531640624603717578)
XLA Ops:
  4.6 1.9 %convolution_bitcast_fusion = f32[2,256,32,32]{1,2,0,3:T(8,128)S(1)} fusion(f32[32,64,32]{2,1,0:T(8,128)S(1)} %reshape.167, f32[1,256,64]{1,2,0:T(8,128)S(1)} %get-tuple-element.23, f32[1,256,64]{1,2,0:T(8,128)S(1)} %get-tuple-element.24), kind=kOutput, calls=%fused_computation.23 | convolution fusion | flops 402685952 | bytes 2490368 | tf_op jit(solution)/shard_map/cua,rab->cubr/dot_general | solution.py:49
  10.6 3.6 %gather_fusion = f32[1024,2,32]{2,1,0:T(2,128)S(1)} fusion(f32[1024,2,32]{2,1,0:T(2,128)S(1)} %copy.48, s32[1024]{0:T(1024)S(1)} %fusion.38), kind=kCustom, calls=%fused_computation.clone | custom fusion | bytes 528384 | tf_op jit(solution)/shard_map/jit(_take)/gather | solution.py:54
  14.2 3.8 %select_multiply_fusion = f32[1024,2,32]{2,1,0:T(2,128)S(1)} fusion(f32[1024,2,32]{2,1,0:T(2,128)S(1)} %gather_fusion, pred[1024]{0:T(1024)(128)(4,1)S(1)} %compare_and_fusion.1), kind=kLoop, calls=%fused_computation.28 | loop fusion | flops 131072 | bytes 525312 | tf_op jit(solution)/shard_map/mul | solution.py:119
  18.0 1.8 %reshape.198 = f32[4,1,16384]{2,1,0:T(1,128)} reshape(f32[1024,2,32]{2,1,0:T(2,128)S(1)} %select_multiply_fusion) | data formatting | bytes 524288
  19.7 5.3 %all-to-all-start = ((f32[4,1,16384]{2,1,0:T(1,128)}), f32[4,1,16384]{2,1,0:T(1,128)S(1)}, u32[]{:S(2)}, u32[]{:S(2)}) async-start(f32[4,1,16384]{2,1,0:T(1,128)} %reshape.198), calls=%async_computation | async-start | bytes 524288 | tf_op jit(solution)/shard_map/all_to_all | solution.py:72
  25.0 7.0 %all-to-all-done = f32[4,1,16384]{2,1,0:T(1,128)S(1)} async-done(((f32[4,1,16384]{2,1,0:T(1,128)}), f32[4,1,16384]{2,1,0:T(1,128)S(1)}, u32[]{:S(2)}, u32[]{:S(2)}) %all-to-all-start) | async-done | bytes 262176 | tf_op jit(solution)/shard_map/all_to_all | solution.py:72
  35.7 15.8 %fusion.51 = f32[256,2,1024]{2,1,0:T(2,128)S(1)} fusion(f32[256,2,32]{2,1,0:T(2,128)S(1)} %reduce_sum.65, f32[256,32,1024]{2,1,0:T(8,128)} %param.9), kind=kOutput, calls=%fused_computation.85 | convolution fusion | flops 100663296 | bytes 35717120 | tf_op jit(solution)/shard_map/krl,kcr->kcl/dot_general | solution.py:120
  52.5 3.0 %collective-permute-done = f32[128,2,1024]{2,1,0:T(2,128)} collective-permute-done((f32[128,2,1024]{2,1,0:T(2,128)}, f32[128,2,1024]{2,1,0:T(2,128)}, u32[]{:S(2)}, u32[]{:S(2)}) %collective-permute-start) | collective-permute-done | bytes 1048608 | tf_op jit(solution)/shard_map/ppermute | solution.py:90
  55.5 1.8 %dynamic-slice_add_fusion = f32[128,2,1024]{2,1,0:T(2,128)S(1)} fusion(f32[128,2,1024]{2,1,0:T(2,128)} %collective-permute-done, f32[256,2,1024]{2,1,0:T(2,128)S(1)} %fusion.51, s32[]{:T(128)S(6)} %select_n.83), kind=kLoop, calls=%fused_computation.30 | loop fusion | flops 262144 | bytes 3145732 | tf_op jit(solution)/shard_map/add | solution.py:90
  57.3 17.4 %all_to_all.20 = f32[128,2,1024]{2,1,0:T(2,128)S(1)} all-to-all(f32[128,2,1024]{2,1,0:T(2,128)S(1)} %dynamic-slice_add_fusion), channel_id=1, replica_groups={{0,8,16,24},{4,12,20,28},{1,9,17,25},{5,13,21,29},{2,10,18,26},{6,14,22..., dimensions={0} | all-to-all | bytes 2097152 | tf_op jit(solution)/shard_map/all_to_all | solution.py:91
  75.6 15.4 %all_to_all.21 = f32[128,2,1024]{2,1,0:T(2,128)S(1)} all-to-all(f32[128,2,1024]{2,1,0:T(2,128)S(1)} %bitcast.50), channel_id=1, replica_groups={{0,8,16,24},{4,12,20,28},{1,9,17,25},{5,13,21,29},{2,10,18,26},{6,14,22..., dimensions={0} | all-to-all | bytes 2097152 | tf_op jit(solution)/shard_map/all_to_all | solution.py:101
  91.8 2.0 %collective-permute-done.1 = f32[128,2,1024]{2,1,0:T(2,128)} collective-permute-done((f32[128,2,1024]{2,1,0:T(2,128)S(1)}, f32[128,2,1024]{2,1,0:T(2,128)}, u32[]{:S(2)}, u32[]{:S(2)}) %collective-permute-start.1) | collective-permute-done | bytes 1048608 | tf_op jit(solution)/shard_map/ppermute | solution.py:102
  93.8 17.7 %fusion.2 = f32[256,2,32]{2,1,0:T(2,128)S(1)} fusion(f32[256,32,1024]{2,1,0:T(8,128)} %param.9, f32[128,2,1024]{2,1,0:T(2,128)} %collective-permute-done.1, f32[128,2,1024]{2,1,0:T(2,128)S(1)} %all_to_all.21, pred[]{:T(512)S(6)} %eq.25, pred[256,1024]{1,0:T(8,128)(4,1)S(1)} %iota_compare_fusion.1, f32[1024]{0:T(1024)S(1)} %copy-done.1), kind=kOutput, calls=%fused_computation.11 | convolution fusion | flops 103284736 | bytes 35983360 | tf_op jit(solution)/shard_map/krl,kcl->kcr/dot_general | solution.py:126
  111.8 1.8 %reshape.200 = f32[4,1,16384]{2,1,0:T(1,128)} reshape(f32[1024,2,32]{2,1,0:T(2,128)S(1)} %bitcast.49) | data formatting | bytes 524288
  113.6 5.2 %all-to-all-start.3 = ((f32[4,1,16384]{2,1,0:T(1,128)}), f32[4,1,16384]{2,1,0:T(1,128)S(1)}, u32[]{:S(2)}, u32[]{:S(2)}) async-start(f32[4,1,16384]{2,1,0:T(1,128)} %reshape.200), calls=%async_computation.3 | async-start | bytes 524288 | tf_op jit(solution)/shard_map/all_to_all | solution.py:79
  118.9 7.5 %all-to-all-done.3 = f32[4,1,16384]{2,1,0:T(1,128)S(1)} async-done(((f32[4,1,16384]{2,1,0:T(1,128)}), f32[4,1,16384]{2,1,0:T(1,128)S(1)}, u32[]{:S(2)}, u32[]{:S(2)}) %all-to-all-start.3) | async-done | bytes 262176 | tf_op jit(solution)/shard_map/all_to_all | solution.py:79
  128.7 3.6 %gather_fusion.1 = f32[1024,2,32]{2,1,0:T(2,128)S(1)} fusion(f32[1024,2,32]{2,1,0:T(2,128)S(1)} %reshape.201, s32[1024]{0:T(1024)S(1)} %fusion.39), kind=kCustom, calls=%fused_computation.1.clone | custom fusion | bytes 528384 | tf_op jit(solution)/shard_map/jit(_take)/gather | solution.py:62
  132.2 3.7 %broadcast_select_fusion = f32[1024,2,32]{2,1,0:T(2,128)S(1)} fusion(f32[1024,2,32]{2,1,0:T(2,128)S(1)} %gather_fusion.1, pred[1024]{0:T(1024)(128)(4,1)S(1)} %compare_and_fusion), kind=kLoop, calls=%fused_computation.33 | loop fusion | flops 65536 | bytes 525312 | tf_op jit(solution)/shard_map/jit(_take)/select_n | solution.py:62
  137.5 1.4 add_reduce_fusion
  138.9 1.8 %multiply_bitcast_fusion = (f32[32,64,32]{1,0,2:T(8,128)S(1)}, f32[32,64,32]{1,0,2:T(8,128)S(1)}) fusion(f32[1,256,64]{1,2,0:T(8,128)S(1)} %get-tuple-element.23, f32[1,256,64]{1,2,0:T(8,128)S(1)} %get-tuple-element.24, f32[1,256,32,32]{1,3,0,2:T(8,128)S(1)} %bitcast.47, f32[1,256,32,32]{1,3,0,2:T(8,128)S(1)} %bitcast.46), kind=kOutput, calls=%fused_computation.34 | convolution fusion | flops 403341312 | bytes 2752512 | tf_op jit(solution)/shard_map/cua,cubr->rab/dot_general | solution.py:66
  141.8 1.9 %collective-permute-start.2 = (f32[1,2048]{1,0:T(1,128)S(1)}, f32[1,2048]{1,0:T(1,128)S(1)}, u32[]{:S(2)}, u32[]{:S(2)}) collective-permute-start(f32[1,2048]{1,0:T(1,128)S(1)} %get-tuple-element.20), channel_id=1, source_target_pairs={{0,4},{4,8},{8,12},{12,16},{16,20},{20,24},{24,28},{1,5},{5,9},{9,... | collective-permute-start | bytes 24584 | tf_op jit(solution)/shard_map/ppermute | solution.py:16
  143.8 4.5 %collective-permute-start.3 = (f32[1,2048]{1,0:T(1,128)S(1)}, f32[1,2048]{1,0:T(1,128)S(1)}, u32[]{:S(2)}, u32[]{:S(2)}) collective-permute-start(f32[1,2048]{1,0:T(1,128)S(1)} %get-tuple-element.19), channel_id=1, source_target_pairs={{4,0},{8,4},{12,8},{16,12},{20,16},{24,20},{28,24},{5,1},{9,5},{13... | collective-permute-start | bytes 24584 | tf_op jit(solution)/shard_map/ppermute | solution.py:17
  148.4 2.3 %collective-permute-start.4 = (f32[32,1]{1,0:T(8,128)S(1)}, f32[32,1]{1,0:T(8,128)S(1)}, u32[]{:S(2)}, u32[]{:S(2)}) collective-permute-start(f32[32,1]{1,0:T(8,128)S(1)} %get-tuple-element.16), channel_id=1, source_target_pairs={{0,1},{1,2},{2,3},{4,5},{5,6},{6,7},{8,9},{9,10},{10,11},{12,13},{... | collective-permute-start | bytes 392 | tf_op jit(solution)/shard_map/ppermute | solution.py:16
  150.6 3.6 %collective-permute-start.5 = (f32[32,1]{1,0:T(8,128)S(1)}, f32[32,1]{1,0:T(8,128)S(1)}, u32[]{:S(2)}, u32[]{:S(2)}) collective-permute-start(f32[32,1]{1,0:T(8,128)S(1)} %get-tuple-element.15), channel_id=1, source_target_pairs={{1,0},{2,1},{3,2},{5,4},{6,5},{7,6},{9,8},{10,9},{11,10},{13,12},{... | collective-permute-start | bytes 392 | tf_op jit(solution)/shard_map/ppermute | solution.py:17
  (61 shorter events, 22.8 us)
Async XLA Ops:
  19.7 12.4 %all-to-all-start = ((f32[4,1,16384]{2,1,0:T(1,128)}), f32[4,1,16384]{2,1,0:T(1,128)S(1)}, u32[]{:S(2)}, u32[]{:S(2)}) async-start(f32[4,1,16384]{2,1,0:T(1,128)} %reshape.198), calls=%async_computation | async-start | bytes 524288 | tf_op jit(solution)/shard_map/all_to_all | solution.py:72
  52.5 3.0 %collective-permute-start = (f32[128,2,1024]{2,1,0:T(2,128)}, f32[128,2,1024]{2,1,0:T(2,128)}, u32[]{:S(2)}, u32[]{:S(2)}) collective-permute-start(f32[128,2,1024]{2,1,0:T(2,128)} %constant_dynamic-slice_fusion), channel_id=1, source_target_pairs={{0,4},{4,0},{8,12},{12,8},{16,20},{20,16},{24,28},{28,24},{1,5},{5... | collective-permute-start | bytes 3145736 | tf_op jit(solution)/shard_map/ppermute | solution.py:90
  57.3 33.7 %copy-start = (s32[1024]{0:T(1024)S(1)}, s32[1024]{0:T(1024)}, u32[]{:S(2)}) copy-start(s32[1024]{0:T(1024)} %param.10) | copy-start | bytes 12292
  57.3 36.5 %copy-start.1 = (f32[1024]{0:T(1024)S(1)}, f32[1024]{0:T(1024)}, u32[]{:S(2)}) copy-start(f32[1024]{0:T(1024)} %param.11) | copy-start | bytes 12292
  91.0 2.8 %collective-permute-start.1 = (f32[128,2,1024]{2,1,0:T(2,128)S(1)}, f32[128,2,1024]{2,1,0:T(2,128)}, u32[]{:S(2)}, u32[]{:S(2)}) collective-permute-start(f32[128,2,1024]{2,1,0:T(2,128)S(1)} %all_to_all.21), channel_id=1, source_target_pairs={{0,4},{4,0},{8,12},{12,8},{16,20},{20,16},{24,28},{28,24},{1,5},{5... | collective-permute-start | bytes 3145736 | tf_op jit(solution)/shard_map/ppermute | solution.py:102
  113.6 12.7 %all-to-all-start.3 = ((f32[4,1,16384]{2,1,0:T(1,128)}), f32[4,1,16384]{2,1,0:T(1,128)S(1)}, u32[]{:S(2)}, u32[]{:S(2)}) async-start(f32[4,1,16384]{2,1,0:T(1,128)} %reshape.200), calls=%async_computation.3 | async-start | bytes 524288 | tf_op jit(solution)/shard_map/all_to_all | solution.py:79
  141.8 14.6 %collective-permute-start.2 = (f32[1,2048]{1,0:T(1,128)S(1)}, f32[1,2048]{1,0:T(1,128)S(1)}, u32[]{:S(2)}, u32[]{:S(2)}) collective-permute-start(f32[1,2048]{1,0:T(1,128)S(1)} %get-tuple-element.20), channel_id=1, source_target_pairs={{0,4},{4,8},{8,12},{12,16},{16,20},{20,24},{24,28},{1,5},{5,9},{9,... | collective-permute-start | bytes 24584 | tf_op jit(solution)/shard_map/ppermute | solution.py:16
  143.8 12.7 %collective-permute-start.3 = (f32[1,2048]{1,0:T(1,128)S(1)}, f32[1,2048]{1,0:T(1,128)S(1)}, u32[]{:S(2)}, u32[]{:S(2)}) collective-permute-start(f32[1,2048]{1,0:T(1,128)S(1)} %get-tuple-element.19), channel_id=1, source_target_pairs={{4,0},{8,4},{12,8},{16,12},{20,16},{24,20},{28,24},{5,1},{9,5},{13... | collective-permute-start | bytes 24584 | tf_op jit(solution)/shard_map/ppermute | solution.py:17
  148.4 7.4 %collective-permute-start.4 = (f32[32,1]{1,0:T(8,128)S(1)}, f32[32,1]{1,0:T(8,128)S(1)}, u32[]{:S(2)}, u32[]{:S(2)}) collective-permute-start(f32[32,1]{1,0:T(8,128)S(1)} %get-tuple-element.16), channel_id=1, source_target_pairs={{0,1},{1,2},{2,3},{4,5},{5,6},{6,7},{8,9},{9,10},{10,11},{12,13},{... | collective-permute-start | bytes 392 | tf_op jit(solution)/shard_map/ppermute | solution.py:16
  150.6 5.8 %collective-permute-start.5 = (f32[32,1]{1,0:T(8,128)S(1)}, f32[32,1]{1,0:T(8,128)S(1)}, u32[]{:S(2)}, u32[]{:S(2)}) collective-permute-start(f32[32,1]{1,0:T(8,128)S(1)} %get-tuple-element.15), channel_id=1, source_target_pairs={{1,0},{2,1},{3,2},{5,4},{6,5},{7,6},{9,8},{10,9},{11,10},{13,12},{... | collective-permute-start | bytes 392 | tf_op jit(solution)/shard_map/ppermute | solution.py:17

commit v6 on v5

--- a/solution.py
+++ b/solution.py
@@ -51,7 +51,7 @@
     fc = (cb[..., None] * gc - sb[..., None] * gs).sum(axis=2)
     fs = (sb[..., None] * gc + cb[..., None] * gs).sum(axis=2)
     by_order = jnp.stack([fc, fs], axis=2).reshape(order_count, 2, cycles)
-    return jnp.take(by_order, slot_order, axis=0)
+    return jnp.take(by_order, slot_order, axis=0, mode="clip", unique_indices=True)
 
 
 def inverse_dft(synthesis, slot_order, lon_start, lon_width, lon_total):
@@ -59,7 +59,7 @@
     rotor, cb, sb = dft_tables(order_count, lon_start, lon_width, lon_total)
     slots = jnp.arange(order_count, dtype=jnp.int32)
     slot_of = jnp.where(slot_order[None, :] == slots[:, None], slots[None, :], 0).sum(axis=1)
-    by_order = jnp.take(synthesis, slot_of, axis=0).reshape(cb.shape[0], cb.shape[1], 2, cycles)
+    by_order = jnp.take(synthesis, slot_of, axis=0, mode="clip", unique_indices=True).reshape(cb.shape[0], cb.shape[1], 2, cycles)
     yc, ys = by_order[:, :, 0, None, :], by_order[:, :, 1, None, :]
     hc = (yc * cb[..., None] + ys * sb[..., None]).sum(axis=0)
     hs = (ys * cb[..., None] - yc * sb[..., None]).sum(axis=0)

time: 159 us -> 150 us (0.943)
  other arithmetic: 21.7 us -> 13.3 us
    select_n x1 -> x0, other arithmetic: 3.74 us -> none  [inverse_dft(): jnp.take(synthesis, slot_of, axis=0)]
    mul x1, other arithmetic: 3.76 us -> 0.54 us  [local(): forward_dft(masked, slot_order, lon_start, lon_total) * forward_scale]
    unnamed x10 -> x8, local copies, waits for them, and re-layouts: 6.04 us -> 5.39 us
where the time goes in v6:
time: 150 us; the launch traced here: 149 us
  matrix products  37.1 us (25%)
  blocking collectives  32.8 us (22%)
  starting transfers between devices  22.9 us (15%)
  local copies, waits for them, and re-layouts  21.4 us (14%)
  waiting for transfers between devices  20.1 us (13%)
  other arithmetic  13.3 us (9%)
    dot_general x1, matrix products, local(): jnp.einsum('krl,kcl->kcr', legendre, spectrum, precision=lax.Precision.HIGH)  17.7 us
    all_to_all x1, blocking collectives, paired_reduce_scatter(): lax.all_to_all(summed, axis, 0, 0, tiled=True, axis_index_groups=groups)  17.4 us
    dot_general x1, matrix products, local(): jnp.einsum('krl,kcr->kcl', legendre, fourier, precision=lax.Precision.HIGH)  15.8 us
    all_to_all x1, blocking collectives, paired_all_gather(): lax.all_to_all(copies, axis, 0, 0, tiled=True, axis_index_groups=groups)  15.4 us
    ppermute x2, starting transfers between devices, halo(): lax.ppermute(head, axis, [((i + 1) % count, i) for i in range(ends)])  8.11 us
    all_to_all x1, waiting for transfers between devices, reduce_scatter(): moved = lax.all_to_all(x, axis, 0, 0, tiled=True)  7.05 us
    all_to_all x1, waiting for transfers between devices, all_gather(): return lax.all_to_all(copies, axis, 0, 0, tiled=True)  6.98 us
    unnamed x8, local copies, waits for them, and re-layouts  5.39 us
  transfers between devices with their start and end apart: 8, of which 5 were waited for; matrix products, arithmetic and copies ran while one was open for 2% of the time, Pallas kernels for 0%

profile of v6, /device:TPU:12, one launch (start us, length us, event | category | flops | bytes accessed | tf_op | source)
XLA Modules:
  0.0 148.7 jit_solution(9127879315378934407)
XLA Ops:
  3.2 1.9 %convolution_bitcast_fusion = f32[2,256,32,32]{1,2,0,3:T(8,128)S(1)} fusion(f32[32,64,32]{2,1,0:T(8,128)S(1)} %reshape.162, f32[1,256,64]{1,2,0:T(8,128)S(1)} %get-tuple-element.22, f32[1,256,64]{1,2,0:T(8,128)S(1)} %get-tuple-element.23), kind=kOutput, calls=%fused_computation.23 | convolution fusion | flops 402685952 | bytes 2490368 | tf_op jit(solution)/shard_map/cua,rab->cubr/dot_general | solution.py:49
  9.3 3.6 %gather_fusion = f32[1024,2,32]{2,1,0:T(2,128)S(1)} fusion(f32[1024,2,32]{2,1,0:T(2,128)S(1)} %copy.39, s32[1024]{0:T(1024)S(1)} %broadcast_clamp_fusion.1), kind=kCustom, calls=%fused_computation | custom fusion | bytes 528384 | tf_op jit(solution)/shard_map/jit(_take)/gather | solution.py:54
  13.4 1.8 %reshape.189 = f32[4,1,16384]{2,1,0:T(1,128)} reshape(f32[1024,2,32]{2,1,0:T(2,128)S(1)} %broadcast_multiply_fusion) | data formatting | bytes 524288
  15.1 5.3 %all-to-all-start = ((f32[4,1,16384]{2,1,0:T(1,128)}), f32[4,1,16384]{2,1,0:T(1,128)S(1)}, u32[]{:S(2)}, u32[]{:S(2)}) async-start(f32[4,1,16384]{2,1,0:T(1,128)} %reshape.189), calls=%async_computation | async-start | bytes 524288 | tf_op jit(solution)/shard_map/all_to_all | solution.py:72
  20.5 7.0 %all-to-all-done = f32[4,1,16384]{2,1,0:T(1,128)S(1)} async-done(((f32[4,1,16384]{2,1,0:T(1,128)}), f32[4,1,16384]{2,1,0:T(1,128)S(1)}, u32[]{:S(2)}, u32[]{:S(2)}) %all-to-all-start) | async-done | bytes 262176 | tf_op jit(solution)/shard_map/all_to_all | solution.py:72
  28.0 1.4 reduce
  31.1 15.8 %fusion.49 = f32[256,2,1024]{2,1,0:T(2,128)S(1)} fusion(f32[256,2,32]{2,1,0:T(2,128)S(1)} %reduce_sum.65, f32[256,32,1024]{2,1,0:T(8,128)} %param.7), kind=kOutput, calls=%fused_computation.80 | convolution fusion | flops 100663296 | bytes 35717120 | tf_op jit(solution)/shard_map/krl,kcr->kcl/dot_general | solution.py:120
  48.0 3.0 %collective-permute-done = f32[128,2,1024]{2,1,0:T(2,128)} collective-permute-done((f32[128,2,1024]{2,1,0:T(2,128)}, f32[128,2,1024]{2,1,0:T(2,128)}, u32[]{:S(2)}, u32[]{:S(2)}) %collective-permute-start) | collective-permute-done | bytes 1048608 | tf_op jit(solution)/shard_map/ppermute | solution.py:90
  51.0 1.8 %dynamic-slice_add_fusion = f32[128,2,1024]{2,1,0:T(2,128)S(1)} fusion(f32[128,2,1024]{2,1,0:T(2,128)} %collective-permute-done, f32[256,2,1024]{2,1,0:T(2,128)S(1)} %fusion.49, s32[]{:T(128)S(6)} %select_n.76), kind=kLoop, calls=%fused_computation.29 | loop fusion | flops 262144 | bytes 3145732 | tf_op jit(solution)/shard_map/add | solution.py:90
  52.8 17.4 %all_to_all.20 = f32[128,2,1024]{2,1,0:T(2,128)S(1)} all-to-all(f32[128,2,1024]{2,1,0:T(2,128)S(1)} %dynamic-slice_add_fusion), channel_id=1, replica_groups={{0,8,16,24},{4,12,20,28},{1,9,17,25},{5,13,21,29},{2,10,18,26},{6,14,22..., dimensions={0} | all-to-all | bytes 2097152 | tf_op jit(solution)/shard_map/all_to_all | solution.py:91
  71.0 15.4 %all_to_all.21 = f32[128,2,1024]{2,1,0:T(2,128)S(1)} all-to-all(f32[128,2,1024]{2,1,0:T(2,128)S(1)} %bitcast.50), channel_id=1, replica_groups={{0,8,16,24},{4,12,20,28},{1,9,17,25},{5,13,21,29},{2,10,18,26},{6,14,22..., dimensions={0} | all-to-all | bytes 2097152 | tf_op jit(solution)/shard_map/all_to_all | solution.py:101
  86.8 2.5 %collective-permute-done.1 = f32[128,2,1024]{2,1,0:T(2,128)} collective-permute-done((f32[128,2,1024]{2,1,0:T(2,128)S(1)}, f32[128,2,1024]{2,1,0:T(2,128)}, u32[]{:S(2)}, u32[]{:S(2)}) %collective-permute-start.1) | collective-permute-done | bytes 1048608 | tf_op jit(solution)/shard_map/ppermute | solution.py:102
  89.3 17.7 %fusion.2 = f32[256,2,32]{2,1,0:T(2,128)S(1)} fusion(f32[256,32,1024]{2,1,0:T(8,128)} %param.7, f32[128,2,1024]{2,1,0:T(2,128)} %collective-permute-done.1, f32[128,2,1024]{2,1,0:T(2,128)S(1)} %all_to_all.21, pred[]{:T(512)S(6)} %eq.25, pred[256,1024]{1,0:T(8,128)(4,1)S(1)} %iota_compare_fusion.1, f32[1024]{0:T(1024)S(1)} %copy-done), kind=kOutput, calls=%fused_computation.11 | convolution fusion | flops 103284736 | bytes 35983360 | tf_op jit(solution)/shard_map/krl,kcl->kcr/dot_general | solution.py:126
  107.3 1.8 %reshape.191 = f32[4,1,16384]{2,1,0:T(1,128)} reshape(f32[1024,2,32]{2,1,0:T(2,128)S(1)} %bitcast.49) | data formatting | bytes 524288
  109.0 5.2 %all-to-all-start.3 = ((f32[4,1,16384]{2,1,0:T(1,128)}), f32[4,1,16384]{2,1,0:T(1,128)S(1)}, u32[]{:S(2)}, u32[]{:S(2)}) async-start(f32[4,1,16384]{2,1,0:T(1,128)} %reshape.191), calls=%async_computation.3 | async-start | bytes 524288 | tf_op jit(solution)/shard_map/all_to_all | solution.py:79
  114.8 7.0 %all-to-all-done.3 = f32[4,1,16384]{2,1,0:T(1,128)S(1)} async-done(((f32[4,1,16384]{2,1,0:T(1,128)}), f32[4,1,16384]{2,1,0:T(1,128)S(1)}, u32[]{:S(2)}, u32[]{:S(2)}) %all-to-all-start.3) | async-done | bytes 262176 | tf_op jit(solution)/shard_map/all_to_all | solution.py:79
  121.8 1.4 reduce.1
  124.1 3.6 %gather_fusion.1 = f32[1024,2,32]{2,1,0:T(2,128)S(1)} fusion(f32[1024,2,32]{2,1,0:T(2,128)S(1)} %reshape.192, s32[1024]{0:T(1024)S(1)} %broadcast_clamp_fusion), kind=kCustom, calls=%fused_computation.1 | custom fusion | bytes 528384 | tf_op jit(solution)/shard_map/jit(_take)/gather | solution.py:62
  128.8 1.4 add_reduce_fusion
  130.2 1.8 %multiply_bitcast_fusion = (f32[32,64,32]{1,0,2:T(8,128)S(1)}, f32[32,64,32]{1,0,2:T(8,128)S(1)}) fusion(f32[1,256,64]{1,2,0:T(8,128)S(1)} %get-tuple-element.22, f32[1,256,64]{1,2,0:T(8,128)S(1)} %get-tuple-element.23, f32[1,256,32,32]{1,3,0,2:T(8,128)S(1)} %bitcast.47, f32[1,256,32,32]{1,3,0,2:T(8,128)S(1)} %bitcast.46), kind=kOutput, calls=%fused_computation.32 | convolution fusion | flops 403341312 | bytes 2752512 | tf_op jit(solution)/shard_map/cua,cubr->rab/dot_general | solution.py:66
  133.1 1.9 %collective-permute-start.2 = (f32[1,2048]{1,0:T(1,128)S(1)}, f32[1,2048]{1,0:T(1,128)S(1)}, u32[]{:S(2)}, u32[]{:S(2)}) collective-permute-start(f32[1,2048]{1,0:T(1,128)S(1)} %get-tuple-element.19), channel_id=1, source_target_pairs={{0,4},{4,8},{8,12},{12,16},{16,20},{20,24},{24,28},{1,5},{5,9},{9,... | collective-permute-start | bytes 24584 | tf_op jit(solution)/shard_map/ppermute | solution.py:16
  135.0 4.5 %collective-permute-start.3 = (f32[1,2048]{1,0:T(1,128)S(1)}, f32[1,2048]{1,0:T(1,128)S(1)}, u32[]{:S(2)}, u32[]{:S(2)}) collective-permute-start(f32[1,2048]{1,0:T(1,128)S(1)} %get-tuple-element.18), channel_id=1, source_target_pairs={{4,0},{8,4},{12,8},{16,12},{20,16},{24,20},{28,24},{5,1},{9,5},{13... | collective-permute-start | bytes 24584 | tf_op jit(solution)/shard_map/ppermute | solution.py:17
  139.7 2.3 %collective-permute-start.4 = (f32[32,1]{1,0:T(8,128)S(1)}, f32[32,1]{1,0:T(8,128)S(1)}, u32[]{:S(2)}, u32[]{:S(2)}) collective-permute-start(f32[32,1]{1,0:T(8,128)S(1)} %get-tuple-element.15), channel_id=1, source_target_pairs={{0,1},{1,2},{2,3},{4,5},{5,6},{6,7},{8,9},{9,10},{10,11},{12,13},{... | collective-permute-start | bytes 392 | tf_op jit(solution)/shard_map/ppermute | solution.py:16
  141.9 3.6 %collective-permute-start.5 = (f32[32,1]{1,0:T(8,128)S(1)}, f32[32,1]{1,0:T(8,128)S(1)}, u32[]{:S(2)}, u32[]{:S(2)}) collective-permute-start(f32[32,1]{1,0:T(8,128)S(1)} %get-tuple-element.14), channel_id=1, source_target_pairs={{1,0},{2,1},{3,2},{5,4},{6,5},{7,6},{9,8},{10,9},{11,10},{13,12},{... | collective-permute-start | bytes 392 | tf_op jit(solution)/shard_map/ppermute | solution.py:17
  (56 shorter events, 18.8 us)
Async XLA Ops:
  5.9 3.4 %copy-start.1 = (s32[1024]{0:T(1024)S(1)}, s32[1024]{0:T(1024)}, u32[]{:S(2)}) copy-start(s32[1024]{0:T(1024)} %param.8) | copy-start | bytes 12292
  15.1 12.4 %all-to-all-start = ((f32[4,1,16384]{2,1,0:T(1,128)}), f32[4,1,16384]{2,1,0:T(1,128)S(1)}, u32[]{:S(2)}, u32[]{:S(2)}) async-start(f32[4,1,16384]{2,1,0:T(1,128)} %reshape.189), calls=%async_computation | async-start | bytes 524288 | tf_op jit(solution)/shard_map/all_to_all | solution.py:72
  48.0 3.0 %collective-permute-start = (f32[128,2,1024]{2,1,0:T(2,128)}, f32[128,2,1024]{2,1,0:T(2,128)}, u32[]{:S(2)}, u32[]{:S(2)}) collective-permute-start(f32[128,2,1024]{2,1,0:T(2,128)} %constant_dynamic-slice_fusion), channel_id=1, source_target_pairs={{0,4},{4,0},{8,12},{12,8},{16,20},{20,16},{24,28},{28,24},{1,5},{5... | collective-permute-start | bytes 3145736 | tf_op jit(solution)/shard_map/ppermute | solution.py:90
  52.7 36.5 %copy-start = (f32[1024]{0:T(1024)S(1)}, f32[1024]{0:T(1024)}, u32[]{:S(2)}) copy-start(f32[1024]{0:T(1024)} %param.9) | copy-start | bytes 12292
  86.5 2.8 %collective-permute-start.1 = (f32[128,2,1024]{2,1,0:T(2,128)S(1)}, f32[128,2,1024]{2,1,0:T(2,128)}, u32[]{:S(2)}, u32[]{:S(2)}) collective-permute-start(f32[128,2,1024]{2,1,0:T(2,128)S(1)} %all_to_all.21), channel_id=1, source_target_pairs={{0,4},{4,0},{8,12},{12,8},{16,20},{20,16},{24,28},{28,24},{1,5},{5... | collective-permute-start | bytes 3145736 | tf_op jit(solution)/shard_map/ppermute | solution.py:102
  109.0 12.7 %all-to-all-start.3 = ((f32[4,1,16384]{2,1,0:T(1,128)}), f32[4,1,16384]{2,1,0:T(1,128)S(1)}, u32[]{:S(2)}, u32[]{:S(2)}) async-start(f32[4,1,16384]{2,1,0:T(1,128)} %reshape.191), calls=%async_computation.3 | async-start | bytes 524288 | tf_op jit(solution)/shard_map/all_to_all | solution.py:79
  133.1 14.6 %collective-permute-start.2 = (f32[1,2048]{1,0:T(1,128)S(1)}, f32[1,2048]{1,0:T(1,128)S(1)}, u32[]{:S(2)}, u32[]{:S(2)}) collective-permute-start(f32[1,2048]{1,0:T(1,128)S(1)} %get-tuple-element.19), channel_id=1, source_target_pairs={{0,4},{4,8},{8,12},{12,16},{16,20},{20,24},{24,28},{1,5},{5,9},{9,... | collective-permute-start | bytes 24584 | tf_op jit(solution)/shard_map/ppermute | solution.py:16
  135.0 12.7 %collective-permute-start.3 = (f32[1,2048]{1,0:T(1,128)S(1)}, f32[1,2048]{1,0:T(1,128)S(1)}, u32[]{:S(2)}, u32[]{:S(2)}) collective-permute-start(f32[1,2048]{1,0:T(1,128)S(1)} %get-tuple-element.18), channel_id=1, source_target_pairs={{4,0},{8,4},{12,8},{16,12},{20,16},{24,20},{28,24},{5,1},{9,5},{13... | collective-permute-start | bytes 24584 | tf_op jit(solution)/shard_map/ppermute | solution.py:17
  139.7 7.4 %collective-permute-start.4 = (f32[32,1]{1,0:T(8,128)S(1)}, f32[32,1]{1,0:T(8,128)S(1)}, u32[]{:S(2)}, u32[]{:S(2)}) collective-permute-start(f32[32,1]{1,0:T(8,128)S(1)} %get-tuple-element.15), channel_id=1, source_target_pairs={{0,1},{1,2},{2,3},{4,5},{5,6},{6,7},{8,9},{9,10},{10,11},{12,13},{... | collective-permute-start | bytes 392 | tf_op jit(solution)/shard_map/ppermute | solution.py:16
  141.9 5.8 %collective-permute-start.5 = (f32[32,1]{1,0:T(8,128)S(1)}, f32[32,1]{1,0:T(8,128)S(1)}, u32[]{:S(2)}, u32[]{:S(2)}) collective-permute-start(f32[32,1]{1,0:T(8,128)S(1)} %get-tuple-element.14), channel_id=1, source_target_pairs={{1,0},{2,1},{3,2},{5,4},{6,5},{7,6},{9,8},{10,9},{11,10},{13,12},{... | collective-permute-start | bytes 392 | tf_op jit(solution)/shard_map/ppermute | solution.py:17

commit v7 on v6

--- a/solution.py
+++ b/solution.py
@@ -79,28 +79,30 @@
     return lax.all_to_all(copies, axis, 0, 0, tiled=True)
 
 
-def paired_reduce_scatter(x, axis):
+def halving_reduce_scatter(x, axis):
     count = lax.axis_size(axis)
-    pairs = [(i, i ^ 1) for i in range(count)]
-    groups = [list(range(side, count, 2)) for side in (0, 1)]
-    side = lax.axis_index(axis) % 2
-    half = x.shape[0] // 2
-    kept = lax.dynamic_slice_in_dim(x, side * half, half)
-    sent = lax.dynamic_slice_in_dim(x, (1 - side) * half, half)
-    summed = kept + lax.ppermute(sent, axis, pairs)
-    moved = lax.all_to_all(summed, axis, 0, 0, tiled=True, axis_index_groups=groups)
-    return moved.reshape((count // 2, half * 2 // count) + x.shape[1:]).sum(axis=0)
+    me = lax.axis_index(axis)
+    step = 1
+    while step < count:
+        half = x.shape[0] // 2
+        bit = me // step % 2
+        kept = lax.dynamic_slice_in_dim(x, bit * half, half)
+        sent = lax.dynamic_slice_in_dim(x, (1 - bit) * half, half)
+        x = kept + lax.ppermute(sent, axis, [(i, i ^ step) for i in range(count)])
+        step *= 2
+    return x
 
 
-def paired_all_gather(x, axis):
+def doubling_all_gather(x, axis):
     count = lax.axis_size(axis)
-    pairs = [(i, i ^ 1) for i in range(count)]
-    groups = [list(range(side, count, 2)) for side in (0, 1)]
-    side = lax.axis_index(axis) % 2
-    copies = jnp.broadcast_to(x[None], (count // 2,) + x.shape).reshape((count // 2 * x.shape[0],) + x.shape[1:])
-    half = lax.all_to_all(copies, axis, 0, 0, tiled=True, axis_index_groups=groups)
-    other = lax.ppermute(half, axis, pairs)
-    return jnp.where(side == 0, jnp.concatenate([half, other]), jnp.concatenate([other, half]))
+    me = lax.axis_index(axis)
+    step = count // 2
+    while step >= 1:
+        bit = me // step % 2
+        other = lax.ppermute(x, axis, [(i, i ^ step) for i in range(count)])
+        x = jnp.where(bit == 0, jnp.concatenate([x, other]), jnp.concatenate([other, x]))
+        step //= 2
+    return x
 
 
 def local(surface, wet_blocks, legendre, slot_order, love_gain):
@@ -118,7 +120,7 @@
     forward_scale = lon_total ** (-0.5)
     fourier = reduce_scatter(forward_dft(masked, slot_order, lon_start, lon_total) * forward_scale, "lon")
     coefficient = jnp.einsum("krl,kcr->kcl", legendre, fourier, precision=lax.Precision.HIGH)
-    degree_whole = paired_all_gather(paired_reduce_scatter(coefficient, "lat"), "lat")
+    degree_whole = doubling_all_gather(halving_reduce_scatter(coefficient, "lat"), "lat")
     degree_count = degree_whole.shape[2]
     degrees = jnp.arange(degree_count, dtype=jnp.int32)
     retained = degrees[None, :] >= own_orders[:, None]

time: 150 us -> 157 us (1.047)
  waiting for transfers between devices: 20.1 us -> 55.1 us
  blocking collectives: 32.8 us -> 0 us
  starting transfers between devices: 22.9 us -> 27.4 us
    ppermute x2 -> x6, waiting for transfers between devices: 5.49 us -> 40.4 us  [the longest x3 22.2 us: halving_reduce_scatter(): x = kept + lax.ppermute(sent, axis, [(i, i ^ step) for i in range(count)])]
    all_to_all x2 -> x0, blocking collectives: 32.8 us -> none  [the longest x1 17.4 us: paired_reduce_scatter(): lax.all_to_all(summed, axis, 0, 0, tiled=True, axis_index_groups=groups)]
    ppermute x2 -> x6, starting transfers between devices: 0.01 us -> 4.42 us  [the longest x3 2.21 us: halving_reduce_scatter(): x = kept + lax.ppermute(sent, axis, [(i, i ^ step) for i in range(count)])]
    unnamed x8 -> x24, local copies, waits for them, and re-layouts: 5.39 us -> 6.12 us
  transfers between devices with their start and end apart: 8 -> 12, of which waited for: 5 -> 9; matrix products, arithmetic and copies ran while one was open for 2% -> 2% of each run, Pallas kernels for 0% -> 0%
where the time goes in v7:
time: 157 us; the launch traced here: 155 us
  waiting for transfers between devices  55.1 us (35%)
  matrix products  36.9 us (24%)
  starting transfers between devices  27.4 us (17%)
  local copies, waits for them, and re-layouts  20.9 us (13%)
  other arithmetic  13.9 us (9%)
    ppermute x3, waiting for transfers between devices, halving_reduce_scatter(): x = kept + lax.ppermute(sent, axis, [(i, i ^ step) for i in range(count)])  22.2 us
    ppermute x3, waiting for transfers between devices, doubling_all_gather(): other = lax.ppermute(x, axis, [(i, i ^ step) for i in range(count)])  18.2 us
    dot_general x1, matrix products, local(): jnp.einsum('krl,kcl->kcr', legendre, spectrum, precision=lax.Precision.HIGH)  17.4 us
    dot_general x1, matrix products, local(): jnp.einsum('krl,kcr->kcl', legendre, fourier, precision=lax.Precision.HIGH)  15.8 us
    ppermute x2, starting transfers between devices, halo(): lax.ppermute(head, axis, [((i + 1) % count, i) for i in range(ends)])  8.11 us
    all_to_all x1, waiting for transfers between devices, reduce_scatter(): moved = lax.all_to_all(x, axis, 0, 0, tiled=True)  7.05 us
    all_to_all x1, waiting for transfers between devices, all_gather(): return lax.all_to_all(copies, axis, 0, 0, tiled=True)  6.98 us
    unnamed x24, local copies, waits for them, and re-layouts  6.12 us
  transfers between devices with their start and end apart: 12, of which 9 were waited for; matrix products, arithmetic and copies ran while one was open for 2% of the time, Pallas kernels for 0%

profile of v7, /device:TPU:12, one launch (start us, length us, event | category | flops | bytes accessed | tf_op | source)
XLA Modules:
  0.0 155.4 jit_solution(2996153358365395431)
XLA Ops:
  4.0 1.8 %convolution_bitcast_fusion = f32[2,256,32,32]{1,2,0,3:T(8,128)S(1)} fusion(f32[32,64,32]{2,1,0:T(8,128)S(1)} %reshape.155, f32[1,256,64]{1,2,0:T(8,128)S(1)} %get-tuple-element.22, f32[1,256,64]{1,2,0:T(8,128)S(1)} %get-tuple-element.23), kind=kOutput, calls=%fused_computation.23 | convolution fusion | flops 402685952 | bytes 2490368 | tf_op jit(solution)/shard_map/cua,rab->cubr/dot_general | solution.py:49
  10.0 3.6 %gather_fusion = f32[1024,2,32]{2,1,0:T(2,128)S(1)} fusion(f32[1024,2,32]{2,1,0:T(2,128)S(1)} %copy.39, s32[1024]{0:T(1024)S(1)} %broadcast_clamp_fusion.1), kind=kCustom, calls=%fused_computation | custom fusion | bytes 528384 | tf_op jit(solution)/shard_map/jit(_take)/gather | solution.py:54
  14.2 1.8 %reshape.180 = f32[4,1,16384]{2,1,0:T(1,128)} reshape(f32[1024,2,32]{2,1,0:T(2,128)S(1)} %broadcast_multiply_fusion) | data formatting | bytes 524288
  15.9 5.3 %all-to-all-start = ((f32[4,1,16384]{2,1,0:T(1,128)}), f32[4,1,16384]{2,1,0:T(1,128)S(1)}, u32[]{:S(2)}, u32[]{:S(2)}) async-start(f32[4,1,16384]{2,1,0:T(1,128)} %reshape.180), calls=%async_computation | async-start | bytes 524288 | tf_op jit(solution)/shard_map/all_to_all | solution.py:72
  21.2 7.0 %all-to-all-done = f32[4,1,16384]{2,1,0:T(1,128)S(1)} async-done(((f32[4,1,16384]{2,1,0:T(1,128)}), f32[4,1,16384]{2,1,0:T(1,128)S(1)}, u32[]{:S(2)}, u32[]{:S(2)}) %all-to-all-start) | async-done | bytes 262176 | tf_op jit(solution)/shard_map/all_to_all | solution.py:72
  31.9 15.8 %fusion.49 = f32[256,2,1024]{2,1,0:T(2,128)S(1)} fusion(f32[256,2,32]{2,1,0:T(2,128)S(1)} %reduce_sum.56, f32[256,32,1024]{2,1,0:T(8,128)} %param.7), kind=kOutput, calls=%fused_computation.86 | convolution fusion | flops 100663296 | bytes 35717120 | tf_op jit(solution)/shard_map/krl,kcr->kcl/dot_general | solution.py:122
  47.9 2.7 %collective-permute-done = f32[128,2,1024]{2,1,0:T(2,128)} collective-permute-done((f32[128,2,1024]{2,1,0:T(2,128)S(1)}, f32[128,2,1024]{2,1,0:T(2,128)}, u32[]{:S(2)}, u32[]{:S(2)}) %collective-permute-start) | collective-permute-done | bytes 1048608 | tf_op jit(solution)/shard_map/ppermute | solution.py:91
  50.6 1.8 %dynamic-slice_add_fusion = f32[128,2,1024]{2,1,0:T(2,128)S(1)} fusion(f32[128,2,1024]{2,1,0:T(2,128)} %collective-permute-done, f32[256,2,1024]{2,1,0:T(2,128)S(1)} %fusion.49, s32[]{:T(128)S(6)} %select_n.133), kind=kLoop, calls=%fused_computation.30 | loop fusion | flops 262144 | bytes 3145732 | tf_op jit(solution)/shard_map/add | solution.py:91
  52.5 1.6 %collective-permute-start.1 = (f32[64,2,1024]{2,1,0:T(2,128)S(1)}, f32[64,2,1024]{2,1,0:T(2,128)S(1)}, u32[]{:S(2)}, u32[]{:S(2)}) collective-permute-start(f32[64,2,1024]{2,1,0:T(2,128)S(1)} %constant_dynamic-slice_fusion.1), channel_id=1, source_target_pairs={{0,8},{4,12},{8,0},{12,4},{16,24},{20,28},{24,16},{28,20},{1,9},{5... | collective-permute-start | bytes 1572872 | tf_op jit(solution)/shard_map/ppermute | solution.py:91
  54.0 12.5 %collective-permute-done.1 = f32[64,2,1024]{2,1,0:T(2,128)S(1)} collective-permute-done((f32[64,2,1024]{2,1,0:T(2,128)S(1)}, f32[64,2,1024]{2,1,0:T(2,128)S(1)}, u32[]{:S(2)}, u32[]{:S(2)}) %collective-permute-start.1) | collective-permute-done | bytes 524320 | tf_op jit(solution)/shard_map/ppermute | solution.py:91
  67.4 7.0 %collective-permute-done.2 = f32[32,2,1024]{2,1,0:T(2,128)S(1)} collective-permute-done((f32[32,2,1024]{2,1,0:T(2,128)S(1)}, f32[32,2,1024]{2,1,0:T(2,128)S(1)}, u32[]{:S(2)}, u32[]{:S(2)}) %collective-permute-start.2) | collective-permute-done | bytes 262176 | tf_op jit(solution)/shard_map/ppermute | solution.py:91
  75.1 6.1 %collective-permute-done.3 = f32[32,2,1024]{2,1,0:T(2,128)S(1)} collective-permute-done((f32[32,2,1024]{2,1,0:T(2,128)S(1)}, f32[32,2,1024]{2,1,0:T(2,128)S(1)}, u32[]{:S(2)}, u32[]{:S(2)}) %collective-permute-start.3) | collective-permute-done | bytes 262176 | tf_op jit(solution)/shard_map/ppermute | solution.py:102
  83.0 9.8 %collective-permute-done.4 = f32[64,2,1024]{2,1,0:T(2,128)S(1)} collective-permute-done((f32[64,2,1024]{2,1,0:T(2,128)S(1)}, f32[64,2,1024]{2,1,0:T(2,128)S(1)}, u32[]{:S(2)}, u32[]{:S(2)}) %collective-permute-start.4) | collective-permute-done | bytes 524320 | tf_op jit(solution)/shard_map/ppermute | solution.py:102
  93.8 2.3 %collective-permute-done.5 = f32[128,2,1024]{2,1,0:T(2,128)S(1)} collective-permute-done((f32[128,2,1024]{2,1,0:T(2,128)S(1)}, f32[128,2,1024]{2,1,0:T(2,128)S(1)}, u32[]{:S(2)}, u32[]{:S(2)}) %collective-permute-start.5) | collective-permute-done | bytes 1048608 | tf_op jit(solution)/shard_map/ppermute | solution.py:102
  96.1 17.4 %fusion.2 = f32[256,2,32]{2,1,0:T(2,128)S(1)} fusion(f32[256,32,1024]{2,1,0:T(8,128)} %param.7, f32[128,2,1024]{2,1,0:T(2,128)S(1)} %collective-permute-done.5, f32[128,2,1024]{2,1,0:T(2,128)S(1)} %maximum_select_fusion.1, pred[]{:T(512)S(6)} %eq.35, pred[256,1024]{1,0:T(8,128)(4,1)S(1)} %iota_compare_fusion.1, f32[1024]{0:T(1024)S(1)} %copy-done.8), kind=kOutput, calls=%fused_computation.11 | convolution fusion | flops 103284736 | bytes 35983360 | tf_op jit(solution)/shard_map/krl,kcl->kcr/dot_general | solution.py:128
  113.8 1.8 %reshape.182 = f32[4,1,16384]{2,1,0:T(1,128)} reshape(f32[1024,2,32]{2,1,0:T(2,128)S(1)} %bitcast.47) | data formatting | bytes 524288
  115.6 5.4 %all-to-all-start.1 = ((f32[4,1,16384]{2,1,0:T(1,128)}), f32[4,1,16384]{2,1,0:T(1,128)S(1)}, u32[]{:S(2)}, u32[]{:S(2)}) async-start(f32[4,1,16384]{2,1,0:T(1,128)} %reshape.182), calls=%async_computation.1 | async-start | bytes 524288 | tf_op jit(solution)/shard_map/all_to_all | solution.py:79
  121.5 7.0 %all-to-all-done.1 = f32[4,1,16384]{2,1,0:T(1,128)S(1)} async-done(((f32[4,1,16384]{2,1,0:T(1,128)}), f32[4,1,16384]{2,1,0:T(1,128)S(1)}, u32[]{:S(2)}, u32[]{:S(2)}) %all-to-all-start.1) | async-done | bytes 262176 | tf_op jit(solution)/shard_map/all_to_all | solution.py:79
  130.8 3.6 %gather_fusion.1 = f32[1024,2,32]{2,1,0:T(2,128)S(1)} fusion(f32[1024,2,32]{2,1,0:T(2,128)S(1)} %reshape.183, s32[1024]{0:T(1024)S(1)} %broadcast_clamp_fusion), kind=kCustom, calls=%fused_computation.1 | custom fusion | bytes 528384 | tf_op jit(solution)/shard_map/jit(_take)/gather | solution.py:62
  136.9 1.8 %multiply_bitcast_fusion = (f32[32,64,32]{1,0,2:T(8,128)S(1)}, f32[32,64,32]{1,0,2:T(8,128)S(1)}) fusion(f32[1,256,64]{1,2,0:T(8,128)S(1)} %copy-done.5, f32[1,256,64]{1,2,0:T(8,128)S(1)} %copy-done.7, f32[1,256,32,32]{1,3,0,2:T(8,128)S(1)} %bitcast.45, f32[1,256,32,32]{1,3,0,2:T(8,128)S(1)} %bitcast.44), kind=kOutput, calls=%fused_computation.34 | convolution fusion | flops 403341312 | bytes 2752512 | tf_op jit(solution)/shard_map/cua,cubr->rab/dot_general | solution.py:66
  139.9 1.9 %collective-permute-start.6 = (f32[1,2048]{1,0:T(1,128)S(1)}, f32[1,2048]{1,0:T(1,128)S(1)}, u32[]{:S(2)}, u32[]{:S(2)}) collective-permute-start(f32[1,2048]{1,0:T(1,128)S(1)} %get-tuple-element.19), channel_id=1, source_target_pairs={{0,4},{4,8},{8,12},{12,16},{16,20},{20,24},{24,28},{1,5},{5,9},{9,... | collective-permute-start | bytes 24584 | tf_op jit(solution)/shard_map/ppermute | solution.py:16
  141.8 4.5 %collective-permute-start.7 = (f32[1,2048]{1,0:T(1,128)S(1)}, f32[1,2048]{1,0:T(1,128)S(1)}, u32[]{:S(2)}, u32[]{:S(2)}) collective-permute-start(f32[1,2048]{1,0:T(1,128)S(1)} %get-tuple-element.18), channel_id=1, source_target_pairs={{4,0},{8,4},{12,8},{16,12},{20,16},{24,20},{28,24},{5,1},{9,5},{13... | collective-permute-start | bytes 24584 | tf_op jit(solution)/shard_map/ppermute | solution.py:17
  146.4 2.3 %collective-permute-start.8 = (f32[32,1]{1,0:T(8,128)S(1)}, f32[32,1]{1,0:T(8,128)S(1)}, u32[]{:S(2)}, u32[]{:S(2)}) collective-permute-start(f32[32,1]{1,0:T(8,128)S(1)} %get-tuple-element.15), channel_id=1, source_target_pairs={{0,1},{1,2},{2,3},{4,5},{5,6},{6,7},{8,9},{9,10},{10,11},{12,13},{... | collective-permute-start | bytes 392 | tf_op jit(solution)/shard_map/ppermute | solution.py:16
  148.7 3.6 %collective-permute-start.9 = (f32[32,1]{1,0:T(8,128)S(1)}, f32[32,1]{1,0:T(8,128)S(1)}, u32[]{:S(2)}, u32[]{:S(2)}) collective-permute-start(f32[32,1]{1,0:T(8,128)S(1)} %get-tuple-element.14), channel_id=1, source_target_pairs={{1,0},{2,1},{3,2},{5,4},{6,5},{7,6},{9,8},{10,9},{11,10},{13,12},{... | collective-permute-start | bytes 392 | tf_op jit(solution)/shard_map/ppermute | solution.py:17
  (82 shorter events, 26.0 us)
Async XLA Ops:
  0.9 3.1 %copy-start.4 = (f32[1,256,64]{1,2,0:T(8,128)}, f32[1,256,64]{1,2,0:T(8,128)S(1)}, u32[]{:S(2)}) copy-start(f32[1,256,64]{1,2,0:T(8,128)S(1)} %get-tuple-element.22) | copy-start | bytes 196612
  0.9 3.1 %copy-start.6 = (f32[1,256,64]{1,2,0:T(8,128)}, f32[1,256,64]{1,2,0:T(8,128)S(1)}, u32[]{:S(2)}) copy-start(f32[1,256,64]{1,2,0:T(8,128)S(1)} %get-tuple-element.23) | copy-start | bytes 196612
  1.9 0.7 copy-start
  6.6 3.4 %copy-start.9 = (s32[1024]{0:T(1024)S(1)}, s32[1024]{0:T(1024)}, u32[]{:S(2)}) copy-start(s32[1024]{0:T(1024)} %param.8) | copy-start | bytes 12292
  7.9 6.3 %copy-start.2 = (f32[4,256,32]{1,2,0:T(8,128)}, f32[4,256,32]{1,2,0:T(8,128)S(1)}, u32[]{:S(2)}) copy-start(f32[4,256,32]{1,2,0:T(8,128)S(1)} %get-tuple-element.21) | copy-start | bytes 393220
  15.9 12.4 %all-to-all-start = ((f32[4,1,16384]{2,1,0:T(1,128)}), f32[4,1,16384]{2,1,0:T(1,128)S(1)}, u32[]{:S(2)}, u32[]{:S(2)}) async-start(f32[4,1,16384]{2,1,0:T(1,128)} %reshape.180), calls=%async_computation | async-start | bytes 524288 | tf_op jit(solution)/shard_map/all_to_all | solution.py:72
  47.8 2.9 %collective-permute-start = (f32[128,2,1024]{2,1,0:T(2,128)S(1)}, f32[128,2,1024]{2,1,0:T(2,128)}, u32[]{:S(2)}, u32[]{:S(2)}) collective-permute-start(f32[128,2,1024]{2,1,0:T(2,128)S(1)} %constant_dynamic-slice_fusion.2), channel_id=1, source_target_pairs={{0,4},{4,0},{8,12},{12,8},{16,20},{20,16},{24,28},{28,24},{1,5},{5... | collective-permute-start | bytes 3145736 | tf_op jit(solution)/shard_map/ppermute | solution.py:91
  52.4 43.7 %copy-start.8 = (f32[1024]{0:T(1024)S(1)}, f32[1024]{0:T(1024)}, u32[]{:S(2)}) copy-start(f32[1024]{0:T(1024)} %param.9) | copy-start | bytes 12292
  52.5 14.0 %collective-permute-start.1 = (f32[64,2,1024]{2,1,0:T(2,128)S(1)}, f32[64,2,1024]{2,1,0:T(2,128)S(1)}, u32[]{:S(2)}, u32[]{:S(2)}) collective-permute-start(f32[64,2,1024]{2,1,0:T(2,128)S(1)} %constant_dynamic-slice_fusion.1), channel_id=1, source_target_pairs={{0,8},{4,12},{8,0},{12,4},{16,24},{20,28},{24,16},{28,20},{1,9},{5... | collective-permute-start | bytes 1572872 | tf_op jit(solution)/shard_map/ppermute | solution.py:91
  66.8 7.6 %collective-permute-start.2 = (f32[32,2,1024]{2,1,0:T(2,128)S(1)}, f32[32,2,1024]{2,1,0:T(2,128)S(1)}, u32[]{:S(2)}, u32[]{:S(2)}) collective-permute-start(f32[32,2,1024]{2,1,0:T(2,128)S(1)} %constant_dynamic-slice_fusion), channel_id=1, source_target_pairs={{0,16},{4,20},{8,24},{12,28},{16,0},{20,4},{24,8},{28,12},{1,17},{... | collective-permute-start | bytes 786440 | tf_op jit(solution)/shard_map/ppermute | solution.py:91
  74.5 6.7 %collective-permute-start.3 = (f32[32,2,1024]{2,1,0:T(2,128)S(1)}, f32[32,2,1024]{2,1,0:T(2,128)S(1)}, u32[]{:S(2)}, u32[]{:S(2)}) collective-permute-start(f32[32,2,1024]{2,1,0:T(2,128)S(1)} %dynamic-slice_add_fusion.2), channel_id=1, source_target_pairs={{0,16},{4,20},{8,24},{12,28},{16,0},{20,4},{24,8},{28,12},{1,17},{... | collective-permute-start | bytes 786440 | tf_op jit(solution)/shard_map/ppermute | solution.py:102
  81.5 11.4 %collective-permute-start.4 = (f32[64,2,1024]{2,1,0:T(2,128)S(1)}, f32[64,2,1024]{2,1,0:T(2,128)S(1)}, u32[]{:S(2)}, u32[]{:S(2)}) collective-permute-start(f32[64,2,1024]{2,1,0:T(2,128)S(1)} %maximum_select_fusion.2), channel_id=1, source_target_pairs={{0,8},{4,12},{8,0},{12,4},{16,24},{20,28},{24,16},{28,20},{1,9},{5... | collective-permute-start | bytes 1572872 | tf_op jit(solution)/shard_map/ppermute | solution.py:102
  93.4 2.7 %collective-permute-start.5 = (f32[128,2,1024]{2,1,0:T(2,128)S(1)}, f32[128,2,1024]{2,1,0:T(2,128)S(1)}, u32[]{:S(2)}, u32[]{:S(2)}) collective-permute-start(f32[128,2,1024]{2,1,0:T(2,128)S(1)} %maximum_select_fusion.1), channel_id=1, source_target_pairs={{0,4},{4,0},{8,12},{12,8},{16,20},{20,16},{24,28},{28,24},{1,5},{5... | collective-permute-start | bytes 3145736 | tf_op jit(solution)/shard_map/ppermute | solution.py:102
  115.6 19.9 %copy-start.3 = (f32[4,256,32]{1,2,0:T(8,128)S(1)}, f32[4,256,32]{1,2,0:T(8,128)}, u32[]{:S(2)}) copy-start(f32[4,256,32]{1,2,0:T(8,128)} %copy-done.2) | copy-start | bytes 393220
  115.6 12.9 %all-to-all-start.1 = ((f32[4,1,16384]{2,1,0:T(1,128)}), f32[4,1,16384]{2,1,0:T(1,128)S(1)}, u32[]{:S(2)}, u32[]{:S(2)}) async-start(f32[4,1,16384]{2,1,0:T(1,128)} %reshape.182), calls=%async_computation.1 | async-start | bytes 524288 | tf_op jit(solution)/shard_map/all_to_all | solution.py:79
  130.7 6.2 %copy-start.5 = (f32[1,256,64]{1,2,0:T(8,128)S(1)}, f32[1,256,64]{1,2,0:T(8,128)}, u32[]{:S(2)}) copy-start(f32[1,256,64]{1,2,0:T(8,128)} %copy-done.4) | copy-start | bytes 196612
  130.8 6.2 %copy-start.7 = (f32[1,256,64]{1,2,0:T(8,128)S(1)}, f32[1,256,64]{1,2,0:T(8,128)}, u32[]{:S(2)}) copy-start(f32[1,256,64]{1,2,0:T(8,128)} %copy-done.6) | copy-start | bytes 196612
  138.7 15.8 %copy-start.1 = (f32[32,16,128]{2,1,0:T(8,128)S(1)}, f32[32,16,128]{2,1,0:T(8,128)}, u32[]{:S(2)}) copy-start(f32[32,16,128]{2,1,0:T(8,128)} %copy-done) | copy-start | bytes 786436
  139.9 14.6 %collective-permute-start.6 = (f32[1,2048]{1,0:T(1,128)S(1)}, f32[1,2048]{1,0:T(1,128)S(1)}, u32[]{:S(2)}, u32[]{:S(2)}) collective-permute-start(f32[1,2048]{1,0:T(1,128)S(1)} %get-tuple-element.19), channel_id=1, source_target_pairs={{0,4},{4,8},{8,12},{12,16},{16,20},{20,24},{24,28},{1,5},{5,9},{9,... | collective-permute-start | bytes 24584 | tf_op jit(solution)/shard_map/ppermute | solution.py:16
  141.8 12.7 %collective-permute-start.7 = (f32[1,2048]{1,0:T(1,128)S(1)}, f32[1,2048]{1,0:T(1,128)S(1)}, u32[]{:S(2)}, u32[]{:S(2)}) collective-permute-start(f32[1,2048]{1,0:T(1,128)S(1)} %get-tuple-element.18), channel_id=1, source_target_pairs={{4,0},{8,4},{12,8},{16,12},{20,16},{24,20},{28,24},{5,1},{9,5},{13... | collective-permute-start | bytes 24584 | tf_op jit(solution)/shard_map/ppermute | solution.py:17
  146.4 7.4 %collective-permute-start.8 = (f32[32,1]{1,0:T(8,128)S(1)}, f32[32,1]{1,0:T(8,128)S(1)}, u32[]{:S(2)}, u32[]{:S(2)}) collective-permute-start(f32[32,1]{1,0:T(8,128)S(1)} %get-tuple-element.15), channel_id=1, source_target_pairs={{0,1},{1,2},{2,3},{4,5},{5,6},{6,7},{8,9},{9,10},{10,11},{12,13},{... | collective-permute-start | bytes 392 | tf_op jit(solution)/shard_map/ppermute | solution.py:16
  148.7 5.8 %collective-permute-start.9 = (f32[32,1]{1,0:T(8,128)S(1)}, f32[32,1]{1,0:T(8,128)S(1)}, u32[]{:S(2)}, u32[]{:S(2)}) collective-permute-start(f32[32,1]{1,0:T(8,128)S(1)} %get-tuple-element.14), channel_id=1, source_target_pairs={{1,0},{2,1},{3,2},{5,4},{6,5},{7,6},{9,8},{10,9},{11,10},{13,12},{... | collective-permute-start | bytes 392 | tf_op jit(solution)/shard_map/ppermute | solution.py:17

commit v8 on v6

--- a/solution.py
+++ b/solution.py
@@ -18,9 +18,8 @@
     return before, after
 
 
-def neighbour_sum(cells):
+def neighbour_sum(cells, left, right):
     up, down = halo(cells, "lat", 0)
-    left, right = halo(cells, "lon", 1)
     rows = jnp.concatenate([up, cells[:-1]], axis=0) + jnp.concatenate([cells[1:], down], axis=0)
     cols = jnp.concatenate([left, cells[:, :-1]], axis=1) + jnp.concatenate([cells[:, 1:], right], axis=1)
     return rows + cols
@@ -111,6 +110,7 @@
     slot_total = slot_count * groups
     wet_cells = jnp.repeat(wet_blocks, BLK, axis=1).astype(jnp.float32)
     masked = wet_cells * surface
+    masked_left, masked_right = halo(masked, "lon", 1)
     lon_start = lax.axis_index("lon") * lon_width
     own_orders = lax.dynamic_slice_in_dim(
         slot_order, lax.axis_index("lon") * slot_count, slot_count
@@ -124,10 +124,20 @@
     retained = degrees[None, :] >= own_orders[:, None]
     spectrum = jnp.where(retained[:, None, :], love_gain[None, None, :] * degree_whole, 0.0)
     synthesis = jnp.einsum("krl,kcl->kcr", legendre, spectrum, precision=lax.Precision.HIGH)
-    summed = inverse_dft(all_gather(synthesis, "lon"), slot_order, lon_start, lon_width, lon_total)
-    loading = summed * (2 * slot_total) ** (-0.5)
+    inverse_scale = (2 * slot_total) ** (-0.5)
+    gathered = all_gather(synthesis, "lon")
+    loading = inverse_dft(gathered, slot_order, lon_start, lon_width, lon_total) * inverse_scale
     potential = masked - 0.6 * loading
-    neighbours = neighbour_sum(potential)
+    outside = jnp.array([-1, lon_width], dtype=jnp.int32)
+    edge_angle = (slot_order[:, None] * ((lon_start + outside) % lon_total)[None, :] % lon_total).astype(jnp.float32)
+    edge_angle = edge_angle * (2.0 * math.pi / lon_total)
+    edge_table = jnp.stack([jnp.cos(edge_angle), jnp.sin(edge_angle)], axis=1)
+    edge_loading = jnp.einsum("kcr,kcj->rj", gathered, edge_table, precision=lax.Precision.HIGHEST) * inverse_scale
+    edge_potential = jnp.concatenate([masked_left, masked_right], axis=1) - 0.6 * edge_loading
+    lon_index = lax.axis_index("lon")
+    inside = jnp.stack([lon_index > 0, lon_index < groups - 1])[None, :]
+    edge_potential = jnp.where(inside, edge_potential, 0.0)
+    neighbours = neighbour_sum(potential, edge_potential[:, :1], edge_potential[:, 1:])
     surface_next = wet_cells * (masked + 0.2 * (neighbours - 4.0 * potential))
     return (surface_next, loading)
 

time: 150 us -> 174 us (1.16)
  local copies, waits for them, and re-layouts: 21.4 us -> 40.3 us
  other arithmetic: 13.3 us -> 20.3 us
  waiting for transfers between devices: 20.1 us -> 15.7 us
  matrix products: 37.1 us -> 39.2 us
    slice x2, local copies, waits for them, and re-layouts: 0.09 us -> 3.19 us  [halo(): head = lax.slice_in_dim(cells, 0, 1, axis=dim)]
    ppermute x0 -> x2, local copies, waits for them, and re-layouts: none -> 2.72 us  [the longest x1 1.38 us: halo(): lax.ppermute(head, axis, [((i + 1) % count, i) for i in range(ends)])]
    mul x1, other arithmetic: 0.94 us -> 3.56 us  [local(): surface_next = wet_cells * (masked + 0.2 * (neighbours - 4.0 * potential))]
    ppermute x1, waiting for transfers between devices: 2.49 us -> 0.01 us  [paired_all_gather(): other = lax.ppermute(half, axis, pairs)]
    unnamed x8 -> x16, local copies, waits for them, and re-layouts: 5.39 us -> 7.69 us
    slice x0 -> x3, local copies, waits for them, and re-layouts: none -> 2.09 us  [the longest x2 2.09 us: halo(): lax.slice_in_dim(cells, cells.shape[dim] - 1, cells.shape[dim], axis=dim)]
    mul x2, local copies, waits for them, and re-layouts: 0.35 us -> 2.42 us  [inverse_dft(): hc = (yc * cb[..., None] + ys * sb[..., None]).sum(axis=0)]
  transfers between devices with their start and end apart: 8 -> 8, of which waited for: 5 -> 3; matrix products, arithmetic and copies ran while one was open for 2% -> 32% of each run, Pallas kernels for 0% -> 0%
where the time goes in v8:
time: 174 us; the launch traced here: 172 us
  local copies, waits for them, and re-layouts  40.3 us (23%)
  matrix products  39.2 us (23%)
  blocking collectives  32.8 us (19%)
  starting transfers between devices  22.7 us (13%)
  other arithmetic  20.3 us (12%)
  waiting for transfers between devices  15.7 us (9%)
    dot_general x1, matrix products, local(): jnp.einsum('krl,kcl->kcr', legendre, spectrum, precision=lax.Precision.HIGH)  17.5 us
    all_to_all x1, blocking collectives, paired_reduce_scatter(): lax.all_to_all(summed, axis, 0, 0, tiled=True, axis_index_groups=groups)  17.4 us
    dot_general x1, matrix products, local(): jnp.einsum('krl,kcr->kcl', legendre, fourier, precision=lax.Precision.HIGH)  16 us
    all_to_all x1, blocking collectives, paired_all_gather(): lax.all_to_all(copies, axis, 0, 0, tiled=True, axis_index_groups=groups)  15.4 us
    ppermute x2, starting transfers between devices, halo(): lax.ppermute(head, axis, [((i + 1) % count, i) for i in range(ends)])  8.98 us
    unnamed x16, local copies, waits for them, and re-layouts  7.69 us
    all_to_all x1, waiting for transfers between devices, reduce_scatter(): moved = lax.all_to_all(x, axis, 0, 0, tiled=True)  7.05 us
    all_to_all x1, waiting for transfers between devices, all_gather(): return lax.all_to_all(copies, axis, 0, 0, tiled=True)  5.65 us
  transfers between devices with their start and end apart: 8, of which 3 were waited for; matrix products, arithmetic and copies ran while one was open for 32% of the time, Pallas kernels for 0%

profile of v8, /device:TPU:12, one launch (start us, length us, event | category | flops | bytes accessed | tf_op | source)
XLA Modules:
  0.0 172.0 jit_solution(13923680293661378459)
XLA Ops:
  4.5 1.8 %convolution_bitcast_fusion = f32[2,256,32,32]{1,2,0,3:T(8,128)S(1)} fusion(f32[32,64,32,1]{1,2,3,0:T(8,128)S(1)} %copy.82, f32[1,256,64]{1,2,0:T(8,128)S(1)} %get-tuple-element.36, f32[1,256,64]{1,2,0:T(8,128)S(1)} %get-tuple-element.37), kind=kOutput, calls=%fused_computation.23 | convolution fusion | flops 402685952 | bytes 2490368 | tf_op jit(solution)/shard_map/cua,rab->cubr/dot_general | solution.py:48
  10.5 3.6 %gather_fusion = f32[1024,2,32]{2,1,0:T(2,128)S(1)} fusion(f32[1024,2,32]{2,1,0:T(2,128)S(1)} %copy.70, s32[1024]{0:T(1024)S(1)} %broadcast_clamp_fusion.1), kind=kCustom, calls=%fused_computation | custom fusion | bytes 528384 | tf_op jit(solution)/shard_map/jit(_take)/gather | solution.py:53
  14.6 1.8 %reshape.307 = f32[4,1,16384]{2,1,0:T(1,128)} reshape(f32[1024,2,32]{2,1,0:T(2,128)S(1)} %broadcast_multiply_fusion) | data formatting | bytes 524288
  16.4 5.3 %all-to-all-start = ((f32[4,1,16384]{2,1,0:T(1,128)}), f32[4,1,16384]{2,1,0:T(1,128)S(1)}, u32[]{:S(2)}, u32[]{:S(2)}) async-start(f32[4,1,16384]{2,1,0:T(1,128)} %reshape.307), calls=%async_computation | async-start | bytes 524288 | tf_op jit(solution)/shard_map/all_to_all | solution.py:71
  21.7 7.0 %all-to-all-done = f32[4,1,16384]{2,1,0:T(1,128)S(1)} async-done(((f32[4,1,16384]{2,1,0:T(1,128)}), f32[4,1,16384]{2,1,0:T(1,128)S(1)}, u32[]{:S(2)}, u32[]{:S(2)}) %all-to-all-start) | async-done | bytes 262176 | tf_op jit(solution)/shard_map/all_to_all | solution.py:71
  33.0 16.0 %fusion.66 = f32[256,2,1024]{2,1,0:T(2,128)S(1)} fusion(f32[256,2,32]{2,1,0:T(2,128)} %reduce_sum.65, f32[256,32,1024]{2,1,0:T(8,128)} %param.8), kind=kOutput, calls=%fused_computation.104 | convolution fusion | flops 100663296 | bytes 35717120 | tf_op jit(solution)/shard_map/krl,kcr->kcl/dot_general | solution.py:120
  50.1 3.0 %collective-permute-done = f32[128,2,1024]{2,1,0:T(2,128)} collective-permute-done((f32[128,2,1024]{2,1,0:T(2,128)}, f32[128,2,1024]{2,1,0:T(2,128)}, u32[]{:S(2)}, u32[]{:S(2)}) %collective-permute-start) | collective-permute-done | bytes 1048608 | tf_op jit(solution)/shard_map/ppermute | solution.py:89
  53.1 1.8 %dynamic-slice_add_fusion = f32[128,2,1024]{2,1,0:T(2,128)S(1)} fusion(f32[128,2,1024]{2,1,0:T(2,128)} %collective-permute-done, f32[256,2,1024]{2,1,0:T(2,128)S(1)} %fusion.66, s32[]{:T(128)S(6)} %select_n.103), kind=kLoop, calls=%fused_computation.40 | loop fusion | flops 262144 | bytes 3145732 | tf_op jit(solution)/shard_map/add | solution.py:89
  54.8 17.4 %all_to_all.20 = f32[128,2,1024]{2,1,0:T(2,128)S(1)} all-to-all(f32[128,2,1024]{2,1,0:T(2,128)S(1)} %dynamic-slice_add_fusion), channel_id=1, replica_groups={{0,8,16,24},{4,12,20,28},{1,9,17,25},{5,13,21,29},{2,10,18,26},{6,14,22..., dimensions={0} | all-to-all | bytes 2097152 | tf_op jit(solution)/shard_map/all_to_all | solution.py:90
  73.1 15.4 %all_to_all.21 = f32[128,2,1024]{2,1,0:T(2,128)S(1)} all-to-all(f32[128,2,1024]{2,1,0:T(2,128)S(1)} %bitcast.59), channel_id=1, replica_groups={{0,8,16,24},{4,12,20,28},{1,9,17,25},{5,13,21,29},{2,10,18,26},{6,14,22..., dimensions={0} | all-to-all | bytes 2097152 | tf_op jit(solution)/shard_map/all_to_all | solution.py:100
  89.1 2.1 %collective-permute-start.4 = (f32[32,1]{0,1:T(1,128)}, f32[32,1]{0,1:T(1,128)}, u32[]{:S(2)}, u32[]{:S(2)}) collective-permute-start(f32[32,1]{0,1:T(1,128)} %get-tuple-element.20), channel_id=1, source_target_pairs={{0,1},{1,2},{2,3},{4,5},{5,6},{6,7},{8,9},{9,10},{10,11},{12,13},{... | collective-permute-start | bytes 392 | tf_op jit(solution)/shard_map/ppermute | solution.py:16
  91.2 4.4 %collective-permute-start.5 = (f32[32,1]{0,1:T(1,128)}, f32[32,1]{0,1:T(1,128)}, u32[]{:S(2)}, u32[]{:S(2)}) collective-permute-start(f32[32,1]{0,1:T(1,128)} %get-tuple-element.21), channel_id=1, source_target_pairs={{1,0},{2,1},{3,2},{5,4},{6,5},{7,6},{9,8},{10,9},{11,10},{13,12},{... | collective-permute-start | bytes 392 | tf_op jit(solution)/shard_map/ppermute | solution.py:17
  97.7 17.5 %fusion.2 = f32[256,2,32]{2,1,0:T(2,128)S(1)} fusion(f32[256,32,1024]{2,1,0:T(8,128)} %param.8, f32[128,2,1024]{2,1,0:T(2,128)S(1)} %collective-permute-done.1, f32[128,2,1024]{2,1,0:T(2,128)S(1)} %all_to_all.21, pred[]{:T(512)S(6)} %eq.29, pred[256,1024]{1,0:T(8,128)(4,1)S(1)} %iota_compare_fusion.1, f32[1024]{0:T(1024)S(1)} %copy-done.2), kind=kOutput, calls=%fused_computation.11 | convolution fusion | flops 103284736 | bytes 35983360 | tf_op jit(solution)/shard_map/krl,kcl->kcr/dot_general | solution.py:126
  115.5 1.8 %reshape.309 = f32[4,1,16384]{2,1,0:T(1,128)} reshape(f32[1024,2,32]{2,1,0:T(2,128)S(1)} %bitcast.58) | data formatting | bytes 524288
  117.2 4.4 %all-to-all-start.3 = ((f32[4,1,16384]{2,1,0:T(1,128)}), f32[4,1,16384]{2,1,0:T(1,128)S(1)}, u32[]{:S(2)}, u32[]{:S(2)}) async-start(f32[4,1,16384]{2,1,0:T(1,128)} %reshape.309), calls=%async_computation.3 | async-start | bytes 524288 | tf_op jit(solution)/shard_map/all_to_all | solution.py:78
  123.1 5.6 %all-to-all-done.3 = f32[4,1,16384]{2,1,0:T(1,128)S(1)} async-done(((f32[4,1,16384]{2,1,0:T(1,128)}), f32[4,1,16384]{2,1,0:T(1,128)S(1)}, u32[]{:S(2)}, u32[]{:S(2)}) %all-to-all-start.3) | async-done | bytes 262176 | tf_op jit(solution)/shard_map/all_to_all | solution.py:78
  131.1 4.0 %gather_fusion.1 = f32[1024,2,32]{2,1,0:T(2,128)S(1)} fusion(f32[1024,2,32]{2,1,0:T(2,128)S(1)} %reshape.310, s32[1024]{0:T(1024)} %broadcast_clamp_fusion), kind=kCustom, calls=%fused_computation.1 | custom fusion | bytes 528384 | tf_op jit(solution)/shard_map/jit(_take)/gather | solution.py:61
  135.1 1.8 %fusion.62 = (f32[4,256,1,32]{3,2,1,0:T(1,128)}, f32[4,256,1,32]{3,2,1,0:T(1,128)}) fusion(f32[4,256,2,32]{3,2,1,0:T(2,128)S(1)} %bitcast.60), kind=kLoop, calls=%fused_computation.102 | loop fusion | bytes 524288 | tf_op jit(solution)/shard_map/slice | solution.py:62
  140.7 2.6 %multiply_bitcast_fusion = (f32[32,64,32]{1,0,2:T(8,128)}, f32[32,64,32]{1,0,2:T(8,128)S(1)}) fusion(f32[1,256,64]{1,2,0:T(8,128)S(1)} %get-tuple-element.36, f32[1,256,64]{1,2,0:T(8,128)S(1)} %get-tuple-element.37, f32[1,256,32,32]{1,3,0,2:T(8,128)S(1)} %bitcast.56, f32[1,256,32,32]{1,3,0,2:T(8,128)S(1)} %bitcast.55), kind=kOutput, calls=%fused_computation.43 | convolution fusion | flops 403341312 | bytes 2752512 | tf_op jit(solution)/shard_map/cua,cubr->rab/dot_general | solution.py:65
  143.3 1.8 %copy.86 = f32[32,64,32]{0,2,1:T(8,128)} copy(f32[32,64,32]{1,0,2:T(8,128)S(1)} %get-tuple-element.29) | data formatting | bytes 524288 | tf_op jit(solution)/shard_map/mul | solution.py:130
  148.0 1.7 fusion.60
  154.3 1.9 %collective-permute-start.2 = (f32[1,2048]{1,0:T(1,128)S(1)}, f32[1,2048]{1,0:T(1,128)S(1)}, u32[]{:S(2)}, u32[]{:S(2)}) collective-permute-start(f32[1,2048]{1,0:T(1,128)S(1)} %copy.75), channel_id=1, source_target_pairs={{0,4},{4,8},{8,12},{12,16},{16,20},{20,24},{24,28},{1,5},{5,9},{9,... | collective-permute-start | bytes 24584 | tf_op jit(solution)/shard_map/ppermute | solution.py:16
  156.2 4.5 %collective-permute-start.3 = (f32[1,2048]{1,0:T(1,128)S(1)}, f32[1,2048]{1,0:T(1,128)S(1)}, u32[]{:S(2)}, u32[]{:S(2)}) collective-permute-start(f32[1,2048]{1,0:T(1,128)S(1)} %copy.77), channel_id=1, source_target_pairs={{4,0},{8,4},{12,8},{16,12},{20,16},{24,20},{28,24},{5,1},{9,5},{13... | collective-permute-start | bytes 24584 | tf_op jit(solution)/shard_map/ppermute | solution.py:17
  167.5 3.6 %bitcast_multiply_fusion = f32[32,2048]{0,1:T(8,128)S(1)} fusion(f32[32,2048]{0,1:T(8,128)S(1)} %bitcast_multiply_fusion.1, f32[31,2048]{0,1:T(8,128)} %get-tuple-element.23, f32[1,2048]{0,1:T(8,128)} %copy.76, f32[1,2048]{0,1:T(8,128)} %copy.78, f32[31,2048]{0,1:T(8,128)} %get-tuple-element.22, f32[32,2047]{0,1:T(8,128)} %get-tuple-element.19, ...), kind=kLoop, calls=%fused_computation.24 | loop fusion | flops 786432 | bytes 1837056 | tf_op jit(solution)/shard_map/mul | solution.py:141
  (70 shorter events, 40.3 us)
Async XLA Ops:
  16.4 12.4 %all-to-all-start = ((f32[4,1,16384]{2,1,0:T(1,128)}), f32[4,1,16384]{2,1,0:T(1,128)S(1)}, u32[]{:S(2)}, u32[]{:S(2)}) async-start(f32[4,1,16384]{2,1,0:T(1,128)} %reshape.307), calls=%async_computation | async-start | bytes 524288 | tf_op jit(solution)/shard_map/all_to_all | solution.py:71
  50.0 3.0 %collective-permute-start = (f32[128,2,1024]{2,1,0:T(2,128)}, f32[128,2,1024]{2,1,0:T(2,128)}, u32[]{:S(2)}, u32[]{:S(2)}) collective-permute-start(f32[128,2,1024]{2,1,0:T(2,128)} %constant_dynamic-slice_fusion), channel_id=1, source_target_pairs={{0,4},{4,0},{8,12},{12,8},{16,20},{20,16},{24,28},{28,24},{1,5},{5... | collective-permute-start | bytes 3145736 | tf_op jit(solution)/shard_map/ppermute | solution.py:89
  54.8 40.8 %copy-start.1 = (s32[1024]{0:T(1024)S(1)}, s32[1024]{0:T(1024)}, u32[]{:S(2)}) copy-start(s32[1024]{0:T(1024)} %param.9) | copy-start | bytes 12292
  54.8 42.9 %copy-start.2 = (f32[1024]{0:T(1024)S(1)}, f32[1024]{0:T(1024)}, u32[]{:S(2)}) copy-start(f32[1024]{0:T(1024)} %param.10) | copy-start | bytes 12292
  88.6 9.2 %collective-permute-start.1 = (f32[128,2,1024]{2,1,0:T(2,128)S(1)}, f32[128,2,1024]{2,1,0:T(2,128)S(1)}, u32[]{:S(2)}, u32[]{:S(2)}) collective-permute-start(f32[128,2,1024]{2,1,0:T(2,128)S(1)} %all_to_all.21), channel_id=1, source_target_pairs={{0,4},{4,0},{8,12},{12,8},{16,20},{20,16},{24,28},{28,24},{1,5},{5... | collective-permute-start | bytes 3145736 | tf_op jit(solution)/shard_map/ppermute | solution.py:101
  89.1 71.7 %collective-permute-start.4 = (f32[32,1]{0,1:T(1,128)}, f32[32,1]{0,1:T(1,128)}, u32[]{:S(2)}, u32[]{:S(2)}) collective-permute-start(f32[32,1]{0,1:T(1,128)} %get-tuple-element.20), channel_id=1, source_target_pairs={{0,1},{1,2},{2,3},{4,5},{5,6},{6,7},{8,9},{9,10},{10,11},{12,13},{... | collective-permute-start | bytes 392 | tf_op jit(solution)/shard_map/ppermute | solution.py:16
  91.2 69.5 %collective-permute-start.5 = (f32[32,1]{0,1:T(1,128)}, f32[32,1]{0,1:T(1,128)}, u32[]{:S(2)}, u32[]{:S(2)}) collective-permute-start(f32[32,1]{0,1:T(1,128)} %get-tuple-element.21), channel_id=1, source_target_pairs={{1,0},{2,1},{3,2},{5,4},{6,5},{7,6},{9,8},{10,9},{11,10},{13,12},{... | collective-permute-start | bytes 392 | tf_op jit(solution)/shard_map/ppermute | solution.py:17
  97.7 23.9 %copy-start.4 = (s32[2]{0:T(128)S(1)}, s32[2]{0:T(128)}, u32[]{:S(2)}) copy-start(s32[2]{0:T(128)} %constant.108.clone) | copy-start | bytes 28
  117.2 11.5 %all-to-all-start.3 = ((f32[4,1,16384]{2,1,0:T(1,128)}), f32[4,1,16384]{2,1,0:T(1,128)S(1)}, u32[]{:S(2)}, u32[]{:S(2)}) async-start(f32[4,1,16384]{2,1,0:T(1,128)} %reshape.309), calls=%async_computation.3 | async-start | bytes 524288 | tf_op jit(solution)/shard_map/all_to_all | solution.py:78
  149.7 11.1 %copy-start = (f32[1024,1,2]{0,2,1:T(2,128)S(1)}, f32[1024,1,2]{0,2,1:T(2,128)}, u32[]{:S(2)}) copy-start(f32[1024,1,2]{0,2,1:T(2,128)} %get-tuple-element.31) | copy-start | bytes 24580
  149.7 11.1 %copy-start.3 = (pred[2]{0:T(512)(128)(4,1)S(1)}, pred[2]{0:T(512)(128)(4,1)}, u32[]{:S(2)}) copy-start(pred[2]{0:T(512)(128)(4,1)} %pad_add_fusion) | copy-start | bytes 10
  154.3 11.9 %collective-permute-start.2 = (f32[1,2048]{1,0:T(1,128)S(1)}, f32[1,2048]{1,0:T(1,128)S(1)}, u32[]{:S(2)}, u32[]{:S(2)}) collective-permute-start(f32[1,2048]{1,0:T(1,128)S(1)} %copy.75), channel_id=1, source_target_pairs={{0,4},{4,8},{8,12},{12,16},{16,20},{20,24},{24,28},{1,5},{5,9},{9,... | collective-permute-start | bytes 24584 | tf_op jit(solution)/shard_map/ppermute | solution.py:16
  156.2 8.6 %collective-permute-start.3 = (f32[1,2048]{1,0:T(1,128)S(1)}, f32[1,2048]{1,0:T(1,128)S(1)}, u32[]{:S(2)}, u32[]{:S(2)}) collective-permute-start(f32[1,2048]{1,0:T(1,128)S(1)} %copy.77), channel_id=1, source_target_pairs={{4,0},{8,4},{12,8},{16,12},{20,16},{24,20},{28,24},{5,1},{9,5},{13... | collective-permute-start | bytes 24584 | tf_op jit(solution)/shard_map/ppermute | solution.py:17

commit v9 on v6

--- a/solution.py
+++ b/solution.py
@@ -123,7 +123,7 @@
     degrees = jnp.arange(degree_count, dtype=jnp.int32)
     retained = degrees[None, :] >= own_orders[:, None]
     spectrum = jnp.where(retained[:, None, :], love_gain[None, None, :] * degree_whole, 0.0)
-    synthesis = jnp.einsum("krl,kcl->kcr", legendre, spectrum, precision=lax.Precision.HIGH)
+    synthesis = (legendre[:, None, :, :] * spectrum[:, :, None, :]).sum(axis=3)
     summed = inverse_dft(all_gather(synthesis, "lon"), slot_order, lon_start, lon_width, lon_total)
     loading = summed * (2 * slot_total) ** (-0.5)
     potential = masked - 0.6 * loading

time: 150 us -> 148 us (0.987)
  matrix products: 37.1 us -> 19.4 us
  other arithmetic: 13.3 us -> 28.4 us
    dot_general x1 -> x0, matrix products: 17.7 us -> none  [local(): jnp.einsum('krl,kcl->kcr', legendre, spectrum, precision=lax.Precision.HIGH)]
    reduce_sum x0 -> x1, other arithmetic: none -> 11.4 us  [local(): synthesis = (legendre[:, None, :, :] * spectrum[:, :, None, :]).sum(axis=3)]
    select_n x0 -> x1, other arithmetic: none -> 3.63 us  [local(): jnp.where(retained[:, None, :], love_gain[None, None, :] * degree_whole,...]
    unnamed x8 -> x24, local copies, waits for them, and re-layouts: 5.39 us -> 6.12 us
where the time goes in v9:
time: 148 us; the launch traced here: 146 us
  blocking collectives  32.8 us (22%)
  other arithmetic  28.4 us (19%)
  starting transfers between devices  23.1 us (16%)
  local copies, waits for them, and re-layouts  21.2 us (14%)
  waiting for transfers between devices  19.9 us (13%)
  matrix products  19.4 us (13%)
    all_to_all x1, blocking collectives, paired_reduce_scatter(): lax.all_to_all(summed, axis, 0, 0, tiled=True, axis_index_groups=groups)  17.4 us
    dot_general x1, matrix products, local(): jnp.einsum('krl,kcr->kcl', legendre, fourier, precision=lax.Precision.HIGH)  15.8 us
    all_to_all x1, blocking collectives, paired_all_gather(): lax.all_to_all(copies, axis, 0, 0, tiled=True, axis_index_groups=groups)  15.4 us
    reduce_sum x1, other arithmetic, local(): synthesis = (legendre[:, None, :, :] * spectrum[:, :, None, :]).sum(axis=3)  11.4 us
    ppermute x2, starting transfers between devices, halo(): lax.ppermute(head, axis, [((i + 1) % count, i) for i in range(ends)])  8.11 us
    all_to_all x1, waiting for transfers between devices, reduce_scatter(): moved = lax.all_to_all(x, axis, 0, 0, tiled=True)  7.05 us
    all_to_all x1, waiting for transfers between devices, all_gather(): return lax.all_to_all(copies, axis, 0, 0, tiled=True)  6.98 us
    unnamed x24, local copies, waits for them, and re-layouts  6.12 us
  transfers between devices with their start and end apart: 8, of which 5 were waited for; matrix products, arithmetic and copies ran while one was open for 2% of the time, Pallas kernels for 0%

profile of v9, /device:TPU:12, one launch (start us, length us, event | category | flops | bytes accessed | tf_op | source)
XLA Modules:
  0.0 146.0 jit_solution(1011697768373044740)
XLA Ops:
  4.0 1.8 %convolution_bitcast_fusion = f32[2,256,32,32]{1,2,0,3:T(8,128)S(1)} fusion(f32[32,64,32]{2,1,0:T(8,128)S(1)} %reshape.194, f32[1,256,64]{1,2,0:T(8,128)S(1)} %get-tuple-element.22, f32[1,256,64]{1,2,0:T(8,128)S(1)} %get-tuple-element.23), kind=kOutput, calls=%fused_computation.16 | convolution fusion | flops 402685952 | bytes 2490368 | tf_op jit(solution)/shard_map/cua,rab->cubr/dot_general | solution.py:49
  10.1 3.6 %gather_fusion = f32[1024,2,32]{2,1,0:T(2,128)S(1)} fusion(f32[1024,2,32]{2,1,0:T(2,128)S(1)} %copy.39, s32[1024]{0:T(1024)S(1)} %broadcast_clamp_fusion.1), kind=kCustom, calls=%fused_computation | custom fusion | bytes 528384 | tf_op jit(solution)/shard_map/jit(_take)/gather | solution.py:54
  14.2 1.8 %reshape.221 = f32[4,1,16384]{2,1,0:T(1,128)} reshape(f32[1024,2,32]{2,1,0:T(2,128)S(1)} %broadcast_multiply_fusion) | data formatting | bytes 524288
  15.9 5.3 %all-to-all-start = ((f32[4,1,16384]{2,1,0:T(1,128)}), f32[4,1,16384]{2,1,0:T(1,128)S(1)}, u32[]{:S(2)}, u32[]{:S(2)}) async-start(f32[4,1,16384]{2,1,0:T(1,128)} %reshape.221), calls=%async_computation | async-start | bytes 524288 | tf_op jit(solution)/shard_map/all_to_all | solution.py:72
  21.3 7.0 %all-to-all-done = f32[4,1,16384]{2,1,0:T(1,128)S(1)} async-done(((f32[4,1,16384]{2,1,0:T(1,128)}), f32[4,1,16384]{2,1,0:T(1,128)S(1)}, u32[]{:S(2)}, u32[]{:S(2)}) %all-to-all-start) | async-done | bytes 262176 | tf_op jit(solution)/shard_map/all_to_all | solution.py:72
  28.9 1.4 reduce
  32.0 15.8 %fusion.36 = f32[256,2,1024]{2,1,0:T(2,128)S(1)} fusion(f32[256,2,32]{2,1,0:T(2,128)S(1)} %reduce_sum.74, f32[256,32,1024]{2,1,0:T(8,128)} %param.7), kind=kOutput, calls=%fused_computation.69 | convolution fusion | flops 100663296 | bytes 35717120 | tf_op jit(solution)/shard_map/krl,kcr->kcl/dot_general | solution.py:120
  48.0 2.8 %collective-permute-done = f32[128,2,1024]{2,1,0:T(2,128)} collective-permute-done((f32[128,2,1024]{2,1,0:T(2,128)S(1)}, f32[128,2,1024]{2,1,0:T(2,128)}, u32[]{:S(2)}, u32[]{:S(2)}) %collective-permute-start) | collective-permute-done | bytes 1048608 | tf_op jit(solution)/shard_map/ppermute | solution.py:90
  50.7 1.8 %dynamic-slice_add_fusion = f32[128,2,1024]{2,1,0:T(2,128)S(1)} fusion(f32[128,2,1024]{2,1,0:T(2,128)} %collective-permute-done, f32[256,2,1024]{2,1,0:T(2,128)S(1)} %fusion.36, s32[]{:T(128)S(6)} %select_n.84), kind=kLoop, calls=%fused_computation.21 | loop fusion | flops 262144 | bytes 3145732 | tf_op jit(solution)/shard_map/add | solution.py:90
  52.5 17.4 %all_to_all.20 = f32[128,2,1024]{2,1,0:T(2,128)S(1)} all-to-all(f32[128,2,1024]{2,1,0:T(2,128)S(1)} %dynamic-slice_add_fusion), channel_id=1, replica_groups={{0,8,16,24},{4,12,20,28},{1,9,17,25},{5,13,21,29},{2,10,18,26},{6,14,22..., dimensions={0} | all-to-all | bytes 2097152 | tf_op jit(solution)/shard_map/all_to_all | solution.py:91
  70.8 15.4 %all_to_all.21 = f32[128,2,1024]{2,1,0:T(2,128)S(1)} all-to-all(f32[128,2,1024]{2,1,0:T(2,128)S(1)} %bitcast.49), channel_id=1, replica_groups={{0,8,16,24},{4,12,20,28},{1,9,17,25},{5,13,21,29},{2,10,18,26},{6,14,22..., dimensions={0} | all-to-all | bytes 2097152 | tf_op jit(solution)/shard_map/all_to_all | solution.py:101
  86.5 2.5 %collective-permute-done.1 = f32[128,2,1024]{2,1,0:T(2,128)} collective-permute-done((f32[128,2,1024]{2,1,0:T(2,128)S(1)}, f32[128,2,1024]{2,1,0:T(2,128)}, u32[]{:S(2)}, u32[]{:S(2)}) %collective-permute-start.1) | collective-permute-done | bytes 1048608 | tf_op jit(solution)/shard_map/ppermute | solution.py:102
  89.0 3.6 %fusion.1 = f32[256,2,1024]{2,1,0:T(2,128)S(1)} fusion(f32[128,2,1024]{2,1,0:T(2,128)} %collective-permute-done.1, f32[128,2,1024]{2,1,0:T(2,128)S(1)} %all_to_all.21, pred[]{:T(512)S(6)} %eq.25, pred[256,1024]{1,0:T(8,128)(4,1)S(1)} %iota_compare_fusion.1, f32[1024]{0:T(1024)S(1)} %copy-done.9), kind=kLoop, calls=%fused_computation.11 | loop fusion | flops 2621440 | bytes 4460545 | tf_op jit(solution)/shard_map/jit(_where)/select_n | solution.py:125
  92.7 11.4 %multiply_reduce_fusion = f32[256,2,32]{2,1,0:T(2,128)S(1)} fusion(f32[256,2,1024]{2,1,0:T(2,128)S(1)} %fusion.1, f32[256,32,1024]{2,1,0:T(8,128)} %param.7), kind=kLoop, calls=%fused_computation.2 | loop fusion | flops 33538048 | bytes 35717120 | tf_op jit(solution)/shard_map/reduce_sum | solution.py:126
  104.3 1.8 %reshape.223 = f32[4,1,16384]{2,1,0:T(1,128)} reshape(f32[1024,2,32]{2,1,0:T(2,128)S(1)} %bitcast.48) | data formatting | bytes 524288
  106.1 5.4 %all-to-all-start.3 = ((f32[4,1,16384]{2,1,0:T(1,128)}), f32[4,1,16384]{2,1,0:T(1,128)S(1)}, u32[]{:S(2)}, u32[]{:S(2)}) async-start(f32[4,1,16384]{2,1,0:T(1,128)} %reshape.223), calls=%async_computation.3 | async-start | bytes 524288 | tf_op jit(solution)/shard_map/all_to_all | solution.py:79
  112.0 7.0 %all-to-all-done.3 = f32[4,1,16384]{2,1,0:T(1,128)S(1)} async-done(((f32[4,1,16384]{2,1,0:T(1,128)}), f32[4,1,16384]{2,1,0:T(1,128)S(1)}, u32[]{:S(2)}, u32[]{:S(2)}) %all-to-all-start.3) | async-done | bytes 262176 | tf_op jit(solution)/shard_map/all_to_all | solution.py:79
  119.0 1.4 reduce.1
  121.3 3.6 %gather_fusion.1 = f32[1024,2,32]{2,1,0:T(2,128)S(1)} fusion(f32[1024,2,32]{2,1,0:T(2,128)S(1)} %reshape.224, s32[1024]{0:T(1024)S(1)} %broadcast_clamp_fusion), kind=kCustom, calls=%fused_computation.1 | custom fusion | bytes 528384 | tf_op jit(solution)/shard_map/jit(_take)/gather | solution.py:62
  127.5 1.8 %multiply_bitcast_fusion = (f32[32,64,32]{1,0,2:T(8,128)S(1)}, f32[32,64,32]{1,0,2:T(8,128)S(1)}) fusion(f32[1,256,64]{1,2,0:T(8,128)S(1)} %copy-done.5, f32[1,256,64]{1,2,0:T(8,128)S(1)} %copy-done.7, f32[1,256,32,32]{1,3,0,2:T(8,128)S(1)} %bitcast.46, f32[1,256,32,32]{1,3,0,2:T(8,128)S(1)} %bitcast.45), kind=kOutput, calls=%fused_computation.23 | convolution fusion | flops 403341312 | bytes 2752512 | tf_op jit(solution)/shard_map/cua,cubr->rab/dot_general | solution.py:66
  130.4 1.9 %collective-permute-start.2 = (f32[1,2048]{1,0:T(1,128)S(1)}, f32[1,2048]{1,0:T(1,128)S(1)}, u32[]{:S(2)}, u32[]{:S(2)}) collective-permute-start(f32[1,2048]{1,0:T(1,128)S(1)} %get-tuple-element.19), channel_id=1, source_target_pairs={{0,4},{4,8},{8,12},{12,16},{16,20},{20,24},{24,28},{1,5},{5,9},{9,... | collective-permute-start | bytes 24584 | tf_op jit(solution)/shard_map/ppermute | solution.py:16
  132.3 4.5 %collective-permute-start.3 = (f32[1,2048]{1,0:T(1,128)S(1)}, f32[1,2048]{1,0:T(1,128)S(1)}, u32[]{:S(2)}, u32[]{:S(2)}) collective-permute-start(f32[1,2048]{1,0:T(1,128)S(1)} %get-tuple-element.18), channel_id=1, source_target_pairs={{4,0},{8,4},{12,8},{16,12},{20,16},{24,20},{28,24},{5,1},{9,5},{13... | collective-permute-start | bytes 24584 | tf_op jit(solution)/shard_map/ppermute | solution.py:17
  137.0 2.3 %collective-permute-start.4 = (f32[32,1]{1,0:T(8,128)S(1)}, f32[32,1]{1,0:T(8,128)S(1)}, u32[]{:S(2)}, u32[]{:S(2)}) collective-permute-start(f32[32,1]{1,0:T(8,128)S(1)} %get-tuple-element.15), channel_id=1, source_target_pairs={{0,1},{1,2},{2,3},{4,5},{5,6},{6,7},{8,9},{9,10},{10,11},{12,13},{... | collective-permute-start | bytes 392 | tf_op jit(solution)/shard_map/ppermute | solution.py:16
  139.2 3.6 %collective-permute-start.5 = (f32[32,1]{1,0:T(8,128)S(1)}, f32[32,1]{1,0:T(8,128)S(1)}, u32[]{:S(2)}, u32[]{:S(2)}) collective-permute-start(f32[32,1]{1,0:T(8,128)S(1)} %get-tuple-element.14), channel_id=1, source_target_pairs={{1,0},{2,1},{3,2},{5,4},{6,5},{7,6},{9,8},{10,9},{11,10},{13,12},{... | collective-permute-start | bytes 392 | tf_op jit(solution)/shard_map/ppermute | solution.py:17
  (73 shorter events, 20.2 us)
Async XLA Ops:
  0.9 3.1 %copy-start.4 = (f32[1,256,64]{1,2,0:T(8,128)}, f32[1,256,64]{1,2,0:T(8,128)S(1)}, u32[]{:S(2)}) copy-start(f32[1,256,64]{1,2,0:T(8,128)S(1)} %get-tuple-element.22) | copy-start | bytes 196612
  0.9 3.1 %copy-start.6 = (f32[1,256,64]{1,2,0:T(8,128)}, f32[1,256,64]{1,2,0:T(8,128)S(1)}, u32[]{:S(2)}) copy-start(f32[1,256,64]{1,2,0:T(8,128)S(1)} %get-tuple-element.23) | copy-start | bytes 196612
  1.9 0.7 copy-start
  6.7 3.4 %copy-start.8 = (s32[1024]{0:T(1024)S(1)}, s32[1024]{0:T(1024)}, u32[]{:S(2)}) copy-start(s32[1024]{0:T(1024)} %param.8) | copy-start | bytes 12292
  7.9 6.3 %copy-start.2 = (f32[4,256,32]{1,2,0:T(8,128)}, f32[4,256,32]{1,2,0:T(8,128)S(1)}, u32[]{:S(2)}) copy-start(f32[4,256,32]{1,2,0:T(8,128)S(1)} %get-tuple-element.21) | copy-start | bytes 393220
  15.9 12.4 %all-to-all-start = ((f32[4,1,16384]{2,1,0:T(1,128)}), f32[4,1,16384]{2,1,0:T(1,128)S(1)}, u32[]{:S(2)}, u32[]{:S(2)}) async-start(f32[4,1,16384]{2,1,0:T(1,128)} %reshape.221), calls=%async_computation | async-start | bytes 524288 | tf_op jit(solution)/shard_map/all_to_all | solution.py:72
  47.9 2.9 %collective-permute-start = (f32[128,2,1024]{2,1,0:T(2,128)S(1)}, f32[128,2,1024]{2,1,0:T(2,128)}, u32[]{:S(2)}, u32[]{:S(2)}) collective-permute-start(f32[128,2,1024]{2,1,0:T(2,128)S(1)} %constant_dynamic-slice_fusion), channel_id=1, source_target_pairs={{0,4},{4,0},{8,12},{12,8},{16,20},{20,16},{24,28},{28,24},{1,5},{5... | collective-permute-start | bytes 3145736 | tf_op jit(solution)/shard_map/ppermute | solution.py:90
  52.5 36.5 %copy-start.9 = (f32[1024]{0:T(1024)S(1)}, f32[1024]{0:T(1024)}, u32[]{:S(2)}) copy-start(f32[1024]{0:T(1024)} %param.9) | copy-start | bytes 12292
  86.2 2.8 %collective-permute-start.1 = (f32[128,2,1024]{2,1,0:T(2,128)S(1)}, f32[128,2,1024]{2,1,0:T(2,128)}, u32[]{:S(2)}, u32[]{:S(2)}) collective-permute-start(f32[128,2,1024]{2,1,0:T(2,128)S(1)} %all_to_all.21), channel_id=1, source_target_pairs={{0,4},{4,0},{8,12},{12,8},{16,20},{20,16},{24,28},{28,24},{1,5},{5... | collective-permute-start | bytes 3145736 | tf_op jit(solution)/shard_map/ppermute | solution.py:102
  106.1 20.0 %copy-start.3 = (f32[4,256,32]{1,2,0:T(8,128)S(1)}, f32[4,256,32]{1,2,0:T(8,128)}, u32[]{:S(2)}) copy-start(f32[4,256,32]{1,2,0:T(8,128)} %copy-done.2) | copy-start | bytes 393220
  106.1 12.9 %all-to-all-start.3 = ((f32[4,1,16384]{2,1,0:T(1,128)}), f32[4,1,16384]{2,1,0:T(1,128)S(1)}, u32[]{:S(2)}, u32[]{:S(2)}) async-start(f32[4,1,16384]{2,1,0:T(1,128)} %reshape.223), calls=%async_computation.3 | async-start | bytes 524288 | tf_op jit(solution)/shard_map/all_to_all | solution.py:79
  121.3 6.2 %copy-start.5 = (f32[1,256,64]{1,2,0:T(8,128)S(1)}, f32[1,256,64]{1,2,0:T(8,128)}, u32[]{:S(2)}) copy-start(f32[1,256,64]{1,2,0:T(8,128)} %copy-done.4) | copy-start | bytes 196612
  121.3 6.2 %copy-start.7 = (f32[1,256,64]{1,2,0:T(8,128)S(1)}, f32[1,256,64]{1,2,0:T(8,128)}, u32[]{:S(2)}) copy-start(f32[1,256,64]{1,2,0:T(8,128)} %copy-done.6) | copy-start | bytes 196612
  129.3 15.8 %copy-start.1 = (f32[32,16,128]{2,1,0:T(8,128)S(1)}, f32[32,16,128]{2,1,0:T(8,128)}, u32[]{:S(2)}) copy-start(f32[32,16,128]{2,1,0:T(8,128)} %copy-done) | copy-start | bytes 786436
  130.4 14.6 %collective-permute-start.2 = (f32[1,2048]{1,0:T(1,128)S(1)}, f32[1,2048]{1,0:T(1,128)S(1)}, u32[]{:S(2)}, u32[]{:S(2)}) collective-permute-start(f32[1,2048]{1,0:T(1,128)S(1)} %get-tuple-element.19), channel_id=1, source_target_pairs={{0,4},{4,8},{8,12},{12,16},{16,20},{20,24},{24,28},{1,5},{5,9},{9,... | collective-permute-start | bytes 24584 | tf_op jit(solution)/shard_map/ppermute | solution.py:16
  132.3 12.7 %collective-permute-start.3 = (f32[1,2048]{1,0:T(1,128)S(1)}, f32[1,2048]{1,0:T(1,128)S(1)}, u32[]{:S(2)}, u32[]{:S(2)}) collective-permute-start(f32[1,2048]{1,0:T(1,128)S(1)} %get-tuple-element.18), channel_id=1, source_target_pairs={{4,0},{8,4},{12,8},{16,12},{20,16},{24,20},{28,24},{5,1},{9,5},{13... | collective-permute-start | bytes 24584 | tf_op jit(solution)/shard_map/ppermute | solution.py:17
  137.0 7.4 %collective-permute-start.4 = (f32[32,1]{1,0:T(8,128)S(1)}, f32[32,1]{1,0:T(8,128)S(1)}, u32[]{:S(2)}, u32[]{:S(2)}) collective-permute-start(f32[32,1]{1,0:T(8,128)S(1)} %get-tuple-element.15), channel_id=1, source_target_pairs={{0,1},{1,2},{2,3},{4,5},{5,6},{6,7},{8,9},{9,10},{10,11},{12,13},{... | collective-permute-start | bytes 392 | tf_op jit(solution)/shard_map/ppermute | solution.py:16
  139.2 5.8 %collective-permute-start.5 = (f32[32,1]{1,0:T(8,128)S(1)}, f32[32,1]{1,0:T(8,128)S(1)}, u32[]{:S(2)}, u32[]{:S(2)}) collective-permute-start(f32[32,1]{1,0:T(8,128)S(1)} %get-tuple-element.14), channel_id=1, source_target_pairs={{1,0},{2,1},{3,2},{5,4},{6,5},{7,6},{9,8},{10,9},{11,10},{13,12},{... | collective-permute-start | bytes 392 | tf_op jit(solution)/shard_map/ppermute | solution.py:17

commit v10 on v9

--- a/solution.py
+++ b/solution.py
@@ -118,11 +118,17 @@
     forward_scale = lon_total ** (-0.5)
     fourier = reduce_scatter(forward_dft(masked, slot_order, lon_start, lon_total) * forward_scale, "lon")
     coefficient = jnp.einsum("krl,kcr->kcl", legendre, fourier, precision=lax.Precision.HIGH)
-    degree_whole = paired_all_gather(paired_reduce_scatter(coefficient, "lat"), "lat")
-    degree_count = degree_whole.shape[2]
-    degrees = jnp.arange(degree_count, dtype=jnp.int32)
-    retained = degrees[None, :] >= own_orders[:, None]
-    spectrum = jnp.where(retained[:, None, :], love_gain[None, None, :] * degree_whole, 0.0)
+    degree_part = paired_reduce_scatter(coefficient, "lat")
+    lat_count = lax.axis_size("lat")
+    lat_index = lax.axis_index("lat")
+    half = slot_count // 2
+    part = degree_part.shape[0]
+    part_orders = lax.dynamic_slice_in_dim(own_orders, lat_index % 2 * half + lat_index // 2 * part, part)
+    degrees = jnp.arange(degree_part.shape[2], dtype=jnp.int32)
+    retained = degrees[None, :] >= part_orders[:, None]
+    spectrum = paired_all_gather(
+        jnp.where(retained[:, None, :], love_gain[None, None, :] * degree_part, 0.0), "lat"
+    )
     synthesis = (legendre[:, None, :, :] * spectrum[:, :, None, :]).sum(axis=3)
     summed = inverse_dft(all_gather(synthesis, "lon"), slot_order, lon_start, lon_width, lon_total)
     loading = summed * (2 * slot_total) ** (-0.5)

time: 148 us -> 149 us (level)
  blocking collectives: 32.8 us -> 15.5 us
  waiting for transfers between devices: 19.9 us -> 33.5 us
  starting transfers between devices: 23.1 us -> 27.3 us
    all_to_all x1 -> x0, blocking collectives: 17.4 us -> none  [paired_reduce_scatter(): lax.all_to_all(summed, axis, 0, 0, tiled=True, axis_index_groups=groups)]
    all_to_all x0 -> x1, waiting for transfers between devices: none -> 13.3 us  [paired_reduce_scatter(): lax.all_to_all(summed, axis, 0, 0, tiled=True, axis_index_groups=groups)]
    all_to_all x0 -> x1, starting transfers between devices: none -> 4.22 us  [paired_reduce_scatter(): lax.all_to_all(summed, axis, 0, 0, tiled=True, axis_index_groups=groups)]
    select_n x1 -> x2, other arithmetic: 3.63 us -> 3.11 us  [the longest x1 2.92 us: paired_all_gather(): jnp.where(side == 0, jnp.concatenate([half, other]), jnp.concatenate([oth...]
  transfers between devices with their start and end apart: 8 -> 9, of which waited for: 5 -> 6; matrix products, arithmetic and copies ran while one was open for 2% -> 2% of each run, Pallas kernels for 0% -> 0%
where the time goes in v10:
time: 149 us; the launch traced here: 147 us
  waiting for transfers between devices  33.5 us (22%)
  other arithmetic  28.8 us (19%)
  starting transfers between devices  27.3 us (18%)
  local copies, waits for them, and re-layouts  21.2 us (14%)
  matrix products  19.4 us (13%)
  blocking collectives  15.5 us (10%)
    dot_general x1, matrix products, local(): jnp.einsum('krl,kcr->kcl', legendre, fourier, precision=lax.Precision.HIGH)  15.8 us
    all_to_all x1, blocking collectives, paired_all_gather(): lax.all_to_all(copies, axis, 0, 0, tiled=True, axis_index_groups=groups)  15.5 us
    all_to_all x1, waiting for transfers between devices, paired_reduce_scatter(): lax.all_to_all(summed, axis, 0, 0, tiled=True, axis_index_groups=groups)  13.3 us
    reduce_sum x1, other arithmetic, local(): synthesis = (legendre[:, None, :, :] * spectrum[:, :, None, :]).sum(axis=3)  11.4 us
    ppermute x2, starting transfers between devices, halo(): lax.ppermute(head, axis, [((i + 1) % count, i) for i in range(ends)])  8.12 us
    all_to_all x1, waiting for transfers between devices, reduce_scatter(): moved = lax.all_to_all(x, axis, 0, 0, tiled=True)  7.05 us
    all_to_all x1, waiting for transfers between devices, all_gather(): return lax.all_to_all(copies, axis, 0, 0, tiled=True)  6.98 us
    unnamed x24, local copies, waits for them, and re-layouts  6.12 us
  transfers between devices with their start and end apart: 9, of which 6 were waited for; matrix products, arithmetic and copies ran while one was open for 2% of the time, Pallas kernels for 0%

profile of v10, /device:TPU:12, one launch (start us, length us, event | category | flops | bytes accessed | tf_op | source)
XLA Modules:
  0.0 146.8 jit_solution(16873133748940642492)
XLA Ops:
  4.0 1.8 %convolution_bitcast_fusion = f32[2,256,32,32]{1,2,0,3:T(8,128)S(1)} fusion(f32[32,64,32]{2,1,0:T(8,128)S(1)} %reshape.195, f32[1,256,64]{1,2,0:T(8,128)S(1)} %get-tuple-element.22, f32[1,256,64]{1,2,0:T(8,128)S(1)} %get-tuple-element.23), kind=kOutput, calls=%fused_computation.14 | convolution fusion | flops 402685952 | bytes 2490368 | tf_op jit(solution)/shard_map/cua,rab->cubr/dot_general | solution.py:49
  10.0 3.6 %gather_fusion = f32[1024,2,32]{2,1,0:T(2,128)S(1)} fusion(f32[1024,2,32]{2,1,0:T(2,128)S(1)} %copy.39, s32[1024]{0:T(1024)S(1)} %broadcast_clamp_fusion.1), kind=kCustom, calls=%fused_computation | custom fusion | bytes 528384 | tf_op jit(solution)/shard_map/jit(_take)/gather | solution.py:54
  14.2 1.8 %reshape.222 = f32[4,1,16384]{2,1,0:T(1,128)} reshape(f32[1024,2,32]{2,1,0:T(2,128)S(1)} %broadcast_multiply_fusion) | data formatting | bytes 524288
  15.9 5.3 %all-to-all-start = ((f32[4,1,16384]{2,1,0:T(1,128)}), f32[4,1,16384]{2,1,0:T(1,128)S(1)}, u32[]{:S(2)}, u32[]{:S(2)}) async-start(f32[4,1,16384]{2,1,0:T(1,128)} %reshape.222), calls=%async_computation | async-start | bytes 524288 | tf_op jit(solution)/shard_map/all_to_all | solution.py:72
  21.2 7.0 %all-to-all-done = f32[4,1,16384]{2,1,0:T(1,128)S(1)} async-done(((f32[4,1,16384]{2,1,0:T(1,128)}), f32[4,1,16384]{2,1,0:T(1,128)S(1)}, u32[]{:S(2)}, u32[]{:S(2)}) %all-to-all-start) | async-done | bytes 262176 | tf_op jit(solution)/shard_map/all_to_all | solution.py:72
  32.0 15.8 %fusion.34 = f32[256,2,1024]{2,1,0:T(2,128)S(1)} fusion(f32[256,2,32]{2,1,0:T(2,128)S(1)} %reduce_sum.74, f32[256,32,1024]{2,1,0:T(8,128)} %param.7), kind=kOutput, calls=%fused_computation.68 | convolution fusion | flops 100663296 | bytes 35717120 | tf_op jit(solution)/shard_map/krl,kcr->kcl/dot_general | solution.py:120
  48.0 2.8 %collective-permute-done = f32[128,2,1024]{2,1,0:T(2,128)} collective-permute-done((f32[128,2,1024]{2,1,0:T(2,128)S(1)}, f32[128,2,1024]{2,1,0:T(2,128)}, u32[]{:S(2)}, u32[]{:S(2)}) %collective-permute-start) | collective-permute-done | bytes 1048608 | tf_op jit(solution)/shard_map/ppermute | solution.py:90
  50.7 2.8 %dynamic-slice_add_fusion = f32[128,2,1024]{2,1,0:T(2,128)} fusion(f32[128,2,1024]{2,1,0:T(2,128)} %collective-permute-done, f32[256,2,1024]{2,1,0:T(2,128)S(1)} %fusion.34, s32[]{:T(128)S(6)} %select_n.101), kind=kLoop, calls=%fused_computation.19 | loop fusion | flops 262144 | bytes 3145732 | tf_op jit(solution)/shard_map/add | solution.py:90
  53.5 4.2 %all-to-all-start.1 = ((f32[128,2,1024]{2,1,0:T(2,128)}), f32[128,2,1024]{2,1,0:T(2,128)S(1)}, u32[]{:S(2)}, u32[]{:S(2)}) async-start(f32[128,2,1024]{2,1,0:T(2,128)} %dynamic-slice_add_fusion), calls=%async_computation.1 | async-start | bytes 2097152 | tf_op jit(solution)/shard_map/all_to_all | solution.py:91
  57.9 13.3 %all-to-all-done.1 = f32[128,2,1024]{2,1,0:T(2,128)S(1)} async-done(((f32[128,2,1024]{2,1,0:T(2,128)}), f32[128,2,1024]{2,1,0:T(2,128)S(1)}, u32[]{:S(2)}, u32[]{:S(2)}) %all-to-all-start.1) | async-done | bytes 1048608 | tf_op jit(solution)/shard_map/all_to_all | solution.py:91
  72.3 15.5 %all_to_all.20 = f32[128,2,1024]{2,1,0:T(2,128)S(1)} all-to-all(f32[128,2,1024]{2,1,0:T(2,128)S(1)} %bitcast.49), channel_id=1, replica_groups={{0,8,16,24},{4,12,20,28},{1,9,17,25},{5,13,21,29},{2,10,18,26},{6,14,22..., dimensions={0} | all-to-all | bytes 2097152 | tf_op jit(solution)/shard_map/all_to_all | solution.py:101
  87.8 2.8 %collective-permute-done.1 = f32[128,2,1024]{2,1,0:T(2,128)} collective-permute-done((f32[128,2,1024]{2,1,0:T(2,128)S(1)}, f32[128,2,1024]{2,1,0:T(2,128)}, u32[]{:S(2)}, u32[]{:S(2)}) %collective-permute-start.1) | collective-permute-done | bytes 1048608 | tf_op jit(solution)/shard_map/ppermute | solution.py:102
  90.6 2.9 %maximum_select_fusion = f32[256,2,1024]{2,1,0:T(2,128)S(1)} fusion(f32[128,2,1024]{2,1,0:T(2,128)} %collective-permute-done.1, f32[128,2,1024]{2,1,0:T(2,128)S(1)} %all_to_all.20, pred[]{:T(512)S(6)} %eq.26), kind=kLoop, calls=%fused_computation.9 | loop fusion | flops 1572864 | bytes 4194305 | tf_op jit(solution)/shard_map/jit(_where)/select_n | solution.py:103
  93.5 11.4 %multiply_reduce_fusion = f32[256,2,32]{2,1,0:T(2,128)S(1)} fusion(f32[256,2,1024]{2,1,0:T(2,128)S(1)} %maximum_select_fusion, f32[256,32,1024]{2,1,0:T(8,128)} %param.7), kind=kLoop, calls=%fused_computation.2 | loop fusion | flops 33538048 | bytes 35717120 | tf_op jit(solution)/shard_map/reduce_sum | solution.py:132
  105.2 1.8 %reshape.224 = f32[4,1,16384]{2,1,0:T(1,128)} reshape(f32[1024,2,32]{2,1,0:T(2,128)S(1)} %bitcast.48) | data formatting | bytes 524288
  107.0 5.4 %all-to-all-start.3 = ((f32[4,1,16384]{2,1,0:T(1,128)}), f32[4,1,16384]{2,1,0:T(1,128)S(1)}, u32[]{:S(2)}, u32[]{:S(2)}) async-start(f32[4,1,16384]{2,1,0:T(1,128)} %reshape.224), calls=%async_computation.3 | async-start | bytes 524288 | tf_op jit(solution)/shard_map/all_to_all | solution.py:79
  112.8 7.0 %all-to-all-done.3 = f32[4,1,16384]{2,1,0:T(1,128)S(1)} async-done(((f32[4,1,16384]{2,1,0:T(1,128)}), f32[4,1,16384]{2,1,0:T(1,128)S(1)}, u32[]{:S(2)}, u32[]{:S(2)}) %all-to-all-start.3) | async-done | bytes 262176 | tf_op jit(solution)/shard_map/all_to_all | solution.py:79
  119.8 1.4 reduce.1
  122.2 3.6 %gather_fusion.1 = f32[1024,2,32]{2,1,0:T(2,128)S(1)} fusion(f32[1024,2,32]{2,1,0:T(2,128)S(1)} %reshape.225, s32[1024]{0:T(1024)S(1)} %broadcast_clamp_fusion), kind=kCustom, calls=%fused_computation.1 | custom fusion | bytes 528384 | tf_op jit(solution)/shard_map/jit(_take)/gather | solution.py:62
  128.3 1.8 %multiply_bitcast_fusion = (f32[32,64,32]{1,0,2:T(8,128)S(1)}, f32[32,64,32]{1,0,2:T(8,128)S(1)}) fusion(f32[1,256,64]{1,2,0:T(8,128)S(1)} %copy-done.5, f32[1,256,64]{1,2,0:T(8,128)S(1)} %copy-done.7, f32[1,256,32,32]{1,3,0,2:T(8,128)S(1)} %bitcast.46, f32[1,256,32,32]{1,3,0,2:T(8,128)S(1)} %bitcast.45), kind=kOutput, calls=%fused_computation.20 | convolution fusion | flops 403341312 | bytes 2752512 | tf_op jit(solution)/shard_map/cua,cubr->rab/dot_general | solution.py:66
  131.3 1.9 %collective-permute-start.2 = (f32[1,2048]{1,0:T(1,128)S(1)}, f32[1,2048]{1,0:T(1,128)S(1)}, u32[]{:S(2)}, u32[]{:S(2)}) collective-permute-start(f32[1,2048]{1,0:T(1,128)S(1)} %get-tuple-element.19), channel_id=1, source_target_pairs={{0,4},{4,8},{8,12},{12,16},{16,20},{20,24},{24,28},{1,5},{5,9},{9,... | collective-permute-start | bytes 24584 | tf_op jit(solution)/shard_map/ppermute | solution.py:16
  133.2 4.5 %collective-permute-start.3 = (f32[1,2048]{1,0:T(1,128)S(1)}, f32[1,2048]{1,0:T(1,128)S(1)}, u32[]{:S(2)}, u32[]{:S(2)}) collective-permute-start(f32[1,2048]{1,0:T(1,128)S(1)} %get-tuple-element.18), channel_id=1, source_target_pairs={{4,0},{8,4},{12,8},{16,12},{20,16},{24,20},{28,24},{5,1},{9,5},{13... | collective-permute-start | bytes 24584 | tf_op jit(solution)/shard_map/ppermute | solution.py:17
  137.8 2.3 %collective-permute-start.4 = (f32[32,1]{1,0:T(8,128)S(1)}, f32[32,1]{1,0:T(8,128)S(1)}, u32[]{:S(2)}, u32[]{:S(2)}) collective-permute-start(f32[32,1]{1,0:T(8,128)S(1)} %get-tuple-element.15), channel_id=1, source_target_pairs={{0,1},{1,2},{2,3},{4,5},{5,6},{6,7},{8,9},{9,10},{10,11},{12,13},{... | collective-permute-start | bytes 392 | tf_op jit(solution)/shard_map/ppermute | solution.py:16
  140.1 3.6 %collective-permute-start.5 = (f32[32,1]{1,0:T(8,128)S(1)}, f32[32,1]{1,0:T(8,128)S(1)}, u32[]{:S(2)}, u32[]{:S(2)}) collective-permute-start(f32[32,1]{1,0:T(8,128)S(1)} %get-tuple-element.14), channel_id=1, source_target_pairs={{1,0},{2,1},{3,2},{5,4},{6,5},{7,6},{9,8},{10,9},{11,10},{13,12},{... | collective-permute-start | bytes 392 | tf_op jit(solution)/shard_map/ppermute | solution.py:17
  (75 shorter events, 21.6 us)
Async XLA Ops:
  0.9 3.1 %copy-start.4 = (f32[1,256,64]{1,2,0:T(8,128)}, f32[1,256,64]{1,2,0:T(8,128)S(1)}, u32[]{:S(2)}) copy-start(f32[1,256,64]{1,2,0:T(8,128)S(1)} %get-tuple-element.22) | copy-start | bytes 196612
  0.9 3.1 %copy-start.6 = (f32[1,256,64]{1,2,0:T(8,128)}, f32[1,256,64]{1,2,0:T(8,128)S(1)}, u32[]{:S(2)}) copy-start(f32[1,256,64]{1,2,0:T(8,128)S(1)} %get-tuple-element.23) | copy-start | bytes 196612
  1.9 0.7 copy-start
  6.6 3.4 %copy-start.9 = (s32[1024]{0:T(1024)S(1)}, s32[1024]{0:T(1024)}, u32[]{:S(2)}) copy-start(s32[1024]{0:T(1024)} %param.8) | copy-start | bytes 12292
  7.9 6.3 %copy-start.2 = (f32[4,256,32]{1,2,0:T(8,128)}, f32[4,256,32]{1,2,0:T(8,128)S(1)}, u32[]{:S(2)}) copy-start(f32[4,256,32]{1,2,0:T(8,128)S(1)} %get-tuple-element.21) | copy-start | bytes 393220
  15.9 12.4 %all-to-all-start = ((f32[4,1,16384]{2,1,0:T(1,128)}), f32[4,1,16384]{2,1,0:T(1,128)S(1)}, u32[]{:S(2)}, u32[]{:S(2)}) async-start(f32[4,1,16384]{2,1,0:T(1,128)} %reshape.222), calls=%async_computation | async-start | bytes 524288 | tf_op jit(solution)/shard_map/all_to_all | solution.py:72
  47.8 24.0 %copy-start.8 = (f32[1024]{0:T(1024)S(1)}, f32[1024]{0:T(1024)}, u32[]{:S(2)}) copy-start(f32[1024]{0:T(1024)} %param.9) | copy-start | bytes 12292
  47.9 2.9 %collective-permute-start = (f32[128,2,1024]{2,1,0:T(2,128)S(1)}, f32[128,2,1024]{2,1,0:T(2,128)}, u32[]{:S(2)}, u32[]{:S(2)}) collective-permute-start(f32[128,2,1024]{2,1,0:T(2,128)S(1)} %constant_dynamic-slice_fusion), channel_id=1, source_target_pairs={{0,4},{4,0},{8,12},{12,8},{16,20},{20,16},{24,28},{28,24},{1,5},{5... | collective-permute-start | bytes 3145736 | tf_op jit(solution)/shard_map/ppermute | solution.py:90
  53.5 17.7 %all-to-all-start.1 = ((f32[128,2,1024]{2,1,0:T(2,128)}), f32[128,2,1024]{2,1,0:T(2,128)S(1)}, u32[]{:S(2)}, u32[]{:S(2)}) async-start(f32[128,2,1024]{2,1,0:T(2,128)} %dynamic-slice_add_fusion), calls=%async_computation.1 | async-start | bytes 2097152 | tf_op jit(solution)/shard_map/all_to_all | solution.py:91
  87.8 2.8 %collective-permute-start.1 = (f32[128,2,1024]{2,1,0:T(2,128)S(1)}, f32[128,2,1024]{2,1,0:T(2,128)}, u32[]{:S(2)}, u32[]{:S(2)}) collective-permute-start(f32[128,2,1024]{2,1,0:T(2,128)S(1)} %all_to_all.20), channel_id=1, source_target_pairs={{0,4},{4,0},{8,12},{12,8},{16,20},{20,16},{24,28},{28,24},{1,5},{5... | collective-permute-start | bytes 3145736 | tf_op jit(solution)/shard_map/ppermute | solution.py:102
  107.0 20.0 %copy-start.3 = (f32[4,256,32]{1,2,0:T(8,128)S(1)}, f32[4,256,32]{1,2,0:T(8,128)}, u32[]{:S(2)}) copy-start(f32[4,256,32]{1,2,0:T(8,128)} %copy-done.2) | copy-start | bytes 393220
  107.0 12.9 %all-to-all-start.3 = ((f32[4,1,16384]{2,1,0:T(1,128)}), f32[4,1,16384]{2,1,0:T(1,128)S(1)}, u32[]{:S(2)}, u32[]{:S(2)}) async-start(f32[4,1,16384]{2,1,0:T(1,128)} %reshape.224), calls=%async_computation.3 | async-start | bytes 524288 | tf_op jit(solution)/shard_map/all_to_all | solution.py:79
  122.2 6.2 %copy-start.5 = (f32[1,256,64]{1,2,0:T(8,128)S(1)}, f32[1,256,64]{1,2,0:T(8,128)}, u32[]{:S(2)}) copy-start(f32[1,256,64]{1,2,0:T(8,128)} %copy-done.4) | copy-start | bytes 196612
  122.2 6.2 %copy-start.7 = (f32[1,256,64]{1,2,0:T(8,128)S(1)}, f32[1,256,64]{1,2,0:T(8,128)}, u32[]{:S(2)}) copy-start(f32[1,256,64]{1,2,0:T(8,128)} %copy-done.6) | copy-start | bytes 196612
  130.1 15.7 %copy-start.1 = (f32[32,16,128]{2,1,0:T(8,128)S(1)}, f32[32,16,128]{2,1,0:T(8,128)}, u32[]{:S(2)}) copy-start(f32[32,16,128]{2,1,0:T(8,128)} %copy-done) | copy-start | bytes 786436
  131.3 14.6 %collective-permute-start.2 = (f32[1,2048]{1,0:T(1,128)S(1)}, f32[1,2048]{1,0:T(1,128)S(1)}, u32[]{:S(2)}, u32[]{:S(2)}) collective-permute-start(f32[1,2048]{1,0:T(1,128)S(1)} %get-tuple-element.19), channel_id=1, source_target_pairs={{0,4},{4,8},{8,12},{12,16},{16,20},{20,24},{24,28},{1,5},{5,9},{9,... | collective-permute-start | bytes 24584 | tf_op jit(solution)/shard_map/ppermute | solution.py:16
  133.2 12.7 %collective-permute-start.3 = (f32[1,2048]{1,0:T(1,128)S(1)}, f32[1,2048]{1,0:T(1,128)S(1)}, u32[]{:S(2)}, u32[]{:S(2)}) collective-permute-start(f32[1,2048]{1,0:T(1,128)S(1)} %get-tuple-element.18), channel_id=1, source_target_pairs={{4,0},{8,4},{12,8},{16,12},{20,16},{24,20},{28,24},{5,1},{9,5},{13... | collective-permute-start | bytes 24584 | tf_op jit(solution)/shard_map/ppermute | solution.py:17
  137.8 7.4 %collective-permute-start.4 = (f32[32,1]{1,0:T(8,128)S(1)}, f32[32,1]{1,0:T(8,128)S(1)}, u32[]{:S(2)}, u32[]{:S(2)}) collective-permute-start(f32[32,1]{1,0:T(8,128)S(1)} %get-tuple-element.15), channel_id=1, source_target_pairs={{0,1},{1,2},{2,3},{4,5},{5,6},{6,7},{8,9},{9,10},{10,11},{12,13},{... | collective-permute-start | bytes 392 | tf_op jit(solution)/shard_map/ppermute | solution.py:16
  140.1 5.8 %collective-permute-start.5 = (f32[32,1]{1,0:T(8,128)S(1)}, f32[32,1]{1,0:T(8,128)S(1)}, u32[]{:S(2)}, u32[]{:S(2)}) collective-permute-start(f32[32,1]{1,0:T(8,128)S(1)} %get-tuple-element.14), channel_id=1, source_target_pairs={{1,0},{2,1},{3,2},{5,4},{6,5},{7,6},{9,8},{10,9},{11,10},{13,12},{... | collective-permute-start | bytes 392 | tf_op jit(solution)/shard_map/ppermute | solution.py:17

commit v11 on v9

--- a/solution.py
+++ b/solution.py
@@ -124,7 +124,7 @@
     retained = degrees[None, :] >= own_orders[:, None]
     spectrum = jnp.where(retained[:, None, :], love_gain[None, None, :] * degree_whole, 0.0)
     synthesis = (legendre[:, None, :, :] * spectrum[:, :, None, :]).sum(axis=3)
-    summed = inverse_dft(all_gather(synthesis, "lon"), slot_order, lon_start, lon_width, lon_total)
+    summed = inverse_dft(lax.all_gather(synthesis, "lon", axis=0, tiled=True), slot_order, lon_start, lon_width, lon_total)
     loading = summed * (2 * slot_total) ** (-0.5)
     potential = masked - 0.6 * loading
     neighbours = neighbour_sum(potential)

time: 148 us -> 144 us (0.973); the launches traced: 146 us -> 144 us
  blocking collectives: 32.8 us -> 46.1 us
  waiting for transfers between devices: 19.9 us -> 13.5 us
  starting transfers between devices: 23.1 us -> 17.7 us
  local copies, waits for them, and re-layouts: 21.2 us -> 18.8 us
    all_gather x0 -> x1, blocking collectives: none -> 13.3 us  [local(): lax.all_gather(synthesis, 'lon', axis=0, tiled=True)]
    all_to_all x1 -> x0, waiting for transfers between devices: 6.98 us -> none  [all_gather(): return lax.all_to_all(copies, axis, 0, 0, tiled=True)]
    all_to_all x1 -> x0, starting transfers between devices: 5.37 us -> none  [all_gather(): return lax.all_to_all(copies, axis, 0, 0, tiled=True)]
    unnamed x24 -> x22, local copies, waits for them, and re-layouts: 6.12 us -> 3.43 us
  transfers between devices with their start and end apart: 8 -> 7, of which waited for: 5 -> 4; matrix products, arithmetic and copies ran while one was open for 2% -> 2% of each run, Pallas kernels for 0% -> 0%
where the time goes in v11:
time: 144 us
  blocking collectives  46.1 us (32%)
  other arithmetic  27 us (19%)
  matrix products  19.4 us (13%)
  local copies, waits for them, and re-layouts  18.8 us (13%)
  starting transfers between devices  17.7 us (12%)
  waiting for transfers between devices  13.5 us (9%)
    all_to_all x1, blocking collectives, paired_reduce_scatter(): lax.all_to_all(summed, axis, 0, 0, tiled=True, axis_index_groups=groups)  17.4 us
    dot_general x1, matrix products, local(): jnp.einsum('krl,kcr->kcl', legendre, fourier, precision=lax.Precision.HIGH)  15.8 us
    all_to_all x1, blocking collectives, paired_all_gather(): lax.all_to_all(copies, axis, 0, 0, tiled=True, axis_index_groups=groups)  15.4 us
    all_gather x1, blocking collectives, local(): lax.all_gather(synthesis, 'lon', axis=0, tiled=True)  13.3 us
    reduce_sum x1, other arithmetic, local(): synthesis = (legendre[:, None, :, :] * spectrum[:, :, None, :]).sum(axis=3)  11.4 us
    all_to_all x1, waiting for transfers between devices, reduce_scatter(): moved = lax.all_to_all(x, axis, 0, 0, tiled=True)  7.05 us
    ppermute x2, starting transfers between devices, halo(): lax.ppermute(head, axis, [((i + 1) % count, i) for i in range(ends)])  6.86 us
    ppermute x2, starting transfers between devices, halo(): lax.ppermute(tail, axis, [(i, (i + 1) % count) for i in range(ends)])  5.43 us
  transfers between devices with their start and end apart: 7, of which 4 were waited for; matrix products, arithmetic and copies ran while one was open for 2% of the time, Pallas kernels for 0%

profile of v11, /device:TPU:12, one launch (start us, length us, event | category | flops | bytes accessed | tf_op | source)
XLA Modules:
  0.0 143.7 jit_solution(22258102371812047)
XLA Ops:
  4.0 1.8 %convolution_bitcast_fusion = f32[2,256,32,32]{1,2,0,3:T(8,128)S(1)} fusion(f32[32,64,32]{2,1,0:T(8,128)S(1)} %reshape.190, f32[1,256,64]{1,2,0:T(8,128)S(1)} %get-tuple-element.22, f32[1,256,64]{1,2,0:T(8,128)S(1)} %get-tuple-element.23), kind=kOutput, calls=%fused_computation.16 | convolution fusion | flops 402685952 | bytes 2490368 | tf_op jit(solution)/shard_map/cua,rab->cubr/dot_general | solution.py:49
  10.1 3.6 %gather_fusion = f32[1024,2,32]{2,1,0:T(2,128)S(1)} fusion(f32[1024,2,32]{2,1,0:T(2,128)S(1)} %copy.42, s32[1024]{0:T(1024)S(1)} %broadcast_clamp_fusion.1), kind=kCustom, calls=%fused_computation | custom fusion | bytes 528384 | tf_op jit(solution)/shard_map/jit(_take)/gather | solution.py:54
  14.2 1.8 %reshape.216 = f32[4,1,16384]{2,1,0:T(1,128)} reshape(f32[1024,2,32]{2,1,0:T(2,128)S(1)} %broadcast_multiply_fusion) | data formatting | bytes 524288
  15.9 5.3 %all-to-all-start = ((f32[4,1,16384]{2,1,0:T(1,128)}), f32[4,1,16384]{2,1,0:T(1,128)S(1)}, u32[]{:S(2)}, u32[]{:S(2)}) async-start(f32[4,1,16384]{2,1,0:T(1,128)} %reshape.216), calls=%async_computation | async-start | bytes 524288 | tf_op jit(solution)/shard_map/all_to_all | solution.py:72
  21.3 7.0 %all-to-all-done = f32[4,1,16384]{2,1,0:T(1,128)S(1)} async-done(((f32[4,1,16384]{2,1,0:T(1,128)}), f32[4,1,16384]{2,1,0:T(1,128)S(1)}, u32[]{:S(2)}, u32[]{:S(2)}) %all-to-all-start) | async-done | bytes 262176 | tf_op jit(solution)/shard_map/all_to_all | solution.py:72
  28.8 1.4 reduce
  31.9 15.8 %fusion.36 = f32[256,2,1024]{2,1,0:T(2,128)S(1)} fusion(f32[256,2,32]{2,1,0:T(2,128)S(1)} %reduce_sum.74, f32[256,32,1024]{2,1,0:T(8,128)} %param.7), kind=kOutput, calls=%fused_computation.69 | convolution fusion | flops 100663296 | bytes 35717120 | tf_op jit(solution)/shard_map/krl,kcr->kcl/dot_general | solution.py:120
  47.9 2.8 %collective-permute-done = f32[128,2,1024]{2,1,0:T(2,128)} collective-permute-done((f32[128,2,1024]{2,1,0:T(2,128)S(1)}, f32[128,2,1024]{2,1,0:T(2,128)}, u32[]{:S(2)}, u32[]{:S(2)}) %collective-permute-start) | collective-permute-done | bytes 1048608 | tf_op jit(solution)/shard_map/ppermute | solution.py:90
  50.6 1.8 %dynamic-slice_add_fusion = f32[128,2,1024]{2,1,0:T(2,128)S(1)} fusion(f32[128,2,1024]{2,1,0:T(2,128)} %collective-permute-done, f32[256,2,1024]{2,1,0:T(2,128)S(1)} %fusion.36, s32[]{:T(128)S(6)} %select_n.84), kind=kLoop, calls=%fused_computation.21 | loop fusion | flops 262144 | bytes 3145732 | tf_op jit(solution)/shard_map/add | solution.py:90
  52.4 17.4 %all_to_all.15 = f32[128,2,1024]{2,1,0:T(2,128)S(1)} all-to-all(f32[128,2,1024]{2,1,0:T(2,128)S(1)} %dynamic-slice_add_fusion), channel_id=1, replica_groups={{0,8,16,24},{4,12,20,28},{1,9,17,25},{5,13,21,29},{2,10,18,26},{6,14,22..., dimensions={0} | all-to-all | bytes 2097152 | tf_op jit(solution)/shard_map/all_to_all | solution.py:91
  70.7 15.4 %all_to_all.16 = f32[128,2,1024]{2,1,0:T(2,128)S(1)} all-to-all(f32[128,2,1024]{2,1,0:T(2,128)S(1)} %bitcast.47), channel_id=1, replica_groups={{0,8,16,24},{4,12,20,28},{1,9,17,25},{5,13,21,29},{2,10,18,26},{6,14,22..., dimensions={0} | all-to-all | bytes 2097152 | tf_op jit(solution)/shard_map/all_to_all | solution.py:101
  86.9 2.0 %collective-permute-done.1 = f32[128,2,1024]{2,1,0:T(2,128)} collective-permute-done((f32[128,2,1024]{2,1,0:T(2,128)S(1)}, f32[128,2,1024]{2,1,0:T(2,128)}, u32[]{:S(2)}, u32[]{:S(2)}) %collective-permute-start.1) | collective-permute-done | bytes 1048608 | tf_op jit(solution)/shard_map/ppermute | solution.py:102
  88.9 3.6 %fusion.1 = f32[256,2,1024]{2,1,0:T(2,128)S(1)} fusion(f32[128,2,1024]{2,1,0:T(2,128)} %collective-permute-done.1, f32[128,2,1024]{2,1,0:T(2,128)S(1)} %all_to_all.16, pred[]{:T(512)S(6)} %eq.25, pred[256,1024]{1,0:T(8,128)(4,1)S(1)} %iota_compare_fusion.1, f32[1024]{0:T(1024)S(1)} %copy-done.9), kind=kLoop, calls=%fused_computation.11 | loop fusion | flops 2621440 | bytes 4460545 | tf_op jit(solution)/shard_map/jit(_where)/select_n | solution.py:125
  92.6 11.4 %multiply_reduce_fusion = f32[256,2,32]{2,1,0:T(2,128)S(1)} fusion(f32[256,2,1024]{2,1,0:T(2,128)S(1)} %fusion.1, f32[256,32,1024]{2,1,0:T(8,128)} %param.7), kind=kLoop, calls=%fused_computation.2 | loop fusion | flops 33538048 | bytes 35717120 | tf_op jit(solution)/shard_map/reduce_sum | solution.py:126
  104.1 13.3 %all_gather.3 = f32[1024,2,32]{0,2,1:T(8,128)S(1)} all-gather(f32[256,2,32]{0,2,1:T(8,128)S(1)} %copy.43), channel_id=1, replica_groups=mesh['lat'=8,'lon'=4] {'lon'}, dimensions={0}, use_global_device_ids=true | all-gather | bytes 327680 | tf_op jit(solution)/shard_map/all_gather | solution.py:127
  117.9 3.6 %gather_fusion.1 = f32[1024,2,32]{2,1,0:T(2,128)S(1)} fusion(f32[1024,2,32]{2,1,0:T(2,128)S(1)} %copy.44, s32[1024]{0:T(1024)S(1)} %broadcast_clamp_fusion), kind=kCustom, calls=%fused_computation.1 | custom fusion | bytes 528384 | tf_op jit(solution)/shard_map/jit(_take)/gather | solution.py:62
  122.7 1.4 add_reduce_fusion
  124.1 1.8 %multiply_bitcast_fusion = (f32[32,64,32]{1,0,2:T(8,128)S(1)}, f32[32,64,32]{1,0,2:T(8,128)S(1)}) fusion(f32[1,256,64]{1,2,0:T(8,128)S(1)} %copy-done.5, f32[1,256,64]{1,2,0:T(8,128)S(1)} %copy-done.7, f32[1,256,32,32]{1,3,0,2:T(8,128)S(1)} %bitcast.45, f32[1,256,32,32]{1,3,0,2:T(8,128)S(1)} %bitcast.44), kind=kOutput, calls=%fused_computation.23 | convolution fusion | flops 403341312 | bytes 2752512 | tf_op jit(solution)/shard_map/cua,cubr->rab/dot_general | solution.py:66
  127.0 1.9 %collective-permute-start.2 = (f32[1,2048]{1,0:T(1,128)S(1)}, f32[1,2048]{1,0:T(1,128)S(1)}, u32[]{:S(2)}, u32[]{:S(2)}) collective-permute-start(f32[1,2048]{1,0:T(1,128)S(1)} %get-tuple-element.19), channel_id=1, source_target_pairs={{0,4},{4,8},{8,12},{12,16},{16,20},{20,24},{24,28},{1,5},{5,9},{9,... | collective-permute-start | bytes 24584 | tf_op jit(solution)/shard_map/ppermute | solution.py:16
  129.0 4.5 %collective-permute-start.3 = (f32[1,2048]{1,0:T(1,128)S(1)}, f32[1,2048]{1,0:T(1,128)S(1)}, u32[]{:S(2)}, u32[]{:S(2)}) collective-permute-start(f32[1,2048]{1,0:T(1,128)S(1)} %get-tuple-element.18), channel_id=1, source_target_pairs={{4,0},{8,4},{12,8},{16,12},{20,16},{24,20},{28,24},{5,1},{9,5},{13... | collective-permute-start | bytes 24584 | tf_op jit(solution)/shard_map/ppermute | solution.py:17
  133.6 3.5 %collective-permute-start.4 = (f32[32,1]{1,0:T(8,128)S(1)}, f32[32,1]{1,0:T(8,128)S(1)}, u32[]{:S(2)}, u32[]{:S(2)}) collective-permute-start(f32[32,1]{1,0:T(8,128)S(1)} %get-tuple-element.15), channel_id=1, source_target_pairs={{0,1},{1,2},{2,3},{4,5},{5,6},{6,7},{8,9},{9,10},{10,11},{12,13},{... | collective-permute-start | bytes 392 | tf_op jit(solution)/shard_map/ppermute | solution.py:16
  137.1 2.3 %collective-permute-start.5 = (f32[32,1]{1,0:T(8,128)S(1)}, f32[32,1]{1,0:T(8,128)S(1)}, u32[]{:S(2)}, u32[]{:S(2)}) collective-permute-start(f32[32,1]{1,0:T(8,128)S(1)} %get-tuple-element.14), channel_id=1, source_target_pairs={{1,0},{2,1},{3,2},{5,4},{6,5},{7,6},{9,8},{10,9},{11,10},{13,12},{... | collective-permute-start | bytes 392 | tf_op jit(solution)/shard_map/ppermute | solution.py:17
  139.8 1.2 mul.330
  141.0 1.7 %collective-permute-done.5 = f32[32,1]{1,0:T(8,128)S(1)} collective-permute-done((f32[32,1]{1,0:T(8,128)S(1)}, f32[32,1]{1,0:T(8,128)S(1)}, u32[]{:S(2)}, u32[]{:S(2)}) %collective-permute-start.5) | collective-permute-done | bytes 160 | tf_op jit(solution)/shard_map/ppermute | solution.py:17
  (70 shorter events, 16.3 us)
Async XLA Ops:
  0.9 3.1 %copy-start.4 = (f32[1,256,64]{1,2,0:T(8,128)}, f32[1,256,64]{1,2,0:T(8,128)S(1)}, u32[]{:S(2)}) copy-start(f32[1,256,64]{1,2,0:T(8,128)S(1)} %get-tuple-element.22) | copy-start | bytes 196612
  0.9 3.1 %copy-start.6 = (f32[1,256,64]{1,2,0:T(8,128)}, f32[1,256,64]{1,2,0:T(8,128)S(1)}, u32[]{:S(2)}) copy-start(f32[1,256,64]{1,2,0:T(8,128)S(1)} %get-tuple-element.23) | copy-start | bytes 196612
  1.9 0.7 copy-start
  6.7 3.4 %copy-start.8 = (s32[1024]{0:T(1024)S(1)}, s32[1024]{0:T(1024)}, u32[]{:S(2)}) copy-start(s32[1024]{0:T(1024)} %param.8) | copy-start | bytes 12292
  7.9 6.3 %copy-start.2 = (f32[4,256,32]{1,2,0:T(8,128)}, f32[4,256,32]{1,2,0:T(8,128)S(1)}, u32[]{:S(2)}) copy-start(f32[4,256,32]{1,2,0:T(8,128)S(1)} %get-tuple-element.21) | copy-start | bytes 393220
  15.9 12.4 %all-to-all-start = ((f32[4,1,16384]{2,1,0:T(1,128)}), f32[4,1,16384]{2,1,0:T(1,128)S(1)}, u32[]{:S(2)}, u32[]{:S(2)}) async-start(f32[4,1,16384]{2,1,0:T(1,128)} %reshape.216), calls=%async_computation | async-start | bytes 524288 | tf_op jit(solution)/shard_map/all_to_all | solution.py:72
  47.8 2.9 %collective-permute-start = (f32[128,2,1024]{2,1,0:T(2,128)S(1)}, f32[128,2,1024]{2,1,0:T(2,128)}, u32[]{:S(2)}, u32[]{:S(2)}) collective-permute-start(f32[128,2,1024]{2,1,0:T(2,128)S(1)} %constant_dynamic-slice_fusion), channel_id=1, source_target_pairs={{0,4},{4,0},{8,12},{12,8},{16,20},{20,16},{24,28},{28,24},{1,5},{5... | collective-permute-start | bytes 3145736 | tf_op jit(solution)/shard_map/ppermute | solution.py:90
  52.4 36.5 %copy-start.9 = (f32[1024]{0:T(1024)S(1)}, f32[1024]{0:T(1024)}, u32[]{:S(2)}) copy-start(f32[1024]{0:T(1024)} %param.9) | copy-start | bytes 12292
  86.1 2.8 %collective-permute-start.1 = (f32[128,2,1024]{2,1,0:T(2,128)S(1)}, f32[128,2,1024]{2,1,0:T(2,128)}, u32[]{:S(2)}, u32[]{:S(2)}) collective-permute-start(f32[128,2,1024]{2,1,0:T(2,128)S(1)} %all_to_all.16), channel_id=1, source_target_pairs={{0,4},{4,0},{8,12},{12,8},{16,20},{20,16},{24,28},{28,24},{1,5},{5... | collective-permute-start | bytes 3145736 | tf_op jit(solution)/shard_map/ppermute | solution.py:102
  103.9 18.7 %copy-start.3 = (f32[4,256,32]{1,2,0:T(8,128)S(1)}, f32[4,256,32]{1,2,0:T(8,128)}, u32[]{:S(2)}) copy-start(f32[4,256,32]{1,2,0:T(8,128)} %copy-done.2) | copy-start | bytes 393220
  117.9 6.2 %copy-start.5 = (f32[1,256,64]{1,2,0:T(8,128)S(1)}, f32[1,256,64]{1,2,0:T(8,128)}, u32[]{:S(2)}) copy-start(f32[1,256,64]{1,2,0:T(8,128)} %copy-done.4) | copy-start | bytes 196612
  117.9 6.2 %copy-start.7 = (f32[1,256,64]{1,2,0:T(8,128)S(1)}, f32[1,256,64]{1,2,0:T(8,128)}, u32[]{:S(2)}) copy-start(f32[1,256,64]{1,2,0:T(8,128)} %copy-done.6) | copy-start | bytes 196612
  125.9 16.9 %copy-start.1 = (f32[32,16,128]{2,1,0:T(8,128)S(1)}, f32[32,16,128]{2,1,0:T(8,128)}, u32[]{:S(2)}) copy-start(f32[32,16,128]{2,1,0:T(8,128)} %copy-done) | copy-start | bytes 786436
  127.0 15.7 %collective-permute-start.2 = (f32[1,2048]{1,0:T(1,128)S(1)}, f32[1,2048]{1,0:T(1,128)S(1)}, u32[]{:S(2)}, u32[]{:S(2)}) collective-permute-start(f32[1,2048]{1,0:T(1,128)S(1)} %get-tuple-element.19), channel_id=1, source_target_pairs={{0,4},{4,8},{8,12},{12,16},{16,20},{20,24},{24,28},{1,5},{5,9},{9,... | collective-permute-start | bytes 24584 | tf_op jit(solution)/shard_map/ppermute | solution.py:16
  129.0 13.8 %collective-permute-start.3 = (f32[1,2048]{1,0:T(1,128)S(1)}, f32[1,2048]{1,0:T(1,128)S(1)}, u32[]{:S(2)}, u32[]{:S(2)}) collective-permute-start(f32[1,2048]{1,0:T(1,128)S(1)} %get-tuple-element.18), channel_id=1, source_target_pairs={{4,0},{8,4},{12,8},{16,12},{20,16},{24,20},{28,24},{5,1},{9,5},{13... | collective-permute-start | bytes 24584 | tf_op jit(solution)/shard_map/ppermute | solution.py:17
  133.6 7.4 %collective-permute-start.4 = (f32[32,1]{1,0:T(8,128)S(1)}, f32[32,1]{1,0:T(8,128)S(1)}, u32[]{:S(2)}, u32[]{:S(2)}) collective-permute-start(f32[32,1]{1,0:T(8,128)S(1)} %get-tuple-element.15), channel_id=1, source_target_pairs={{0,1},{1,2},{2,3},{4,5},{5,6},{6,7},{8,9},{9,10},{10,11},{12,13},{... | collective-permute-start | bytes 392 | tf_op jit(solution)/shard_map/ppermute | solution.py:16
  137.1 5.6 %collective-permute-start.5 = (f32[32,1]{1,0:T(8,128)S(1)}, f32[32,1]{1,0:T(8,128)S(1)}, u32[]{:S(2)}, u32[]{:S(2)}) collective-permute-start(f32[32,1]{1,0:T(8,128)S(1)} %get-tuple-element.14), channel_id=1, source_target_pairs={{1,0},{2,1},{3,2},{5,4},{6,5},{7,6},{9,8},{10,9},{11,10},{13,12},{... | collective-permute-start | bytes 392 | tf_op jit(solution)/shard_map/ppermute | solution.py:17

commit v12 on v11

--- a/solution.py
+++ b/solution.py
@@ -41,9 +41,8 @@
     return jnp.stack([jnp.cos(alpha), jnp.sin(alpha)]), jnp.cos(beta), jnp.sin(beta)
 
 
-def forward_dft(masked, slot_order, lon_start, lon_total):
+def forward_dft(masked, slot_order, order_count, lon_start, lon_total):
     cycles, lon_width = masked.shape
-    order_count = slot_order.shape[0]
     rotor, cb, sb = dft_tables(order_count, lon_start, lon_width, lon_total)
     blocks = masked.reshape(cycles, lon_width // INNER, INNER)
     partial = jnp.einsum("cua,rab->cubr", rotor, blocks, precision=lax.Precision.HIGHEST)
@@ -116,7 +115,8 @@
         slot_order, lax.axis_index("lon") * slot_count, slot_count
     )
     forward_scale = lon_total ** (-0.5)
-    fourier = reduce_scatter(forward_dft(masked, slot_order, lon_start, lon_total) * forward_scale, "lon")
+    masked_row = lax.all_gather(masked, "lon", axis=1, tiled=True)
+    fourier = forward_dft(masked_row, own_orders, slot_total, 0, lon_total) * forward_scale
     coefficient = jnp.einsum("krl,kcr->kcl", legendre, fourier, precision=lax.Precision.HIGH)
     degree_whole = paired_all_gather(paired_reduce_scatter(coefficient, "lat"), "lat")
     degree_count = degree_whole.shape[2]

time: 144 us -> 181 us (1.26)
  waiting for transfers between devices: 13.5 us -> 30.8 us
  matrix products: 19.4 us -> 33 us
  between operations: 1.12 us -> 14.4 us
  starting transfers between devices: 17.7 us -> 12.4 us
  local copies, waits for them, and re-layouts: 18.8 us -> 16.4 us
    all_gather x0 -> x1, waiting for transfers between devices: none -> 25.7 us  [local(): masked_row = lax.all_gather(masked, 'lon', axis=1, tiled=True)]
    dot_general x1, matrix products: 1.84 us -> 15.2 us  [forward_dft(): jnp.einsum('cua,rab->cubr', rotor, blocks, precision=lax.Precision.HIGHEST)]
    all_to_all x1 -> x0, waiting for transfers between devices: 7.05 us -> none  [reduce_scatter(): moved = lax.all_to_all(x, axis, 0, 0, tiled=True)]
    all_to_all x1 -> x0, starting transfers between devices: 5.32 us -> none  [reduce_scatter(): moved = lax.all_to_all(x, axis, 0, 0, tiled=True)]
    reshape x1, local copies, waits for them, and re-layouts: 0.34 us -> 3.75 us  [forward_dft(): blocks = masked.reshape(cycles, lon_width // INNER, INNER)]
    unnamed x22 -> x12, local copies, waits for them, and re-layouts: 3.43 us -> 0.04 us
    gather x1, local copies, waits for them, and re-layouts: 3.55 us -> 0.98 us  [forward_dft(): jnp.take(by_order, slot_order, axis=0, mode='clip', unique_indices=True)]
  transfers between devices with their start and end apart: 7 -> 7, of which waited for: 4 -> 4; matrix products, arithmetic and copies ran while one was open for 2% -> 4% of each run, Pallas kernels for 0% -> 0%
where the time goes in v12:
time: 181 us; the launch traced here: 180 us
  blocking collectives  45.3 us (25%)
  matrix products  33 us (18%)
  waiting for transfers between devices  30.8 us (17%)
  other arithmetic  27.9 us (15%)
  local copies, waits for them, and re-layouts  16.4 us (9%)
  between operations  14.4 us (8%)
  starting transfers between devices  12.4 us (7%)
    all_gather x1, waiting for transfers between devices, local(): masked_row = lax.all_gather(masked, 'lon', axis=1, tiled=True)  25.7 us
    all_to_all x1, blocking collectives, paired_reduce_scatter(): lax.all_to_all(summed, axis, 0, 0, tiled=True, axis_index_groups=groups)  17.3 us
    dot_general x1, matrix products, local(): jnp.einsum('krl,kcr->kcl', legendre, fourier, precision=lax.Precision.HIGH)  16 us
    all_to_all x1, blocking collectives, paired_all_gather(): lax.all_to_all(copies, axis, 0, 0, tiled=True, axis_index_groups=groups)  15.4 us
    dot_general x1, matrix products, forward_dft(): jnp.einsum('cua,rab->cubr', rotor, blocks, precision=lax.Precision.HIGHEST)  15.2 us
    all_gather x1, blocking collectives, local(): lax.all_gather(synthesis, 'lon', axis=0, tiled=True)  12.5 us
    reduce_sum x1, other arithmetic, local(): synthesis = (legendre[:, None, :, :] * spectrum[:, :, None, :]).sum(axis=3)  11.4 us
    ppermute x2, starting transfers between devices, halo(): lax.ppermute(head, axis, [((i + 1) % count, i) for i in range(ends)])  7.35 us
  transfers between devices with their start and end apart: 7, of which 4 were waited for; matrix products, arithmetic and copies ran while one was open for 4% of the time, Pallas kernels for 0%

profile of v12, /device:TPU:12, one launch (start us, length us, event | category | flops | bytes accessed | tf_op | source)
XLA Modules:
  0.0 180.2 jit_solution(1363750176208509001)
XLA Ops:
  8.1 1.8 bitcast_multiply_fusion.1
  11.7 1.8 fusion.50
  13.5 25.7 %all-gather.2.cloned.1.call-done = f32[32,8192]{1,0:T(8,128)} async-done(((f32[32,2048]{1,0:T(8,128)}), f32[32,8192]{1,0:T(8,128)}) %all-gather.2.cloned.1.call-update) | async-done | bytes 1048592 | tf_op jit(solution)/shard_map/all_gather | solution.py:118
  39.2 3.7 %reshape.283 = f32[32,256,32]{2,1,0:T(8,128)} reshape(f32[32,8192]{1,0:T(8,128)} %all-gather.2.cloned.1.call-done) | data formatting | bytes 2097152 | tf_op jit(solution)/shard_map/reshape | solution.py:47
  42.9 15.2 %fusion.8 = f32[2,256,32,32]{1,2,0,3:T(8,128)S(1)} fusion(f32[32,256,32]{2,1,0:T(8,128)} %reshape.283, f32[1,256,256]{2,1,0:T(8,128)S(1)} %get-tuple-element.24, f32[1,256,256]{2,1,0:T(8,128)S(1)} %get-tuple-element.25), kind=kOutput, calls=%fused_computation.18 | convolution fusion | flops 1610743808 | bytes 3670016 | tf_op jit(solution)/shard_map/cua,rab->cubr/dot_general | solution.py:48
  59.5 1.2 subtract_reduce_fusion.1
  62.6 16.0 %fusion.23 = f32[256,2,1024]{2,1,0:T(2,128)S(1)} fusion(f32[256,32,1024]{2,1,0:T(8,128)} %param.7, f32[256,2,32]{2,1,0:T(2,128)S(1)} %gather_fusion), kind=kOutput, calls=%fused_computation.44 | convolution fusion | flops 100679680 | bytes 35717120 | tf_op jit(solution)/shard_map/krl,kcr->kcl/dot_general | solution.py:120
  78.8 2.8 %collective-permute-done = f32[128,2,1024]{2,1,0:T(2,128)} collective-permute-done((f32[128,2,1024]{2,1,0:T(2,128)S(1)}, f32[128,2,1024]{2,1,0:T(2,128)}, u32[]{:S(2)}, u32[]{:S(2)}) %collective-permute-start) | collective-permute-done | bytes 1048608 | tf_op jit(solution)/shard_map/ppermute | solution.py:89
  81.6 1.8 dynamic-slice_add_fusion
  83.3 17.3 %all_to_all.10 = f32[128,2,1024]{2,1,0:T(2,128)S(1)} all-to-all(f32[128,2,1024]{2,1,0:T(2,128)S(1)} %dynamic-slice_add_fusion), channel_id=1, replica_groups={{0,8,16,24},{4,12,20,28},{1,9,17,25},{5,13,21,29},{2,10,18,26},{6,14,22..., dimensions={0} | all-to-all | bytes 2097152 | tf_op jit(solution)/shard_map/all_to_all | solution.py:90
  101.6 15.4 %all_to_all.11 = f32[128,2,1024]{2,1,0:T(2,128)S(1)} all-to-all(f32[128,2,1024]{2,1,0:T(2,128)S(1)} %bitcast.48), channel_id=1, replica_groups={{0,8,16,24},{4,12,20,28},{1,9,17,25},{5,13,21,29},{2,10,18,26},{6,14,22..., dimensions={0} | all-to-all | bytes 2097152 | tf_op jit(solution)/shard_map/all_to_all | solution.py:100
  118.7 1.1 collective-permute-done.1
  119.8 3.7 %fusion.3 = f32[256,2,1024]{2,1,0:T(2,128)S(1)} fusion(f32[128,2,1024]{2,1,0:T(2,128)} %collective-permute-done.1, f32[128,2,1024]{2,1,0:T(2,128)S(1)} %all_to_all.11, pred[]{:T(512)S(6)} %eq.26, pred[256,1024]{1,0:T(8,128)(4,1)S(1)} %iota_compare_fusion.1, f32[1024]{0:T(1024)S(1)} %copy-done.4), kind=kLoop, calls=%fused_computation.13 | loop fusion | flops 2621440 | bytes 4460545 | tf_op jit(solution)/shard_map/jit(_where)/select_n | solution.py:125
  123.5 11.4 %multiply_reduce_fusion = f32[256,2,32]{2,1,0:T(2,128)S(1)} fusion(f32[256,2,1024]{2,1,0:T(2,128)S(1)} %fusion.3, f32[256,32,1024]{2,1,0:T(8,128)} %param.7), kind=kLoop, calls=%fused_computation.2 | loop fusion | flops 33538048 | bytes 35717120 | tf_op jit(solution)/shard_map/reduce_sum | solution.py:126
  135.0 12.5 %all_gather.7 = f32[1024,2,32]{0,2,1:T(8,128)S(1)} all-gather(f32[256,2,32]{0,2,1:T(8,128)S(1)} %copy.51), channel_id=1, replica_groups=mesh['lat'=8,'lon'=4] {'lon'}, dimensions={0}, use_global_device_ids=true | all-gather | bytes 327680 | tf_op jit(solution)/shard_map/all_gather | solution.py:127
  148.1 3.6 %gather_fusion.1 = f32[1024,2,32]{2,1,0:T(2,128)S(1)} fusion(f32[1024,2,32]{2,1,0:T(2,128)S(1)} %copy.52, s32[1024]{0:T(1024)S(1)} %broadcast_clamp_fusion), kind=kCustom, calls=%fused_computation.1 | custom fusion | bytes 528384 | tf_op jit(solution)/shard_map/jit(_take)/gather | solution.py:61
  152.8 1.4 add_reduce_fusion
  154.2 1.8 multiply_bitcast_fusion
  157.1 1.9 %collective-permute-start.2 = (f32[1,2048]{1,0:T(1,128)S(1)}, f32[1,2048]{1,0:T(1,128)S(1)}, u32[]{:S(2)}, u32[]{:S(2)}) collective-permute-start(f32[1,2048]{1,0:T(1,128)S(1)} %get-tuple-element.19), channel_id=1, source_target_pairs={{0,4},{4,8},{8,12},{12,16},{16,20},{20,24},{24,28},{1,5},{5,9},{9,... | collective-permute-start | bytes 24584 | tf_op jit(solution)/shard_map/ppermute | solution.py:16
  159.1 4.5 %collective-permute-start.3 = (f32[1,2048]{1,0:T(1,128)S(1)}, f32[1,2048]{1,0:T(1,128)S(1)}, u32[]{:S(2)}, u32[]{:S(2)}) collective-permute-start(f32[1,2048]{1,0:T(1,128)S(1)} %get-tuple-element.18), channel_id=1, source_target_pairs={{4,0},{8,4},{12,8},{16,12},{20,16},{24,20},{28,24},{5,1},{9,5},{13... | collective-permute-start | bytes 24584 | tf_op jit(solution)/shard_map/ppermute | solution.py:17
  163.7 3.0 %collective-permute-start.4 = (f32[32,1]{1,0:T(8,128)S(1)}, f32[32,1]{1,0:T(8,128)S(1)}, u32[]{:S(2)}, u32[]{:S(2)}) collective-permute-start(f32[32,1]{1,0:T(8,128)S(1)} %get-tuple-element.15), channel_id=1, source_target_pairs={{0,1},{1,2},{2,3},{4,5},{5,6},{6,7},{8,9},{9,10},{10,11},{12,13},{... | collective-permute-start | bytes 392 | tf_op jit(solution)/shard_map/ppermute | solution.py:16
  166.7 2.8 %collective-permute-start.5 = (f32[32,1]{1,0:T(8,128)S(1)}, f32[32,1]{1,0:T(8,128)S(1)}, u32[]{:S(2)}, u32[]{:S(2)}) collective-permute-start(f32[32,1]{1,0:T(8,128)S(1)} %get-tuple-element.14), channel_id=1, source_target_pairs={{1,0},{2,1},{3,2},{5,4},{6,5},{7,6},{9,8},{10,9},{11,10},{13,12},{... | collective-permute-start | bytes 392 | tf_op jit(solution)/shard_map/ppermute | solution.py:17
  169.9 1.2 mul.457
  171.1 1.2 collective-permute-done.5
  (58 shorter events, 13.0 us)
Async XLA Ops:
  7.2 32.0 %all-gather.2.cloned.1.call-start = ((), (), s32[]{:S(2)}) async-start(), calls=%async_computation.2 | async-start | bytes 1310720 | tf_op jit(solution)/shard_map/all_gather | solution.py:118
  78.7 2.9 %collective-permute-start = (f32[128,2,1024]{2,1,0:T(2,128)S(1)}, f32[128,2,1024]{2,1,0:T(2,128)}, u32[]{:S(2)}, u32[]{:S(2)}) collective-permute-start(f32[128,2,1024]{2,1,0:T(2,128)S(1)} %constant_dynamic-slice_fusion), channel_id=1, source_target_pairs={{0,4},{4,0},{8,12},{12,8},{16,20},{20,16},{24,28},{28,24},{1,5},{5... | collective-permute-start | bytes 3145736 | tf_op jit(solution)/shard_map/ppermute | solution.py:89
  83.3 34.6 %copy-start.5 = (s32[1024]{0:T(1024)S(1)}, s32[1024]{0:T(1024)}, u32[]{:S(2)}) copy-start(s32[1024]{0:T(1024)} %param.8) | copy-start | bytes 12292
  83.3 36.5 %copy-start.4 = (f32[1024]{0:T(1024)S(1)}, f32[1024]{0:T(1024)}, u32[]{:S(2)}) copy-start(f32[1024]{0:T(1024)} %param.9) | copy-start | bytes 12292
  117.0 2.8 %collective-permute-start.1 = (f32[128,2,1024]{2,1,0:T(2,128)S(1)}, f32[128,2,1024]{2,1,0:T(2,128)}, u32[]{:S(2)}, u32[]{:S(2)}) collective-permute-start(f32[128,2,1024]{2,1,0:T(2,128)S(1)} %all_to_all.11), channel_id=1, source_target_pairs={{0,4},{4,0},{8,12},{12,8},{16,20},{20,16},{24,28},{28,24},{1,5},{5... | collective-permute-start | bytes 3145736 | tf_op jit(solution)/shard_map/ppermute | solution.py:101
  134.9 17.9 %copy-start.1 = (f32[4,256,32]{1,2,0:T(8,128)S(1)}, f32[4,256,32]{1,2,0:T(8,128)}, u32[]{:S(2)}) copy-start(f32[4,256,32]{1,2,0:T(8,128)} %get-tuple-element.21) | copy-start | bytes 393220
  148.0 6.2 %copy-start.2 = (f32[1,256,64]{1,2,0:T(8,128)S(1)}, f32[1,256,64]{1,2,0:T(8,128)}, u32[]{:S(2)}) copy-start(f32[1,256,64]{1,2,0:T(8,128)} %get-tuple-element.26) | copy-start | bytes 196612
  148.0 6.2 %copy-start.3 = (f32[1,256,64]{1,2,0:T(8,128)S(1)}, f32[1,256,64]{1,2,0:T(8,128)}, u32[]{:S(2)}) copy-start(f32[1,256,64]{1,2,0:T(8,128)} %get-tuple-element.27) | copy-start | bytes 196612
  152.8 4.1 %copy-start = (f32[32,2048]{1,0:T(8,128)S(1)}, f32[32,2048]{1,0:T(8,128)}, u32[]{:S(2)}) copy-start(f32[32,2048]{1,0:T(8,128)} %bitcast_multiply_fusion.1) | copy-start | bytes 786436
  157.1 15.2 %collective-permute-start.2 = (f32[1,2048]{1,0:T(1,128)S(1)}, f32[1,2048]{1,0:T(1,128)S(1)}, u32[]{:S(2)}, u32[]{:S(2)}) collective-permute-start(f32[1,2048]{1,0:T(1,128)S(1)} %get-tuple-element.19), channel_id=1, source_target_pairs={{0,4},{4,8},{8,12},{12,16},{16,20},{20,24},{24,28},{1,5},{5,9},{9,... | collective-permute-start | bytes 24584 | tf_op jit(solution)/shard_map/ppermute | solution.py:16
  159.1 13.3 %collective-permute-start.3 = (f32[1,2048]{1,0:T(1,128)S(1)}, f32[1,2048]{1,0:T(1,128)S(1)}, u32[]{:S(2)}, u32[]{:S(2)}) collective-permute-start(f32[1,2048]{1,0:T(1,128)S(1)} %get-tuple-element.18), channel_id=1, source_target_pairs={{4,0},{8,4},{12,8},{16,12},{20,16},{24,20},{28,24},{5,1},{9,5},{13... | collective-permute-start | bytes 24584 | tf_op jit(solution)/shard_map/ppermute | solution.py:17
  163.7 7.4 %collective-permute-start.4 = (f32[32,1]{1,0:T(8,128)S(1)}, f32[32,1]{1,0:T(8,128)S(1)}, u32[]{:S(2)}, u32[]{:S(2)}) collective-permute-start(f32[32,1]{1,0:T(8,128)S(1)} %get-tuple-element.15), channel_id=1, source_target_pairs={{0,1},{1,2},{2,3},{4,5},{5,6},{6,7},{8,9},{9,10},{10,11},{12,13},{... | collective-permute-start | bytes 392 | tf_op jit(solution)/shard_map/ppermute | solution.py:16
  166.7 5.6 %collective-permute-start.5 = (f32[32,1]{1,0:T(8,128)S(1)}, f32[32,1]{1,0:T(8,128)S(1)}, u32[]{:S(2)}, u32[]{:S(2)}) collective-permute-start(f32[32,1]{1,0:T(8,128)S(1)} %get-tuple-element.14), channel_id=1, source_target_pairs={{1,0},{2,1},{3,2},{5,4},{6,5},{7,6},{9,8},{10,9},{11,10},{13,12},{... | collective-permute-start | bytes 392 | tf_op jit(solution)/shard_map/ppermute | solution.py:17
Sparse Core Ops, SparseCore 0:
  10.1 28.9 all-gather.1

commit v13 on v11

--- a/solution.py
+++ b/solution.py
@@ -50,7 +50,7 @@
     gc, gs = partial[0][None], partial[1][None]
     fc = (cb[..., None] * gc - sb[..., None] * gs).sum(axis=2)
     fs = (sb[..., None] * gc + cb[..., None] * gs).sum(axis=2)
-    by_order = jnp.stack([fc, fs], axis=2).reshape(order_count, 2, cycles)
+    by_order = jnp.stack([fc, fs], axis=2).reshape(order_count, 2 * cycles)
     return jnp.take(by_order, slot_order, axis=0, mode="clip", unique_indices=True)
 
 
@@ -117,6 +117,7 @@
     )
     forward_scale = lon_total ** (-0.5)
     fourier = reduce_scatter(forward_dft(masked, slot_order, lon_start, lon_total) * forward_scale, "lon")
+    fourier = fourier.reshape(slot_count, 2, cycle_count)
     coefficient = jnp.einsum("krl,kcr->kcl", legendre, fourier, precision=lax.Precision.HIGH)
     degree_whole = paired_all_gather(paired_reduce_scatter(coefficient, "lat"), "lat")
     degree_count = degree_whole.shape[2]

time: 144 us -> 138 us (0.958)
  local copies, waits for them, and re-layouts: 18.8 us -> 15.5 us
  other arithmetic: 27 us -> 24.4 us
    unnamed x22 -> x21, local copies, waits for them, and re-layouts: 3.43 us -> 0.79 us
where the time goes in v13:
time: 138 us
  blocking collectives  46.3 us (34%)
  other arithmetic  24.4 us (18%)
  matrix products  19.4 us (14%)
  starting transfers between devices  17.7 us (13%)
  local copies, waits for them, and re-layouts  15.5 us (11%)
  waiting for transfers between devices  13.5 us (10%)
    all_to_all x1, blocking collectives, paired_reduce_scatter(): lax.all_to_all(summed, axis, 0, 0, tiled=True, axis_index_groups=groups)  17.4 us
    dot_general x1, matrix products, local(): jnp.einsum('krl,kcr->kcl', legendre, fourier, precision=lax.Precision.HIGH)  15.8 us
    all_to_all x1, blocking collectives, paired_all_gather(): lax.all_to_all(copies, axis, 0, 0, tiled=True, axis_index_groups=groups)  15.4 us
    all_gather x1, blocking collectives, local(): lax.all_gather(synthesis, 'lon', axis=0, tiled=True)  13.5 us
    reduce_sum x1, other arithmetic, local(): synthesis = (legendre[:, None, :, :] * spectrum[:, :, None, :]).sum(axis=3)  11.4 us
    all_to_all x1, waiting for transfers between devices, reduce_scatter(): moved = lax.all_to_all(x, axis, 0, 0, tiled=True)  7.05 us
    ppermute x2, starting transfers between devices, halo(): lax.ppermute(head, axis, [((i + 1) % count, i) for i in range(ends)])  6.85 us
    ppermute x2, starting transfers between devices, halo(): lax.ppermute(tail, axis, [(i, (i + 1) % count) for i in range(ends)])  5.44 us
  transfers between devices with their start and end apart: 7, of which 4 were waited for; matrix products, arithmetic and copies ran while one was open for 2% of the time, Pallas kernels for 0%

profile of v13, /device:TPU:12, one launch (start us, length us, event | category | flops | bytes accessed | tf_op | source)
XLA Modules:
  0.0 137.9 jit_solution(16198514489690938704)
XLA Ops:
  2.6 1.1 bitcast_multiply_fusion.1
  4.0 1.8 %convolution_bitcast_fusion = f32[2,256,32,32]{1,2,0,3:T(8,128)S(1)} fusion(f32[32,64,32]{2,1,0:T(8,128)S(1)} %reshape.195, f32[1,256,64]{1,2,0:T(8,128)S(1)} %get-tuple-element.22, f32[1,256,64]{1,2,0:T(8,128)S(1)} %get-tuple-element.23), kind=kOutput, calls=%fused_computation.16 | convolution fusion | flops 402685952 | bytes 2490368 | tf_op jit(solution)/shard_map/cua,rab->cubr/dot_general | solution.py:49
  7.9 1.2 subtract_reduce_fusion.1
  9.6 2.8 %gather_fusion = f32[1024,64]{1,0:T(8,128)S(1)} fusion(f32[1024,64]{1,0:T(8,128)S(1)} %copy.36, s32[1024]{0:T(1024)S(1)} %broadcast_clamp_fusion.1), kind=kCustom, calls=%fused_computation | custom fusion | bytes 528384 | tf_op jit(solution)/shard_map/jit(_take)/gather | solution.py:54
  13.4 5.3 %all-to-all-start = ((f32[4,256,64]{1,2,0:T(8,128)}), f32[4,256,64]{1,2,0:T(8,128)S(1)}, u32[]{:S(2)}, u32[]{:S(2)}) async-start(f32[4,256,64]{1,2,0:T(8,128)} %copy.37), calls=%async_computation | async-start | bytes 524288 | tf_op jit(solution)/shard_map/all_to_all | solution.py:72
  18.7 7.0 %all-to-all-done = f32[4,256,64]{1,2,0:T(8,128)S(1)} async-done(((f32[4,256,64]{1,2,0:T(8,128)}), f32[4,256,64]{1,2,0:T(8,128)S(1)}, u32[]{:S(2)}, u32[]{:S(2)}) %all-to-all-start) | async-done | bytes 262176 | tf_op jit(solution)/shard_map/all_to_all | solution.py:72
  25.9 15.8 %fusion.36 = f32[256,2,1024]{2,1,0:T(2,128)S(1)} fusion(f32[256,2,32]{2,1,0:T(2,128)S(1)} %copy.40, f32[256,32,1024]{2,1,0:T(8,128)} %param.7), kind=kOutput, calls=%fused_computation.69 | convolution fusion | flops 100663296 | bytes 35717120 | tf_op jit(solution)/shard_map/krl,kcr->kcl/dot_general | solution.py:121
  41.9 2.8 %collective-permute-done = f32[128,2,1024]{2,1,0:T(2,128)} collective-permute-done((f32[128,2,1024]{2,1,0:T(2,128)S(1)}, f32[128,2,1024]{2,1,0:T(2,128)}, u32[]{:S(2)}, u32[]{:S(2)}) %collective-permute-start) | collective-permute-done | bytes 1048608 | tf_op jit(solution)/shard_map/ppermute | solution.py:90
  44.7 1.8 %dynamic-slice_add_fusion = f32[128,2,1024]{2,1,0:T(2,128)S(1)} fusion(f32[128,2,1024]{2,1,0:T(2,128)} %collective-permute-done, f32[256,2,1024]{2,1,0:T(2,128)S(1)} %fusion.36, s32[]{:T(128)S(6)} %select_n.84), kind=kLoop, calls=%fused_computation.21 | loop fusion | flops 262144 | bytes 3145732 | tf_op jit(solution)/shard_map/add | solution.py:90
  46.4 17.4 %all_to_all.16 = f32[128,2,1024]{2,1,0:T(2,128)S(1)} all-to-all(f32[128,2,1024]{2,1,0:T(2,128)S(1)} %dynamic-slice_add_fusion), channel_id=1, replica_groups={{0,8,16,24},{4,12,20,28},{1,9,17,25},{5,13,21,29},{2,10,18,26},{6,14,22..., dimensions={0} | all-to-all | bytes 2097152 | tf_op jit(solution)/shard_map/all_to_all | solution.py:91
  64.7 15.4 %all_to_all.17 = f32[128,2,1024]{2,1,0:T(2,128)S(1)} all-to-all(f32[128,2,1024]{2,1,0:T(2,128)S(1)} %bitcast.50), channel_id=1, replica_groups={{0,8,16,24},{4,12,20,28},{1,9,17,25},{5,13,21,29},{2,10,18,26},{6,14,22..., dimensions={0} | all-to-all | bytes 2097152 | tf_op jit(solution)/shard_map/all_to_all | solution.py:101
  81.0 2.0 %collective-permute-done.1 = f32[128,2,1024]{2,1,0:T(2,128)} collective-permute-done((f32[128,2,1024]{2,1,0:T(2,128)S(1)}, f32[128,2,1024]{2,1,0:T(2,128)}, u32[]{:S(2)}, u32[]{:S(2)}) %collective-permute-start.1) | collective-permute-done | bytes 1048608 | tf_op jit(solution)/shard_map/ppermute | solution.py:102
  83.0 3.6 %fusion.1 = f32[256,2,1024]{2,1,0:T(2,128)S(1)} fusion(f32[128,2,1024]{2,1,0:T(2,128)} %collective-permute-done.1, f32[128,2,1024]{2,1,0:T(2,128)S(1)} %all_to_all.17, pred[]{:T(512)S(6)} %eq.25, pred[256,1024]{1,0:T(8,128)(4,1)S(1)} %iota_compare_fusion.1, f32[1024]{0:T(1024)S(1)} %copy-done.9), kind=kLoop, calls=%fused_computation.11 | loop fusion | flops 2621440 | bytes 4460545 | tf_op jit(solution)/shard_map/jit(_where)/select_n | solution.py:126
  86.6 11.4 %multiply_reduce_fusion = f32[256,2,32]{2,1,0:T(2,128)S(1)} fusion(f32[256,2,1024]{2,1,0:T(2,128)S(1)} %fusion.1, f32[256,32,1024]{2,1,0:T(8,128)} %param.7), kind=kLoop, calls=%fused_computation.2 | loop fusion | flops 33538048 | bytes 35717120 | tf_op jit(solution)/shard_map/reduce_sum | solution.py:127
  98.1 13.5 %all_gather.3 = f32[1024,2,32]{0,2,1:T(8,128)S(1)} all-gather(f32[256,2,32]{0,2,1:T(8,128)S(1)} %copy.41), channel_id=1, replica_groups=mesh['lat'=8,'lon'=4] {'lon'}, dimensions={0}, use_global_device_ids=true | all-gather | bytes 327680 | tf_op jit(solution)/shard_map/all_gather | solution.py:128
  112.2 3.5 %gather_fusion.1 = f32[1024,2,32]{2,1,0:T(2,128)S(1)} fusion(f32[1024,2,32]{2,1,0:T(2,128)S(1)} %copy.42, s32[1024]{0:T(1024)S(1)} %broadcast_clamp_fusion), kind=kCustom, calls=%fused_computation.1 | custom fusion | bytes 528384 | tf_op jit(solution)/shard_map/jit(_take)/gather | solution.py:62
  116.9 1.4 %add_reduce_fusion = (f32[256,32,32]{0,2,1:T(8,128)S(1)}, f32[256,32,32]{0,2,1:T(8,128)S(1)}) fusion(f32[4,256,32]{1,2,0:T(8,128)S(1)} %copy.44, f32[4,256,32]{1,2,0:T(8,128)S(1)} %copy.43, f32[4,256,32]{1,2,0:T(8,128)S(1)} %copy-done.3, f32[4,256,32]{1,2,0:T(8,128)S(1)} %get-tuple-element.20), kind=kLoop, calls=%fused_computation.4 | loop fusion | flops 7864320 | bytes 2621440 | tf_op jit(solution)/shard_map/reduce_sum | solution.py:64
  118.3 1.8 %multiply_bitcast_fusion = (f32[32,64,32]{1,0,2:T(8,128)S(1)}, f32[32,64,32]{1,0,2:T(8,128)S(1)}) fusion(f32[1,256,64]{1,2,0:T(8,128)S(1)} %copy-done.5, f32[1,256,64]{1,2,0:T(8,128)S(1)} %copy-done.7, f32[1,256,32,32]{1,3,0,2:T(8,128)S(1)} %bitcast.49, f32[1,256,32,32]{1,3,0,2:T(8,128)S(1)} %bitcast.48), kind=kOutput, calls=%fused_computation.23 | convolution fusion | flops 403341312 | bytes 2752512 | tf_op jit(solution)/shard_map/cua,cubr->rab/dot_general | solution.py:66
  121.3 1.9 %collective-permute-start.2 = (f32[1,2048]{1,0:T(1,128)S(1)}, f32[1,2048]{1,0:T(1,128)S(1)}, u32[]{:S(2)}, u32[]{:S(2)}) collective-permute-start(f32[1,2048]{1,0:T(1,128)S(1)} %get-tuple-element.19), channel_id=1, source_target_pairs={{0,4},{4,8},{8,12},{12,16},{16,20},{20,24},{24,28},{1,5},{5,9},{9,... | collective-permute-start | bytes 24584 | tf_op jit(solution)/shard_map/ppermute | solution.py:16
  123.2 4.5 %collective-permute-start.3 = (f32[1,2048]{1,0:T(1,128)S(1)}, f32[1,2048]{1,0:T(1,128)S(1)}, u32[]{:S(2)}, u32[]{:S(2)}) collective-permute-start(f32[1,2048]{1,0:T(1,128)S(1)} %get-tuple-element.18), channel_id=1, source_target_pairs={{4,0},{8,4},{12,8},{16,12},{20,16},{24,20},{28,24},{5,1},{9,5},{13... | collective-permute-start | bytes 24584 | tf_op jit(solution)/shard_map/ppermute | solution.py:17
  127.8 3.5 %collective-permute-start.4 = (f32[32,1]{1,0:T(8,128)S(1)}, f32[32,1]{1,0:T(8,128)S(1)}, u32[]{:S(2)}, u32[]{:S(2)}) collective-permute-start(f32[32,1]{1,0:T(8,128)S(1)} %get-tuple-element.15), channel_id=1, source_target_pairs={{0,1},{1,2},{2,3},{4,5},{5,6},{6,7},{8,9},{9,10},{10,11},{12,13},{... | collective-permute-start | bytes 392 | tf_op jit(solution)/shard_map/ppermute | solution.py:16
  131.3 2.3 %collective-permute-start.5 = (f32[32,1]{1,0:T(8,128)S(1)}, f32[32,1]{1,0:T(8,128)S(1)}, u32[]{:S(2)}, u32[]{:S(2)}) collective-permute-start(f32[32,1]{1,0:T(8,128)S(1)} %get-tuple-element.14), channel_id=1, source_target_pairs={{1,0},{2,1},{3,2},{5,4},{6,5},{7,6},{9,8},{10,9},{11,10},{13,12},{... | collective-permute-start | bytes 392 | tf_op jit(solution)/shard_map/ppermute | solution.py:17
  134.1 1.2 mul.335
  135.3 1.7 %collective-permute-done.5 = f32[32,1]{1,0:T(8,128)S(1)} collective-permute-done((f32[32,1]{1,0:T(8,128)S(1)}, f32[32,1]{1,0:T(8,128)S(1)}, u32[]{:S(2)}, u32[]{:S(2)}) %collective-permute-start.5) | collective-permute-done | bytes 160 | tf_op jit(solution)/shard_map/ppermute | solution.py:17
  (66 shorter events, 12.0 us)
Async XLA Ops:
  0.9 3.1 %copy-start.4 = (f32[1,256,64]{1,2,0:T(8,128)}, f32[1,256,64]{1,2,0:T(8,128)S(1)}, u32[]{:S(2)}) copy-start(f32[1,256,64]{1,2,0:T(8,128)S(1)} %get-tuple-element.22) | copy-start | bytes 196612
  0.9 3.1 %copy-start.6 = (f32[1,256,64]{1,2,0:T(8,128)}, f32[1,256,64]{1,2,0:T(8,128)S(1)}, u32[]{:S(2)}) copy-start(f32[1,256,64]{1,2,0:T(8,128)S(1)} %get-tuple-element.23) | copy-start | bytes 196612
  1.9 0.7 copy-start
  6.7 2.9 %copy-start.8 = (s32[1024]{0:T(1024)S(1)}, s32[1024]{0:T(1024)}, u32[]{:S(2)}) copy-start(s32[1024]{0:T(1024)} %param.8) | copy-start | bytes 12292
  7.9 4.5 %copy-start.2 = (f32[4,256,32]{1,2,0:T(8,128)}, f32[4,256,32]{1,2,0:T(8,128)S(1)}, u32[]{:S(2)}) copy-start(f32[4,256,32]{1,2,0:T(8,128)S(1)} %get-tuple-element.21) | copy-start | bytes 393220
  13.4 12.4 %all-to-all-start = ((f32[4,256,64]{1,2,0:T(8,128)}), f32[4,256,64]{1,2,0:T(8,128)S(1)}, u32[]{:S(2)}, u32[]{:S(2)}) async-start(f32[4,256,64]{1,2,0:T(8,128)} %copy.37), calls=%async_computation | async-start | bytes 524288 | tf_op jit(solution)/shard_map/all_to_all | solution.py:72
  41.8 2.9 %collective-permute-start = (f32[128,2,1024]{2,1,0:T(2,128)S(1)}, f32[128,2,1024]{2,1,0:T(2,128)}, u32[]{:S(2)}, u32[]{:S(2)}) collective-permute-start(f32[128,2,1024]{2,1,0:T(2,128)S(1)} %constant_dynamic-slice_fusion), channel_id=1, source_target_pairs={{0,4},{4,0},{8,12},{12,8},{16,20},{20,16},{24,28},{28,24},{1,5},{5... | collective-permute-start | bytes 3145736 | tf_op jit(solution)/shard_map/ppermute | solution.py:90
  46.4 36.5 %copy-start.9 = (f32[1024]{0:T(1024)S(1)}, f32[1024]{0:T(1024)}, u32[]{:S(2)}) copy-start(f32[1024]{0:T(1024)} %param.9) | copy-start | bytes 12292
  80.2 2.8 %collective-permute-start.1 = (f32[128,2,1024]{2,1,0:T(2,128)S(1)}, f32[128,2,1024]{2,1,0:T(2,128)}, u32[]{:S(2)}, u32[]{:S(2)}) collective-permute-start(f32[128,2,1024]{2,1,0:T(2,128)S(1)} %all_to_all.17), channel_id=1, source_target_pairs={{0,4},{4,0},{8,12},{12,8},{16,20},{20,16},{24,28},{28,24},{1,5},{5... | collective-permute-start | bytes 3145736 | tf_op jit(solution)/shard_map/ppermute | solution.py:102
  98.0 18.9 %copy-start.3 = (f32[4,256,32]{1,2,0:T(8,128)S(1)}, f32[4,256,32]{1,2,0:T(8,128)}, u32[]{:S(2)}) copy-start(f32[4,256,32]{1,2,0:T(8,128)} %copy-done.2) | copy-start | bytes 393220
  112.2 6.2 %copy-start.5 = (f32[1,256,64]{1,2,0:T(8,128)S(1)}, f32[1,256,64]{1,2,0:T(8,128)}, u32[]{:S(2)}) copy-start(f32[1,256,64]{1,2,0:T(8,128)} %copy-done.4) | copy-start | bytes 196612
  112.2 6.2 %copy-start.7 = (f32[1,256,64]{1,2,0:T(8,128)S(1)}, f32[1,256,64]{1,2,0:T(8,128)}, u32[]{:S(2)}) copy-start(f32[1,256,64]{1,2,0:T(8,128)} %copy-done.6) | copy-start | bytes 196612
  120.1 16.9 %copy-start.1 = (f32[32,16,128]{2,1,0:T(8,128)S(1)}, f32[32,16,128]{2,1,0:T(8,128)}, u32[]{:S(2)}) copy-start(f32[32,16,128]{2,1,0:T(8,128)} %copy-done) | copy-start | bytes 786436
  121.3 15.7 %collective-permute-start.2 = (f32[1,2048]{1,0:T(1,128)S(1)}, f32[1,2048]{1,0:T(1,128)S(1)}, u32[]{:S(2)}, u32[]{:S(2)}) collective-permute-start(f32[1,2048]{1,0:T(1,128)S(1)} %get-tuple-element.19), channel_id=1, source_target_pairs={{0,4},{4,8},{8,12},{12,16},{16,20},{20,24},{24,28},{1,5},{5,9},{9,... | collective-permute-start | bytes 24584 | tf_op jit(solution)/shard_map/ppermute | solution.py:16
  123.2 13.8 %collective-permute-start.3 = (f32[1,2048]{1,0:T(1,128)S(1)}, f32[1,2048]{1,0:T(1,128)S(1)}, u32[]{:S(2)}, u32[]{:S(2)}) collective-permute-start(f32[1,2048]{1,0:T(1,128)S(1)} %get-tuple-element.18), channel_id=1, source_target_pairs={{4,0},{8,4},{12,8},{16,12},{20,16},{24,20},{28,24},{5,1},{9,5},{13... | collective-permute-start | bytes 24584 | tf_op jit(solution)/shard_map/ppermute | solution.py:17
  127.8 7.4 %collective-permute-start.4 = (f32[32,1]{1,0:T(8,128)S(1)}, f32[32,1]{1,0:T(8,128)S(1)}, u32[]{:S(2)}, u32[]{:S(2)}) collective-permute-start(f32[32,1]{1,0:T(8,128)S(1)} %get-tuple-element.15), channel_id=1, source_target_pairs={{0,1},{1,2},{2,3},{4,5},{5,6},{6,7},{8,9},{9,10},{10,11},{12,13},{... | collective-permute-start | bytes 392 | tf_op jit(solution)/shard_map/ppermute | solution.py:16
  131.3 5.6 %collective-permute-start.5 = (f32[32,1]{1,0:T(8,128)S(1)}, f32[32,1]{1,0:T(8,128)S(1)}, u32[]{:S(2)}, u32[]{:S(2)}) collective-permute-start(f32[32,1]{1,0:T(8,128)S(1)} %get-tuple-element.14), channel_id=1, source_target_pairs={{1,0},{2,1},{3,2},{5,4},{6,5},{7,6},{9,8},{10,9},{11,10},{13,12},{... | collective-permute-start | bytes 392 | tf_op jit(solution)/shard_map/ppermute | solution.py:17

commit v14 on v13

--- a/solution.py
+++ b/solution.py
@@ -55,7 +55,8 @@
 
 
 def inverse_dft(synthesis, slot_order, lon_start, lon_width, lon_total):
-    order_count, _, cycles = synthesis.shape
+    order_count, width = synthesis.shape
+    cycles = width // 2
     rotor, cb, sb = dft_tables(order_count, lon_start, lon_width, lon_total)
     slots = jnp.arange(order_count, dtype=jnp.int32)
     slot_of = jnp.where(slot_order[None, :] == slots[:, None], slots[None, :], 0).sum(axis=1)
@@ -125,7 +126,7 @@
     retained = degrees[None, :] >= own_orders[:, None]
     spectrum = jnp.where(retained[:, None, :], love_gain[None, None, :] * degree_whole, 0.0)
     synthesis = (legendre[:, None, :, :] * spectrum[:, :, None, :]).sum(axis=3)
-    summed = inverse_dft(lax.all_gather(synthesis, "lon", axis=0, tiled=True), slot_order, lon_start, lon_width, lon_total)
+    summed = inverse_dft(lax.all_gather(synthesis.reshape(slot_count, -1), "lon", axis=0, tiled=True), slot_order, lon_start, lon_width, lon_total)
     loading = summed * (2 * slot_total) ** (-0.5)
     potential = masked - 0.6 * loading
     neighbours = neighbour_sum(potential)

time: 138 us -> 139 us (level)
  local copies, waits for them, and re-layouts: 15.5 us -> 13.5 us
  blocking collectives: 46.3 us -> 48 us
    all_gather x1, blocking collectives: 13.5 us -> 15.2 us  [local(): lax.all_gather(synthesis.reshape(slot_count, -1), 'lon', axis=0, tiled=True)]
    gather x1 -> x2, local copies, waits for them, and re-layouts: 3.55 us -> 2.98 us  [inverse_dft(): jnp.take(synthesis, slot_of, axis=0, mode='clip', unique_indices=True)]
where the time goes in v14:
time: 139 us; the launch traced here: 138 us
  blocking collectives  48 us (35%)
  other arithmetic  24.4 us (18%)
  matrix products  19.4 us (14%)
  starting transfers between devices  18 us (13%)
  waiting for transfers between devices  13.8 us (10%)
  local copies, waits for them, and re-layouts  13.5 us (10%)
    all_to_all x1, blocking collectives, paired_reduce_scatter(): lax.all_to_all(summed, axis, 0, 0, tiled=True, axis_index_groups=groups)  17.4 us
    dot_general x1, matrix products, local(): jnp.einsum('krl,kcr->kcl', legendre, fourier, precision=lax.Precision.HIGH)  15.8 us
    all_to_all x1, blocking collectives, paired_all_gather(): lax.all_to_all(copies, axis, 0, 0, tiled=True, axis_index_groups=groups)  15.4 us
    all_gather x1, blocking collectives, local(): lax.all_gather(synthesis.reshape(slot_count, -1), 'lon', axis=0, tiled=True)  15.2 us
    reduce_sum x1, other arithmetic, local(): synthesis = (legendre[:, None, :, :] * spectrum[:, :, None, :]).sum(axis=3)  11.4 us
    all_to_all x1, waiting for transfers between devices, reduce_scatter(): moved = lax.all_to_all(x, axis, 0, 0, tiled=True)  7.05 us
    ppermute x2, starting transfers between devices, halo(): lax.ppermute(head, axis, [((i + 1) % count, i) for i in range(ends)])  6.55 us
    ppermute x2, starting transfers between devices, halo(): lax.ppermute(tail, axis, [(i, (i + 1) % count) for i in range(ends)])  6 us
  transfers between devices with their start and end apart: 7, of which 4 were waited for; matrix products, arithmetic and copies ran while one was open for 2% of the time, Pallas kernels for 0%

profile of v14, /device:TPU:12, one launch (start us, length us, event | category | flops | bytes accessed | tf_op | source)
XLA Modules:
  0.0 138.2 jit_solution(14475564918151505909)
XLA Ops:
  2.6 1.1 bitcast_multiply_fusion.1
  4.0 1.8 %convolution_bitcast_fusion = f32[2,256,32,32]{1,2,0,3:T(8,128)S(1)} fusion(f32[32,64,32]{2,1,0:T(8,128)S(1)} %reshape.198, f32[1,256,64]{1,2,0:T(8,128)S(1)} %get-tuple-element.22, f32[1,256,64]{1,2,0:T(8,128)S(1)} %get-tuple-element.23), kind=kOutput, calls=%fused_computation.16 | convolution fusion | flops 402685952 | bytes 2490368 | tf_op jit(solution)/shard_map/cua,rab->cubr/dot_general | solution.py:49
  7.9 1.2 subtract_reduce_fusion.1
  9.6 2.8 %gather_fusion = f32[1024,64]{1,0:T(8,128)S(1)} fusion(f32[1024,64]{1,0:T(8,128)S(1)} %copy.43, s32[1024]{0:T(1024)S(1)} %broadcast_clamp_fusion.1), kind=kCustom, calls=%fused_computation | custom fusion | bytes 528384 | tf_op jit(solution)/shard_map/jit(_take)/gather | solution.py:54
  13.4 5.3 %all-to-all-start = ((f32[4,256,64]{1,2,0:T(8,128)}), f32[4,256,64]{1,2,0:T(8,128)S(1)}, u32[]{:S(2)}, u32[]{:S(2)}) async-start(f32[4,256,64]{1,2,0:T(8,128)} %copy.44), calls=%async_computation | async-start | bytes 524288 | tf_op jit(solution)/shard_map/all_to_all | solution.py:73
  18.7 7.0 %all-to-all-done = f32[4,256,64]{1,2,0:T(8,128)S(1)} async-done(((f32[4,256,64]{1,2,0:T(8,128)}), f32[4,256,64]{1,2,0:T(8,128)S(1)}, u32[]{:S(2)}, u32[]{:S(2)}) %all-to-all-start) | async-done | bytes 262176 | tf_op jit(solution)/shard_map/all_to_all | solution.py:73
  25.9 15.8 %fusion.35 = f32[256,2,1024]{2,1,0:T(2,128)S(1)} fusion(f32[256,2,32]{2,1,0:T(2,128)S(1)} %copy.47, f32[256,32,1024]{2,1,0:T(8,128)} %param.7), kind=kOutput, calls=%fused_computation.70 | convolution fusion | flops 100663296 | bytes 35717120 | tf_op jit(solution)/shard_map/krl,kcr->kcl/dot_general | solution.py:122
  41.9 2.8 %collective-permute-done = f32[128,2,1024]{2,1,0:T(2,128)} collective-permute-done((f32[128,2,1024]{2,1,0:T(2,128)S(1)}, f32[128,2,1024]{2,1,0:T(2,128)}, u32[]{:S(2)}, u32[]{:S(2)}) %collective-permute-start) | collective-permute-done | bytes 1048608 | tf_op jit(solution)/shard_map/ppermute | solution.py:91
  44.7 1.8 %dynamic-slice_add_fusion = f32[128,2,1024]{2,1,0:T(2,128)S(1)} fusion(f32[128,2,1024]{2,1,0:T(2,128)} %collective-permute-done, f32[256,2,1024]{2,1,0:T(2,128)S(1)} %fusion.35, s32[]{:T(128)S(6)} %select_n.84), kind=kLoop, calls=%fused_computation.21 | loop fusion | flops 262144 | bytes 3145732 | tf_op jit(solution)/shard_map/add | solution.py:91
  46.4 17.4 %all_to_all.16 = f32[128,2,1024]{2,1,0:T(2,128)S(1)} all-to-all(f32[128,2,1024]{2,1,0:T(2,128)S(1)} %dynamic-slice_add_fusion), channel_id=1, replica_groups={{0,8,16,24},{4,12,20,28},{1,9,17,25},{5,13,21,29},{2,10,18,26},{6,14,22..., dimensions={0} | all-to-all | bytes 2097152 | tf_op jit(solution)/shard_map/all_to_all | solution.py:92
  64.7 15.4 %all_to_all.17 = f32[128,2,1024]{2,1,0:T(2,128)S(1)} all-to-all(f32[128,2,1024]{2,1,0:T(2,128)S(1)} %bitcast.54), channel_id=1, replica_groups={{0,8,16,24},{4,12,20,28},{1,9,17,25},{5,13,21,29},{2,10,18,26},{6,14,22..., dimensions={0} | all-to-all | bytes 2097152 | tf_op jit(solution)/shard_map/all_to_all | solution.py:102
  81.0 2.0 %collective-permute-done.1 = f32[128,2,1024]{2,1,0:T(2,128)} collective-permute-done((f32[128,2,1024]{2,1,0:T(2,128)S(1)}, f32[128,2,1024]{2,1,0:T(2,128)}, u32[]{:S(2)}, u32[]{:S(2)}) %collective-permute-start.1) | collective-permute-done | bytes 1048608 | tf_op jit(solution)/shard_map/ppermute | solution.py:103
  83.0 3.6 %fusion.1 = f32[256,2,1024]{2,1,0:T(2,128)S(1)} fusion(f32[128,2,1024]{2,1,0:T(2,128)} %collective-permute-done.1, f32[128,2,1024]{2,1,0:T(2,128)S(1)} %all_to_all.17, pred[]{:T(512)S(6)} %eq.25, pred[256,1024]{1,0:T(8,128)(4,1)S(1)} %iota_compare_fusion.1, f32[1024]{0:T(1024)S(1)} %copy-done.9), kind=kLoop, calls=%fused_computation.11 | loop fusion | flops 2621440 | bytes 4460545 | tf_op jit(solution)/shard_map/jit(_where)/select_n | solution.py:127
  86.6 11.4 %multiply_reduce_fusion = f32[256,2,32]{2,1,0:T(2,128)S(1)} fusion(f32[256,2,1024]{2,1,0:T(2,128)S(1)} %fusion.1, f32[256,32,1024]{2,1,0:T(8,128)} %param.7), kind=kLoop, calls=%fused_computation.2 | loop fusion | flops 33538048 | bytes 35717120 | tf_op jit(solution)/shard_map/reduce_sum | solution.py:128
  98.2 15.2 %all_gather.3 = f32[1024,64]{1,0:T(8,128)S(1)} all-gather(f32[256,64]{1,0:T(8,128)S(1)} %copy.49), channel_id=1, replica_groups=mesh['lat'=8,'lon'=4] {'lon'}, dimensions={0}, use_global_device_ids=true | all-gather | bytes 327680 | tf_op jit(solution)/shard_map/all_gather | solution.py:129
  113.3 2.8 %gather_fusion.1 = f32[1024,64]{1,0:T(8,128)S(1)} fusion(f32[1024,64]{1,0:T(8,128)S(1)} %all_gather.3, s32[1024]{0:T(1024)S(1)} %broadcast_clamp_fusion), kind=kCustom, calls=%fused_computation.1 | custom fusion | bytes 528384 | tf_op jit(solution)/shard_map/jit(_take)/gather | solution.py:63
  116.6 1.4 %add_reduce_fusion = (f32[256,32,32]{0,2,1:T(8,128)S(1)}, f32[256,32,32]{0,2,1:T(8,128)S(1)}) fusion(f32[4,256,32]{1,2,0:T(8,128)S(1)} %copy.52, f32[4,256,32]{1,2,0:T(8,128)S(1)} %copy.51, f32[4,256,32]{1,2,0:T(8,128)S(1)} %copy-done.3, f32[4,256,32]{1,2,0:T(8,128)S(1)} %get-tuple-element.20), kind=kLoop, calls=%fused_computation.4 | loop fusion | flops 7864320 | bytes 2621440 | tf_op jit(solution)/shard_map/reduce_sum | solution.py:65
  118.0 1.8 %multiply_bitcast_fusion = (f32[32,64,32]{1,0,2:T(8,128)S(1)}, f32[32,64,32]{1,0,2:T(8,128)S(1)}) fusion(f32[1,256,64]{1,2,0:T(8,128)S(1)} %copy-done.5, f32[1,256,64]{1,2,0:T(8,128)S(1)} %copy-done.7, f32[1,256,32,32]{1,3,0,2:T(8,128)S(1)} %bitcast.53, f32[1,256,32,32]{1,3,0,2:T(8,128)S(1)} %bitcast.52), kind=kOutput, calls=%fused_computation.23 | convolution fusion | flops 403341312 | bytes 2752512 | tf_op jit(solution)/shard_map/cua,cubr->rab/dot_general | solution.py:67
  120.9 1.9 %collective-permute-start.2 = (f32[1,2048]{1,0:T(1,128)S(1)}, f32[1,2048]{1,0:T(1,128)S(1)}, u32[]{:S(2)}, u32[]{:S(2)}) collective-permute-start(f32[1,2048]{1,0:T(1,128)S(1)} %get-tuple-element.17), channel_id=1, source_target_pairs={{0,4},{4,8},{8,12},{12,16},{16,20},{20,24},{24,28},{1,5},{5,9},{9,... | collective-permute-start | bytes 24584 | tf_op jit(solution)/shard_map/ppermute | solution.py:16
  122.9 4.5 %collective-permute-start.3 = (f32[1,2048]{1,0:T(1,128)S(1)}, f32[1,2048]{1,0:T(1,128)S(1)}, u32[]{:S(2)}, u32[]{:S(2)}) collective-permute-start(f32[1,2048]{1,0:T(1,128)S(1)} %get-tuple-element.16), channel_id=1, source_target_pairs={{4,0},{8,4},{12,8},{16,12},{20,16},{24,20},{28,24},{5,1},{9,5},{13... | collective-permute-start | bytes 24584 | tf_op jit(solution)/shard_map/ppermute | solution.py:17
  127.5 4.1 %collective-permute-start.4 = (f32[32,1]{1,0:T(8,128)S(1)}, f32[32,1]{1,0:T(8,128)S(1)}, u32[]{:S(2)}, u32[]{:S(2)}) collective-permute-start(f32[32,1]{1,0:T(8,128)S(1)} %get-tuple-element.13), channel_id=1, source_target_pairs={{0,1},{1,2},{2,3},{4,5},{5,6},{6,7},{8,9},{9,10},{10,11},{12,13},{... | collective-permute-start | bytes 392 | tf_op jit(solution)/shard_map/ppermute | solution.py:16
  131.6 2.0 %collective-permute-start.5 = (f32[32,1]{1,0:T(8,128)S(1)}, f32[32,1]{1,0:T(8,128)S(1)}, u32[]{:S(2)}, u32[]{:S(2)}) collective-permute-start(f32[32,1]{1,0:T(8,128)S(1)} %get-tuple-element.12), channel_id=1, source_target_pairs={{1,0},{2,1},{3,2},{5,4},{6,5},{7,6},{9,8},{10,9},{11,10},{13,12},{... | collective-permute-start | bytes 392 | tf_op jit(solution)/shard_map/ppermute | solution.py:17
  134.0 1.2 mul.335
  135.2 2.0 %collective-permute-done.5 = f32[32,1]{1,0:T(8,128)S(1)} collective-permute-done((f32[32,1]{1,0:T(8,128)S(1)}, f32[32,1]{1,0:T(8,128)S(1)}, u32[]{:S(2)}, u32[]{:S(2)}) %collective-permute-start.5) | collective-permute-done | bytes 160 | tf_op jit(solution)/shard_map/ppermute | solution.py:17
  (68 shorter events, 10.8 us)
Async XLA Ops:
  0.9 3.1 %copy-start.4 = (f32[1,256,64]{1,2,0:T(8,128)}, f32[1,256,64]{1,2,0:T(8,128)S(1)}, u32[]{:S(2)}) copy-start(f32[1,256,64]{1,2,0:T(8,128)S(1)} %get-tuple-element.22) | copy-start | bytes 196612
  0.9 3.1 %copy-start.6 = (f32[1,256,64]{1,2,0:T(8,128)}, f32[1,256,64]{1,2,0:T(8,128)S(1)}, u32[]{:S(2)}) copy-start(f32[1,256,64]{1,2,0:T(8,128)S(1)} %get-tuple-element.23) | copy-start | bytes 196612
  1.9 0.7 copy-start
  6.7 2.9 %copy-start.8 = (s32[1024]{0:T(1024)S(1)}, s32[1024]{0:T(1024)}, u32[]{:S(2)}) copy-start(s32[1024]{0:T(1024)} %param.8) | copy-start | bytes 12292
  7.9 4.5 %copy-start.2 = (f32[4,256,32]{1,2,0:T(8,128)}, f32[4,256,32]{1,2,0:T(8,128)S(1)}, u32[]{:S(2)}) copy-start(f32[4,256,32]{1,2,0:T(8,128)S(1)} %get-tuple-element.21) | copy-start | bytes 393220
  13.4 12.4 %all-to-all-start = ((f32[4,256,64]{1,2,0:T(8,128)}), f32[4,256,64]{1,2,0:T(8,128)S(1)}, u32[]{:S(2)}, u32[]{:S(2)}) async-start(f32[4,256,64]{1,2,0:T(8,128)} %copy.44), calls=%async_computation | async-start | bytes 524288 | tf_op jit(solution)/shard_map/all_to_all | solution.py:73
  41.8 2.9 %collective-permute-start = (f32[128,2,1024]{2,1,0:T(2,128)S(1)}, f32[128,2,1024]{2,1,0:T(2,128)}, u32[]{:S(2)}, u32[]{:S(2)}) collective-permute-start(f32[128,2,1024]{2,1,0:T(2,128)S(1)} %constant_dynamic-slice_fusion), channel_id=1, source_target_pairs={{0,4},{4,0},{8,12},{12,8},{16,20},{20,16},{24,28},{28,24},{1,5},{5... | collective-permute-start | bytes 3145736 | tf_op jit(solution)/shard_map/ppermute | solution.py:91
  46.4 36.5 %copy-start.9 = (f32[1024]{0:T(1024)S(1)}, f32[1024]{0:T(1024)}, u32[]{:S(2)}) copy-start(f32[1024]{0:T(1024)} %param.9) | copy-start | bytes 12292
  80.2 2.8 %collective-permute-start.1 = (f32[128,2,1024]{2,1,0:T(2,128)S(1)}, f32[128,2,1024]{2,1,0:T(2,128)}, u32[]{:S(2)}, u32[]{:S(2)}) collective-permute-start(f32[128,2,1024]{2,1,0:T(2,128)S(1)} %all_to_all.17), channel_id=1, source_target_pairs={{0,4},{4,0},{8,12},{12,8},{16,20},{20,16},{24,28},{28,24},{1,5},{5... | collective-permute-start | bytes 3145736 | tf_op jit(solution)/shard_map/ppermute | solution.py:103
  98.0 18.6 %copy-start.3 = (f32[4,256,32]{1,2,0:T(8,128)S(1)}, f32[4,256,32]{1,2,0:T(8,128)}, u32[]{:S(2)}) copy-start(f32[4,256,32]{1,2,0:T(8,128)} %copy-done.2) | copy-start | bytes 393220
  113.3 4.6 %copy-start.5 = (f32[1,256,64]{1,2,0:T(8,128)S(1)}, f32[1,256,64]{1,2,0:T(8,128)}, u32[]{:S(2)}) copy-start(f32[1,256,64]{1,2,0:T(8,128)} %copy-done.4) | copy-start | bytes 196612
  113.3 4.6 %copy-start.7 = (f32[1,256,64]{1,2,0:T(8,128)S(1)}, f32[1,256,64]{1,2,0:T(8,128)}, u32[]{:S(2)}) copy-start(f32[1,256,64]{1,2,0:T(8,128)} %copy-done.6) | copy-start | bytes 196612
  119.8 17.4 %copy-start.1 = (f32[32,16,128]{2,1,0:T(8,128)S(1)}, f32[32,16,128]{2,1,0:T(8,128)}, u32[]{:S(2)}) copy-start(f32[32,16,128]{2,1,0:T(8,128)} %copy-done) | copy-start | bytes 786436
  120.9 16.3 %collective-permute-start.2 = (f32[1,2048]{1,0:T(1,128)S(1)}, f32[1,2048]{1,0:T(1,128)S(1)}, u32[]{:S(2)}, u32[]{:S(2)}) collective-permute-start(f32[1,2048]{1,0:T(1,128)S(1)} %get-tuple-element.17), channel_id=1, source_target_pairs={{0,4},{4,8},{8,12},{12,16},{16,20},{20,24},{24,28},{1,5},{5,9},{9,... | collective-permute-start | bytes 24584 | tf_op jit(solution)/shard_map/ppermute | solution.py:16
  122.9 14.4 %collective-permute-start.3 = (f32[1,2048]{1,0:T(1,128)S(1)}, f32[1,2048]{1,0:T(1,128)S(1)}, u32[]{:S(2)}, u32[]{:S(2)}) collective-permute-start(f32[1,2048]{1,0:T(1,128)S(1)} %get-tuple-element.16), channel_id=1, source_target_pairs={{4,0},{8,4},{12,8},{16,12},{20,16},{24,20},{28,24},{5,1},{9,5},{13... | collective-permute-start | bytes 24584 | tf_op jit(solution)/shard_map/ppermute | solution.py:17
  127.5 7.7 %collective-permute-start.4 = (f32[32,1]{1,0:T(8,128)S(1)}, f32[32,1]{1,0:T(8,128)S(1)}, u32[]{:S(2)}, u32[]{:S(2)}) collective-permute-start(f32[32,1]{1,0:T(8,128)S(1)} %get-tuple-element.13), channel_id=1, source_target_pairs={{0,1},{1,2},{2,3},{4,5},{5,6},{6,7},{8,9},{9,10},{10,11},{12,13},{... | collective-permute-start | bytes 392 | tf_op jit(solution)/shard_map/ppermute | solution.py:16
  131.6 5.6 %collective-permute-start.5 = (f32[32,1]{1,0:T(8,128)S(1)}, f32[32,1]{1,0:T(8,128)S(1)}, u32[]{:S(2)}, u32[]{:S(2)}) collective-permute-start(f32[32,1]{1,0:T(8,128)S(1)} %get-tuple-element.12), channel_id=1, source_target_pairs={{1,0},{2,1},{3,2},{5,4},{6,5},{7,6},{9,8},{10,9},{11,10},{13,12},{... | collective-permute-start | bytes 392 | tf_op jit(solution)/shard_map/ppermute | solution.py:17

commit v15 on v14

--- a/solution.py
+++ b/solution.py
@@ -126,7 +126,7 @@
     retained = degrees[None, :] >= own_orders[:, None]
     spectrum = jnp.where(retained[:, None, :], love_gain[None, None, :] * degree_whole, 0.0)
     synthesis = (legendre[:, None, :, :] * spectrum[:, :, None, :]).sum(axis=3)
-    summed = inverse_dft(lax.all_gather(synthesis.reshape(slot_count, -1), "lon", axis=0, tiled=True), slot_order, lon_start, lon_width, lon_total)
+    summed = inverse_dft(all_gather(synthesis.reshape(slot_count, -1), "lon"), slot_order, lon_start, lon_width, lon_total)
     loading = summed * (2 * slot_total) ** (-0.5)
     potential = masked - 0.6 * loading
     neighbours = neighbour_sum(potential)

time: 139 us -> 137 us (0.986)
  blocking collectives: 48 us -> 32.8 us
  waiting for transfers between devices: 13.8 us -> 19.9 us
  starting transfers between devices: 18 us -> 23.1 us
    all_gather x1 -> x0, blocking collectives: 15.2 us -> none  [local(): lax.all_gather(synthesis.reshape(slot_count, -1), 'lon', axis=0, tiled=True)]
    all_to_all x0 -> x1, waiting for transfers between devices: none -> 6.98 us  [all_gather(): return lax.all_to_all(copies, axis, 0, 0, tiled=True)]
    all_to_all x0 -> x1, starting transfers between devices: none -> 5.37 us  [all_gather(): return lax.all_to_all(copies, axis, 0, 0, tiled=True)]
    ppermute x2, starting transfers between devices: 6 us -> 4.18 us  [halo(): lax.ppermute(tail, axis, [(i, (i + 1) % count) for i in range(ends)])]
    ppermute x2, starting transfers between devices: 6.55 us -> 8.12 us  [halo(): lax.ppermute(head, axis, [((i + 1) % count, i) for i in range(ends)])]
    ppermute x2, waiting for transfers between devices: 2.02 us -> 0.61 us  [halo(): lax.ppermute(head, axis, [((i + 1) % count, i) for i in range(ends)])]
  transfers between devices with their start and end apart: 7 -> 8, of which waited for: 4 -> 5; matrix products, arithmetic and copies ran while one was open for 2% -> 2% of each run, Pallas kernels for 0% -> 0%
where the time goes in v15:
time: 137 us; the launch traced here: 135 us
  blocking collectives  32.8 us (24%)
  other arithmetic  24.4 us (18%)
  starting transfers between devices  23.1 us (17%)
  waiting for transfers between devices  19.9 us (15%)
  matrix products  19.4 us (14%)
  local copies, waits for them, and re-layouts  14.4 us (11%)
    all_to_all x1, blocking collectives, paired_reduce_scatter(): lax.all_to_all(summed, axis, 0, 0, tiled=True, axis_index_groups=groups)  17.4 us
    dot_general x1, matrix products, local(): jnp.einsum('krl,kcr->kcl', legendre, fourier, precision=lax.Precision.HIGH)  15.8 us
    all_to_all x1, blocking collectives, paired_all_gather(): lax.all_to_all(copies, axis, 0, 0, tiled=True, axis_index_groups=groups)  15.4 us
    reduce_sum x1, other arithmetic, local(): synthesis = (legendre[:, None, :, :] * spectrum[:, :, None, :]).sum(axis=3)  11.4 us
    ppermute x2, starting transfers between devices, halo(): lax.ppermute(head, axis, [((i + 1) % count, i) for i in range(ends)])  8.12 us
    all_to_all x1, waiting for transfers between devices, reduce_scatter(): moved = lax.all_to_all(x, axis, 0, 0, tiled=True)  7.05 us
    all_to_all x1, waiting for transfers between devices, all_gather(): return lax.all_to_all(copies, axis, 0, 0, tiled=True)  6.98 us
    all_to_all x1, starting transfers between devices, all_gather(): return lax.all_to_all(copies, axis, 0, 0, tiled=True)  5.37 us
  transfers between devices with their start and end apart: 8, of which 5 were waited for; matrix products, arithmetic and copies ran while one was open for 2% of the time, Pallas kernels for 0%

profile of v15, /device:TPU:12, one launch (start us, length us, event | category | flops | bytes accessed | tf_op | source)
XLA Modules:
  0.0 135.1 jit_solution(1309728297976285723)
XLA Ops:
  2.6 1.1 bitcast_multiply_fusion.1
  4.0 1.8 %convolution_bitcast_fusion = f32[2,256,32,32]{1,2,0,3:T(8,128)S(1)} fusion(f32[32,64,32]{2,1,0:T(8,128)S(1)} %reshape.200, f32[1,256,64]{1,2,0:T(8,128)S(1)} %get-tuple-element.22, f32[1,256,64]{1,2,0:T(8,128)S(1)} %get-tuple-element.23), kind=kOutput, calls=%fused_computation.16 | convolution fusion | flops 402685952 | bytes 2490368 | tf_op jit(solution)/shard_map/cua,rab->cubr/dot_general | solution.py:49
  7.9 1.2 subtract_reduce_fusion.1
  9.6 2.8 %gather_fusion = f32[1024,64]{1,0:T(8,128)S(1)} fusion(f32[1024,64]{1,0:T(8,128)S(1)} %copy.43, s32[1024]{0:T(1024)S(1)} %broadcast_clamp_fusion.1), kind=kCustom, calls=%fused_computation | custom fusion | bytes 528384 | tf_op jit(solution)/shard_map/jit(_take)/gather | solution.py:54
  13.4 5.3 %all-to-all-start = ((f32[4,256,64]{1,2,0:T(8,128)}), f32[4,256,64]{1,2,0:T(8,128)S(1)}, u32[]{:S(2)}, u32[]{:S(2)}) async-start(f32[4,256,64]{1,2,0:T(8,128)} %copy.44), calls=%async_computation | async-start | bytes 524288 | tf_op jit(solution)/shard_map/all_to_all | solution.py:73
  18.7 7.0 %all-to-all-done = f32[4,256,64]{1,2,0:T(8,128)S(1)} async-done(((f32[4,256,64]{1,2,0:T(8,128)}), f32[4,256,64]{1,2,0:T(8,128)S(1)}, u32[]{:S(2)}, u32[]{:S(2)}) %all-to-all-start) | async-done | bytes 262176 | tf_op jit(solution)/shard_map/all_to_all | solution.py:73
  25.9 15.8 %fusion.35 = f32[256,2,1024]{2,1,0:T(2,128)S(1)} fusion(f32[256,2,32]{2,1,0:T(2,128)S(1)} %copy.47, f32[256,32,1024]{2,1,0:T(8,128)} %param.7), kind=kOutput, calls=%fused_computation.70 | convolution fusion | flops 100663296 | bytes 35717120 | tf_op jit(solution)/shard_map/krl,kcr->kcl/dot_general | solution.py:122
  41.9 2.8 %collective-permute-done = f32[128,2,1024]{2,1,0:T(2,128)} collective-permute-done((f32[128,2,1024]{2,1,0:T(2,128)S(1)}, f32[128,2,1024]{2,1,0:T(2,128)}, u32[]{:S(2)}, u32[]{:S(2)}) %collective-permute-start) | collective-permute-done | bytes 1048608 | tf_op jit(solution)/shard_map/ppermute | solution.py:91
  44.7 1.8 %dynamic-slice_add_fusion = f32[128,2,1024]{2,1,0:T(2,128)S(1)} fusion(f32[128,2,1024]{2,1,0:T(2,128)} %collective-permute-done, f32[256,2,1024]{2,1,0:T(2,128)S(1)} %fusion.35, s32[]{:T(128)S(6)} %select_n.84), kind=kLoop, calls=%fused_computation.21 | loop fusion | flops 262144 | bytes 3145732 | tf_op jit(solution)/shard_map/add | solution.py:91
  46.4 17.4 %all_to_all.25 = f32[128,2,1024]{2,1,0:T(2,128)S(1)} all-to-all(f32[128,2,1024]{2,1,0:T(2,128)S(1)} %dynamic-slice_add_fusion), channel_id=1, replica_groups={{0,8,16,24},{4,12,20,28},{1,9,17,25},{5,13,21,29},{2,10,18,26},{6,14,22..., dimensions={0} | all-to-all | bytes 2097152 | tf_op jit(solution)/shard_map/all_to_all | solution.py:92
  64.7 15.4 %all_to_all.26 = f32[128,2,1024]{2,1,0:T(2,128)S(1)} all-to-all(f32[128,2,1024]{2,1,0:T(2,128)S(1)} %bitcast.56), channel_id=1, replica_groups={{0,8,16,24},{4,12,20,28},{1,9,17,25},{5,13,21,29},{2,10,18,26},{6,14,22..., dimensions={0} | all-to-all | bytes 2097152 | tf_op jit(solution)/shard_map/all_to_all | solution.py:102
  80.5 2.5 %collective-permute-done.1 = f32[128,2,1024]{2,1,0:T(2,128)} collective-permute-done((f32[128,2,1024]{2,1,0:T(2,128)S(1)}, f32[128,2,1024]{2,1,0:T(2,128)}, u32[]{:S(2)}, u32[]{:S(2)}) %collective-permute-start.1) | collective-permute-done | bytes 1048608 | tf_op jit(solution)/shard_map/ppermute | solution.py:103
  83.0 3.6 %fusion.1 = f32[256,2,1024]{2,1,0:T(2,128)S(1)} fusion(f32[128,2,1024]{2,1,0:T(2,128)} %collective-permute-done.1, f32[128,2,1024]{2,1,0:T(2,128)S(1)} %all_to_all.26, pred[]{:T(512)S(6)} %eq.25, pred[256,1024]{1,0:T(8,128)(4,1)S(1)} %iota_compare_fusion.1, f32[1024]{0:T(1024)S(1)} %copy-done.9), kind=kLoop, calls=%fused_computation.11 | loop fusion | flops 2621440 | bytes 4460545 | tf_op jit(solution)/shard_map/jit(_where)/select_n | solution.py:127
  86.6 11.4 %multiply_reduce_fusion = f32[256,2,32]{2,1,0:T(2,128)S(1)} fusion(f32[256,2,1024]{2,1,0:T(2,128)S(1)} %fusion.1, f32[256,32,1024]{2,1,0:T(8,128)} %param.7), kind=kLoop, calls=%fused_computation.2 | loop fusion | flops 33538048 | bytes 35717120 | tf_op jit(solution)/shard_map/reduce_sum | solution.py:128
  98.8 5.4 %all-to-all-start.3 = ((f32[4,256,64]{1,2,0:T(8,128)}), f32[4,256,64]{1,2,0:T(8,128)S(1)}, u32[]{:S(2)}, u32[]{:S(2)}) async-start(f32[4,256,64]{1,2,0:T(8,128)} %broadcast_in_dim.41), calls=%async_computation.3 | async-start | bytes 524288 | tf_op jit(solution)/shard_map/all_to_all | solution.py:80
  104.7 7.0 %all-to-all-done.3 = f32[4,256,64]{1,2,0:T(8,128)S(1)} async-done(((f32[4,256,64]{1,2,0:T(8,128)}), f32[4,256,64]{1,2,0:T(8,128)S(1)}, u32[]{:S(2)}, u32[]{:S(2)}) %all-to-all-start.3) | async-done | bytes 262176 | tf_op jit(solution)/shard_map/all_to_all | solution.py:80
  111.9 2.8 %gather_fusion.1 = f32[1024,64]{1,0:T(8,128)S(1)} fusion(f32[1024,64]{1,0:T(8,128)S(1)} %bitcast.53, s32[1024]{0:T(1024)S(1)} %broadcast_clamp_fusion), kind=kCustom, calls=%fused_computation.1 | custom fusion | bytes 528384 | tf_op jit(solution)/shard_map/jit(_take)/gather | solution.py:63
  115.2 1.4 %add_reduce_fusion = (f32[256,32,32]{0,2,1:T(8,128)S(1)}, f32[256,32,32]{0,2,1:T(8,128)S(1)}) fusion(f32[4,256,32]{1,2,0:T(8,128)S(1)} %copy.52, f32[4,256,32]{1,2,0:T(8,128)S(1)} %copy.51, f32[4,256,32]{1,2,0:T(8,128)S(1)} %copy-done.3, f32[4,256,32]{1,2,0:T(8,128)S(1)} %get-tuple-element.20), kind=kLoop, calls=%fused_computation.4 | loop fusion | flops 7864320 | bytes 2621440 | tf_op jit(solution)/shard_map/reduce_sum | solution.py:65
  116.6 1.8 %multiply_bitcast_fusion = (f32[32,64,32]{1,0,2:T(8,128)S(1)}, f32[32,64,32]{1,0,2:T(8,128)S(1)}) fusion(f32[1,256,64]{1,2,0:T(8,128)S(1)} %copy-done.5, f32[1,256,64]{1,2,0:T(8,128)S(1)} %copy-done.7, f32[1,256,32,32]{1,3,0,2:T(8,128)S(1)} %bitcast.55, f32[1,256,32,32]{1,3,0,2:T(8,128)S(1)} %bitcast.54), kind=kOutput, calls=%fused_computation.23 | convolution fusion | flops 403341312 | bytes 2752512 | tf_op jit(solution)/shard_map/cua,cubr->rab/dot_general | solution.py:67
  119.5 1.9 %collective-permute-start.2 = (f32[1,2048]{1,0:T(1,128)S(1)}, f32[1,2048]{1,0:T(1,128)S(1)}, u32[]{:S(2)}, u32[]{:S(2)}) collective-permute-start(f32[1,2048]{1,0:T(1,128)S(1)} %get-tuple-element.17), channel_id=1, source_target_pairs={{0,4},{4,8},{8,12},{12,16},{16,20},{20,24},{24,28},{1,5},{5,9},{9,... | collective-permute-start | bytes 24584 | tf_op jit(solution)/shard_map/ppermute | solution.py:16
  121.4 4.5 %collective-permute-start.3 = (f32[1,2048]{1,0:T(1,128)S(1)}, f32[1,2048]{1,0:T(1,128)S(1)}, u32[]{:S(2)}, u32[]{:S(2)}) collective-permute-start(f32[1,2048]{1,0:T(1,128)S(1)} %get-tuple-element.16), channel_id=1, source_target_pairs={{4,0},{8,4},{12,8},{16,12},{20,16},{24,20},{28,24},{5,1},{9,5},{13... | collective-permute-start | bytes 24584 | tf_op jit(solution)/shard_map/ppermute | solution.py:17
  126.0 2.3 %collective-permute-start.4 = (f32[32,1]{1,0:T(8,128)S(1)}, f32[32,1]{1,0:T(8,128)S(1)}, u32[]{:S(2)}, u32[]{:S(2)}) collective-permute-start(f32[32,1]{1,0:T(8,128)S(1)} %get-tuple-element.13), channel_id=1, source_target_pairs={{0,1},{1,2},{2,3},{4,5},{5,6},{6,7},{8,9},{9,10},{10,11},{12,13},{... | collective-permute-start | bytes 392 | tf_op jit(solution)/shard_map/ppermute | solution.py:16
  128.3 3.6 %collective-permute-start.5 = (f32[32,1]{1,0:T(8,128)S(1)}, f32[32,1]{1,0:T(8,128)S(1)}, u32[]{:S(2)}, u32[]{:S(2)}) collective-permute-start(f32[32,1]{1,0:T(8,128)S(1)} %get-tuple-element.12), channel_id=1, source_target_pairs={{1,0},{2,1},{3,2},{5,4},{6,5},{7,6},{9,8},{10,9},{11,10},{13,12},{... | collective-permute-start | bytes 392 | tf_op jit(solution)/shard_map/ppermute | solution.py:17
  132.3 1.2 mul.335
  (70 shorter events, 12.2 us)
Async XLA Ops:
  0.9 3.1 %copy-start.4 = (f32[1,256,64]{1,2,0:T(8,128)}, f32[1,256,64]{1,2,0:T(8,128)S(1)}, u32[]{:S(2)}) copy-start(f32[1,256,64]{1,2,0:T(8,128)S(1)} %get-tuple-element.22) | copy-start | bytes 196612
  0.9 3.1 %copy-start.6 = (f32[1,256,64]{1,2,0:T(8,128)}, f32[1,256,64]{1,2,0:T(8,128)S(1)}, u32[]{:S(2)}) copy-start(f32[1,256,64]{1,2,0:T(8,128)S(1)} %get-tuple-element.23) | copy-start | bytes 196612
  1.9 0.7 copy-start
  6.7 2.9 %copy-start.8 = (s32[1024]{0:T(1024)S(1)}, s32[1024]{0:T(1024)}, u32[]{:S(2)}) copy-start(s32[1024]{0:T(1024)} %param.8) | copy-start | bytes 12292
  7.9 4.5 %copy-start.2 = (f32[4,256,32]{1,2,0:T(8,128)}, f32[4,256,32]{1,2,0:T(8,128)S(1)}, u32[]{:S(2)}) copy-start(f32[4,256,32]{1,2,0:T(8,128)S(1)} %get-tuple-element.21) | copy-start | bytes 393220
  13.4 12.4 %all-to-all-start = ((f32[4,256,64]{1,2,0:T(8,128)}), f32[4,256,64]{1,2,0:T(8,128)S(1)}, u32[]{:S(2)}, u32[]{:S(2)}) async-start(f32[4,256,64]{1,2,0:T(8,128)} %copy.44), calls=%async_computation | async-start | bytes 524288 | tf_op jit(solution)/shard_map/all_to_all | solution.py:73
  41.8 2.9 %collective-permute-start = (f32[128,2,1024]{2,1,0:T(2,128)S(1)}, f32[128,2,1024]{2,1,0:T(2,128)}, u32[]{:S(2)}, u32[]{:S(2)}) collective-permute-start(f32[128,2,1024]{2,1,0:T(2,128)S(1)} %constant_dynamic-slice_fusion), channel_id=1, source_target_pairs={{0,4},{4,0},{8,12},{12,8},{16,20},{20,16},{24,28},{28,24},{1,5},{5... | collective-permute-start | bytes 3145736 | tf_op jit(solution)/shard_map/ppermute | solution.py:91
  46.4 36.5 %copy-start.9 = (f32[1024]{0:T(1024)S(1)}, f32[1024]{0:T(1024)}, u32[]{:S(2)}) copy-start(f32[1024]{0:T(1024)} %param.9) | copy-start | bytes 12292
  80.2 2.8 %collective-permute-start.1 = (f32[128,2,1024]{2,1,0:T(2,128)S(1)}, f32[128,2,1024]{2,1,0:T(2,128)}, u32[]{:S(2)}, u32[]{:S(2)}) collective-permute-start(f32[128,2,1024]{2,1,0:T(2,128)S(1)} %all_to_all.26), channel_id=1, source_target_pairs={{0,4},{4,0},{8,12},{12,8},{16,20},{20,16},{24,28},{28,24},{1,5},{5... | collective-permute-start | bytes 3145736 | tf_op jit(solution)/shard_map/ppermute | solution.py:103
  98.8 16.3 %copy-start.3 = (f32[4,256,32]{1,2,0:T(8,128)S(1)}, f32[4,256,32]{1,2,0:T(8,128)}, u32[]{:S(2)}) copy-start(f32[4,256,32]{1,2,0:T(8,128)} %copy-done.2) | copy-start | bytes 393220
  98.8 12.9 %all-to-all-start.3 = ((f32[4,256,64]{1,2,0:T(8,128)}), f32[4,256,64]{1,2,0:T(8,128)S(1)}, u32[]{:S(2)}, u32[]{:S(2)}) async-start(f32[4,256,64]{1,2,0:T(8,128)} %broadcast_in_dim.41), calls=%async_computation.3 | async-start | bytes 524288 | tf_op jit(solution)/shard_map/all_to_all | solution.py:80
  111.9 4.7 %copy-start.5 = (f32[1,256,64]{1,2,0:T(8,128)S(1)}, f32[1,256,64]{1,2,0:T(8,128)}, u32[]{:S(2)}) copy-start(f32[1,256,64]{1,2,0:T(8,128)} %copy-done.4) | copy-start | bytes 196612
  111.9 4.7 %copy-start.7 = (f32[1,256,64]{1,2,0:T(8,128)S(1)}, f32[1,256,64]{1,2,0:T(8,128)}, u32[]{:S(2)}) copy-start(f32[1,256,64]{1,2,0:T(8,128)} %copy-done.6) | copy-start | bytes 196612
  118.4 15.7 %copy-start.1 = (f32[32,16,128]{2,1,0:T(8,128)S(1)}, f32[32,16,128]{2,1,0:T(8,128)}, u32[]{:S(2)}) copy-start(f32[32,16,128]{2,1,0:T(8,128)} %copy-done) | copy-start | bytes 786436
  119.5 14.6 %collective-permute-start.2 = (f32[1,2048]{1,0:T(1,128)S(1)}, f32[1,2048]{1,0:T(1,128)S(1)}, u32[]{:S(2)}, u32[]{:S(2)}) collective-permute-start(f32[1,2048]{1,0:T(1,128)S(1)} %get-tuple-element.17), channel_id=1, source_target_pairs={{0,4},{4,8},{8,12},{12,16},{16,20},{20,24},{24,28},{1,5},{5,9},{9,... | collective-permute-start | bytes 24584 | tf_op jit(solution)/shard_map/ppermute | solution.py:16
  121.4 12.7 %collective-permute-start.3 = (f32[1,2048]{1,0:T(1,128)S(1)}, f32[1,2048]{1,0:T(1,128)S(1)}, u32[]{:S(2)}, u32[]{:S(2)}) collective-permute-start(f32[1,2048]{1,0:T(1,128)S(1)} %get-tuple-element.16), channel_id=1, source_target_pairs={{4,0},{8,4},{12,8},{16,12},{20,16},{24,20},{28,24},{5,1},{9,5},{13... | collective-permute-start | bytes 24584 | tf_op jit(solution)/shard_map/ppermute | solution.py:17
  126.0 7.4 %collective-permute-start.4 = (f32[32,1]{1,0:T(8,128)S(1)}, f32[32,1]{1,0:T(8,128)S(1)}, u32[]{:S(2)}, u32[]{:S(2)}) collective-permute-start(f32[32,1]{1,0:T(8,128)S(1)} %get-tuple-element.13), channel_id=1, source_target_pairs={{0,1},{1,2},{2,3},{4,5},{5,6},{6,7},{8,9},{9,10},{10,11},{12,13},{... | collective-permute-start | bytes 392 | tf_op jit(solution)/shard_map/ppermute | solution.py:16
  128.3 5.8 %collective-permute-start.5 = (f32[32,1]{1,0:T(8,128)S(1)}, f32[32,1]{1,0:T(8,128)S(1)}, u32[]{:S(2)}, u32[]{:S(2)}) collective-permute-start(f32[32,1]{1,0:T(8,128)S(1)} %get-tuple-element.12), channel_id=1, source_target_pairs={{1,0},{2,1},{3,2},{5,4},{6,5},{7,6},{9,8},{10,9},{11,10},{13,12},{... | collective-permute-start | bytes 392 | tf_op jit(solution)/shard_map/ppermute | solution.py:17

commit v16 on v15

--- a/solution.py
+++ b/solution.py
@@ -119,7 +119,7 @@
     forward_scale = lon_total ** (-0.5)
     fourier = reduce_scatter(forward_dft(masked, slot_order, lon_start, lon_total) * forward_scale, "lon")
     fourier = fourier.reshape(slot_count, 2, cycle_count)
-    coefficient = jnp.einsum("krl,kcr->kcl", legendre, fourier, precision=lax.Precision.HIGH)
+    coefficient = (legendre[:, None, :, :] * fourier[:, :, :, None]).sum(axis=2)
     degree_whole = paired_all_gather(paired_reduce_scatter(coefficient, "lat"), "lat")
     degree_count = degree_whole.shape[2]
     degrees = jnp.arange(degree_count, dtype=jnp.int32)

time: 137 us -> 138 us (level)
  other arithmetic: 24.4 us -> 41.1 us
  matrix products: 19.4 us -> 3.63 us
    reduce_sum x0 -> x1, other arithmetic: none -> 16.8 us  [local(): coefficient = (legendre[:, None, :, :] * fourier[:, :, :, None]).sum(axis=2)]
    dot_general x1 -> x0, matrix products: 15.8 us -> none  [local(): jnp.einsum('krl,kcr->kcl', legendre, fourier, precision=lax.Precision.HIGH)]
where the time goes in v16:
time: 138 us; the launch traced here: 136 us
  other arithmetic  41.1 us (30%)
  blocking collectives  32.8 us (24%)
  starting transfers between devices  23.1 us (17%)
  waiting for transfers between devices  19.9 us (14%)
  local copies, waits for them, and re-layouts  14.4 us (10%)
  matrix products  3.63 us (3%)
    all_to_all x1, blocking collectives, paired_reduce_scatter(): lax.all_to_all(summed, axis, 0, 0, tiled=True, axis_index_groups=groups)  17.4 us
    reduce_sum x1, other arithmetic, local(): coefficient = (legendre[:, None, :, :] * fourier[:, :, :, None]).sum(axis=2)  16.8 us
    all_to_all x1, blocking collectives, paired_all_gather(): lax.all_to_all(copies, axis, 0, 0, tiled=True, axis_index_groups=groups)  15.4 us
    reduce_sum x1, other arithmetic, local(): synthesis = (legendre[:, None, :, :] * spectrum[:, :, None, :]).sum(axis=3)  11.4 us
    ppermute x2, starting transfers between devices, halo(): lax.ppermute(head, axis, [((i + 1) % count, i) for i in range(ends)])  8.11 us
    all_to_all x1, waiting for transfers between devices, reduce_scatter(): moved = lax.all_to_all(x, axis, 0, 0, tiled=True)  7.05 us
    all_to_all x1, waiting for transfers between devices, all_gather(): return lax.all_to_all(copies, axis, 0, 0, tiled=True)  6.98 us
    all_to_all x1, starting transfers between devices, all_gather(): return lax.all_to_all(copies, axis, 0, 0, tiled=True)  5.37 us
  transfers between devices with their start and end apart: 8, of which 5 were waited for; matrix products, arithmetic and copies ran while one was open for 2% of the time, Pallas kernels for 0%

profile of v16, /device:TPU:12, one launch (start us, length us, event | category | flops | bytes accessed | tf_op | source)
XLA Modules:
  0.0 136.0 jit_solution(2808113827973588478)
XLA Ops:
  2.6 1.1 bitcast_multiply_fusion.1
  4.0 1.8 %convolution_bitcast_fusion = f32[2,256,32,32]{1,2,0,3:T(8,128)S(1)} fusion(f32[32,64,32]{2,1,0:T(8,128)S(1)} %reshape.198, f32[1,256,64]{1,2,0:T(8,128)S(1)} %get-tuple-element.22, f32[1,256,64]{1,2,0:T(8,128)S(1)} %get-tuple-element.23), kind=kOutput, calls=%fused_computation.17 | convolution fusion | flops 402685952 | bytes 2490368 | tf_op jit(solution)/shard_map/cua,rab->cubr/dot_general | solution.py:49
  7.9 1.2 subtract_reduce_fusion.1
  9.6 2.8 %gather_fusion = f32[1024,64]{1,0:T(8,128)S(1)} fusion(f32[1024,64]{1,0:T(8,128)S(1)} %copy.43, s32[1024]{0:T(1024)S(1)} %broadcast_clamp_fusion.1), kind=kCustom, calls=%fused_computation | custom fusion | bytes 528384 | tf_op jit(solution)/shard_map/jit(_take)/gather | solution.py:54
  13.4 5.3 %all-to-all-start = ((f32[4,256,64]{1,2,0:T(8,128)}), f32[4,256,64]{1,2,0:T(8,128)S(1)}, u32[]{:S(2)}, u32[]{:S(2)}) async-start(f32[4,256,64]{1,2,0:T(8,128)} %copy.44), calls=%async_computation | async-start | bytes 524288 | tf_op jit(solution)/shard_map/all_to_all | solution.py:73
  18.7 7.0 %all-to-all-done = f32[4,256,64]{1,2,0:T(8,128)S(1)} async-done(((f32[4,256,64]{1,2,0:T(8,128)}), f32[4,256,64]{1,2,0:T(8,128)S(1)}, u32[]{:S(2)}, u32[]{:S(2)}) %all-to-all-start) | async-done | bytes 262176 | tf_op jit(solution)/shard_map/all_to_all | solution.py:73
  25.9 16.8 %multiply_reduce_fusion.1 = f32[256,2,1024]{2,1,0:T(2,128)S(1)} fusion(f32[256,2,32]{2,1,0:T(2,128)S(1)} %copy.47, f32[256,32,1024]{2,1,0:T(8,128)} %param.7), kind=kLoop, calls=%fused_computation.3 | loop fusion | flops 33030144 | bytes 35717120 | tf_op jit(solution)/shard_map/reduce_sum | solution.py:122
  42.9 2.8 %collective-permute-done = f32[128,2,1024]{2,1,0:T(2,128)} collective-permute-done((f32[128,2,1024]{2,1,0:T(2,128)S(1)}, f32[128,2,1024]{2,1,0:T(2,128)}, u32[]{:S(2)}, u32[]{:S(2)}) %collective-permute-start) | collective-permute-done | bytes 1048608 | tf_op jit(solution)/shard_map/ppermute | solution.py:91
  45.6 1.8 %dynamic-slice_add_fusion = f32[128,2,1024]{2,1,0:T(2,128)S(1)} fusion(f32[128,2,1024]{2,1,0:T(2,128)} %collective-permute-done, f32[256,2,1024]{2,1,0:T(2,128)S(1)} %multiply_reduce_fusion.1, s32[]{:T(128)S(6)} %select_n.84), kind=kLoop, calls=%fused_computation.22 | loop fusion | flops 262144 | bytes 3145732 | tf_op jit(solution)/shard_map/add | solution.py:91
  47.4 17.4 %all_to_all.25 = f32[128,2,1024]{2,1,0:T(2,128)S(1)} all-to-all(f32[128,2,1024]{2,1,0:T(2,128)S(1)} %dynamic-slice_add_fusion), channel_id=1, replica_groups={{0,8,16,24},{4,12,20,28},{1,9,17,25},{5,13,21,29},{2,10,18,26},{6,14,22..., dimensions={0} | all-to-all | bytes 2097152 | tf_op jit(solution)/shard_map/all_to_all | solution.py:92
  65.7 15.4 %all_to_all.26 = f32[128,2,1024]{2,1,0:T(2,128)S(1)} all-to-all(f32[128,2,1024]{2,1,0:T(2,128)S(1)} %bitcast.54), channel_id=1, replica_groups={{0,8,16,24},{4,12,20,28},{1,9,17,25},{5,13,21,29},{2,10,18,26},{6,14,22..., dimensions={0} | all-to-all | bytes 2097152 | tf_op jit(solution)/shard_map/all_to_all | solution.py:102
  81.4 2.5 %collective-permute-done.1 = f32[128,2,1024]{2,1,0:T(2,128)} collective-permute-done((f32[128,2,1024]{2,1,0:T(2,128)S(1)}, f32[128,2,1024]{2,1,0:T(2,128)}, u32[]{:S(2)}, u32[]{:S(2)}) %collective-permute-start.1) | collective-permute-done | bytes 1048608 | tf_op jit(solution)/shard_map/ppermute | solution.py:103
  83.9 3.6 %fusion.1 = f32[256,2,1024]{2,1,0:T(2,128)S(1)} fusion(f32[128,2,1024]{2,1,0:T(2,128)} %collective-permute-done.1, f32[128,2,1024]{2,1,0:T(2,128)S(1)} %all_to_all.26, pred[]{:T(512)S(6)} %eq.25, pred[256,1024]{1,0:T(8,128)(4,1)S(1)} %iota_compare_fusion.1, f32[1024]{0:T(1024)S(1)} %copy-done.9), kind=kLoop, calls=%fused_computation.12 | loop fusion | flops 2621440 | bytes 4460545 | tf_op jit(solution)/shard_map/jit(_where)/select_n | solution.py:127
  87.6 11.4 %multiply_reduce_fusion = f32[256,2,32]{2,1,0:T(2,128)S(1)} fusion(f32[256,2,1024]{2,1,0:T(2,128)S(1)} %fusion.1, f32[256,32,1024]{2,1,0:T(8,128)} %param.7), kind=kLoop, calls=%fused_computation.2 | loop fusion | flops 33538048 | bytes 35717120 | tf_op jit(solution)/shard_map/reduce_sum | solution.py:128
  99.8 5.4 %all-to-all-start.3 = ((f32[4,256,64]{1,2,0:T(8,128)}), f32[4,256,64]{1,2,0:T(8,128)S(1)}, u32[]{:S(2)}, u32[]{:S(2)}) async-start(f32[4,256,64]{1,2,0:T(8,128)} %broadcast_in_dim.41), calls=%async_computation.3 | async-start | bytes 524288 | tf_op jit(solution)/shard_map/all_to_all | solution.py:80
  105.7 7.0 %all-to-all-done.3 = f32[4,256,64]{1,2,0:T(8,128)S(1)} async-done(((f32[4,256,64]{1,2,0:T(8,128)}), f32[4,256,64]{1,2,0:T(8,128)S(1)}, u32[]{:S(2)}, u32[]{:S(2)}) %all-to-all-start.3) | async-done | bytes 262176 | tf_op jit(solution)/shard_map/all_to_all | solution.py:80
  112.9 2.8 %gather_fusion.1 = f32[1024,64]{1,0:T(8,128)S(1)} fusion(f32[1024,64]{1,0:T(8,128)S(1)} %bitcast.51, s32[1024]{0:T(1024)S(1)} %broadcast_clamp_fusion), kind=kCustom, calls=%fused_computation.1 | custom fusion | bytes 528384 | tf_op jit(solution)/shard_map/jit(_take)/gather | solution.py:63
  116.1 1.4 %add_reduce_fusion = (f32[256,32,32]{0,2,1:T(8,128)S(1)}, f32[256,32,32]{0,2,1:T(8,128)S(1)}) fusion(f32[4,256,32]{1,2,0:T(8,128)S(1)} %copy.54, f32[4,256,32]{1,2,0:T(8,128)S(1)} %copy.53, f32[4,256,32]{1,2,0:T(8,128)S(1)} %copy-done.3, f32[4,256,32]{1,2,0:T(8,128)S(1)} %get-tuple-element.20), kind=kLoop, calls=%fused_computation.5 | loop fusion | flops 7864320 | bytes 2621440 | tf_op jit(solution)/shard_map/reduce_sum | solution.py:65
  117.5 1.8 %multiply_bitcast_fusion = (f32[32,64,32]{1,0,2:T(8,128)S(1)}, f32[32,64,32]{1,0,2:T(8,128)S(1)}) fusion(f32[1,256,64]{1,2,0:T(8,128)S(1)} %copy-done.5, f32[1,256,64]{1,2,0:T(8,128)S(1)} %copy-done.7, f32[1,256,32,32]{1,3,0,2:T(8,128)S(1)} %bitcast.53, f32[1,256,32,32]{1,3,0,2:T(8,128)S(1)} %bitcast.52), kind=kOutput, calls=%fused_computation.24 | convolution fusion | flops 403341312 | bytes 2752512 | tf_op jit(solution)/shard_map/cua,cubr->rab/dot_general | solution.py:67
  120.5 1.9 %collective-permute-start.2 = (f32[1,2048]{1,0:T(1,128)S(1)}, f32[1,2048]{1,0:T(1,128)S(1)}, u32[]{:S(2)}, u32[]{:S(2)}) collective-permute-start(f32[1,2048]{1,0:T(1,128)S(1)} %get-tuple-element.17), channel_id=1, source_target_pairs={{0,4},{4,8},{8,12},{12,16},{16,20},{20,24},{24,28},{1,5},{5,9},{9,... | collective-permute-start | bytes 24584 | tf_op jit(solution)/shard_map/ppermute | solution.py:16
  122.4 4.5 %collective-permute-start.3 = (f32[1,2048]{1,0:T(1,128)S(1)}, f32[1,2048]{1,0:T(1,128)S(1)}, u32[]{:S(2)}, u32[]{:S(2)}) collective-permute-start(f32[1,2048]{1,0:T(1,128)S(1)} %get-tuple-element.16), channel_id=1, source_target_pairs={{4,0},{8,4},{12,8},{16,12},{20,16},{24,20},{28,24},{5,1},{9,5},{13... | collective-permute-start | bytes 24584 | tf_op jit(solution)/shard_map/ppermute | solution.py:17
  127.0 2.3 %collective-permute-start.4 = (f32[32,1]{1,0:T(8,128)S(1)}, f32[32,1]{1,0:T(8,128)S(1)}, u32[]{:S(2)}, u32[]{:S(2)}) collective-permute-start(f32[32,1]{1,0:T(8,128)S(1)} %get-tuple-element.13), channel_id=1, source_target_pairs={{0,1},{1,2},{2,3},{4,5},{5,6},{6,7},{8,9},{9,10},{10,11},{12,13},{... | collective-permute-start | bytes 392 | tf_op jit(solution)/shard_map/ppermute | solution.py:16
  129.3 3.6 %collective-permute-start.5 = (f32[32,1]{1,0:T(8,128)S(1)}, f32[32,1]{1,0:T(8,128)S(1)}, u32[]{:S(2)}, u32[]{:S(2)}) collective-permute-start(f32[32,1]{1,0:T(8,128)S(1)} %get-tuple-element.12), channel_id=1, source_target_pairs={{1,0},{2,1},{3,2},{5,4},{6,5},{7,6},{9,8},{10,9},{11,10},{13,12},{... | collective-permute-start | bytes 392 | tf_op jit(solution)/shard_map/ppermute | solution.py:17
  133.3 1.2 mul.351
  (70 shorter events, 12.2 us)
Async XLA Ops:
  0.9 3.1 %copy-start.4 = (f32[1,256,64]{1,2,0:T(8,128)}, f32[1,256,64]{1,2,0:T(8,128)S(1)}, u32[]{:S(2)}) copy-start(f32[1,256,64]{1,2,0:T(8,128)S(1)} %get-tuple-element.22) | copy-start | bytes 196612
  0.9 3.1 %copy-start.6 = (f32[1,256,64]{1,2,0:T(8,128)}, f32[1,256,64]{1,2,0:T(8,128)S(1)}, u32[]{:S(2)}) copy-start(f32[1,256,64]{1,2,0:T(8,128)S(1)} %get-tuple-element.23) | copy-start | bytes 196612
  1.9 0.7 copy-start
  6.7 2.9 %copy-start.8 = (s32[1024]{0:T(1024)S(1)}, s32[1024]{0:T(1024)}, u32[]{:S(2)}) copy-start(s32[1024]{0:T(1024)} %param.8) | copy-start | bytes 12292
  7.9 4.5 %copy-start.2 = (f32[4,256,32]{1,2,0:T(8,128)}, f32[4,256,32]{1,2,0:T(8,128)S(1)}, u32[]{:S(2)}) copy-start(f32[4,256,32]{1,2,0:T(8,128)S(1)} %get-tuple-element.21) | copy-start | bytes 393220
  13.4 12.4 %all-to-all-start = ((f32[4,256,64]{1,2,0:T(8,128)}), f32[4,256,64]{1,2,0:T(8,128)S(1)}, u32[]{:S(2)}, u32[]{:S(2)}) async-start(f32[4,256,64]{1,2,0:T(8,128)} %copy.44), calls=%async_computation | async-start | bytes 524288 | tf_op jit(solution)/shard_map/all_to_all | solution.py:73
  42.8 2.9 %collective-permute-start = (f32[128,2,1024]{2,1,0:T(2,128)S(1)}, f32[128,2,1024]{2,1,0:T(2,128)}, u32[]{:S(2)}, u32[]{:S(2)}) collective-permute-start(f32[128,2,1024]{2,1,0:T(2,128)S(1)} %constant_dynamic-slice_fusion), channel_id=1, source_target_pairs={{0,4},{4,0},{8,12},{12,8},{16,20},{20,16},{24,28},{28,24},{1,5},{5... | collective-permute-start | bytes 3145736 | tf_op jit(solution)/shard_map/ppermute | solution.py:91
  47.4 36.5 %copy-start.9 = (f32[1024]{0:T(1024)S(1)}, f32[1024]{0:T(1024)}, u32[]{:S(2)}) copy-start(f32[1024]{0:T(1024)} %param.9) | copy-start | bytes 12292
  81.1 2.8 %collective-permute-start.1 = (f32[128,2,1024]{2,1,0:T(2,128)S(1)}, f32[128,2,1024]{2,1,0:T(2,128)}, u32[]{:S(2)}, u32[]{:S(2)}) collective-permute-start(f32[128,2,1024]{2,1,0:T(2,128)S(1)} %all_to_all.26), channel_id=1, source_target_pairs={{0,4},{4,0},{8,12},{12,8},{16,20},{20,16},{24,28},{28,24},{1,5},{5... | collective-permute-start | bytes 3145736 | tf_op jit(solution)/shard_map/ppermute | solution.py:103
  99.8 16.3 %copy-start.3 = (f32[4,256,32]{1,2,0:T(8,128)S(1)}, f32[4,256,32]{1,2,0:T(8,128)}, u32[]{:S(2)}) copy-start(f32[4,256,32]{1,2,0:T(8,128)} %copy-done.2) | copy-start | bytes 393220
  99.8 12.9 %all-to-all-start.3 = ((f32[4,256,64]{1,2,0:T(8,128)}), f32[4,256,64]{1,2,0:T(8,128)S(1)}, u32[]{:S(2)}, u32[]{:S(2)}) async-start(f32[4,256,64]{1,2,0:T(8,128)} %broadcast_in_dim.41), calls=%async_computation.3 | async-start | bytes 524288 | tf_op jit(solution)/shard_map/all_to_all | solution.py:80
  112.9 4.7 %copy-start.5 = (f32[1,256,64]{1,2,0:T(8,128)S(1)}, f32[1,256,64]{1,2,0:T(8,128)}, u32[]{:S(2)}) copy-start(f32[1,256,64]{1,2,0:T(8,128)} %copy-done.4) | copy-start | bytes 196612
  112.9 4.7 %copy-start.7 = (f32[1,256,64]{1,2,0:T(8,128)S(1)}, f32[1,256,64]{1,2,0:T(8,128)}, u32[]{:S(2)}) copy-start(f32[1,256,64]{1,2,0:T(8,128)} %copy-done.6) | copy-start | bytes 196612
  119.3 15.8 %copy-start.1 = (f32[32,16,128]{2,1,0:T(8,128)S(1)}, f32[32,16,128]{2,1,0:T(8,128)}, u32[]{:S(2)}) copy-start(f32[32,16,128]{2,1,0:T(8,128)} %copy-done) | copy-start | bytes 786436
  120.5 14.6 %collective-permute-start.2 = (f32[1,2048]{1,0:T(1,128)S(1)}, f32[1,2048]{1,0:T(1,128)S(1)}, u32[]{:S(2)}, u32[]{:S(2)}) collective-permute-start(f32[1,2048]{1,0:T(1,128)S(1)} %get-tuple-element.17), channel_id=1, source_target_pairs={{0,4},{4,8},{8,12},{12,16},{16,20},{20,24},{24,28},{1,5},{5,9},{9,... | collective-permute-start | bytes 24584 | tf_op jit(solution)/shard_map/ppermute | solution.py:16
  122.4 12.7 %collective-permute-start.3 = (f32[1,2048]{1,0:T(1,128)S(1)}, f32[1,2048]{1,0:T(1,128)S(1)}, u32[]{:S(2)}, u32[]{:S(2)}) collective-permute-start(f32[1,2048]{1,0:T(1,128)S(1)} %get-tuple-element.16), channel_id=1, source_target_pairs={{4,0},{8,4},{12,8},{16,12},{20,16},{24,20},{28,24},{5,1},{9,5},{13... | collective-permute-start | bytes 24584 | tf_op jit(solution)/shard_map/ppermute | solution.py:17
  127.0 7.4 %collective-permute-start.4 = (f32[32,1]{1,0:T(8,128)S(1)}, f32[32,1]{1,0:T(8,128)S(1)}, u32[]{:S(2)}, u32[]{:S(2)}) collective-permute-start(f32[32,1]{1,0:T(8,128)S(1)} %get-tuple-element.13), channel_id=1, source_target_pairs={{0,1},{1,2},{2,3},{4,5},{5,6},{6,7},{8,9},{9,10},{10,11},{12,13},{... | collective-permute-start | bytes 392 | tf_op jit(solution)/shard_map/ppermute | solution.py:16
  129.3 5.8 %collective-permute-start.5 = (f32[32,1]{1,0:T(8,128)S(1)}, f32[32,1]{1,0:T(8,128)S(1)}, u32[]{:S(2)}, u32[]{:S(2)}) collective-permute-start(f32[32,1]{1,0:T(8,128)S(1)} %get-tuple-element.12), channel_id=1, source_target_pairs={{1,0},{2,1},{3,2},{5,4},{6,5},{7,6},{9,8},{10,9},{11,10},{13,12},{... | collective-permute-start | bytes 392 | tf_op jit(solution)/shard_map/ppermute | solution.py:17

commit v17 on v15

--- a/solution.py
+++ b/solution.py
@@ -120,7 +120,8 @@
     fourier = reduce_scatter(forward_dft(masked, slot_order, lon_start, lon_total) * forward_scale, "lon")
     fourier = fourier.reshape(slot_count, 2, cycle_count)
     coefficient = jnp.einsum("krl,kcr->kcl", legendre, fourier, precision=lax.Precision.HIGH)
-    degree_whole = paired_all_gather(paired_reduce_scatter(coefficient, "lat"), "lat")
+    flat = coefficient.reshape(slot_count, -1)
+    degree_whole = paired_all_gather(paired_reduce_scatter(flat, "lat"), "lat").reshape(coefficient.shape)
     degree_count = degree_whole.shape[2]
     degrees = jnp.arange(degree_count, dtype=jnp.int32)
     retained = degrees[None, :] >= own_orders[:, None]

time: 137 us -> 140 us (1.022)
  local copies, waits for them, and re-layouts: 14.4 us -> 19.2 us
  waiting for transfers between devices: 19.9 us -> 18.1 us
    concatenate x0 -> x2, local copies, waits for them, and re-layouts: none -> 2.74 us  [paired_all_gather(): jnp.concatenate([half, other])]
    unnamed x21 -> x24, local copies, waits for them, and re-layouts: 0.79 us -> 3.01 us
    ppermute x1, waiting for transfers between devices: 2.49 us -> 0.77 us  [paired_all_gather(): other = lax.ppermute(half, axis, pairs)]
  transfers between devices with their start and end apart: 8 -> 8, of which waited for: 5 -> 5; matrix products, arithmetic and copies ran while one was open for 2% -> 3% of each run, Pallas kernels for 0% -> 0%
where the time goes in v17:
time: 140 us; the launch traced here: 138 us
  blocking collectives  32.8 us (23%)
  other arithmetic  24.2 us (17%)
  starting transfers between devices  23.1 us (16%)
  matrix products  19.4 us (14%)
  local copies, waits for them, and re-layouts  19.2 us (14%)
  waiting for transfers between devices  18.1 us (13%)
    all_to_all x1, blocking collectives, paired_reduce_scatter(): lax.all_to_all(summed, axis, 0, 0, tiled=True, axis_index_groups=groups)  17.4 us
    dot_general x1, matrix products, local(): jnp.einsum('krl,kcr->kcl', legendre, fourier, precision=lax.Precision.HIGH)  15.8 us
    all_to_all x1, blocking collectives, paired_all_gather(): lax.all_to_all(copies, axis, 0, 0, tiled=True, axis_index_groups=groups)  15.4 us
    reduce_sum x1, other arithmetic, local(): synthesis = (legendre[:, None, :, :] * spectrum[:, :, None, :]).sum(axis=3)  11.4 us
    ppermute x2, starting transfers between devices, halo(): lax.ppermute(head, axis, [((i + 1) % count, i) for i in range(ends)])  8.11 us
    all_to_all x1, waiting for transfers between devices, reduce_scatter(): moved = lax.all_to_all(x, axis, 0, 0, tiled=True)  7.05 us
    all_to_all x1, waiting for transfers between devices, all_gather(): return lax.all_to_all(copies, axis, 0, 0, tiled=True)  6.98 us
    all_to_all x1, starting transfers between devices, all_gather(): return lax.all_to_all(copies, axis, 0, 0, tiled=True)  5.37 us
  transfers between devices with their start and end apart: 8, of which 5 were waited for; matrix products, arithmetic and copies ran while one was open for 3% of the time, Pallas kernels for 0%

profile of v17, /device:TPU:12, one launch (start us, length us, event | category | flops | bytes accessed | tf_op | source)
XLA Modules:
  0.0 137.9 jit_solution(13160852755040671618)
XLA Ops:
  4.0 1.9 %convolution_bitcast_fusion = f32[2,256,32,32]{1,2,0,3:T(8,128)S(1)} fusion(f32[32,64,32]{2,1,0:T(8,128)S(1)} %reshape.216, f32[1,256,64]{1,2,0:T(8,128)S(1)} %get-tuple-element.22, f32[1,256,64]{1,2,0:T(8,128)S(1)} %get-tuple-element.23), kind=kOutput, calls=%fused_computation.16 | convolution fusion | flops 402685952 | bytes 2490368 | tf_op jit(solution)/shard_map/cua,rab->cubr/dot_general | solution.py:49
  8.0 1.2 subtract_reduce_fusion.1
  9.7 2.8 %gather_fusion = f32[1024,64]{1,0:T(8,128)S(1)} fusion(f32[1024,64]{1,0:T(8,128)S(1)} %copy.43, s32[1024]{0:T(1024)S(1)} %broadcast_clamp_fusion.1), kind=kCustom, calls=%fused_computation | custom fusion | bytes 528384 | tf_op jit(solution)/shard_map/jit(_take)/gather | solution.py:54
  13.5 5.3 %all-to-all-start = ((f32[4,256,64]{1,2,0:T(8,128)}), f32[4,256,64]{1,2,0:T(8,128)S(1)}, u32[]{:S(2)}, u32[]{:S(2)}) async-start(f32[4,256,64]{1,2,0:T(8,128)} %copy.44), calls=%async_computation | async-start | bytes 524288 | tf_op jit(solution)/shard_map/all_to_all | solution.py:73
  18.8 7.0 %all-to-all-done = f32[4,256,64]{1,2,0:T(8,128)S(1)} async-done(((f32[4,256,64]{1,2,0:T(8,128)}), f32[4,256,64]{1,2,0:T(8,128)S(1)}, u32[]{:S(2)}, u32[]{:S(2)}) %all-to-all-start) | async-done | bytes 262176 | tf_op jit(solution)/shard_map/all_to_all | solution.py:73
  26.0 15.8 %fusion.35 = f32[256,2,1024]{2,1,0:T(2,128)S(1)} fusion(f32[256,2,32]{2,1,0:T(2,128)S(1)} %copy.47, f32[256,32,1024]{2,1,0:T(8,128)} %param.7), kind=kOutput, calls=%fused_computation.70 | convolution fusion | flops 100663296 | bytes 35717120 | tf_op jit(solution)/shard_map/krl,kcr->kcl/dot_general | solution.py:122
  42.7 1.3 copy-done
  44.2 2.6 %collective-permute-done = f32[128,2048]{1,0:T(8,128)S(1)} collective-permute-done((f32[128,2048]{1,0:T(8,128)S(1)}, f32[128,2048]{1,0:T(8,128)S(1)}, u32[]{:S(2)}, u32[]{:S(2)}) %collective-permute-start) | collective-permute-done | bytes 1048608 | tf_op jit(solution)/shard_map/ppermute | solution.py:91
  46.8 1.3 dynamic-slice_add_fusion
  48.2 17.4 %all_to_all.33 = f32[4,32,2048]{2,1,0:T(8,128)S(1)} all-to-all(f32[4,32,2048]{2,1,0:T(8,128)S(1)} %bitcast.62), channel_id=1, replica_groups={{0,8,16,24},{4,12,20,28},{1,9,17,25},{5,13,21,29},{2,10,18,26},{6,14,22..., dimensions={0} | all-to-all | bytes 2097152 | tf_op jit(solution)/shard_map/all_to_all | solution.py:92
  65.7 15.4 %all_to_all.34 = f32[4,32,2048]{2,1,0:T(8,128)S(1)} all-to-all(f32[4,32,2048]{2,1,0:T(8,128)S(1)} %broadcast_in_dim.38), channel_id=1, replica_groups={{0,8,16,24},{4,12,20,28},{1,9,17,25},{5,13,21,29},{2,10,18,26},{6,14,22..., dimensions={0} | all-to-all | bytes 2097152 | tf_op jit(solution)/shard_map/all_to_all | solution.py:102
  83.8 1.9 %concatenate.33 = f32[128,2,1024]{2,1,0:T(2,128)} reshape(f32[128,2048]{1,0:T(8,128)S(1)} %collective-permute-done.1) | data formatting | bytes 2097152 | tf_op jit(solution)/shard_map/concatenate | solution.py:104
  85.7 3.7 %fusion.1 = f32[256,2,1024]{2,1,0:T(2,128)S(1)} fusion(f32[128,2,1024]{2,1,0:T(2,128)} %concatenate.33, f32[128,2,1024]{2,1,0:T(2,128)S(1)} %concatenate.32, pred[]{:T(512)S(6)} %eq.25, pred[256,1024]{1,0:T(8,128)(4,1)} %iota_compare_fusion.1, f32[1024]{0:T(1024)S(1)} %copy-done.10), kind=kLoop, calls=%fused_computation.11 | loop fusion | flops 2621440 | bytes 4460545 | tf_op jit(solution)/shard_map/jit(_where)/select_n | solution.py:128
  89.4 11.4 %multiply_reduce_fusion = f32[256,2,32]{2,1,0:T(2,128)S(1)} fusion(f32[256,2,1024]{2,1,0:T(2,128)S(1)} %fusion.1, f32[256,32,1024]{2,1,0:T(8,128)} %param.7), kind=kLoop, calls=%fused_computation.2 | loop fusion | flops 33538048 | bytes 35717120 | tf_op jit(solution)/shard_map/reduce_sum | solution.py:129
  101.6 5.4 %all-to-all-start.3 = ((f32[4,256,64]{1,2,0:T(8,128)}), f32[4,256,64]{1,2,0:T(8,128)S(1)}, u32[]{:S(2)}, u32[]{:S(2)}) async-start(f32[4,256,64]{1,2,0:T(8,128)} %broadcast_in_dim.41), calls=%async_computation.3 | async-start | bytes 524288 | tf_op jit(solution)/shard_map/all_to_all | solution.py:80
  107.5 7.0 %all-to-all-done.3 = f32[4,256,64]{1,2,0:T(8,128)S(1)} async-done(((f32[4,256,64]{1,2,0:T(8,128)}), f32[4,256,64]{1,2,0:T(8,128)S(1)}, u32[]{:S(2)}, u32[]{:S(2)}) %all-to-all-start.3) | async-done | bytes 262176 | tf_op jit(solution)/shard_map/all_to_all | solution.py:80
  114.7 2.8 %gather_fusion.1 = f32[1024,64]{1,0:T(8,128)S(1)} fusion(f32[1024,64]{1,0:T(8,128)S(1)} %bitcast.55, s32[1024]{0:T(1024)S(1)} %broadcast_clamp_fusion), kind=kCustom, calls=%fused_computation.1 | custom fusion | bytes 528384 | tf_op jit(solution)/shard_map/jit(_take)/gather | solution.py:63
  118.0 1.4 %add_reduce_fusion = (f32[256,32,32]{0,2,1:T(8,128)S(1)}, f32[256,32,32]{0,2,1:T(8,128)S(1)}) fusion(f32[4,256,32]{1,2,0:T(8,128)S(1)} %copy.52, f32[4,256,32]{1,2,0:T(8,128)S(1)} %copy.51, f32[4,256,32]{1,2,0:T(8,128)S(1)} %copy-done.4, f32[4,256,32]{1,2,0:T(8,128)S(1)} %get-tuple-element.20), kind=kLoop, calls=%fused_computation.4 | loop fusion | flops 7864320 | bytes 2621440 | tf_op jit(solution)/shard_map/reduce_sum | solution.py:65
  119.4 1.8 %multiply_bitcast_fusion = (f32[32,64,32]{1,0,2:T(8,128)S(1)}, f32[32,64,32]{1,0,2:T(8,128)S(1)}) fusion(f32[1,256,64]{1,2,0:T(8,128)S(1)} %copy-done.6, f32[1,256,64]{1,2,0:T(8,128)S(1)} %copy-done.8, f32[1,256,32,32]{1,3,0,2:T(8,128)S(1)} %bitcast.60, f32[1,256,32,32]{1,3,0,2:T(8,128)S(1)} %bitcast.59), kind=kOutput, calls=%fused_computation.23 | convolution fusion | flops 403341312 | bytes 2752512 | tf_op jit(solution)/shard_map/cua,cubr->rab/dot_general | solution.py:67
  122.3 1.9 %collective-permute-start.2 = (f32[1,2048]{1,0:T(1,128)S(1)}, f32[1,2048]{1,0:T(1,128)S(1)}, u32[]{:S(2)}, u32[]{:S(2)}) collective-permute-start(f32[1,2048]{1,0:T(1,128)S(1)} %get-tuple-element.17), channel_id=1, source_target_pairs={{0,4},{4,8},{8,12},{12,16},{16,20},{20,24},{24,28},{1,5},{5,9},{9,... | collective-permute-start | bytes 24584 | tf_op jit(solution)/shard_map/ppermute | solution.py:16
  124.2 4.5 %collective-permute-start.3 = (f32[1,2048]{1,0:T(1,128)S(1)}, f32[1,2048]{1,0:T(1,128)S(1)}, u32[]{:S(2)}, u32[]{:S(2)}) collective-permute-start(f32[1,2048]{1,0:T(1,128)S(1)} %get-tuple-element.16), channel_id=1, source_target_pairs={{4,0},{8,4},{12,8},{16,12},{20,16},{24,20},{28,24},{5,1},{9,5},{13... | collective-permute-start | bytes 24584 | tf_op jit(solution)/shard_map/ppermute | solution.py:17
  128.8 2.3 %collective-permute-start.4 = (f32[32,1]{1,0:T(8,128)S(1)}, f32[32,1]{1,0:T(8,128)S(1)}, u32[]{:S(2)}, u32[]{:S(2)}) collective-permute-start(f32[32,1]{1,0:T(8,128)S(1)} %get-tuple-element.13), channel_id=1, source_target_pairs={{0,1},{1,2},{2,3},{4,5},{5,6},{6,7},{8,9},{9,10},{10,11},{12,13},{... | collective-permute-start | bytes 392 | tf_op jit(solution)/shard_map/ppermute | solution.py:16
  131.1 3.6 %collective-permute-start.5 = (f32[32,1]{1,0:T(8,128)S(1)}, f32[32,1]{1,0:T(8,128)S(1)}, u32[]{:S(2)}, u32[]{:S(2)}) collective-permute-start(f32[32,1]{1,0:T(8,128)S(1)} %get-tuple-element.12), channel_id=1, source_target_pairs={{1,0},{2,1},{3,2},{5,4},{6,5},{7,6},{9,8},{10,9},{11,10},{13,12},{... | collective-permute-start | bytes 392 | tf_op jit(solution)/shard_map/ppermute | solution.py:17
  135.1 1.2 mul.335
  (75 shorter events, 15.8 us)
Async XLA Ops:
  0.9 5.2 %copy-start.5 = (f32[1,256,64]{1,2,0:T(8,128)}, f32[1,256,64]{1,2,0:T(8,128)S(1)}, u32[]{:S(2)}) copy-start(f32[1,256,64]{1,2,0:T(8,128)S(1)} %get-tuple-element.22) | copy-start | bytes 196612
  0.9 5.2 %copy-start.7 = (f32[1,256,64]{1,2,0:T(8,128)}, f32[1,256,64]{1,2,0:T(8,128)S(1)}, u32[]{:S(2)}) copy-start(f32[1,256,64]{1,2,0:T(8,128)S(1)} %get-tuple-element.23) | copy-start | bytes 196612
  1.9 0.7 copy-start.1
  6.7 2.9 %copy-start.9 = (s32[1024]{0:T(1024)S(1)}, s32[1024]{0:T(1024)}, u32[]{:S(2)}) copy-start(s32[1024]{0:T(1024)} %param.8) | copy-start | bytes 12292
  8.0 4.5 %copy-start.3 = (f32[4,256,32]{1,2,0:T(8,128)}, f32[4,256,32]{1,2,0:T(8,128)S(1)}, u32[]{:S(2)}) copy-start(f32[4,256,32]{1,2,0:T(8,128)S(1)} %get-tuple-element.21) | copy-start | bytes 393220
  13.5 12.4 %all-to-all-start = ((f32[4,256,64]{1,2,0:T(8,128)}), f32[4,256,64]{1,2,0:T(8,128)S(1)}, u32[]{:S(2)}, u32[]{:S(2)}) async-start(f32[4,256,64]{1,2,0:T(8,128)} %copy.44), calls=%async_computation | async-start | bytes 524288 | tf_op jit(solution)/shard_map/all_to_all | solution.py:73
  42.7 1.3 copy-start
  44.1 2.7 %collective-permute-start = (f32[128,2048]{1,0:T(8,128)S(1)}, f32[128,2048]{1,0:T(8,128)S(1)}, u32[]{:S(2)}, u32[]{:S(2)}) collective-permute-start(f32[128,2048]{1,0:T(8,128)S(1)} %constant_dynamic-slice_fusion), channel_id=1, source_target_pairs={{0,4},{4,0},{8,12},{12,8},{16,20},{20,16},{24,28},{28,24},{1,5},{5... | collective-permute-start | bytes 3145736 | tf_op jit(solution)/shard_map/ppermute | solution.py:91
  65.6 20.1 %copy-start.10 = (f32[1024]{0:T(1024)S(1)}, f32[1024]{0:T(1024)}, u32[]{:S(2)}) copy-start(f32[1024]{0:T(1024)} %param.9) | copy-start | bytes 12292
  81.2 2.7 %collective-permute-start.1 = (f32[128,2048]{1,0:T(8,128)S(1)}, f32[128,2048]{1,0:T(8,128)S(1)}, u32[]{:S(2)}, u32[]{:S(2)}) collective-permute-start(f32[128,2048]{1,0:T(8,128)S(1)} %bitcast.61), channel_id=1, source_target_pairs={{0,4},{4,0},{8,12},{12,8},{16,20},{20,16},{24,28},{28,24},{1,5},{5... | collective-permute-start | bytes 3145736 | tf_op jit(solution)/shard_map/ppermute | solution.py:103
  101.6 16.3 %copy-start.4 = (f32[4,256,32]{1,2,0:T(8,128)S(1)}, f32[4,256,32]{1,2,0:T(8,128)}, u32[]{:S(2)}) copy-start(f32[4,256,32]{1,2,0:T(8,128)} %copy-done.3) | copy-start | bytes 393220
  101.6 12.9 %all-to-all-start.3 = ((f32[4,256,64]{1,2,0:T(8,128)}), f32[4,256,64]{1,2,0:T(8,128)S(1)}, u32[]{:S(2)}, u32[]{:S(2)}) async-start(f32[4,256,64]{1,2,0:T(8,128)} %broadcast_in_dim.41), calls=%async_computation.3 | async-start | bytes 524288 | tf_op jit(solution)/shard_map/all_to_all | solution.py:80
  114.7 4.7 %copy-start.6 = (f32[1,256,64]{1,2,0:T(8,128)S(1)}, f32[1,256,64]{1,2,0:T(8,128)}, u32[]{:S(2)}) copy-start(f32[1,256,64]{1,2,0:T(8,128)} %copy-done.5) | copy-start | bytes 196612
  114.7 4.7 %copy-start.8 = (f32[1,256,64]{1,2,0:T(8,128)S(1)}, f32[1,256,64]{1,2,0:T(8,128)}, u32[]{:S(2)}) copy-start(f32[1,256,64]{1,2,0:T(8,128)} %copy-done.7) | copy-start | bytes 196612
  121.2 15.7 %copy-start.2 = (f32[32,16,128]{2,1,0:T(8,128)S(1)}, f32[32,16,128]{2,1,0:T(8,128)}, u32[]{:S(2)}) copy-start(f32[32,16,128]{2,1,0:T(8,128)} %copy-done.1) | copy-start | bytes 786436
  122.3 14.6 %collective-permute-start.2 = (f32[1,2048]{1,0:T(1,128)S(1)}, f32[1,2048]{1,0:T(1,128)S(1)}, u32[]{:S(2)}, u32[]{:S(2)}) collective-permute-start(f32[1,2048]{1,0:T(1,128)S(1)} %get-tuple-element.17), channel_id=1, source_target_pairs={{0,4},{4,8},{8,12},{12,16},{16,20},{20,24},{24,28},{1,5},{5,9},{9,... | collective-permute-start | bytes 24584 | tf_op jit(solution)/shard_map/ppermute | solution.py:16
  124.2 12.7 %collective-permute-start.3 = (f32[1,2048]{1,0:T(1,128)S(1)}, f32[1,2048]{1,0:T(1,128)S(1)}, u32[]{:S(2)}, u32[]{:S(2)}) collective-permute-start(f32[1,2048]{1,0:T(1,128)S(1)} %get-tuple-element.16), channel_id=1, source_target_pairs={{4,0},{8,4},{12,8},{16,12},{20,16},{24,20},{28,24},{5,1},{9,5},{13... | collective-permute-start | bytes 24584 | tf_op jit(solution)/shard_map/ppermute | solution.py:17
  128.8 7.4 %collective-permute-start.4 = (f32[32,1]{1,0:T(8,128)S(1)}, f32[32,1]{1,0:T(8,128)S(1)}, u32[]{:S(2)}, u32[]{:S(2)}) collective-permute-start(f32[32,1]{1,0:T(8,128)S(1)} %get-tuple-element.13), channel_id=1, source_target_pairs={{0,1},{1,2},{2,3},{4,5},{5,6},{6,7},{8,9},{9,10},{10,11},{12,13},{... | collective-permute-start | bytes 392 | tf_op jit(solution)/shard_map/ppermute | solution.py:16
  131.1 5.8 %collective-permute-start.5 = (f32[32,1]{1,0:T(8,128)S(1)}, f32[32,1]{1,0:T(8,128)S(1)}, u32[]{:S(2)}, u32[]{:S(2)}) collective-permute-start(f32[32,1]{1,0:T(8,128)S(1)} %get-tuple-element.12), channel_id=1, source_target_pairs={{1,0},{2,1},{3,2},{5,4},{6,5},{7,6},{9,8},{10,9},{11,10},{13,12},{... | collective-permute-start | bytes 392 | tf_op jit(solution)/shard_map/ppermute | solution.py:17

commit v18 on v15

--- a/solution.py
+++ b/solution.py
@@ -46,7 +46,7 @@
     order_count = slot_order.shape[0]
     rotor, cb, sb = dft_tables(order_count, lon_start, lon_width, lon_total)
     blocks = masked.reshape(cycles, lon_width // INNER, INNER)
-    partial = jnp.einsum("cua,rab->cubr", rotor, blocks, precision=lax.Precision.HIGHEST)
+    partial = jnp.einsum("cua,rab->cubr", rotor, blocks, precision=lax.Precision.HIGH)
     gc, gs = partial[0][None], partial[1][None]
     fc = (cb[..., None] * gc - sb[..., None] * gs).sum(axis=2)
     fs = (sb[..., None] * gc + cb[..., None] * gs).sum(axis=2)
@@ -64,7 +64,7 @@
     yc, ys = by_order[:, :, 0, None, :], by_order[:, :, 1, None, :]
     hc = (yc * cb[..., None] + ys * sb[..., None]).sum(axis=0)
     hs = (ys * cb[..., None] - yc * sb[..., None]).sum(axis=0)
-    out = jnp.einsum("cua,cubr->rab", rotor, jnp.stack([hc, hs]), precision=lax.Precision.HIGHEST)
+    out = jnp.einsum("cua,cubr->rab", rotor, jnp.stack([hc, hs]), precision=lax.Precision.HIGH)
     return out.reshape(cycles, lon_width)
 
 

time: 137 us -> 135 us (0.985)
  matrix products: 19.4 us -> 17.8 us
where the time goes in v18:
time: 135 us; the launch traced here: 133 us
  blocking collectives  32.8 us (24%)
  other arithmetic  24.4 us (18%)
  starting transfers between devices  23.1 us (17%)
  waiting for transfers between devices  19.9 us (15%)
  matrix products  17.8 us (13%)
  local copies, waits for them, and re-layouts  14.4 us (11%)
    all_to_all x1, blocking collectives, paired_reduce_scatter(): lax.all_to_all(summed, axis, 0, 0, tiled=True, axis_index_groups=groups)  17.4 us
    dot_general x1, matrix products, local(): jnp.einsum('krl,kcr->kcl', legendre, fourier, precision=lax.Precision.HIGH)  15.8 us
    all_to_all x1, blocking collectives, paired_all_gather(): lax.all_to_all(copies, axis, 0, 0, tiled=True, axis_index_groups=groups)  15.4 us
    reduce_sum x1, other arithmetic, local(): synthesis = (legendre[:, None, :, :] * spectrum[:, :, None, :]).sum(axis=3)  11.4 us
    ppermute x2, starting transfers between devices, halo(): lax.ppermute(head, axis, [((i + 1) % count, i) for i in range(ends)])  8.11 us
    all_to_all x1, waiting for transfers between devices, reduce_scatter(): moved = lax.all_to_all(x, axis, 0, 0, tiled=True)  7.05 us
    all_to_all x1, waiting for transfers between devices, all_gather(): return lax.all_to_all(copies, axis, 0, 0, tiled=True)  6.98 us
    all_to_all x1, starting transfers between devices, all_gather(): return lax.all_to_all(copies, axis, 0, 0, tiled=True)  5.37 us
  transfers between devices with their start and end apart: 8, of which 5 were waited for; matrix products, arithmetic and copies ran while one was open for 2% of the time, Pallas kernels for 0%

profile of v18, /device:TPU:12, one launch (start us, length us, event | category | flops | bytes accessed | tf_op | source)
XLA Modules:
  0.0 133.4 jit_solution(9794706620866520540)
XLA Ops:
  2.6 1.1 bitcast_multiply_fusion.1
  4.0 1.0 convolution_bitcast_fusion
  7.1 1.2 subtract_reduce_fusion.1
  8.8 2.8 %gather_fusion = f32[1024,64]{1,0:T(8,128)S(1)} fusion(f32[1024,64]{1,0:T(8,128)S(1)} %copy.43, s32[1024]{0:T(1024)S(1)} %broadcast_clamp_fusion.1), kind=kCustom, calls=%fused_computation | custom fusion | bytes 528384 | tf_op jit(solution)/shard_map/jit(_take)/gather | solution.py:54
  12.6 5.3 %all-to-all-start = ((f32[4,256,64]{1,2,0:T(8,128)}), f32[4,256,64]{1,2,0:T(8,128)S(1)}, u32[]{:S(2)}, u32[]{:S(2)}) async-start(f32[4,256,64]{1,2,0:T(8,128)} %copy.44), calls=%async_computation | async-start | bytes 524288 | tf_op jit(solution)/shard_map/all_to_all | solution.py:73
  17.9 7.0 %all-to-all-done = f32[4,256,64]{1,2,0:T(8,128)S(1)} async-done(((f32[4,256,64]{1,2,0:T(8,128)}), f32[4,256,64]{1,2,0:T(8,128)S(1)}, u32[]{:S(2)}, u32[]{:S(2)}) %all-to-all-start) | async-done | bytes 262176 | tf_op jit(solution)/shard_map/all_to_all | solution.py:73
  25.1 15.8 %fusion.35 = f32[256,2,1024]{2,1,0:T(2,128)S(1)} fusion(f32[256,2,32]{2,1,0:T(2,128)S(1)} %copy.47, f32[256,32,1024]{2,1,0:T(8,128)} %param.7), kind=kOutput, calls=%fused_computation.70 | convolution fusion | flops 100663296 | bytes 35717120 | tf_op jit(solution)/shard_map/krl,kcr->kcl/dot_general | solution.py:122
  41.1 2.8 %collective-permute-done = f32[128,2,1024]{2,1,0:T(2,128)} collective-permute-done((f32[128,2,1024]{2,1,0:T(2,128)S(1)}, f32[128,2,1024]{2,1,0:T(2,128)}, u32[]{:S(2)}, u32[]{:S(2)}) %collective-permute-start) | collective-permute-done | bytes 1048608 | tf_op jit(solution)/shard_map/ppermute | solution.py:91
  43.9 1.8 %dynamic-slice_add_fusion = f32[128,2,1024]{2,1,0:T(2,128)S(1)} fusion(f32[128,2,1024]{2,1,0:T(2,128)} %collective-permute-done, f32[256,2,1024]{2,1,0:T(2,128)S(1)} %fusion.35, s32[]{:T(128)S(6)} %select_n.84), kind=kLoop, calls=%fused_computation.21 | loop fusion | flops 262144 | bytes 3145732 | tf_op jit(solution)/shard_map/add | solution.py:91
  45.6 17.4 %all_to_all.25 = f32[128,2,1024]{2,1,0:T(2,128)S(1)} all-to-all(f32[128,2,1024]{2,1,0:T(2,128)S(1)} %dynamic-slice_add_fusion), channel_id=1, replica_groups={{0,8,16,24},{4,12,20,28},{1,9,17,25},{5,13,21,29},{2,10,18,26},{6,14,22..., dimensions={0} | all-to-all | bytes 2097152 | tf_op jit(solution)/shard_map/all_to_all | solution.py:92
  63.9 15.4 %all_to_all.26 = f32[128,2,1024]{2,1,0:T(2,128)S(1)} all-to-all(f32[128,2,1024]{2,1,0:T(2,128)S(1)} %bitcast.56), channel_id=1, replica_groups={{0,8,16,24},{4,12,20,28},{1,9,17,25},{5,13,21,29},{2,10,18,26},{6,14,22..., dimensions={0} | all-to-all | bytes 2097152 | tf_op jit(solution)/shard_map/all_to_all | solution.py:102
  79.6 2.5 %collective-permute-done.1 = f32[128,2,1024]{2,1,0:T(2,128)} collective-permute-done((f32[128,2,1024]{2,1,0:T(2,128)S(1)}, f32[128,2,1024]{2,1,0:T(2,128)}, u32[]{:S(2)}, u32[]{:S(2)}) %collective-permute-start.1) | collective-permute-done | bytes 1048608 | tf_op jit(solution)/shard_map/ppermute | solution.py:103
  82.1 3.6 %fusion.1 = f32[256,2,1024]{2,1,0:T(2,128)S(1)} fusion(f32[128,2,1024]{2,1,0:T(2,128)} %collective-permute-done.1, f32[128,2,1024]{2,1,0:T(2,128)S(1)} %all_to_all.26, pred[]{:T(512)S(6)} %eq.25, pred[256,1024]{1,0:T(8,128)(4,1)S(1)} %iota_compare_fusion.1, f32[1024]{0:T(1024)S(1)} %copy-done.9), kind=kLoop, calls=%fused_computation.11 | loop fusion | flops 2621440 | bytes 4460545 | tf_op jit(solution)/shard_map/jit(_where)/select_n | solution.py:127
  85.8 11.4 %multiply_reduce_fusion = f32[256,2,32]{2,1,0:T(2,128)S(1)} fusion(f32[256,2,1024]{2,1,0:T(2,128)S(1)} %fusion.1, f32[256,32,1024]{2,1,0:T(8,128)} %param.7), kind=kLoop, calls=%fused_computation.2 | loop fusion | flops 33538048 | bytes 35717120 | tf_op jit(solution)/shard_map/reduce_sum | solution.py:128
  98.0 5.4 %all-to-all-start.3 = ((f32[4,256,64]{1,2,0:T(8,128)}), f32[4,256,64]{1,2,0:T(8,128)S(1)}, u32[]{:S(2)}, u32[]{:S(2)}) async-start(f32[4,256,64]{1,2,0:T(8,128)} %broadcast_in_dim.41), calls=%async_computation.3 | async-start | bytes 524288 | tf_op jit(solution)/shard_map/all_to_all | solution.py:80
  103.9 7.0 %all-to-all-done.3 = f32[4,256,64]{1,2,0:T(8,128)S(1)} async-done(((f32[4,256,64]{1,2,0:T(8,128)}), f32[4,256,64]{1,2,0:T(8,128)S(1)}, u32[]{:S(2)}, u32[]{:S(2)}) %all-to-all-start.3) | async-done | bytes 262176 | tf_op jit(solution)/shard_map/all_to_all | solution.py:80
  111.1 2.8 %gather_fusion.1 = f32[1024,64]{1,0:T(8,128)S(1)} fusion(f32[1024,64]{1,0:T(8,128)S(1)} %bitcast.53, s32[1024]{0:T(1024)S(1)} %broadcast_clamp_fusion), kind=kCustom, calls=%fused_computation.1 | custom fusion | bytes 528384 | tf_op jit(solution)/shard_map/jit(_take)/gather | solution.py:63
  114.3 1.4 %add_reduce_fusion = (f32[256,32,32]{0,2,1:T(8,128)S(1)}, f32[256,32,32]{0,2,1:T(8,128)S(1)}) fusion(f32[4,256,32]{1,2,0:T(8,128)S(1)} %copy.52, f32[4,256,32]{1,2,0:T(8,128)S(1)} %copy.51, f32[4,256,32]{1,2,0:T(8,128)S(1)} %copy-done.3, f32[4,256,32]{1,2,0:T(8,128)S(1)} %get-tuple-element.20), kind=kLoop, calls=%fused_computation.4 | loop fusion | flops 7864320 | bytes 2621440 | tf_op jit(solution)/shard_map/reduce_sum | solution.py:65
  115.8 1.0 multiply_bitcast_fusion
  117.9 1.9 %collective-permute-start.2 = (f32[1,2048]{1,0:T(1,128)S(1)}, f32[1,2048]{1,0:T(1,128)S(1)}, u32[]{:S(2)}, u32[]{:S(2)}) collective-permute-start(f32[1,2048]{1,0:T(1,128)S(1)} %get-tuple-element.17), channel_id=1, source_target_pairs={{0,4},{4,8},{8,12},{12,16},{16,20},{20,24},{24,28},{1,5},{5,9},{9,... | collective-permute-start | bytes 24584 | tf_op jit(solution)/shard_map/ppermute | solution.py:16
  119.8 4.5 %collective-permute-start.3 = (f32[1,2048]{1,0:T(1,128)S(1)}, f32[1,2048]{1,0:T(1,128)S(1)}, u32[]{:S(2)}, u32[]{:S(2)}) collective-permute-start(f32[1,2048]{1,0:T(1,128)S(1)} %get-tuple-element.16), channel_id=1, source_target_pairs={{4,0},{8,4},{12,8},{16,12},{20,16},{24,20},{28,24},{5,1},{9,5},{13... | collective-permute-start | bytes 24584 | tf_op jit(solution)/shard_map/ppermute | solution.py:17
  124.4 2.3 %collective-permute-start.4 = (f32[32,1]{1,0:T(8,128)S(1)}, f32[32,1]{1,0:T(8,128)S(1)}, u32[]{:S(2)}, u32[]{:S(2)}) collective-permute-start(f32[32,1]{1,0:T(8,128)S(1)} %get-tuple-element.13), channel_id=1, source_target_pairs={{0,1},{1,2},{2,3},{4,5},{5,6},{6,7},{8,9},{9,10},{10,11},{12,13},{... | collective-permute-start | bytes 392 | tf_op jit(solution)/shard_map/ppermute | solution.py:16
  126.7 3.6 %collective-permute-start.5 = (f32[32,1]{1,0:T(8,128)S(1)}, f32[32,1]{1,0:T(8,128)S(1)}, u32[]{:S(2)}, u32[]{:S(2)}) collective-permute-start(f32[32,1]{1,0:T(8,128)S(1)} %get-tuple-element.12), channel_id=1, source_target_pairs={{1,0},{2,1},{3,2},{5,4},{6,5},{7,6},{9,8},{10,9},{11,10},{13,12},{... | collective-permute-start | bytes 392 | tf_op jit(solution)/shard_map/ppermute | solution.py:17
  130.7 1.2 mul.335
  (70 shorter events, 12.2 us)
Async XLA Ops:
  0.9 3.1 %copy-start.4 = (f32[1,256,64]{1,2,0:T(8,128)}, f32[1,256,64]{1,2,0:T(8,128)S(1)}, u32[]{:S(2)}) copy-start(f32[1,256,64]{1,2,0:T(8,128)S(1)} %get-tuple-element.22) | copy-start | bytes 196612
  0.9 3.1 %copy-start.6 = (f32[1,256,64]{1,2,0:T(8,128)}, f32[1,256,64]{1,2,0:T(8,128)S(1)}, u32[]{:S(2)}) copy-start(f32[1,256,64]{1,2,0:T(8,128)S(1)} %get-tuple-element.23) | copy-start | bytes 196612
  1.9 0.7 copy-start
  5.9 2.9 %copy-start.8 = (s32[1024]{0:T(1024)S(1)}, s32[1024]{0:T(1024)}, u32[]{:S(2)}) copy-start(s32[1024]{0:T(1024)} %param.8) | copy-start | bytes 12292
  7.1 4.5 %copy-start.2 = (f32[4,256,32]{1,2,0:T(8,128)}, f32[4,256,32]{1,2,0:T(8,128)S(1)}, u32[]{:S(2)}) copy-start(f32[4,256,32]{1,2,0:T(8,128)S(1)} %get-tuple-element.21) | copy-start | bytes 393220
  12.6 12.4 %all-to-all-start = ((f32[4,256,64]{1,2,0:T(8,128)}), f32[4,256,64]{1,2,0:T(8,128)S(1)}, u32[]{:S(2)}, u32[]{:S(2)}) async-start(f32[4,256,64]{1,2,0:T(8,128)} %copy.44), calls=%async_computation | async-start | bytes 524288 | tf_op jit(solution)/shard_map/all_to_all | solution.py:73
  41.0 2.9 %collective-permute-start = (f32[128,2,1024]{2,1,0:T(2,128)S(1)}, f32[128,2,1024]{2,1,0:T(2,128)}, u32[]{:S(2)}, u32[]{:S(2)}) collective-permute-start(f32[128,2,1024]{2,1,0:T(2,128)S(1)} %constant_dynamic-slice_fusion), channel_id=1, source_target_pairs={{0,4},{4,0},{8,12},{12,8},{16,20},{20,16},{24,28},{28,24},{1,5},{5... | collective-permute-start | bytes 3145736 | tf_op jit(solution)/shard_map/ppermute | solution.py:91
  45.6 36.5 %copy-start.9 = (f32[1024]{0:T(1024)S(1)}, f32[1024]{0:T(1024)}, u32[]{:S(2)}) copy-start(f32[1024]{0:T(1024)} %param.9) | copy-start | bytes 12292
  79.3 2.8 %collective-permute-start.1 = (f32[128,2,1024]{2,1,0:T(2,128)S(1)}, f32[128,2,1024]{2,1,0:T(2,128)}, u32[]{:S(2)}, u32[]{:S(2)}) collective-permute-start(f32[128,2,1024]{2,1,0:T(2,128)S(1)} %all_to_all.26), channel_id=1, source_target_pairs={{0,4},{4,0},{8,12},{12,8},{16,20},{20,16},{24,28},{28,24},{1,5},{5... | collective-permute-start | bytes 3145736 | tf_op jit(solution)/shard_map/ppermute | solution.py:103
  98.0 16.3 %copy-start.3 = (f32[4,256,32]{1,2,0:T(8,128)S(1)}, f32[4,256,32]{1,2,0:T(8,128)}, u32[]{:S(2)}) copy-start(f32[4,256,32]{1,2,0:T(8,128)} %copy-done.2) | copy-start | bytes 393220
  98.0 12.9 %all-to-all-start.3 = ((f32[4,256,64]{1,2,0:T(8,128)}), f32[4,256,64]{1,2,0:T(8,128)S(1)}, u32[]{:S(2)}, u32[]{:S(2)}) async-start(f32[4,256,64]{1,2,0:T(8,128)} %broadcast_in_dim.41), calls=%async_computation.3 | async-start | bytes 524288 | tf_op jit(solution)/shard_map/all_to_all | solution.py:80
  111.1 4.7 %copy-start.5 = (f32[1,256,64]{1,2,0:T(8,128)S(1)}, f32[1,256,64]{1,2,0:T(8,128)}, u32[]{:S(2)}) copy-start(f32[1,256,64]{1,2,0:T(8,128)} %copy-done.4) | copy-start | bytes 196612
  111.1 4.7 %copy-start.7 = (f32[1,256,64]{1,2,0:T(8,128)S(1)}, f32[1,256,64]{1,2,0:T(8,128)}, u32[]{:S(2)}) copy-start(f32[1,256,64]{1,2,0:T(8,128)} %copy-done.6) | copy-start | bytes 196612
  116.7 15.7 %copy-start.1 = (f32[32,16,128]{2,1,0:T(8,128)S(1)}, f32[32,16,128]{2,1,0:T(8,128)}, u32[]{:S(2)}) copy-start(f32[32,16,128]{2,1,0:T(8,128)} %copy-done) | copy-start | bytes 786436
  117.9 14.6 %collective-permute-start.2 = (f32[1,2048]{1,0:T(1,128)S(1)}, f32[1,2048]{1,0:T(1,128)S(1)}, u32[]{:S(2)}, u32[]{:S(2)}) collective-permute-start(f32[1,2048]{1,0:T(1,128)S(1)} %get-tuple-element.17), channel_id=1, source_target_pairs={{0,4},{4,8},{8,12},{12,16},{16,20},{20,24},{24,28},{1,5},{5,9},{9,... | collective-permute-start | bytes 24584 | tf_op jit(solution)/shard_map/ppermute | solution.py:16
  119.8 12.7 %collective-permute-start.3 = (f32[1,2048]{1,0:T(1,128)S(1)}, f32[1,2048]{1,0:T(1,128)S(1)}, u32[]{:S(2)}, u32[]{:S(2)}) collective-permute-start(f32[1,2048]{1,0:T(1,128)S(1)} %get-tuple-element.16), channel_id=1, source_target_pairs={{4,0},{8,4},{12,8},{16,12},{20,16},{24,20},{28,24},{5,1},{9,5},{13... | collective-permute-start | bytes 24584 | tf_op jit(solution)/shard_map/ppermute | solution.py:17
  124.4 7.4 %collective-permute-start.4 = (f32[32,1]{1,0:T(8,128)S(1)}, f32[32,1]{1,0:T(8,128)S(1)}, u32[]{:S(2)}, u32[]{:S(2)}) collective-permute-start(f32[32,1]{1,0:T(8,128)S(1)} %get-tuple-element.13), channel_id=1, source_target_pairs={{0,1},{1,2},{2,3},{4,5},{5,6},{6,7},{8,9},{9,10},{10,11},{12,13},{... | collective-permute-start | bytes 392 | tf_op jit(solution)/shard_map/ppermute | solution.py:16
  126.7 5.8 %collective-permute-start.5 = (f32[32,1]{1,0:T(8,128)S(1)}, f32[32,1]{1,0:T(8,128)S(1)}, u32[]{:S(2)}, u32[]{:S(2)}) collective-permute-start(f32[32,1]{1,0:T(8,128)S(1)} %get-tuple-element.12), channel_id=1, source_target_pairs={{1,0},{2,1},{3,2},{5,4},{6,5},{7,6},{9,8},{10,9},{11,10},{13,12},{... | collective-permute-start | bytes 392 | tf_op jit(solution)/shard_map/ppermute | solution.py:17

commit v19 on v18

--- a/solution.py
+++ b/solution.py
@@ -95,13 +95,12 @@
 
 def paired_all_gather(x, axis):
     count = lax.axis_size(axis)
-    pairs = [(i, i ^ 1) for i in range(count)]
     groups = [list(range(side, count, 2)) for side in (0, 1)]
-    side = lax.axis_index(axis) % 2
     copies = jnp.broadcast_to(x[None], (count // 2,) + x.shape).reshape((count // 2 * x.shape[0],) + x.shape[1:])
     half = lax.all_to_all(copies, axis, 0, 0, tiled=True, axis_index_groups=groups)
-    other = lax.ppermute(half, axis, pairs)
-    return jnp.where(side == 0, jnp.concatenate([half, other]), jnp.concatenate([other, half]))
+    couples = [[i, i + 1] for i in range(0, count, 2)]
+    both = jnp.broadcast_to(half[None], (2,) + half.shape).reshape((2 * half.shape[0],) + half.shape[1:])
+    return lax.all_to_all(both, axis, 0, 0, tiled=True, axis_index_groups=couples)
 
 
 def local(surface, wet_blocks, legendre, slot_order, love_gain):

time: 135 us -> 138 us (1.022)
  blocking collectives: 32.8 us -> 22.8 us
  waiting for transfers between devices: 19.9 us -> 29.3 us
  starting transfers between devices: 23.1 us -> 27.4 us
  other arithmetic: 24.4 us -> 22.1 us
  local copies, waits for them, and re-layouts: 14.4 us -> 16.2 us
    all_to_all x0 -> x1, waiting for transfers between devices: none -> 11.7 us  [paired_all_gather(): lax.all_to_all(copies, axis, 0, 0, tiled=True, axis_index_groups=groups)]
    all_to_all x1, blocking collectives: 15.4 us -> 5.42 us  [paired_all_gather(): lax.all_to_all(both, axis, 0, 0, tiled=True, axis_index_groups=couples)]
    all_to_all x0 -> x1, starting transfers between devices: none -> 4.6 us  [paired_all_gather(): lax.all_to_all(copies, axis, 0, 0, tiled=True, axis_index_groups=groups)]
    ppermute x1 -> x0, waiting for transfers between devices: 2.49 us -> none  [paired_all_gather(): other = lax.ppermute(half, axis, pairs)]
    select_n x1, other arithmetic: 3.63 us -> 1.45 us  [local(): jnp.where(retained[:, None, :], love_gain[None, None, :] * degree_whole,...]
where the time goes in v19:
time: 138 us; the launch traced here: 137 us
  waiting for transfers between devices  29.3 us (21%)
  starting transfers between devices  27.4 us (20%)
  blocking collectives  22.8 us (17%)
  other arithmetic  22.1 us (16%)
  matrix products  17.8 us (13%)
  local copies, waits for them, and re-layouts  16.2 us (12%)
    all_to_all x1, blocking collectives, paired_reduce_scatter(): lax.all_to_all(summed, axis, 0, 0, tiled=True, axis_index_groups=groups)  17.4 us
    dot_general x1, matrix products, local(): jnp.einsum('krl,kcr->kcl', legendre, fourier, precision=lax.Precision.HIGH)  15.8 us
    all_to_all x1, waiting for transfers between devices, paired_all_gather(): lax.all_to_all(copies, axis, 0, 0, tiled=True, axis_index_groups=groups)  11.7 us
    reduce_sum x1, other arithmetic, local(): synthesis = (legendre[:, None, :, :] * spectrum[:, :, None, :]).sum(axis=3)  11.4 us
    ppermute x2, starting transfers between devices, halo(): lax.ppermute(head, axis, [((i + 1) % count, i) for i in range(ends)])  8.12 us
    all_to_all x1, waiting for transfers between devices, reduce_scatter(): moved = lax.all_to_all(x, axis, 0, 0, tiled=True)  7.05 us
    all_to_all x1, waiting for transfers between devices, all_gather(): return lax.all_to_all(copies, axis, 0, 0, tiled=True)  6.98 us
    all_to_all x1, blocking collectives, paired_all_gather(): lax.all_to_all(both, axis, 0, 0, tiled=True, axis_index_groups=couples)  5.42 us
  transfers between devices with their start and end apart: 8, of which 5 were waited for; matrix products, arithmetic and copies ran while one was open for 2% of the time, Pallas kernels for 0%

profile of v19, /device:TPU:12, one launch (start us, length us, event | category | flops | bytes accessed | tf_op | source)
XLA Modules:
  0.0 136.6 jit_solution(2304341820145015143)
XLA Ops:
  6.3 1.2 subtract_reduce_fusion.1
  8.0 2.8 %gather_fusion = f32[1024,64]{1,0:T(8,128)S(1)} fusion(f32[1024,64]{1,0:T(8,128)S(1)} %copy.43, s32[1024]{0:T(1024)S(1)} %broadcast_clamp_fusion.1), kind=kCustom, calls=%fused_computation | custom fusion | bytes 528384 | tf_op jit(solution)/shard_map/jit(_take)/gather | solution.py:54
  11.8 5.3 %all-to-all-start = ((f32[4,256,64]{1,2,0:T(8,128)}), f32[4,256,64]{1,2,0:T(8,128)S(1)}, u32[]{:S(2)}, u32[]{:S(2)}) async-start(f32[4,256,64]{1,2,0:T(8,128)} %copy.44), calls=%async_computation | async-start | bytes 524288 | tf_op jit(solution)/shard_map/all_to_all | solution.py:73
  17.1 7.0 %all-to-all-done = f32[4,256,64]{1,2,0:T(8,128)S(1)} async-done(((f32[4,256,64]{1,2,0:T(8,128)}), f32[4,256,64]{1,2,0:T(8,128)S(1)}, u32[]{:S(2)}, u32[]{:S(2)}) %all-to-all-start) | async-done | bytes 262176 | tf_op jit(solution)/shard_map/all_to_all | solution.py:73
  24.3 15.8 %fusion.33 = f32[256,2,1024]{2,1,0:T(2,128)S(1)} fusion(f32[256,2,32]{2,1,0:T(2,128)S(1)} %copy.47, f32[256,32,1024]{2,1,0:T(8,128)} %param.7), kind=kOutput, calls=%fused_computation.68 | convolution fusion | flops 100663296 | bytes 35717120 | tf_op jit(solution)/shard_map/krl,kcr->kcl/dot_general | solution.py:121
  40.1 1.1 constant_dynamic-slice_fusion
  41.2 3.0 %collective-permute-done = f32[128,2,1024]{2,1,0:T(2,128)} collective-permute-done((f32[128,2,1024]{2,1,0:T(2,128)}, f32[128,2,1024]{2,1,0:T(2,128)}, u32[]{:S(2)}, u32[]{:S(2)}) %collective-permute-start) | collective-permute-done | bytes 1048608 | tf_op jit(solution)/shard_map/ppermute | solution.py:91
  44.2 1.8 %dynamic-slice_add_fusion = f32[128,2,1024]{2,1,0:T(2,128)S(1)} fusion(f32[128,2,1024]{2,1,0:T(2,128)} %collective-permute-done, f32[256,2,1024]{2,1,0:T(2,128)S(1)} %fusion.33, s32[]{:T(128)S(6)} %select_n.65), kind=kLoop, calls=%fused_computation.19 | loop fusion | flops 262144 | bytes 3145732 | tf_op jit(solution)/shard_map/add | solution.py:91
  45.9 17.4 %all_to_all.30 = f32[128,2,1024]{2,1,0:T(2,128)S(1)} all-to-all(f32[128,2,1024]{2,1,0:T(2,128)S(1)} %dynamic-slice_add_fusion), channel_id=1, replica_groups={{0,8,16,24},{4,12,20,28},{1,9,17,25},{5,13,21,29},{2,10,18,26},{6,14,22..., dimensions={0} | all-to-all | bytes 2097152 | tf_op jit(solution)/shard_map/all_to_all | solution.py:92
  63.9 1.3 broadcast_in_dim.40
  65.2 4.6 %all-to-all-start.2 = ((f32[128,2,1024]{2,1,0:T(2,128)}), f32[128,2,1024]{2,1,0:T(2,128)S(1)}, u32[]{:S(2)}, u32[]{:S(2)}) async-start(f32[128,2,1024]{2,1,0:T(2,128)} %bitcast.10), calls=%async_computation.2 | async-start | bytes 2097152 | tf_op jit(solution)/shard_map/all_to_all | solution.py:100
  70.1 11.7 %all-to-all-done.2 = f32[128,2,1024]{2,1,0:T(2,128)S(1)} async-done(((f32[128,2,1024]{2,1,0:T(2,128)}), f32[128,2,1024]{2,1,0:T(2,128)S(1)}, u32[]{:S(2)}, u32[]{:S(2)}) %all-to-all-start.2) | async-done | bytes 1048608 | tf_op jit(solution)/shard_map/all_to_all | solution.py:100
  82.3 5.4 %all_to_all.31 = f32[256,2,1024]{2,1,0:T(2,128)S(1)} all-to-all(f32[256,2,1024]{2,1,0:T(2,128)S(1)} %bitcast.55), channel_id=1, replica_groups={{0,4},{8,12},{16,20},{24,28},{1,5},{9,13},{17,21},{25,29},{2,6},{10,14}..., dimensions={0} | all-to-all | bytes 4194304 | tf_op jit(solution)/shard_map/all_to_all | solution.py:103
  87.7 1.4 %multiply_select_fusion = f32[256,2,1024]{2,1,0:T(2,128)S(1)} fusion(f32[256,2,1024]{2,1,0:T(2,128)S(1)} %all_to_all.31, pred[256,1024]{1,0:T(8,128)(4,1)S(1)} %iota_compare_fusion.1, f32[1024]{0:T(1024)S(1)} %copy-done.1), kind=kLoop, calls=%fused_computation.13 | loop fusion | flops 1048576 | bytes 4460544 | tf_op jit(solution)/shard_map/jit(_where)/select_n | solution.py:126
  89.2 11.4 %multiply_reduce_fusion = f32[256,2,32]{2,1,0:T(2,128)S(1)} fusion(f32[256,2,1024]{2,1,0:T(2,128)S(1)} %multiply_select_fusion, f32[256,32,1024]{2,1,0:T(8,128)} %param.7), kind=kLoop, calls=%fused_computation.2 | loop fusion | flops 33538048 | bytes 35717120 | tf_op jit(solution)/shard_map/reduce_sum | solution.py:127
  101.4 5.2 %all-to-all-start.4 = ((f32[4,256,64]{1,2,0:T(8,128)}), f32[4,256,64]{1,2,0:T(8,128)S(1)}, u32[]{:S(2)}, u32[]{:S(2)}) async-start(f32[4,256,64]{1,2,0:T(8,128)} %broadcast_in_dim.44), calls=%async_computation.4 | async-start | bytes 524288 | tf_op jit(solution)/shard_map/all_to_all | solution.py:80
  107.1 7.0 %all-to-all-done.4 = f32[4,256,64]{1,2,0:T(8,128)S(1)} async-done(((f32[4,256,64]{1,2,0:T(8,128)}), f32[4,256,64]{1,2,0:T(8,128)S(1)}, u32[]{:S(2)}, u32[]{:S(2)}) %all-to-all-start.4) | async-done | bytes 262176 | tf_op jit(solution)/shard_map/all_to_all | solution.py:80
  114.3 2.8 %gather_fusion.1 = f32[1024,64]{1,0:T(8,128)S(1)} fusion(f32[1024,64]{1,0:T(8,128)S(1)} %bitcast.54, s32[1024]{0:T(1024)S(1)} %broadcast_clamp_fusion), kind=kCustom, calls=%fused_computation.1 | custom fusion | bytes 528384 | tf_op jit(solution)/shard_map/jit(_take)/gather | solution.py:63
  117.6 1.4 %add_reduce_fusion = (f32[256,32,32]{0,2,1:T(8,128)S(1)}, f32[256,32,32]{0,2,1:T(8,128)S(1)}) fusion(f32[4,256,32]{1,2,0:T(8,128)S(1)} %copy.52, f32[4,256,32]{1,2,0:T(8,128)S(1)} %copy.51, f32[4,256,32]{1,2,0:T(8,128)S(1)} %get-tuple-element.21, f32[4,256,32]{1,2,0:T(8,128)S(1)} %get-tuple-element.20), kind=kLoop, calls=%fused_computation.4 | loop fusion | flops 7864320 | bytes 2621440 | tf_op jit(solution)/shard_map/reduce_sum | solution.py:65
  121.1 1.9 %collective-permute-start.1 = (f32[1,2048]{1,0:T(1,128)S(1)}, f32[1,2048]{1,0:T(1,128)S(1)}, u32[]{:S(2)}, u32[]{:S(2)}) collective-permute-start(f32[1,2048]{1,0:T(1,128)S(1)} %get-tuple-element.17), channel_id=1, source_target_pairs={{0,4},{4,8},{8,12},{12,16},{16,20},{20,24},{24,28},{1,5},{5,9},{9,... | collective-permute-start | bytes 24584 | tf_op jit(solution)/shard_map/ppermute | solution.py:16
  123.0 4.5 %collective-permute-start.2 = (f32[1,2048]{1,0:T(1,128)S(1)}, f32[1,2048]{1,0:T(1,128)S(1)}, u32[]{:S(2)}, u32[]{:S(2)}) collective-permute-start(f32[1,2048]{1,0:T(1,128)S(1)} %get-tuple-element.16), channel_id=1, source_target_pairs={{4,0},{8,4},{12,8},{16,12},{20,16},{24,20},{28,24},{5,1},{9,5},{13... | collective-permute-start | bytes 24584 | tf_op jit(solution)/shard_map/ppermute | solution.py:17
  127.6 2.3 %collective-permute-start.3 = (f32[32,1]{1,0:T(8,128)S(1)}, f32[32,1]{1,0:T(8,128)S(1)}, u32[]{:S(2)}, u32[]{:S(2)}) collective-permute-start(f32[32,1]{1,0:T(8,128)S(1)} %get-tuple-element.13), channel_id=1, source_target_pairs={{0,1},{1,2},{2,3},{4,5},{5,6},{6,7},{8,9},{9,10},{10,11},{12,13},{... | collective-permute-start | bytes 392 | tf_op jit(solution)/shard_map/ppermute | solution.py:16
  129.9 3.6 %collective-permute-start.4 = (f32[32,1]{1,0:T(8,128)S(1)}, f32[32,1]{1,0:T(8,128)S(1)}, u32[]{:S(2)}, u32[]{:S(2)}) collective-permute-start(f32[32,1]{1,0:T(8,128)S(1)} %get-tuple-element.12), channel_id=1, source_target_pairs={{1,0},{2,1},{3,2},{5,4},{6,5},{7,6},{9,8},{10,9},{11,10},{13,12},{... | collective-permute-start | bytes 392 | tf_op jit(solution)/shard_map/ppermute | solution.py:17
  133.9 1.2 mul.331
  (55 shorter events, 14.6 us)
Async XLA Ops:
  5.1 2.9 %copy-start = (s32[1024]{0:T(1024)S(1)}, s32[1024]{0:T(1024)}, u32[]{:S(2)}) copy-start(s32[1024]{0:T(1024)} %param.8) | copy-start | bytes 12292
  11.8 12.4 %all-to-all-start = ((f32[4,256,64]{1,2,0:T(8,128)}), f32[4,256,64]{1,2,0:T(8,128)S(1)}, u32[]{:S(2)}, u32[]{:S(2)}) async-start(f32[4,256,64]{1,2,0:T(8,128)} %copy.44), calls=%async_computation | async-start | bytes 524288 | tf_op jit(solution)/shard_map/all_to_all | solution.py:73
  41.2 3.0 %collective-permute-start = (f32[128,2,1024]{2,1,0:T(2,128)}, f32[128,2,1024]{2,1,0:T(2,128)}, u32[]{:S(2)}, u32[]{:S(2)}) collective-permute-start(f32[128,2,1024]{2,1,0:T(2,128)} %constant_dynamic-slice_fusion), channel_id=1, source_target_pairs={{0,4},{4,0},{8,12},{12,8},{16,20},{20,16},{24,28},{28,24},{1,5},{5... | collective-permute-start | bytes 3145736 | tf_op jit(solution)/shard_map/ppermute | solution.py:91
  65.2 16.6 %all-to-all-start.2 = ((f32[128,2,1024]{2,1,0:T(2,128)}), f32[128,2,1024]{2,1,0:T(2,128)S(1)}, u32[]{:S(2)}, u32[]{:S(2)}) async-start(f32[128,2,1024]{2,1,0:T(2,128)} %bitcast.10), calls=%async_computation.2 | async-start | bytes 2097152 | tf_op jit(solution)/shard_map/all_to_all | solution.py:100
  69.8 17.9 %copy-start.1 = (f32[1024]{0:T(1024)S(1)}, f32[1024]{0:T(1024)}, u32[]{:S(2)}) copy-start(f32[1024]{0:T(1024)} %param.9) | copy-start | bytes 12292
  101.4 12.7 %all-to-all-start.4 = ((f32[4,256,64]{1,2,0:T(8,128)}), f32[4,256,64]{1,2,0:T(8,128)S(1)}, u32[]{:S(2)}, u32[]{:S(2)}) async-start(f32[4,256,64]{1,2,0:T(8,128)} %broadcast_in_dim.44), calls=%async_computation.4 | async-start | bytes 524288 | tf_op jit(solution)/shard_map/all_to_all | solution.py:80
  121.1 14.6 %collective-permute-start.1 = (f32[1,2048]{1,0:T(1,128)S(1)}, f32[1,2048]{1,0:T(1,128)S(1)}, u32[]{:S(2)}, u32[]{:S(2)}) collective-permute-start(f32[1,2048]{1,0:T(1,128)S(1)} %get-tuple-element.17), channel_id=1, source_target_pairs={{0,4},{4,8},{8,12},{12,16},{16,20},{20,24},{24,28},{1,5},{5,9},{9,... | collective-permute-start | bytes 24584 | tf_op jit(solution)/shard_map/ppermute | solution.py:16
  123.0 12.7 %collective-permute-start.2 = (f32[1,2048]{1,0:T(1,128)S(1)}, f32[1,2048]{1,0:T(1,128)S(1)}, u32[]{:S(2)}, u32[]{:S(2)}) collective-permute-start(f32[1,2048]{1,0:T(1,128)S(1)} %get-tuple-element.16), channel_id=1, source_target_pairs={{4,0},{8,4},{12,8},{16,12},{20,16},{24,20},{28,24},{5,1},{9,5},{13... | collective-permute-start | bytes 24584 | tf_op jit(solution)/shard_map/ppermute | solution.py:17
  127.6 7.4 %collective-permute-start.3 = (f32[32,1]{1,0:T(8,128)S(1)}, f32[32,1]{1,0:T(8,128)S(1)}, u32[]{:S(2)}, u32[]{:S(2)}) collective-permute-start(f32[32,1]{1,0:T(8,128)S(1)} %get-tuple-element.13), channel_id=1, source_target_pairs={{0,1},{1,2},{2,3},{4,5},{5,6},{6,7},{8,9},{9,10},{10,11},{12,13},{... | collective-permute-start | bytes 392 | tf_op jit(solution)/shard_map/ppermute | solution.py:16
  129.9 5.8 %collective-permute-start.4 = (f32[32,1]{1,0:T(8,128)S(1)}, f32[32,1]{1,0:T(8,128)S(1)}, u32[]{:S(2)}, u32[]{:S(2)}) collective-permute-start(f32[32,1]{1,0:T(8,128)S(1)} %get-tuple-element.12), channel_id=1, source_target_pairs={{1,0},{2,1},{3,2},{5,4},{6,5},{7,6},{9,8},{10,9},{11,10},{13,12},{... | collective-permute-start | bytes 392 | tf_op jit(solution)/shard_map/ppermute | solution.py:17

commit v20 on v18

--- a/solution.py
+++ b/solution.py
@@ -41,10 +41,11 @@
     return jnp.stack([jnp.cos(alpha), jnp.sin(alpha)]), jnp.cos(beta), jnp.sin(beta)
 
 
-def forward_dft(masked, slot_order, lon_start, lon_total):
+def forward_dft(masked, slot_order, lon_start, lon_total, scale):
     cycles, lon_width = masked.shape
     order_count = slot_order.shape[0]
     rotor, cb, sb = dft_tables(order_count, lon_start, lon_width, lon_total)
+    rotor = rotor * scale
     blocks = masked.reshape(cycles, lon_width // INNER, INNER)
     partial = jnp.einsum("cua,rab->cubr", rotor, blocks, precision=lax.Precision.HIGH)
     gc, gs = partial[0][None], partial[1][None]
@@ -54,10 +55,11 @@
     return jnp.take(by_order, slot_order, axis=0, mode="clip", unique_indices=True)
 
 
-def inverse_dft(synthesis, slot_order, lon_start, lon_width, lon_total):
+def inverse_dft(synthesis, slot_order, lon_start, lon_width, lon_total, scale):
     order_count, width = synthesis.shape
     cycles = width // 2
     rotor, cb, sb = dft_tables(order_count, lon_start, lon_width, lon_total)
+    rotor = rotor * scale
     slots = jnp.arange(order_count, dtype=jnp.int32)
     slot_of = jnp.where(slot_order[None, :] == slots[:, None], slots[None, :], 0).sum(axis=1)
     by_order = jnp.take(synthesis, slot_of, axis=0, mode="clip", unique_indices=True).reshape(cb.shape[0], cb.shape[1], 2, cycles)
@@ -117,7 +119,7 @@
         slot_order, lax.axis_index("lon") * slot_count, slot_count
     )
     forward_scale = lon_total ** (-0.5)
-    fourier = reduce_scatter(forward_dft(masked, slot_order, lon_start, lon_total) * forward_scale, "lon")
+    fourier = reduce_scatter(forward_dft(masked, slot_order, lon_start, lon_total, forward_scale), "lon")
     fourier = fourier.reshape(slot_count, 2, cycle_count)
     coefficient = jnp.einsum("krl,kcr->kcl", legendre, fourier, precision=lax.Precision.HIGH)
     degree_whole = paired_all_gather(paired_reduce_scatter(coefficient, "lat"), "lat")
@@ -126,8 +128,8 @@
     retained = degrees[None, :] >= own_orders[:, None]
     spectrum = jnp.where(retained[:, None, :], love_gain[None, None, :] * degree_whole, 0.0)
     synthesis = (legendre[:, None, :, :] * spectrum[:, :, None, :]).sum(axis=3)
-    summed = inverse_dft(all_gather(synthesis.reshape(slot_count, -1), "lon"), slot_order, lon_start, lon_width, lon_total)
-    loading = summed * (2 * slot_total) ** (-0.5)
+    summed = inverse_dft(all_gather(synthesis.reshape(slot_count, -1), "lon"), slot_order, lon_start, lon_width, lon_total, (2 * slot_total) ** (-0.5))
+    loading = summed
     potential = masked - 0.6 * loading
     neighbours = neighbour_sum(potential)
     surface_next = wet_cells * (masked + 0.2 * (neighbours - 4.0 * potential))

time: 135 us -> 135 us (level)
  local copies, waits for them, and re-layouts: 14.4 us -> 12.8 us
    mul x5 -> x0, local copies, waits for them, and re-layouts: 3.37 us -> none  [the longest x2 1.59 us: local(): loading = summed * (2 * slot_total) ** (-0.5)]
  transfers between devices with their start and end apart: 8 -> 8, of which waited for: 5 -> 5; matrix products, arithmetic and copies ran while one was open for 2% -> 1% of each run, Pallas kernels for 0% -> 0%
where the time goes in v20:
time: 135 us; the launch traced here: 132 us
  blocking collectives  32.8 us (24%)
  other arithmetic  24.4 us (18%)
  starting transfers between devices  23.1 us (17%)
  waiting for transfers between devices  20.5 us (15%)
  matrix products  17.8 us (13%)
  local copies, waits for them, and re-layouts  12.8 us (9%)
    all_to_all x1, blocking collectives, paired_reduce_scatter(): lax.all_to_all(summed, axis, 0, 0, tiled=True, axis_index_groups=groups)  17.4 us
    dot_general x1, matrix products, local(): jnp.einsum('krl,kcr->kcl', legendre, fourier, precision=lax.Precision.HIGH)  15.8 us
    all_to_all x1, blocking collectives, paired_all_gather(): lax.all_to_all(copies, axis, 0, 0, tiled=True, axis_index_groups=groups)  15.4 us
    reduce_sum x1, other arithmetic, local(): synthesis = (legendre[:, None, :, :] * spectrum[:, :, None, :]).sum(axis=3)  11.4 us
    ppermute x2, starting transfers between devices, halo(): lax.ppermute(head, axis, [((i + 1) % count, i) for i in range(ends)])  8.12 us
    all_to_all x1, waiting for transfers between devices, reduce_scatter(): moved = lax.all_to_all(x, axis, 0, 0, tiled=True)  7.05 us
    all_to_all x1, waiting for transfers between devices, all_gather(): return lax.all_to_all(copies, axis, 0, 0, tiled=True)  6.98 us
    all_to_all x1, starting transfers between devices, all_gather(): return lax.all_to_all(copies, axis, 0, 0, tiled=True)  5.37 us
  transfers between devices with their start and end apart: 8, of which 5 were waited for; matrix products, arithmetic and copies ran while one was open for 1% of the time, Pallas kernels for 0%

profile of v20, /device:TPU:12, one launch (start us, length us, event | category | flops | bytes accessed | tf_op | source)
XLA Modules:
  0.0 132.4 jit_solution(1195900999278426198)
XLA Ops:
  2.6 1.1 bitcast_multiply_fusion.1
  4.0 1.0 convolution_bitcast_fusion
  7.1 1.2 subtract_reduce_fusion.1
  8.8 2.8 %gather_fusion = f32[1024,64]{1,0:T(8,128)S(1)} fusion(f32[1024,64]{1,0:T(8,128)S(1)} %copy.41, s32[1024]{0:T(1024)S(1)} %broadcast_clamp_fusion.1), kind=kCustom, calls=%fused_computation | custom fusion | bytes 528384 | tf_op jit(solution)/shard_map/jit(_take)/gather | solution.py:55
  12.5 5.3 %all-to-all-start = ((f32[4,256,64]{1,2,0:T(8,128)}), f32[4,256,64]{1,2,0:T(8,128)S(1)}, u32[]{:S(2)}, u32[]{:S(2)}) async-start(f32[4,256,64]{1,2,0:T(8,128)} %copy.42), calls=%async_computation | async-start | bytes 524288 | tf_op jit(solution)/shard_map/all_to_all | solution.py:75
  17.8 7.0 %all-to-all-done = f32[4,256,64]{1,2,0:T(8,128)S(1)} async-done(((f32[4,256,64]{1,2,0:T(8,128)}), f32[4,256,64]{1,2,0:T(8,128)S(1)}, u32[]{:S(2)}, u32[]{:S(2)}) %all-to-all-start) | async-done | bytes 262176 | tf_op jit(solution)/shard_map/all_to_all | solution.py:75
  25.1 15.8 %fusion.41 = f32[256,2,1024]{2,1,0:T(2,128)S(1)} fusion(f32[256,2,32]{2,1,0:T(2,128)S(1)} %copy.45, f32[256,32,1024]{2,1,0:T(8,128)} %param.7), kind=kOutput, calls=%fused_computation.76 | convolution fusion | flops 100663296 | bytes 35717120 | tf_op jit(solution)/shard_map/krl,kcr->kcl/dot_general | solution.py:124
  41.0 2.8 %collective-permute-done = f32[128,2,1024]{2,1,0:T(2,128)} collective-permute-done((f32[128,2,1024]{2,1,0:T(2,128)S(1)}, f32[128,2,1024]{2,1,0:T(2,128)}, u32[]{:S(2)}, u32[]{:S(2)}) %collective-permute-start) | collective-permute-done | bytes 1048608 | tf_op jit(solution)/shard_map/ppermute | solution.py:93
  43.8 1.8 %dynamic-slice_add_fusion = f32[128,2,1024]{2,1,0:T(2,128)S(1)} fusion(f32[128,2,1024]{2,1,0:T(2,128)} %collective-permute-done, f32[256,2,1024]{2,1,0:T(2,128)S(1)} %fusion.41, s32[]{:T(128)S(6)} %select_n.84), kind=kLoop, calls=%fused_computation.21 | loop fusion | flops 262144 | bytes 3145732 | tf_op jit(solution)/shard_map/add | solution.py:93
  45.6 17.4 %all_to_all.28 = f32[128,2,1024]{2,1,0:T(2,128)S(1)} all-to-all(f32[128,2,1024]{2,1,0:T(2,128)S(1)} %dynamic-slice_add_fusion), channel_id=1, replica_groups={{0,8,16,24},{4,12,20,28},{1,9,17,25},{5,13,21,29},{2,10,18,26},{6,14,22..., dimensions={0} | all-to-all | bytes 2097152 | tf_op jit(solution)/shard_map/all_to_all | solution.py:94
  63.8 15.4 %all_to_all.29 = f32[128,2,1024]{2,1,0:T(2,128)S(1)} all-to-all(f32[128,2,1024]{2,1,0:T(2,128)S(1)} %bitcast.50), channel_id=1, replica_groups={{0,8,16,24},{4,12,20,28},{1,9,17,25},{5,13,21,29},{2,10,18,26},{6,14,22..., dimensions={0} | all-to-all | bytes 2097152 | tf_op jit(solution)/shard_map/all_to_all | solution.py:104
  79.6 2.5 %collective-permute-done.1 = f32[128,2,1024]{2,1,0:T(2,128)} collective-permute-done((f32[128,2,1024]{2,1,0:T(2,128)S(1)}, f32[128,2,1024]{2,1,0:T(2,128)}, u32[]{:S(2)}, u32[]{:S(2)}) %collective-permute-start.1) | collective-permute-done | bytes 1048608 | tf_op jit(solution)/shard_map/ppermute | solution.py:105
  82.1 3.6 %fusion.1 = f32[256,2,1024]{2,1,0:T(2,128)S(1)} fusion(f32[128,2,1024]{2,1,0:T(2,128)} %collective-permute-done.1, f32[128,2,1024]{2,1,0:T(2,128)S(1)} %all_to_all.29, pred[]{:T(512)S(6)} %eq.25, pred[256,1024]{1,0:T(8,128)(4,1)S(1)} %iota_compare_fusion.1, f32[1024]{0:T(1024)S(1)} %copy-done.10), kind=kLoop, calls=%fused_computation.11 | loop fusion | flops 2621440 | bytes 4460545 | tf_op jit(solution)/shard_map/jit(_where)/select_n | solution.py:129
  85.7 11.4 %multiply_reduce_fusion = f32[256,2,32]{2,1,0:T(2,128)S(1)} fusion(f32[256,2,1024]{2,1,0:T(2,128)S(1)} %fusion.1, f32[256,32,1024]{2,1,0:T(8,128)} %param.7), kind=kLoop, calls=%fused_computation.2 | loop fusion | flops 33538048 | bytes 35717120 | tf_op jit(solution)/shard_map/reduce_sum | solution.py:130
  97.9 5.4 %all-to-all-start.3 = ((f32[4,256,64]{1,2,0:T(8,128)}), f32[4,256,64]{1,2,0:T(8,128)S(1)}, u32[]{:S(2)}, u32[]{:S(2)}) async-start(f32[4,256,64]{1,2,0:T(8,128)} %broadcast_in_dim.41), calls=%async_computation.3 | async-start | bytes 524288 | tf_op jit(solution)/shard_map/all_to_all | solution.py:82
  103.8 7.0 %all-to-all-done.3 = f32[4,256,64]{1,2,0:T(8,128)S(1)} async-done(((f32[4,256,64]{1,2,0:T(8,128)}), f32[4,256,64]{1,2,0:T(8,128)S(1)}, u32[]{:S(2)}, u32[]{:S(2)}) %all-to-all-start.3) | async-done | bytes 262176 | tf_op jit(solution)/shard_map/all_to_all | solution.py:82
  111.0 2.8 %gather_fusion.1 = f32[1024,64]{1,0:T(8,128)S(1)} fusion(f32[1024,64]{1,0:T(8,128)S(1)} %bitcast.49, s32[1024]{0:T(1024)S(1)} %broadcast_clamp_fusion), kind=kCustom, calls=%fused_computation.1 | custom fusion | bytes 528384 | tf_op jit(solution)/shard_map/jit(_take)/gather | solution.py:65
  114.3 1.4 %add_reduce_fusion = (f32[256,32,32]{0,2,1:T(8,128)S(1)}, f32[256,32,32]{0,2,1:T(8,128)S(1)}) fusion(f32[4,256,32]{1,2,0:T(8,128)S(1)} %copy.50, f32[4,256,32]{1,2,0:T(8,128)S(1)} %copy.49, f32[4,256,32]{1,2,0:T(8,128)S(1)} %copy-done.4, f32[4,256,32]{1,2,0:T(8,128)S(1)} %get-tuple-element.18), kind=kLoop, calls=%fused_computation.4 | loop fusion | flops 7864320 | bytes 2621440 | tf_op jit(solution)/shard_map/reduce_sum | solution.py:67
  115.7 1.0 fusion.6
  117.8 2.3 %collective-permute-start.4 = (f32[32,1]{1,0:T(8,128)S(1)}, f32[32,1]{1,0:T(8,128)S(1)}, u32[]{:S(2)}, u32[]{:S(2)}) collective-permute-start(f32[32,1]{1,0:T(8,128)S(1)} %get-tuple-element.11), channel_id=1, source_target_pairs={{0,1},{1,2},{2,3},{4,5},{5,6},{6,7},{8,9},{9,10},{10,11},{12,13},{... | collective-permute-start | bytes 392 | tf_op jit(solution)/shard_map/ppermute | solution.py:16
  120.0 3.6 %collective-permute-start.5 = (f32[32,1]{1,0:T(8,128)S(1)}, f32[32,1]{1,0:T(8,128)S(1)}, u32[]{:S(2)}, u32[]{:S(2)}) collective-permute-start(f32[32,1]{1,0:T(8,128)S(1)} %get-tuple-element.10), channel_id=1, source_target_pairs={{1,0},{2,1},{3,2},{5,4},{6,5},{7,6},{9,8},{10,9},{11,10},{13,12},{... | collective-permute-start | bytes 392 | tf_op jit(solution)/shard_map/ppermute | solution.py:17
  123.6 1.9 %collective-permute-start.2 = (f32[1,2048]{1,0:T(1,128)S(1)}, f32[1,2048]{1,0:T(1,128)S(1)}, u32[]{:S(2)}, u32[]{:S(2)}) collective-permute-start(f32[1,2048]{1,0:T(1,128)S(1)} %get-tuple-element.15), channel_id=1, source_target_pairs={{0,4},{4,8},{8,12},{12,16},{16,20},{20,24},{24,28},{1,5},{5,9},{9,... | collective-permute-start | bytes 24584 | tf_op jit(solution)/shard_map/ppermute | solution.py:16
  125.5 4.5 %collective-permute-start.3 = (f32[1,2048]{1,0:T(1,128)S(1)}, f32[1,2048]{1,0:T(1,128)S(1)}, u32[]{:S(2)}, u32[]{:S(2)}) collective-permute-start(f32[1,2048]{1,0:T(1,128)S(1)} %get-tuple-element.14), channel_id=1, source_target_pairs={{4,0},{8,4},{12,8},{16,12},{20,16},{24,20},{28,24},{5,1},{9,5},{13... | collective-permute-start | bytes 24584 | tf_op jit(solution)/shard_map/ppermute | solution.py:17
  130.3 1.2 collective-permute-done.3
  (69 shorter events, 11.2 us)
Async XLA Ops:
  0.9 3.1 %copy-start.5 = (f32[1,256,64]{1,2,0:T(8,128)}, f32[1,256,64]{1,2,0:T(8,128)S(1)}, u32[]{:S(2)}) copy-start(f32[1,256,64]{1,2,0:T(8,128)S(1)} %get-tuple-element.20) | copy-start | bytes 196612
  0.9 3.1 %copy-start.7 = (f32[1,256,64]{1,2,0:T(8,128)}, f32[1,256,64]{1,2,0:T(8,128)S(1)}, u32[]{:S(2)}) copy-start(f32[1,256,64]{1,2,0:T(8,128)S(1)} %get-tuple-element.21) | copy-start | bytes 196612
  1.9 0.7 copy-start.1
  5.9 2.9 %copy-start.9 = (s32[1024]{0:T(1024)S(1)}, s32[1024]{0:T(1024)}, u32[]{:S(2)}) copy-start(s32[1024]{0:T(1024)} %param.8) | copy-start | bytes 12292
  7.1 4.5 %copy-start.3 = (f32[4,256,32]{1,2,0:T(8,128)}, f32[4,256,32]{1,2,0:T(8,128)S(1)}, u32[]{:S(2)}) copy-start(f32[4,256,32]{1,2,0:T(8,128)S(1)} %get-tuple-element.19) | copy-start | bytes 393220
  12.5 12.4 %all-to-all-start = ((f32[4,256,64]{1,2,0:T(8,128)}), f32[4,256,64]{1,2,0:T(8,128)S(1)}, u32[]{:S(2)}, u32[]{:S(2)}) async-start(f32[4,256,64]{1,2,0:T(8,128)} %copy.42), calls=%async_computation | async-start | bytes 524288 | tf_op jit(solution)/shard_map/all_to_all | solution.py:75
  40.9 2.9 %collective-permute-start = (f32[128,2,1024]{2,1,0:T(2,128)S(1)}, f32[128,2,1024]{2,1,0:T(2,128)}, u32[]{:S(2)}, u32[]{:S(2)}) collective-permute-start(f32[128,2,1024]{2,1,0:T(2,128)S(1)} %constant_dynamic-slice_fusion), channel_id=1, source_target_pairs={{0,4},{4,0},{8,12},{12,8},{16,20},{20,16},{24,28},{28,24},{1,5},{5... | collective-permute-start | bytes 3145736 | tf_op jit(solution)/shard_map/ppermute | solution.py:93
  45.6 36.5 %copy-start.10 = (f32[1024]{0:T(1024)S(1)}, f32[1024]{0:T(1024)}, u32[]{:S(2)}) copy-start(f32[1024]{0:T(1024)} %param.9) | copy-start | bytes 12292
  79.3 2.8 %collective-permute-start.1 = (f32[128,2,1024]{2,1,0:T(2,128)S(1)}, f32[128,2,1024]{2,1,0:T(2,128)}, u32[]{:S(2)}, u32[]{:S(2)}) collective-permute-start(f32[128,2,1024]{2,1,0:T(2,128)S(1)} %all_to_all.29), channel_id=1, source_target_pairs={{0,4},{4,0},{8,12},{12,8},{16,20},{20,16},{24,28},{28,24},{1,5},{5... | collective-permute-start | bytes 3145736 | tf_op jit(solution)/shard_map/ppermute | solution.py:105
  97.9 16.3 %copy-start.4 = (f32[4,256,32]{1,2,0:T(8,128)S(1)}, f32[4,256,32]{1,2,0:T(8,128)}, u32[]{:S(2)}) copy-start(f32[4,256,32]{1,2,0:T(8,128)} %copy-done.3) | copy-start | bytes 393220
  97.9 12.9 %all-to-all-start.3 = ((f32[4,256,64]{1,2,0:T(8,128)}), f32[4,256,64]{1,2,0:T(8,128)S(1)}, u32[]{:S(2)}, u32[]{:S(2)}) async-start(f32[4,256,64]{1,2,0:T(8,128)} %broadcast_in_dim.41), calls=%async_computation.3 | async-start | bytes 524288 | tf_op jit(solution)/shard_map/all_to_all | solution.py:82
  111.0 4.7 %copy-start.6 = (f32[1,256,64]{1,2,0:T(8,128)S(1)}, f32[1,256,64]{1,2,0:T(8,128)}, u32[]{:S(2)}) copy-start(f32[1,256,64]{1,2,0:T(8,128)} %copy-done.5) | copy-start | bytes 196612
  111.0 4.7 %copy-start.8 = (f32[1,256,64]{1,2,0:T(8,128)S(1)}, f32[1,256,64]{1,2,0:T(8,128)}, u32[]{:S(2)}) copy-start(f32[1,256,64]{1,2,0:T(8,128)} %copy-done.7) | copy-start | bytes 196612
  115.7 15.7 %copy-start.2 = (f32[32,16,128]{2,1,0:T(8,128)S(1)}, f32[32,16,128]{2,1,0:T(8,128)}, u32[]{:S(2)}) copy-start(f32[32,16,128]{2,1,0:T(8,128)} %copy-done.1) | copy-start | bytes 786436
  117.6 14.8 %copy-start = (f32[32,2048]{1,0:T(8,128)}, f32[32,2048]{1,0:T(8,128)S(1)}, u32[]{:S(2)}) copy-start(f32[32,2048]{1,0:T(8,128)S(1)} %reshape.201) | copy-start | bytes 786436
  117.8 12.5 %collective-permute-start.4 = (f32[32,1]{1,0:T(8,128)S(1)}, f32[32,1]{1,0:T(8,128)S(1)}, u32[]{:S(2)}, u32[]{:S(2)}) collective-permute-start(f32[32,1]{1,0:T(8,128)S(1)} %get-tuple-element.11), channel_id=1, source_target_pairs={{0,1},{1,2},{2,3},{4,5},{5,6},{6,7},{8,9},{9,10},{10,11},{12,13},{... | collective-permute-start | bytes 392 | tf_op jit(solution)/shard_map/ppermute | solution.py:16
  120.0 10.2 %collective-permute-start.5 = (f32[32,1]{1,0:T(8,128)S(1)}, f32[32,1]{1,0:T(8,128)S(1)}, u32[]{:S(2)}, u32[]{:S(2)}) collective-permute-start(f32[32,1]{1,0:T(8,128)S(1)} %get-tuple-element.10), channel_id=1, source_target_pairs={{1,0},{2,1},{3,2},{5,4},{6,5},{7,6},{9,8},{10,9},{11,10},{13,12},{... | collective-permute-start | bytes 392 | tf_op jit(solution)/shard_map/ppermute | solution.py:17
  123.6 6.6 %collective-permute-start.2 = (f32[1,2048]{1,0:T(1,128)S(1)}, f32[1,2048]{1,0:T(1,128)S(1)}, u32[]{:S(2)}, u32[]{:S(2)}) collective-permute-start(f32[1,2048]{1,0:T(1,128)S(1)} %get-tuple-element.15), channel_id=1, source_target_pairs={{0,4},{4,8},{8,12},{12,16},{16,20},{20,24},{24,28},{1,5},{5,9},{9,... | collective-permute-start | bytes 24584 | tf_op jit(solution)/shard_map/ppermute | solution.py:16
  125.5 5.9 %collective-permute-start.3 = (f32[1,2048]{1,0:T(1,128)S(1)}, f32[1,2048]{1,0:T(1,128)S(1)}, u32[]{:S(2)}, u32[]{:S(2)}) collective-permute-start(f32[1,2048]{1,0:T(1,128)S(1)} %get-tuple-element.14), channel_id=1, source_target_pairs={{4,0},{8,4},{12,8},{16,12},{20,16},{24,20},{28,24},{5,1},{9,5},{13... | collective-permute-start | bytes 24584 | tf_op jit(solution)/shard_map/ppermute | solution.py:17

commit v21 on v20

--- a/solution.py
+++ b/solution.py
@@ -103,7 +103,9 @@
     copies = jnp.broadcast_to(x[None], (count // 2,) + x.shape).reshape((count // 2 * x.shape[0],) + x.shape[1:])
     half = lax.all_to_all(copies, axis, 0, 0, tiled=True, axis_index_groups=groups)
     other = lax.ppermute(half, axis, pairs)
-    return jnp.where(side == 0, jnp.concatenate([half, other]), jnp.concatenate([other, half]))
+    mine_first = (jnp.arange(2) == side)[:, None, None, None]
+    joined = jnp.where(mine_first, half[None], other[None])
+    return joined.reshape((2 * half.shape[0],) + half.shape[1:])
 
 
 def local(surface, wet_blocks, legendre, slot_order, love_gain):

time: 135 us -> 134 us (level)
  no operation moved by 1% of the time
where the time goes in v21:
time: 134 us; the launch traced here: 132 us
  blocking collectives  32.8 us (24%)
  other arithmetic  23.9 us (18%)
  starting transfers between devices  23.1 us (17%)
  waiting for transfers between devices  20.4 us (15%)
  matrix products  17.8 us (13%)
  local copies, waits for them, and re-layouts  12.9 us (10%)
    all_to_all x1, blocking collectives, paired_reduce_scatter(): lax.all_to_all(summed, axis, 0, 0, tiled=True, axis_index_groups=groups)  17.4 us
    dot_general x1, matrix products, local(): jnp.einsum('krl,kcr->kcl', legendre, fourier, precision=lax.Precision.HIGH)  15.8 us
    all_to_all x1, blocking collectives, paired_all_gather(): lax.all_to_all(copies, axis, 0, 0, tiled=True, axis_index_groups=groups)  15.4 us
    reduce_sum x1, other arithmetic, local(): synthesis = (legendre[:, None, :, :] * spectrum[:, :, None, :]).sum(axis=3)  11.4 us
    ppermute x2, starting transfers between devices, halo(): lax.ppermute(head, axis, [((i + 1) % count, i) for i in range(ends)])  8.12 us
    all_to_all x1, waiting for transfers between devices, reduce_scatter(): moved = lax.all_to_all(x, axis, 0, 0, tiled=True)  7.05 us
    all_to_all x1, waiting for transfers between devices, all_gather(): return lax.all_to_all(copies, axis, 0, 0, tiled=True)  6.98 us
    all_to_all x1, starting transfers between devices, all_gather(): return lax.all_to_all(copies, axis, 0, 0, tiled=True)  5.37 us
  transfers between devices with their start and end apart: 8, of which 5 were waited for; matrix products, arithmetic and copies ran while one was open for 1% of the time, Pallas kernels for 0%

profile of v21, /device:TPU:12, one launch (start us, length us, event | category | flops | bytes accessed | tf_op | source)
XLA Modules:
  0.0 132.0 jit_solution(15042101969723793939)
XLA Ops:
  2.6 1.1 bitcast_multiply_fusion.1
  4.0 1.0 convolution_bitcast_fusion
  7.1 1.2 subtract_reduce_fusion.1
  8.8 2.8 %gather_fusion = f32[1024,64]{1,0:T(8,128)S(1)} fusion(f32[1024,64]{1,0:T(8,128)S(1)} %copy.41, s32[1024]{0:T(1024)S(1)} %broadcast_clamp_fusion.1), kind=kCustom, calls=%fused_computation | custom fusion | bytes 528384 | tf_op jit(solution)/shard_map/jit(_take)/gather | solution.py:55
  12.5 5.3 %all-to-all-start = ((f32[4,256,64]{1,2,0:T(8,128)}), f32[4,256,64]{1,2,0:T(8,128)S(1)}, u32[]{:S(2)}, u32[]{:S(2)}) async-start(f32[4,256,64]{1,2,0:T(8,128)} %copy.42), calls=%async_computation | async-start | bytes 524288 | tf_op jit(solution)/shard_map/all_to_all | solution.py:75
  17.8 7.0 %all-to-all-done = f32[4,256,64]{1,2,0:T(8,128)S(1)} async-done(((f32[4,256,64]{1,2,0:T(8,128)}), f32[4,256,64]{1,2,0:T(8,128)S(1)}, u32[]{:S(2)}, u32[]{:S(2)}) %all-to-all-start) | async-done | bytes 262176 | tf_op jit(solution)/shard_map/all_to_all | solution.py:75
  25.1 15.8 %fusion.40 = f32[256,2,1024]{2,1,0:T(2,128)S(1)} fusion(f32[256,2,32]{2,1,0:T(2,128)S(1)} %copy.45, f32[256,32,1024]{2,1,0:T(8,128)} %param.7), kind=kOutput, calls=%fused_computation.78 | convolution fusion | flops 100663296 | bytes 35717120 | tf_op jit(solution)/shard_map/krl,kcr->kcl/dot_general | solution.py:126
  41.0 2.8 %collective-permute-done = f32[128,2,1024]{2,1,0:T(2,128)} collective-permute-done((f32[128,2,1024]{2,1,0:T(2,128)S(1)}, f32[128,2,1024]{2,1,0:T(2,128)}, u32[]{:S(2)}, u32[]{:S(2)}) %collective-permute-start) | collective-permute-done | bytes 1048608 | tf_op jit(solution)/shard_map/ppermute | solution.py:93
  43.8 1.8 %dynamic-slice_add_fusion = f32[128,2,1024]{2,1,0:T(2,128)S(1)} fusion(f32[128,2,1024]{2,1,0:T(2,128)} %collective-permute-done, f32[256,2,1024]{2,1,0:T(2,128)S(1)} %fusion.40, s32[]{:T(128)S(6)} %select_n.80), kind=kLoop, calls=%fused_computation.21 | loop fusion | flops 262144 | bytes 3145732 | tf_op jit(solution)/shard_map/add | solution.py:93
  45.6 17.4 %all_to_all.28 = f32[128,2,1024]{2,1,0:T(2,128)S(1)} all-to-all(f32[128,2,1024]{2,1,0:T(2,128)S(1)} %dynamic-slice_add_fusion), channel_id=1, replica_groups={{0,8,16,24},{4,12,20,28},{1,9,17,25},{5,13,21,29},{2,10,18,26},{6,14,22..., dimensions={0} | all-to-all | bytes 2097152 | tf_op jit(solution)/shard_map/all_to_all | solution.py:94
  63.8 15.4 %all_to_all.29 = f32[128,2,1024]{2,1,0:T(2,128)S(1)} all-to-all(f32[128,2,1024]{2,1,0:T(2,128)S(1)} %bitcast.62), channel_id=1, replica_groups={{0,8,16,24},{4,12,20,28},{1,9,17,25},{5,13,21,29},{2,10,18,26},{6,14,22..., dimensions={0} | all-to-all | bytes 2097152 | tf_op jit(solution)/shard_map/all_to_all | solution.py:104
  79.7 2.4 %collective-permute-done.1 = f32[128,2,1024]{2,1,0:T(2,128)} collective-permute-done((f32[128,2,1024]{2,1,0:T(2,128)S(1)}, f32[128,2,1024]{2,1,0:T(2,128)}, u32[]{:S(2)}, u32[]{:S(2)}) %collective-permute-start.1) | collective-permute-done | bytes 1048608 | tf_op jit(solution)/shard_map/ppermute | solution.py:105
  82.1 3.2 %broadcast_select_fusion = f32[256,2,1024]{2,1,0:T(2,128)S(1)} fusion(pred[256,1024]{1,0:T(8,128)(4,1)S(1)} %iota_compare_fusion.1, f32[128,2,1024]{2,1,0:T(2,128)} %collective-permute-done.1, pred[256]{0:T(512)(128)(4,1)S(1)} %broadcast_bitcast_fusion, f32[128,2,1024]{2,1,0:T(2,128)S(1)} %all_to_all.29, f32[1024]{0:T(1024)S(1)} %copy-done.10), kind=kLoop, calls=%fused_computation.15 | loop fusion | flops 1572864 | bytes 4460800 | tf_op jit(solution)/shard_map/jit(_where)/select_n | solution.py:131
  85.3 11.4 %multiply_reduce_fusion = f32[256,2,32]{2,1,0:T(2,128)S(1)} fusion(f32[256,2,1024]{2,1,0:T(2,128)S(1)} %broadcast_select_fusion, f32[256,32,1024]{2,1,0:T(8,128)} %param.7), kind=kLoop, calls=%fused_computation.2 | loop fusion | flops 33538048 | bytes 35717120 | tf_op jit(solution)/shard_map/reduce_sum | solution.py:132
  97.5 5.4 %all-to-all-start.3 = ((f32[4,256,64]{1,2,0:T(8,128)}), f32[4,256,64]{1,2,0:T(8,128)S(1)}, u32[]{:S(2)}, u32[]{:S(2)}) async-start(f32[4,256,64]{1,2,0:T(8,128)} %broadcast_in_dim.120), calls=%async_computation.3 | async-start | bytes 524288 | tf_op jit(solution)/shard_map/all_to_all | solution.py:82
  103.4 7.0 %all-to-all-done.3 = f32[4,256,64]{1,2,0:T(8,128)S(1)} async-done(((f32[4,256,64]{1,2,0:T(8,128)}), f32[4,256,64]{1,2,0:T(8,128)S(1)}, u32[]{:S(2)}, u32[]{:S(2)}) %all-to-all-start.3) | async-done | bytes 262176 | tf_op jit(solution)/shard_map/all_to_all | solution.py:82
  110.6 2.8 %gather_fusion.1 = f32[1024,64]{1,0:T(8,128)S(1)} fusion(f32[1024,64]{1,0:T(8,128)S(1)} %bitcast.61, s32[1024]{0:T(1024)S(1)} %broadcast_clamp_fusion), kind=kCustom, calls=%fused_computation.1 | custom fusion | bytes 528384 | tf_op jit(solution)/shard_map/jit(_take)/gather | solution.py:65
  113.9 1.4 %add_reduce_fusion = (f32[256,32,32]{0,2,1:T(8,128)S(1)}, f32[256,32,32]{0,2,1:T(8,128)S(1)}) fusion(f32[4,256,32]{1,2,0:T(8,128)S(1)} %copy.50, f32[4,256,32]{1,2,0:T(8,128)S(1)} %copy.49, f32[4,256,32]{1,2,0:T(8,128)S(1)} %copy-done.4, f32[4,256,32]{1,2,0:T(8,128)S(1)} %get-tuple-element.18), kind=kLoop, calls=%fused_computation.4 | loop fusion | flops 7864320 | bytes 2621440 | tf_op jit(solution)/shard_map/reduce_sum | solution.py:67
  115.3 1.0 fusion.5
  117.3 2.3 %collective-permute-start.4 = (f32[32,1]{1,0:T(8,128)S(1)}, f32[32,1]{1,0:T(8,128)S(1)}, u32[]{:S(2)}, u32[]{:S(2)}) collective-permute-start(f32[32,1]{1,0:T(8,128)S(1)} %get-tuple-element.11), channel_id=1, source_target_pairs={{0,1},{1,2},{2,3},{4,5},{5,6},{6,7},{8,9},{9,10},{10,11},{12,13},{... | collective-permute-start | bytes 392 | tf_op jit(solution)/shard_map/ppermute | solution.py:16
  119.6 3.6 %collective-permute-start.5 = (f32[32,1]{1,0:T(8,128)S(1)}, f32[32,1]{1,0:T(8,128)S(1)}, u32[]{:S(2)}, u32[]{:S(2)}) collective-permute-start(f32[32,1]{1,0:T(8,128)S(1)} %get-tuple-element.10), channel_id=1, source_target_pairs={{1,0},{2,1},{3,2},{5,4},{6,5},{7,6},{9,8},{10,9},{11,10},{13,12},{... | collective-permute-start | bytes 392 | tf_op jit(solution)/shard_map/ppermute | solution.py:17
  123.2 1.9 %collective-permute-start.2 = (f32[1,2048]{1,0:T(1,128)S(1)}, f32[1,2048]{1,0:T(1,128)S(1)}, u32[]{:S(2)}, u32[]{:S(2)}) collective-permute-start(f32[1,2048]{1,0:T(1,128)S(1)} %get-tuple-element.15), channel_id=1, source_target_pairs={{0,4},{4,8},{8,12},{12,16},{16,20},{20,24},{24,28},{1,5},{5,9},{9,... | collective-permute-start | bytes 24584 | tf_op jit(solution)/shard_map/ppermute | solution.py:16
  125.1 4.5 %collective-permute-start.3 = (f32[1,2048]{1,0:T(1,128)S(1)}, f32[1,2048]{1,0:T(1,128)S(1)}, u32[]{:S(2)}, u32[]{:S(2)}) collective-permute-start(f32[1,2048]{1,0:T(1,128)S(1)} %get-tuple-element.14), channel_id=1, source_target_pairs={{4,0},{8,4},{12,8},{16,12},{20,16},{24,20},{28,24},{5,1},{9,5},{13... | collective-permute-start | bytes 24584 | tf_op jit(solution)/shard_map/ppermute | solution.py:17
  129.8 1.2 collective-permute-done.3
  (71 shorter events, 11.3 us)
Async XLA Ops:
  0.9 3.1 %copy-start.5 = (f32[1,256,64]{1,2,0:T(8,128)}, f32[1,256,64]{1,2,0:T(8,128)S(1)}, u32[]{:S(2)}) copy-start(f32[1,256,64]{1,2,0:T(8,128)S(1)} %get-tuple-element.20) | copy-start | bytes 196612
  0.9 3.1 %copy-start.7 = (f32[1,256,64]{1,2,0:T(8,128)}, f32[1,256,64]{1,2,0:T(8,128)S(1)}, u32[]{:S(2)}) copy-start(f32[1,256,64]{1,2,0:T(8,128)S(1)} %get-tuple-element.21) | copy-start | bytes 196612
  1.9 0.7 copy-start.1
  5.9 2.9 %copy-start.9 = (s32[1024]{0:T(1024)S(1)}, s32[1024]{0:T(1024)}, u32[]{:S(2)}) copy-start(s32[1024]{0:T(1024)} %param.8) | copy-start | bytes 12292
  7.1 4.5 %copy-start.3 = (f32[4,256,32]{1,2,0:T(8,128)}, f32[4,256,32]{1,2,0:T(8,128)S(1)}, u32[]{:S(2)}) copy-start(f32[4,256,32]{1,2,0:T(8,128)S(1)} %get-tuple-element.19) | copy-start | bytes 393220
  12.5 12.4 %all-to-all-start = ((f32[4,256,64]{1,2,0:T(8,128)}), f32[4,256,64]{1,2,0:T(8,128)S(1)}, u32[]{:S(2)}, u32[]{:S(2)}) async-start(f32[4,256,64]{1,2,0:T(8,128)} %copy.42), calls=%async_computation | async-start | bytes 524288 | tf_op jit(solution)/shard_map/all_to_all | solution.py:75
  40.9 2.9 %collective-permute-start = (f32[128,2,1024]{2,1,0:T(2,128)S(1)}, f32[128,2,1024]{2,1,0:T(2,128)}, u32[]{:S(2)}, u32[]{:S(2)}) collective-permute-start(f32[128,2,1024]{2,1,0:T(2,128)S(1)} %constant_dynamic-slice_fusion), channel_id=1, source_target_pairs={{0,4},{4,0},{8,12},{12,8},{16,20},{20,16},{24,28},{28,24},{1,5},{5... | collective-permute-start | bytes 3145736 | tf_op jit(solution)/shard_map/ppermute | solution.py:93
  45.6 36.5 %copy-start.10 = (f32[1024]{0:T(1024)S(1)}, f32[1024]{0:T(1024)}, u32[]{:S(2)}) copy-start(f32[1024]{0:T(1024)} %param.9) | copy-start | bytes 12292
  79.3 2.8 %collective-permute-start.1 = (f32[128,2,1024]{2,1,0:T(2,128)S(1)}, f32[128,2,1024]{2,1,0:T(2,128)}, u32[]{:S(2)}, u32[]{:S(2)}) collective-permute-start(f32[128,2,1024]{2,1,0:T(2,128)S(1)} %all_to_all.29), channel_id=1, source_target_pairs={{0,4},{4,0},{8,12},{12,8},{16,20},{20,16},{24,28},{28,24},{1,5},{5... | collective-permute-start | bytes 3145736 | tf_op jit(solution)/shard_map/ppermute | solution.py:105
  97.5 16.3 %copy-start.4 = (f32[4,256,32]{1,2,0:T(8,128)S(1)}, f32[4,256,32]{1,2,0:T(8,128)}, u32[]{:S(2)}) copy-start(f32[4,256,32]{1,2,0:T(8,128)} %copy-done.3) | copy-start | bytes 393220
  97.5 12.9 %all-to-all-start.3 = ((f32[4,256,64]{1,2,0:T(8,128)}), f32[4,256,64]{1,2,0:T(8,128)S(1)}, u32[]{:S(2)}, u32[]{:S(2)}) async-start(f32[4,256,64]{1,2,0:T(8,128)} %broadcast_in_dim.120), calls=%async_computation.3 | async-start | bytes 524288 | tf_op jit(solution)/shard_map/all_to_all | solution.py:82
  110.6 4.7 %copy-start.6 = (f32[1,256,64]{1,2,0:T(8,128)S(1)}, f32[1,256,64]{1,2,0:T(8,128)}, u32[]{:S(2)}) copy-start(f32[1,256,64]{1,2,0:T(8,128)} %copy-done.5) | copy-start | bytes 196612
  110.6 4.7 %copy-start.8 = (f32[1,256,64]{1,2,0:T(8,128)S(1)}, f32[1,256,64]{1,2,0:T(8,128)}, u32[]{:S(2)}) copy-start(f32[1,256,64]{1,2,0:T(8,128)} %copy-done.7) | copy-start | bytes 196612
  115.3 15.7 %copy-start.2 = (f32[32,16,128]{2,1,0:T(8,128)S(1)}, f32[32,16,128]{2,1,0:T(8,128)}, u32[]{:S(2)}) copy-start(f32[32,16,128]{2,1,0:T(8,128)} %copy-done.1) | copy-start | bytes 786436
  117.2 14.8 %copy-start = (f32[32,2048]{1,0:T(8,128)}, f32[32,2048]{1,0:T(8,128)S(1)}, u32[]{:S(2)}) copy-start(f32[32,2048]{1,0:T(8,128)S(1)} %reshape.191) | copy-start | bytes 786436
  117.3 12.5 %collective-permute-start.4 = (f32[32,1]{1,0:T(8,128)S(1)}, f32[32,1]{1,0:T(8,128)S(1)}, u32[]{:S(2)}, u32[]{:S(2)}) collective-permute-start(f32[32,1]{1,0:T(8,128)S(1)} %get-tuple-element.11), channel_id=1, source_target_pairs={{0,1},{1,2},{2,3},{4,5},{5,6},{6,7},{8,9},{9,10},{10,11},{12,13},{... | collective-permute-start | bytes 392 | tf_op jit(solution)/shard_map/ppermute | solution.py:16
  119.6 10.2 %collective-permute-start.5 = (f32[32,1]{1,0:T(8,128)S(1)}, f32[32,1]{1,0:T(8,128)S(1)}, u32[]{:S(2)}, u32[]{:S(2)}) collective-permute-start(f32[32,1]{1,0:T(8,128)S(1)} %get-tuple-element.10), channel_id=1, source_target_pairs={{1,0},{2,1},{3,2},{5,4},{6,5},{7,6},{9,8},{10,9},{11,10},{13,12},{... | collective-permute-start | bytes 392 | tf_op jit(solution)/shard_map/ppermute | solution.py:17
  123.2 6.6 %collective-permute-start.2 = (f32[1,2048]{1,0:T(1,128)S(1)}, f32[1,2048]{1,0:T(1,128)S(1)}, u32[]{:S(2)}, u32[]{:S(2)}) collective-permute-start(f32[1,2048]{1,0:T(1,128)S(1)} %get-tuple-element.15), channel_id=1, source_target_pairs={{0,4},{4,8},{8,12},{12,16},{16,20},{20,24},{24,28},{1,5},{5,9},{9,... | collective-permute-start | bytes 24584 | tf_op jit(solution)/shard_map/ppermute | solution.py:16
  125.1 5.9 %collective-permute-start.3 = (f32[1,2048]{1,0:T(1,128)S(1)}, f32[1,2048]{1,0:T(1,128)S(1)}, u32[]{:S(2)}, u32[]{:S(2)}) collective-permute-start(f32[1,2048]{1,0:T(1,128)S(1)} %get-tuple-element.14), channel_id=1, source_target_pairs={{4,0},{8,4},{12,8},{16,12},{20,16},{24,20},{28,24},{5,1},{9,5},{13... | collective-permute-start | bytes 24584 | tf_op jit(solution)/shard_map/ppermute | solution.py:17
